TPU v7x, 768 devices: a whole 4x8x12 slice. The times are simulated.
768 devices in a mesh: seq: 64 (over x, y, core), head: 12 (over z).
Axes of the slice: x: 4, y: 8, z: 12, core: 2. Of those that a mesh axis runs over, the one named last changes fastest.
Arguments:
- queries: bfloat16 [24576, 3072], P('seq', 'head'), may hold values from -6 to 6
- key_rows: bfloat16 [24576, 3072], P('seq', 'head'), may hold values from -6 to 6
- value_rows: bfloat16 [24576, 3072], P('seq', 'head'), may hold values from -6 to 6
- out_weight: bfloat16 [4096, 3072], P(None, 'head'), may hold values from -0.109375 to 0.109375
- out_grad: bfloat16 [24576, 4096], P('seq'), may hold values from -16 to 16
Outputs:
- output: bfloat16 [24576, 4096], P(('seq', 'head'))
- query_grad: bfloat16 [24576, 3072], P('seq', 'head')
- key_grad: bfloat16 [24576, 3072], P('seq', 'head')
- value_grad: bfloat16 [24576, 3072], P('seq', 'head')
- weight_grad: float32 [4096, 3072], P('seq', 'head')
All inputs are finite; a program needn't handle non-finite values.
Results may differ from a plain program's by a relative error of at most 0.02.
Values may be sent and summed in bfloat16 or wider, within the bound.
No kernel may reach another device: no remote copies, remote signals or barrier semaphores. Data moves between devices by JAX's collectives and lax.ppermute only.
A program may use at most 64 MiB of HBM per device.

v0:
```python
import jax
import jax.numpy as jnp
from jax import lax
from jax.sharding import PartitionSpec as P

HD = 128
CH = 64


def swapped(block, axis, distance):
    count = lax.axis_size(axis)
    route = []
    for low in range(count):
        high = low | 1 << distance
        if high != low and high < count:
            route += [(low, high), (high, low)]
    return lax.ppermute(block, axis, route)


def split_state(state):
    upper = state.astype(jnp.bfloat16)
    lower = (state - upper.astype(jnp.float32)).astype(jnp.bfloat16)
    return (upper, lower)


def state_product(form, operand, parts):
    first = jnp.einsum(form, operand, parts[0], preferred_element_type=jnp.float32)
    return first + jnp.einsum(form, operand, parts[1], preferred_element_type=jnp.float32)


def local(queries, key_rows, value_rows, out_weight, out_grad):
    local_rows = queries.shape[0]
    head_count = queries.shape[1] // HD
    blocks = local_rows // CH
    total_rows = local_rows * lax.axis_size("seq")
    factor = (HD * total_rows) ** (-0.5)
    block_shape = (blocks, CH, head_count, HD)
    flat_shape = (local_rows, head_count * HD)
    query_blocks = queries.reshape(block_shape)
    key_blocks = key_rows.reshape(block_shape)
    value_blocks = value_rows.reshape(block_shape)
    causal = (jnp.arange(CH)[:, None] >= jnp.arange(CH)[None, :])[None, None]
    grad_rows = jnp.dot(out_grad, out_weight, preferred_element_type=jnp.float32).astype(
        jnp.bfloat16
    )
    grad_blocks = grad_rows.reshape(block_shape)
    key_value = jnp.einsum(
        "cshd,cshe->chde", key_blocks, value_blocks, preferred_element_type=jnp.float32
    )
    query_pairs = jnp.einsum(
        "cthd,cthe->chde", query_blocks, grad_blocks, preferred_element_type=jnp.float32
    )
    own_state = jnp.sum(key_value, 0)
    own_pairs = jnp.sum(query_pairs, 0)
    empty_state = jnp.zeros_like(own_state)
    position = lax.axis_index("seq")
    level_count = lax.axis_size("seq").bit_length() - 1
    inflow = empty_state
    outflow = empty_state
    state_total = own_state
    pairs_total = own_pairs
    for level in range(level_count):
        other_state, other_pairs = (
            swapped(state_total.astype(jnp.bfloat16), "seq", level).astype(state_total.dtype),
            swapped(pairs_total.astype(jnp.bfloat16), "seq", level).astype(pairs_total.dtype),
        )
        upper_half = position >> level & 1 == 1
        inflow = inflow + jnp.where(upper_half, other_state, 0.0)
        outflow = outflow + jnp.where(upper_half, 0.0, other_pairs)
        state_total = state_total + other_state
        pairs_total = pairs_total + other_pairs
    before = inflow[None] + jnp.cumsum(key_value, 0) - key_value
    later_state = outflow[None] + own_pairs[None] - jnp.cumsum(query_pairs, 0)
    before_parts = split_state(before)
    later_parts = split_state(later_state)
    scores = jnp.einsum(
        "cthd,cshd->chts", query_blocks, key_blocks, preferred_element_type=jnp.float32
    )
    weights = jnp.where(causal, factor * scores, 0.0).astype(jnp.bfloat16)
    within = jnp.einsum(
        "chts,cshe->cthe", weights, value_blocks, preferred_element_type=jnp.float32
    )
    carried = factor * state_product("cthd,chde->cthe", query_blocks, before_parts)
    attention = (within + carried).astype(jnp.bfloat16).reshape(flat_shape)
    output = lax.psum_scatter(
        lax.dot_general(
            attention, out_weight, (((1,), (1,)), ((), ())), preferred_element_type=jnp.float32
        ).astype(jnp.bfloat16),
        "head",
        scatter_dimension=0,
        tiled=True,
    )
    grad_scores = jnp.einsum(
        "cthe,cshe->chts", grad_blocks, value_blocks, preferred_element_type=jnp.float32
    )
    grad_weights = jnp.where(causal, factor * grad_scores, 0.0).astype(jnp.bfloat16)
    query_grad = jnp.einsum(
        "chts,cshd->cthd", grad_weights, key_blocks, preferred_element_type=jnp.float32
    )
    query_grad = query_grad + factor * state_product("cthe,chde->cthd", grad_blocks, before_parts)
    key_grad = jnp.einsum(
        "chts,cthd->cshd", grad_weights, query_blocks, preferred_element_type=jnp.float32
    )
    key_grad = key_grad + factor * state_product("cshe,chde->cshd", value_blocks, later_parts)
    value_grad = jnp.einsum(
        "chts,cthe->cshe", weights, grad_blocks, preferred_element_type=jnp.float32
    )
    value_grad = value_grad + factor * state_product("cshd,chde->cshe", key_blocks, later_parts)
    weight_grad = lax.psum_scatter(
        lax.dot_general(
            out_grad, attention, (((0,), (0,)), ((), ())), preferred_element_type=jnp.float32
        ),
        "seq",
        scatter_dimension=0,
        tiled=True,
    ) * total_rows ** (-0.5)
    return (
        output,
        query_grad.astype(jnp.bfloat16).reshape(flat_shape),
        key_grad.astype(jnp.bfloat16).reshape(flat_shape),
        value_grad.astype(jnp.bfloat16).reshape(flat_shape),
        weight_grad,
    )


def solution(mesh):
    return jax.shard_map(
        local,
        mesh=mesh,
        in_specs=(
            P("seq", "head"),
            P("seq", "head"),
            P("seq", "head"),
            P(None, "head"),
            P("seq", None),
        ),
        out_specs=(
            P(("seq", "head"), None),
            P("seq", "head"),
            P("seq", "head"),
            P("seq", "head"),
            P("seq", "head"),
        ),
        check_vma=False,
    )
```

profile of v0, /device:TPU:6, one launch (start us, length us, event | category | flops | bytes accessed | tf_op | source)
XLA Modules:
  0.0 326.4 jit_solution(16353234806278116308)
XLA Ops:
  7.2 1.1 reshape.49
  8.4 0.8 copy-done
  9.2 3.3 %convolution_convert_fusion.1 = bf16[384,256]{1,0:T(8,128)(2,1)} fusion(bf16[384,4096]{1,0:T(8,128)(2,1)S(1)} %copy-done, bf16[4096,256]{1,0:T(8,128)(2,1)} %param.8), kind=kOutput, calls=%fused_computation.32 | convolution fusion | flops 805404672 | bytes 5439488 | tf_op jit(solution)/shard_map/dot_general | solution.py:43
  12.5 1.0 reshape.53
  13.5 1.9 fusion.74
  15.4 1.0 copy.120
  16.4 0.7 convert_element_type.138
  17.1 1.9 collective-permute-start.6
  19.0 1.0 reshape.50
  20.0 1.0 reshape.51
  21.3 2.4 collective-permute-start
  23.8 1.0 fusion.75
  24.8 0.9 fusion.64
  25.6 3.5 %collective-permute-start.7 = (bf16[2,128,128]{2,1,0:T(8,128)(2,1)S(1)}, bf16[2,128,128]{2,1,0:T(8,128)(2,1)S(1)}, u32[]{:S(2)}, u32[]{:S(2)}) collective-permute-start(bf16[2,128,128]{2,1,0:T(8,128)(2,1)S(1)} %fusion.64), channel_id=1, source_target_pairs={{0,24},{24,0},{12,36},{36,12},{48,72},{72,48},{60,84},{84,60},{96,... | collective-permute-start | bytes 196616 | tf_op jit(solution)/shard_map/ppermute | solution.py:17
  29.2 2.3 collective-permute-start.1
  31.8 0.9 fusion.70
  32.7 4.5 %collective-permute-start.8 = (bf16[2,128,128]{2,1,0:T(8,128)(2,1)S(1)}, bf16[2,128,128]{2,1,0:T(8,128)(2,1)S(1)}, u32[]{:S(2)}, u32[]{:S(2)}) collective-permute-start(bf16[2,128,128]{2,1,0:T(8,128)(2,1)S(1)} %get-tuple-element.25), channel_id=1, source_target_pairs={{0,48},{48,0},{12,60},{60,12},{24,72},{72,24},{36,84},{84,36},{96,... | collective-permute-start | bytes 196616 | tf_op jit(solution)/shard_map/ppermute | solution.py:17
  37.3 2.6 collective-permute-start.2
  40.0 9.5 %collective-permute-start.9 = (bf16[2,128,128]{2,1,0:T(8,128)(2,1)S(1)}, bf16[2,128,128]{2,1,0:T(8,128)(2,1)S(1)}, u32[]{:S(2)}, u32[]{:S(2)}) collective-permute-start(bf16[2,128,128]{2,1,0:T(8,128)(2,1)S(1)} %fusion.65), channel_id=1, source_target_pairs={{0,96},{96,0},{12,108},{108,12},{24,120},{120,24},{36,132},{132,36... | collective-permute-start | bytes 196616 | tf_op jit(solution)/shard_map/ppermute | solution.py:17
  49.5 1.9 collective-permute-start.3
  51.8 2.7 collective-permute-start.10
  54.5 5.0 %collective-permute-done.3 = bf16[2,128,128]{2,1,0:T(8,128)(2,1)S(1)} collective-permute-done((bf16[2,128,128]{2,1,0:T(8,128)(2,1)S(1)}, bf16[2,128,128]{2,1,0:T(8,128)(2,1)S(1)}, u32[]{:S(2)}, u32[]{:S(2)}) %collective-permute-start.3) | collective-permute-done | bytes 65568 | tf_op jit(solution)/shard_map/ppermute | solution.py:17
  59.6 2.7 collective-permute-start.4
  62.3 0.7 fusion.36
  63.0 8.6 %collective-permute-start.11 = (bf16[2,128,128]{2,1,0:T(8,128)(2,1)}, bf16[2,128,128]{2,1,0:T(8,128)(2,1)}, u32[]{:S(2)}, u32[]{:S(2)}) collective-permute-start(bf16[2,128,128]{2,1,0:T(8,128)(2,1)} %fusion.36), channel_id=1, source_target_pairs={{0,384},{384,0},{12,396},{396,12},{24,408},{408,24},{36,420},{420,... | collective-permute-start | bytes 196616 | tf_op jit(solution)/shard_map/ppermute | solution.py:17
  71.6 0.7 fusion.29
  72.3 2.9 collective-permute-start.5
  75.3 0.9 fusion.13
  76.3 4.0 %collective-permute-done.5 = bf16[2,128,128]{2,1,0:T(8,128)(2,1)} collective-permute-done((bf16[2,128,128]{2,1,0:T(8,128)(2,1)}, bf16[2,128,128]{2,1,0:T(8,128)(2,1)}, u32[]{:S(2)}, u32[]{:S(2)}) %collective-permute-start.5) | collective-permute-done | bytes 65568 | tf_op jit(solution)/shard_map/ppermute | solution.py:17
  80.3 2.0 fusion.28
  82.3 1.6 subtract_convert_fusion.1
  85.1 0.7 copy-done.14
  85.7 3.3 %convolution_bitcast_fusion = f32[4096,256]{0,1:T(8,128)} fusion(bf16[384,4096]{1,0:T(8,128)(2,1)S(1)} %copy-done, bf16[48,8,2,128]{3,2,1,0:T(2,128)(2,1)S(1)} %bitcast.67), kind=kOutput, calls=%fused_computation.1 | convolution fusion | flops 805306368 | bytes 7536640 | tf_op jit(solution)/shard_map/dot_general | solution.py:110
  89.0 5.6 %copy.143 = f32[4096,256]{1,0:T(8,128)} copy(f32[4096,256]{0,1:T(8,128)} %convolution_bitcast_fusion) | data formatting | bytes 8388608
  94.7 4.4 %convolution_convert_fusion = bf16[384,4096]{1,0:T(8,128)(2,1)} fusion(bf16[4096,256]{1,0:T(8,128)(2,1)} %param.8, bf16[48,8,2,128]{3,2,1,0:T(2,128)(2,1)} %bitcast.68), kind=kOutput, calls=%fused_computation | convolution fusion | flops 806879232 | bytes 5439488 | tf_op jit(solution)/shard_map/dot_general | solution.py:86
  99.1 1.8 fusion.12
  101.0 1.6 copy.123
  102.6 1.3 reduce-window_subtract_fusion
  104.3 0.4 fusion.5
  105.1 0.7 copy.208
  106.8 0.7 copy.209
  107.5 0.4 fusion.40
  107.9 0.4 fusion.4
  108.7 0.7 copy.210
  109.4 141.6 %reduce-scatter.7.cloned.1.call-done = f32[64,256]{1,0:T(8,128)} async-done(((f32[4096,256]{1,0:T(8,128)}), f32[64,256]{1,0:T(8,128)}) %reduce-scatter.7.cloned.1.call-update) | async-done | bytes 65552
  251.0 0.9 copy.144
  251.9 0.7 copy.136
  252.7 66.9 %reduce-scatter.5.cloned.1.call-done = bf16[32,4096]{1,0:T(8,128)(2,1)} async-done(((bf16[384,4096]{1,0:T(8,128)(2,1)}), bf16[32,4096]{1,0:T(8,128)(2,1)}) %reduce-scatter.5.cloned.1.call-update) | async-done | bytes 262160 | tf_op jit(solution)/shard_map/reduce_scatter | solution.py:85
  (89 shorter events, 4.6 us)
Async XLA Ops:
  7.2 2.0 copy-start
  7.2 243.8 %reduce-scatter.7.cloned.1.call-start = ((), (), s32[]{:S(2)}) async-start(), calls=%async_computation.3 | async-start | bytes 4259840
  9.2 4.3 %copy-start.4 = (bf16[6,64,2,128]{3,2,1,0:T(2,128)(2,1)}, bf16[6,64,2,128]{3,2,1,0:T(2,128)(2,1)S(1)}, u32[]{:S(2)}) copy-start(bf16[6,64,2,128]{3,2,1,0:T(2,128)(2,1)S(1)} %reshape.49) | copy-start | bytes 589828
  13.5 3.6 %copy-start.2 = (bf16[6,64,2,128]{3,2,1,0:T(2,128)(2,1)}, bf16[6,64,2,128]{3,2,1,0:T(2,128)(2,1)S(1)}, u32[]{:S(2)}) copy-start(bf16[6,64,2,128]{3,2,1,0:T(2,128)(2,1)S(1)} %reshape.53) | copy-start | bytes 589828
  16.4 2.6 copy-start.12
  17.1 7.7 %collective-permute-start.6 = (bf16[2,128,128]{2,1,0:T(8,128)(2,1)}, bf16[2,128,128]{2,1,0:T(8,128)(2,1)}, u32[]{:S(2)}, u32[]{:S(2)}) collective-permute-start(bf16[2,128,128]{2,1,0:T(8,128)(2,1)} %convert_element_type.138), channel_id=1, source_target_pairs={{0,12},{12,0},{24,36},{36,24},{48,60},{60,48},{72,84},{84,72},{96,... | collective-permute-start | bytes 196616 | tf_op jit(solution)/shard_map/ppermute | solution.py:17
  21.0 3.8 %copy-start.13 = (f32[2,128,128]{2,1,0:T(8,128)S(1)}, f32[2,128,128]{2,1,0:T(8,128)}, u32[]{:S(2)}) copy-start(f32[2,128,128]{2,1,0:T(8,128)} %copy-done.12) | copy-start | bytes 393220
  21.0 54.3 %copy-start.5 = (bf16[6,64,2,128]{3,2,1,0:T(2,128)(2,1)S(1)}, bf16[6,64,2,128]{3,2,1,0:T(2,128)(2,1)}, u32[]{:S(2)}) copy-start(bf16[6,64,2,128]{3,2,1,0:T(2,128)(2,1)} %copy-done.4) | copy-start | bytes 589828
  21.3 2.4 copy-start.1
  21.3 7.8 %collective-permute-start = (bf16[2,128,128]{2,1,0:T(8,128)(2,1)S(1)}, bf16[2,128,128]{2,1,0:T(8,128)(2,1)S(1)}, u32[]{:S(2)}, u32[]{:S(2)}) collective-permute-start(bf16[2,128,128]{2,1,0:T(8,128)(2,1)S(1)} %convert_element_type.118), channel_id=1, source_target_pairs={{0,12},{12,0},{24,36},{36,24},{48,60},{60,48},{72,84},{84,72},{96,... | collective-permute-start | bytes 196616 | tf_op jit(solution)/shard_map/ppermute | solution.py:17
  25.6 6.2 %collective-permute-start.7 = (bf16[2,128,128]{2,1,0:T(8,128)(2,1)S(1)}, bf16[2,128,128]{2,1,0:T(8,128)(2,1)S(1)}, u32[]{:S(2)}, u32[]{:S(2)}) collective-permute-start(bf16[2,128,128]{2,1,0:T(8,128)(2,1)S(1)} %fusion.64), channel_id=1, source_target_pairs={{0,24},{24,0},{12,36},{36,12},{48,72},{72,48},{60,84},{84,60},{96,... | collective-permute-start | bytes 196616 | tf_op jit(solution)/shard_map/ppermute | solution.py:17
  29.2 47.0 %copy-start.20 = (bf16[2,128,128]{2,1,0:T(8,128)(2,1)}, bf16[2,128,128]{2,1,0:T(8,128)(2,1)S(1)}, u32[]{:S(2)}) copy-start(bf16[2,128,128]{2,1,0:T(8,128)(2,1)S(1)} %collective-permute-done) | copy-start | bytes 196612
  29.2 8.0 %collective-permute-start.1 = (bf16[2,128,128]{2,1,0:T(8,128)(2,1)S(1)}, bf16[2,128,128]{2,1,0:T(8,128)(2,1)S(1)}, u32[]{:S(2)}, u32[]{:S(2)}) collective-permute-start(bf16[2,128,128]{2,1,0:T(8,128)(2,1)S(1)} %fusion.62), channel_id=1, source_target_pairs={{0,24},{24,0},{12,36},{36,12},{48,72},{72,48},{60,84},{84,60},{96,... | collective-permute-start | bytes 196616 | tf_op jit(solution)/shard_map/ppermute | solution.py:17
  31.8 0.9 copy-start.23
  32.7 7.2 %collective-permute-start.8 = (bf16[2,128,128]{2,1,0:T(8,128)(2,1)S(1)}, bf16[2,128,128]{2,1,0:T(8,128)(2,1)S(1)}, u32[]{:S(2)}, u32[]{:S(2)}) collective-permute-start(bf16[2,128,128]{2,1,0:T(8,128)(2,1)S(1)} %get-tuple-element.25), channel_id=1, source_target_pairs={{0,48},{48,0},{12,60},{60,12},{24,72},{72,24},{36,84},{84,36},{96,... | collective-permute-start | bytes 196616 | tf_op jit(solution)/shard_map/ppermute | solution.py:17
  37.2 2.7 copy-start.24
  37.3 12.1 %collective-permute-start.2 = (bf16[2,128,128]{2,1,0:T(8,128)(2,1)S(1)}, bf16[2,128,128]{2,1,0:T(8,128)(2,1)S(1)}, u32[]{:S(2)}, u32[]{:S(2)}) collective-permute-start(bf16[2,128,128]{2,1,0:T(8,128)(2,1)S(1)} %get-tuple-element.29), channel_id=1, source_target_pairs={{0,48},{48,0},{12,60},{60,12},{24,72},{72,24},{36,84},{84,36},{96,... | collective-permute-start | bytes 196616 | tf_op jit(solution)/shard_map/ppermute | solution.py:17
  39.9 36.3 %copy-start.15 = (bf16[2,128,128]{2,1,0:T(8,128)(2,1)}, bf16[2,128,128]{2,1,0:T(8,128)(2,1)S(1)}, u32[]{:S(2)}) copy-start(bf16[2,128,128]{2,1,0:T(8,128)(2,1)S(1)} %collective-permute-done.8) | copy-start | bytes 196612
  40.0 11.8 %collective-permute-start.9 = (bf16[2,128,128]{2,1,0:T(8,128)(2,1)S(1)}, bf16[2,128,128]{2,1,0:T(8,128)(2,1)S(1)}, u32[]{:S(2)}, u32[]{:S(2)}) collective-permute-start(bf16[2,128,128]{2,1,0:T(8,128)(2,1)S(1)} %fusion.65), channel_id=1, source_target_pairs={{0,96},{96,0},{12,108},{108,12},{24,120},{120,24},{36,132},{132,36... | collective-permute-start | bytes 196616 | tf_op jit(solution)/shard_map/ppermute | solution.py:17
  49.4 22.9 %copy-start.16 = (bf16[2,128,128]{2,1,0:T(8,128)(2,1)}, bf16[2,128,128]{2,1,0:T(8,128)(2,1)S(1)}, u32[]{:S(2)}) copy-start(bf16[2,128,128]{2,1,0:T(8,128)(2,1)S(1)} %collective-permute-done.2) | copy-start | bytes 196612
  49.5 10.1 %collective-permute-start.3 = (bf16[2,128,128]{2,1,0:T(8,128)(2,1)S(1)}, bf16[2,128,128]{2,1,0:T(8,128)(2,1)S(1)}, u32[]{:S(2)}, u32[]{:S(2)}) collective-permute-start(bf16[2,128,128]{2,1,0:T(8,128)(2,1)S(1)} %fusion.63), channel_id=1, source_target_pairs={{0,96},{96,0},{12,108},{108,12},{24,120},{120,24},{36,132},{132,36... | collective-permute-start | bytes 196616 | tf_op jit(solution)/shard_map/ppermute | solution.py:17
  51.7 24.4 %copy-start.21 = (bf16[2,128,128]{2,1,0:T(8,128)(2,1)}, bf16[2,128,128]{2,1,0:T(8,128)(2,1)S(1)}, u32[]{:S(2)}) copy-start(bf16[2,128,128]{2,1,0:T(8,128)(2,1)S(1)} %collective-permute-done.9) | copy-start | bytes 196612
  51.8 10.5 %collective-permute-start.10 = (bf16[2,128,128]{2,1,0:T(8,128)(2,1)S(1)}, bf16[2,128,128]{2,1,0:T(8,128)(2,1)S(1)}, u32[]{:S(2)}, u32[]{:S(2)}) collective-permute-start(bf16[2,128,128]{2,1,0:T(8,128)(2,1)S(1)} %fusion.67), channel_id=1, source_target_pairs={{0,192},{192,0},{12,204},{204,12},{24,216},{216,24},{36,228},{228,... | collective-permute-start | bytes 196616 | tf_op jit(solution)/shard_map/ppermute | solution.py:17
  59.5 16.6 %copy-start.22 = (bf16[2,128,128]{2,1,0:T(8,128)(2,1)}, bf16[2,128,128]{2,1,0:T(8,128)(2,1)S(1)}, u32[]{:S(2)}) copy-start(bf16[2,128,128]{2,1,0:T(8,128)(2,1)S(1)} %collective-permute-done.3) | copy-start | bytes 196612
  59.6 12.0 %collective-permute-start.4 = (bf16[2,128,128]{2,1,0:T(8,128)(2,1)S(1)}, bf16[2,128,128]{2,1,0:T(8,128)(2,1)S(1)}, u32[]{:S(2)}, u32[]{:S(2)}) collective-permute-start(bf16[2,128,128]{2,1,0:T(8,128)(2,1)S(1)} %fusion.66), channel_id=1, source_target_pairs={{0,192},{192,0},{12,204},{204,12},{24,216},{216,24},{36,228},{228,... | collective-permute-start | bytes 196616 | tf_op jit(solution)/shard_map/ppermute | solution.py:17
  62.3 13.9 %copy-start.25 = (bf16[2,128,128]{2,1,0:T(8,128)(2,1)}, bf16[2,128,128]{2,1,0:T(8,128)(2,1)S(1)}, u32[]{:S(2)}) copy-start(bf16[2,128,128]{2,1,0:T(8,128)(2,1)S(1)} %collective-permute-done.10) | copy-start | bytes 196612
  63.0 13.2 %collective-permute-start.11 = (bf16[2,128,128]{2,1,0:T(8,128)(2,1)}, bf16[2,128,128]{2,1,0:T(8,128)(2,1)}, u32[]{:S(2)}, u32[]{:S(2)}) collective-permute-start(bf16[2,128,128]{2,1,0:T(8,128)(2,1)} %fusion.36), channel_id=1, source_target_pairs={{0,384},{384,0},{12,396},{396,12},{24,408},{408,24},{36,420},{420,... | collective-permute-start | bytes 196616 | tf_op jit(solution)/shard_map/ppermute | solution.py:17
  71.6 4.6 %copy-start.26 = (bf16[2,128,128]{2,1,0:T(8,128)(2,1)}, bf16[2,128,128]{2,1,0:T(8,128)(2,1)S(1)}, u32[]{:S(2)}) copy-start(bf16[2,128,128]{2,1,0:T(8,128)(2,1)S(1)} %collective-permute-done.4) | copy-start | bytes 196612
  72.3 8.0 %collective-permute-start.5 = (bf16[2,128,128]{2,1,0:T(8,128)(2,1)}, bf16[2,128,128]{2,1,0:T(8,128)(2,1)}, u32[]{:S(2)}, u32[]{:S(2)}) collective-permute-start(bf16[2,128,128]{2,1,0:T(8,128)(2,1)} %fusion.29), channel_id=1, source_target_pairs={{0,384},{384,0},{12,396},{396,12},{24,408},{408,24},{36,420},{420,... | collective-permute-start | bytes 196616 | tf_op jit(solution)/shard_map/ppermute | solution.py:17
  76.2 7.7 %copy-start.6 = (bf16[6,64,2,128]{3,2,1,0:T(2,128)(2,1)S(1)}, bf16[6,64,2,128]{3,2,1,0:T(2,128)(2,1)}, u32[]{:S(2)}) copy-start(bf16[6,64,2,128]{3,2,1,0:T(2,128)(2,1)} %copy-done.4) | copy-start | bytes 589828
  76.2 8.4 %copy-start.17 = (bf16[6,2,64,64]{3,2,1,0:T(8,128)(2,1)S(1)}, bf16[6,2,64,64]{3,2,1,0:T(8,128)(2,1)}, u32[]{:S(2)}) copy-start(bf16[6,2,64,64]{3,2,1,0:T(8,128)(2,1)} %fusion.13) | copy-start | bytes 294916
  83.9 0.8 copy-start.8
  83.9 1.0 copy-start.10
  85.0 0.7 copy-start.14
  94.7 225.0 %reduce-scatter.5.cloned.1.call-start = ((), (), s32[]{:S(2)}) async-start(), calls=%async_computation.2 | async-start | bytes 3407872 | tf_op jit(solution)/shard_map/reduce_scatter | solution.py:85
  102.6 2.0 copy-start.3
  102.6 2.0 copy-start.18
  104.2 2.1 copy-start.7
  104.2 2.1 copy-start.19
  104.7 2.9 copy-start.11
  105.1 2.8 copy-start.9
Sparse Core Ops, SparseCore 0:
  94.8 156.1 reduce-scatter.6
  255.0 64.5 reduce-scatter.4
where the time goes:
time: 328 us; the launch traced here: 326 us
  waiting for transfers between devices  218 us (66%)
  starting transfers between devices  45.7 us (14%)
  matrix products  19.3 us (6%)
  local copies, waits for them, and re-layouts  18.7 us (6%)
  between operations  14.7 us (4%)
  other arithmetic  9.71 us (3%)
    unnamed x3, waiting for transfers between devices  142 us
    reduce_scatter x1, waiting for transfers between devices, local(): lax.psum_scatter(lax.dot_general(attention, out_weight, (((1,), (1,)), ((...  66.9 us
    ppermute x12, starting transfers between devices, swapped(): return lax.ppermute(block, axis, route)  45.7 us
    unnamed x60, local copies, waits for them, and re-layouts  11.2 us
    ppermute x12, waiting for transfers between devices, swapped(): return lax.ppermute(block, axis, route)  9.66 us
  transfers between devices with their start and end apart: 14, of which 6 were waited for; matrix products, arithmetic and copies ran while one was open for 7% of the time, Pallas kernels for 0%

commit v1 on v0

--- a/solution.py
+++ b/solution.py
@@ -1,20 +1,21 @@
 import jax
 import jax.numpy as jnp
 from jax import lax
+from jax.sharding import Mesh
 from jax.sharding import PartitionSpec as P
 
 HD = 128
 CH = 64
+SEQ = ("xy", "c")
 
 
-def swapped(block, axis, distance):
-    count = lax.axis_size(axis)
+def swapped(block, count, distance):
     route = []
     for low in range(count):
         high = low | 1 << distance
         if high != low and high < count:
             route += [(low, high), (high, low)]
-    return lax.ppermute(block, axis, route)
+    return lax.ppermute(block, SEQ, route)
 
 
 def split_state(state):
@@ -28,11 +29,34 @@
     return first + jnp.einsum(form, operand, parts[1], preferred_element_type=jnp.float32)
 
 
-def local(queries, key_rows, value_rows, out_weight, out_grad):
+def ring_scatter(partial, count):
+    position = lax.axis_index("head")
+    rows = partial.shape[0] // count
+    half = partial.shape[1] // 2
+    chunks = partial.reshape(count, rows, partial.shape[1])
+    up_own = chunks[:, :, :half]
+    down_own = chunks[:, :, half:]
+    up_route = [(i, (i + 1) % count) for i in range(count)]
+    down_route = [(i, (i - 1) % count) for i in range(count)]
+
+    def pick(own, index):
+        return lax.dynamic_index_in_dim(own, index % count, 0, keepdims=False).astype(jnp.float32)
+
+    up_acc = pick(up_own, position - 1)
+    down_acc = pick(down_own, position + 1)
+    for step in range(count - 1):
+        up_in = lax.ppermute(up_acc.astype(jnp.bfloat16), "head", up_route)
+        down_in = lax.ppermute(down_acc.astype(jnp.bfloat16), "head", down_route)
+        up_acc = up_in.astype(jnp.float32) + pick(up_own, position - 2 - step)
+        down_acc = down_in.astype(jnp.float32) + pick(down_own, position + 2 + step)
+    return jnp.concatenate([up_acc, down_acc], 1).astype(jnp.bfloat16)
+
+
+def local(queries, key_rows, value_rows, out_weight, out_grad, seq_count, head_count_axis):
     local_rows = queries.shape[0]
     head_count = queries.shape[1] // HD
     blocks = local_rows // CH
-    total_rows = local_rows * lax.axis_size("seq")
+    total_rows = local_rows * seq_count
     factor = (HD * total_rows) ** (-0.5)
     block_shape = (blocks, CH, head_count, HD)
     flat_shape = (local_rows, head_count * HD)
@@ -52,23 +76,17 @@
     )
     own_state = jnp.sum(key_value, 0)
     own_pairs = jnp.sum(query_pairs, 0)
-    empty_state = jnp.zeros_like(own_state)
-    position = lax.axis_index("seq")
-    level_count = lax.axis_size("seq").bit_length() - 1
-    inflow = empty_state
-    outflow = empty_state
-    state_total = own_state
-    pairs_total = own_pairs
+    position = lax.axis_index(SEQ)
+    level_count = seq_count.bit_length() - 1
+    inflow = jnp.zeros_like(own_state)
+    outflow = jnp.zeros_like(own_state)
+    totals = jnp.stack([own_state, own_pairs])
     for level in range(level_count):
-        other_state, other_pairs = (
-            swapped(state_total.astype(jnp.bfloat16), "seq", level).astype(state_total.dtype),
-            swapped(pairs_total.astype(jnp.bfloat16), "seq", level).astype(pairs_total.dtype),
-        )
+        other = swapped(totals.astype(jnp.bfloat16), seq_count, level).astype(jnp.float32)
         upper_half = position >> level & 1 == 1
-        inflow = inflow + jnp.where(upper_half, other_state, 0.0)
-        outflow = outflow + jnp.where(upper_half, 0.0, other_pairs)
-        state_total = state_total + other_state
-        pairs_total = pairs_total + other_pairs
+        inflow = inflow + jnp.where(upper_half, other[0], 0.0)
+        outflow = outflow + jnp.where(upper_half, 0.0, other[1])
+        totals = totals + other
     before = inflow[None] + jnp.cumsum(key_value, 0) - key_value
     later_state = outflow[None] + own_pairs[None] - jnp.cumsum(query_pairs, 0)
     before_parts = split_state(before)
@@ -82,14 +100,9 @@
     )
     carried = factor * state_product("cthd,chde->cthe", query_blocks, before_parts)
     attention = (within + carried).astype(jnp.bfloat16).reshape(flat_shape)
-    output = lax.psum_scatter(
-        lax.dot_general(
-            attention, out_weight, (((1,), (1,)), ((), ())), preferred_element_type=jnp.float32
-        ).astype(jnp.bfloat16),
-        "head",
-        scatter_dimension=0,
-        tiled=True,
-    )
+    partial_output = lax.dot_general(
+        attention, out_weight, (((1,), (1,)), ((), ())), preferred_element_type=jnp.float32
+    ).astype(jnp.bfloat16)
     grad_scores = jnp.einsum(
         "cthe,cshe->chts", grad_blocks, value_blocks, preferred_element_type=jnp.float32
     )
@@ -106,11 +119,19 @@
         "chts,cthe->cshe", weights, grad_blocks, preferred_element_type=jnp.float32
     )
     value_grad = value_grad + factor * state_product("cshd,chde->cshe", key_blocks, later_parts)
+    weight_partial = lax.dot_general(
+        out_grad, attention, (((0,), (0,)), ((), ())), preferred_element_type=jnp.float32
+    )
+    core = lax.axis_index("c")
+    halves = weight_partial.reshape(-1, 2, weight_partial.shape[0] // (2 * lax.axis_size("xy")), weight_partial.shape[1])
+    kept = lax.dynamic_index_in_dim(halves, core, 1, keepdims=False)
+    sent = lax.dynamic_index_in_dim(halves, 1 - core, 1, keepdims=False)
+    kept = kept + lax.ppermute(sent, "c", [(0, 1), (1, 0)])
+    kept, partial_output = lax.optimization_barrier((kept, partial_output))
+    output = ring_scatter(partial_output, head_count_axis)
     weight_grad = lax.psum_scatter(
-        lax.dot_general(
-            out_grad, attention, (((0,), (0,)), ((), ())), preferred_element_type=jnp.float32
-        ),
-        "seq",
+        kept.reshape(-1, weight_partial.shape[1]),
+        "xy",
         scatter_dimension=0,
         tiled=True,
     ) * total_rows ** (-0.5)
@@ -124,22 +145,30 @@
 
 
 def solution(mesh):
+    seq_count, head_count_axis = mesh.devices.shape
+    split_mesh = Mesh(
+        mesh.devices.reshape(seq_count // 2, 2, head_count_axis), ("xy", "c", "head")
+    )
+
+    def body(queries, key_rows, value_rows, out_weight, out_grad):
+        return local(queries, key_rows, value_rows, out_weight, out_grad, seq_count, head_count_axis)
+
     return jax.shard_map(
-        local,
-        mesh=mesh,
+        body,
+        mesh=split_mesh,
         in_specs=(
-            P("seq", "head"),
-            P("seq", "head"),
-            P("seq", "head"),
+            P(SEQ, "head"),
+            P(SEQ, "head"),
+            P(SEQ, "head"),
             P(None, "head"),
-            P("seq", None),
+            P(SEQ, None),
         ),
         out_specs=(
-            P(("seq", "head"), None),
-            P("seq", "head"),
-            P("seq", "head"),
-            P("seq", "head"),
-            P("seq", "head"),
+            P(SEQ + ("head",), None),
+            P(SEQ, "head"),
+            P(SEQ, "head"),
+            P(SEQ, "head"),
+            P(SEQ, "head"),
         ),
         check_vma=False,
     )

time: 328 us -> 354 us (1.079)
  starting transfers between devices: 45.7 us -> 116 us
  waiting for transfers between devices: 218 us -> 160 us
  other arithmetic: 9.71 us -> 19.1 us
  local copies, waits for them, and re-layouts: 18.7 us -> 22.9 us
    unnamed x3 -> x1, waiting for transfers between devices: 142 us -> 0.02 us
    ppermute x12 -> x29, starting transfers between devices: 45.7 us -> 116 us  [the longest x11 64.3 us: ring_scatter(): down_in = lax.ppermute(down_acc.astype(jnp.bfloat16), 'head', down_route)]
    reduce_scatter x1, waiting for transfers between devices: 66.9 us -> 128 us  [local(): lax.psum_scatter(kept.reshape(-1, weight_partial.shape[1]), 'xy', scatter...]
    ppermute x12 -> x29, waiting for transfers between devices: 9.66 us -> 32.4 us  [the longest x6 20.3 us: swapped(): return lax.ppermute(block, SEQ, route)]
    convert_element_type x13 -> x32, other arithmetic: 5.46 us -> 13 us  [the longest x6 4.86 us: local(): totals.astype(jnp.bfloat16)]
    unnamed x60 -> x67, local copies, waits for them, and re-layouts: 11.2 us -> 5.16 us
    dot_general x0 -> x1, local copies, waits for them, and re-layouts: none -> 5.62 us  [local(): lax.dot_general(out_grad, attention, (((0,), (0,)), ((), ())), preferred_...]
  transfers between devices with their start and end apart: 14 -> 30, of which waited for: 6 -> 17; matrix products, arithmetic and copies ran while one was open for 7% -> 5% of each run, Pallas kernels for 0% -> 0%
where the time goes in v1:
time: 354 us; the launch traced here: 352 us
  waiting for transfers between devices  160 us (45%)
  starting transfers between devices  116 us (33%)
  local copies, waits for them, and re-layouts  22.9 us (6%)
  other arithmetic  19.1 us (5%)
  matrix products  18.2 us (5%)
  between operations  15.5 us (4%)
    reduce_scatter x1, waiting for transfers between devices, local(): lax.psum_scatter(kept.reshape(-1, weight_partial.shape[1]), 'xy', scatter...  128 us
    ppermute x11, starting transfers between devices, ring_scatter(): down_in = lax.ppermute(down_acc.astype(jnp.bfloat16), 'head', down_route)  64.3 us
    ppermute x6, starting transfers between devices, swapped(): return lax.ppermute(block, SEQ, route)  28.4 us
    ppermute x11, starting transfers between devices, ring_scatter(): up_in = lax.ppermute(up_acc.astype(jnp.bfloat16), 'head', up_route)  21.1 us
    ppermute x6, waiting for transfers between devices, swapped(): return lax.ppermute(block, SEQ, route)  20.3 us
    ppermute x11, waiting for transfers between devices, ring_scatter(): up_in = lax.ppermute(up_acc.astype(jnp.bfloat16), 'head', up_route)  10.1 us
  transfers between devices with their start and end apart: 30, of which 17 were waited for; matrix products, arithmetic and copies ran while one was open for 5% of the time, Pallas kernels for 0%

profile of v1, /device:TPU:6, one launch (start us, length us, event | category | flops | bytes accessed | tf_op | source)
XLA Modules:
  0.0 351.6 jit_solution(12024015293525122602)
XLA Ops:
  7.2 1.8 copy-done
  9.1 2.6 convolution_convert_fusion.1
  12.7 1.9 fusion.97
  14.6 1.7 copy.108
  18.9 2.2 fusion.98
  22.0 1.9 collective-permute-start
  26.2 3.5 collective-permute-start.1
  29.7 3.9 %collective-permute-done.1 = bf16[2,2,128,128]{3,2,1,0:T(8,128)(2,1)S(1)} collective-permute-done((bf16[2,2,128,128]{3,2,1,0:T(8,128)(2,1)S(1)}, bf16[2,2,128,128]{3,2,1,0:T(8,128)(2,1)S(1)}, u32[]{:S(2)}, u32[]{:S(2)}) %collective-permute-start.1) | collective-permute-done | bytes 131104 | tf_op jit(solution)/shard_map/ppermute | solution.py:18
  33.7 4.5 %collective-permute-start.2 = (bf16[2,2,128,128]{3,2,1,0:T(8,128)(2,1)S(1)}, bf16[2,2,128,128]{3,2,1,0:T(8,128)(2,1)S(1)}, u32[]{:S(2)}, u32[]{:S(2)}) collective-permute-start(bf16[2,2,128,128]{3,2,1,0:T(8,128)(2,1)S(1)} %get-tuple-element.9), channel_id=1, source_target_pairs={{0,48},{48,0},{12,60},{60,12},{24,72},{72,24},{36,84},{84,36},{96,... | collective-permute-start | bytes 393224 | tf_op jit(solution)/shard_map/ppermute | solution.py:18
  38.2 5.8 %collective-permute-done.2 = bf16[2,2,128,128]{3,2,1,0:T(8,128)(2,1)S(1)} collective-permute-done((bf16[2,2,128,128]{3,2,1,0:T(8,128)(2,1)S(1)}, bf16[2,2,128,128]{3,2,1,0:T(8,128)(2,1)S(1)}, u32[]{:S(2)}, u32[]{:S(2)}) %collective-permute-start.2) | collective-permute-done | bytes 131104 | tf_op jit(solution)/shard_map/ppermute | solution.py:18
  44.7 7.7 %collective-permute-start.3 = (bf16[2,2,128,128]{3,2,1,0:T(8,128)(2,1)}, bf16[2,2,128,128]{3,2,1,0:T(8,128)(2,1)}, u32[]{:S(2)}, u32[]{:S(2)}) collective-permute-start(bf16[2,2,128,128]{3,2,1,0:T(8,128)(2,1)} %fusion.89), channel_id=1, source_target_pairs={{0,96},{96,0},{12,108},{108,12},{24,120},{120,24},{36,132},{132,36... | collective-permute-start | bytes 393224 | tf_op jit(solution)/shard_map/ppermute | solution.py:18
  53.1 6.0 %collective-permute-done.3 = bf16[2,2,128,128]{3,2,1,0:T(8,128)(2,1)} collective-permute-done((bf16[2,2,128,128]{3,2,1,0:T(8,128)(2,1)}, bf16[2,2,128,128]{3,2,1,0:T(8,128)(2,1)}, u32[]{:S(2)}, u32[]{:S(2)}) %collective-permute-start.3) | collective-permute-done | bytes 131104 | tf_op jit(solution)/shard_map/ppermute | solution.py:18
  60.2 2.7 collective-permute-start.4
  63.0 1.8 fusion.13
  64.8 2.3 collective-permute-done.4
  68.2 8.0 %collective-permute-start.5 = (bf16[2,2,128,128]{3,2,1,0:T(8,128)(2,1)S(1)}, bf16[2,2,128,128]{3,2,1,0:T(8,128)(2,1)S(1)}, u32[]{:S(2)}, u32[]{:S(2)}) collective-permute-start(bf16[2,2,128,128]{3,2,1,0:T(8,128)(2,1)S(1)} %add_convert_fusion), channel_id=1, source_target_pairs={{0,384},{384,0},{12,396},{396,12},{24,408},{408,24},{36,420},{420,... | collective-permute-start | bytes 393224 | tf_op jit(solution)/shard_map/ppermute | solution.py:18
  80.0 1.7 copy.121
  88.2 3.3 convolution_bitcast_fusion
  91.5 5.6 %copy.112 = f32[4096,256]{1,0:T(8,128)} copy(f32[4096,256]{0,1:T(8,128)} %convolution_bitcast_fusion) | data formatting | bytes 8388608 | tf_op jit(solution)/shard_map/dot_general | solution.py:122
  97.1 1.8 dynamic-slice_bitcast_fusion
  99.0 2.1 collective-permute-start.6
  107.2 1.7 bitcast_add_fusion
  109.9 1.9 collective-permute-start.7
  111.9 12.0 %collective-permute-start.18 = (bf16[32,2048]{1,0:T(8,128)(2,1)S(1)}, bf16[32,2048]{1,0:T(8,128)(2,1)S(1)}, u32[]{:S(2)}, u32[]{:S(2)}) collective-permute-start(bf16[32,2048]{1,0:T(8,128)(2,1)S(1)} %dynamic-slice_bitcast_fusion.1), channel_id=1, source_target_pairs={{0,11},{1,0},{2,1},{3,2},{4,3},{5,4},{6,5},{7,6},{8,7},{9,8},{10,9... | collective-permute-start | bytes 393224 | tf_op jit(solution)/shard_map/ppermute | solution.py:49
  123.9 2.3 collective-permute-done.7
  127.2 1.9 collective-permute-start.8
  130.1 5.1 %collective-permute-start.19 = (bf16[32,2048]{1,0:T(8,128)(2,1)S(1)}, bf16[32,2048]{1,0:T(8,128)(2,1)S(1)}, u32[]{:S(2)}, u32[]{:S(2)}) collective-permute-start(bf16[32,2048]{1,0:T(8,128)(2,1)S(1)} %fusion.30), channel_id=1, source_target_pairs={{0,11},{1,0},{2,1},{3,2},{4,3},{5,4},{6,5},{7,6},{8,7},{9,8},{10,9... | collective-permute-start | bytes 393224 | tf_op jit(solution)/shard_map/ppermute | solution.py:49
  136.6 1.9 collective-permute-start.9
  139.5 5.1 %collective-permute-start.20 = (bf16[32,2048]{1,0:T(8,128)(2,1)S(1)}, bf16[32,2048]{1,0:T(8,128)(2,1)S(1)}, u32[]{:S(2)}, u32[]{:S(2)}) collective-permute-start(bf16[32,2048]{1,0:T(8,128)(2,1)S(1)} %fusion.29), channel_id=1, source_target_pairs={{0,11},{1,0},{2,1},{3,2},{4,3},{5,4},{6,5},{7,6},{8,7},{9,8},{10,9... | collective-permute-start | bytes 393224 | tf_op jit(solution)/shard_map/ppermute | solution.py:49
  145.6 1.9 collective-permute-start.10
  148.5 5.1 %collective-permute-start.21 = (bf16[32,2048]{1,0:T(8,128)(2,1)S(1)}, bf16[32,2048]{1,0:T(8,128)(2,1)S(1)}, u32[]{:S(2)}, u32[]{:S(2)}) collective-permute-start(bf16[32,2048]{1,0:T(8,128)(2,1)S(1)} %fusion.28), channel_id=1, source_target_pairs={{0,11},{1,0},{2,1},{3,2},{4,3},{5,4},{6,5},{7,6},{8,7},{9,8},{10,9... | collective-permute-start | bytes 393224 | tf_op jit(solution)/shard_map/ppermute | solution.py:49
  154.6 1.9 collective-permute-start.11
  156.6 5.1 %collective-permute-start.22 = (bf16[32,2048]{1,0:T(8,128)(2,1)S(1)}, bf16[32,2048]{1,0:T(8,128)(2,1)S(1)}, u32[]{:S(2)}, u32[]{:S(2)}) collective-permute-start(bf16[32,2048]{1,0:T(8,128)(2,1)S(1)} %fusion.27), channel_id=1, source_target_pairs={{0,11},{1,0},{2,1},{3,2},{4,3},{5,4},{6,5},{7,6},{8,7},{9,8},{10,9... | collective-permute-start | bytes 393224 | tf_op jit(solution)/shard_map/ppermute | solution.py:49
  162.7 1.9 collective-permute-start.12
  164.7 5.1 %collective-permute-start.23 = (bf16[32,2048]{1,0:T(8,128)(2,1)S(1)}, bf16[32,2048]{1,0:T(8,128)(2,1)S(1)}, u32[]{:S(2)}, u32[]{:S(2)}) collective-permute-start(bf16[32,2048]{1,0:T(8,128)(2,1)S(1)} %fusion.26), channel_id=1, source_target_pairs={{0,11},{1,0},{2,1},{3,2},{4,3},{5,4},{6,5},{7,6},{8,7},{9,8},{10,9... | collective-permute-start | bytes 393224 | tf_op jit(solution)/shard_map/ppermute | solution.py:49
  170.9 1.9 collective-permute-start.13
  172.8 5.1 %collective-permute-start.24 = (bf16[32,2048]{1,0:T(8,128)(2,1)S(1)}, bf16[32,2048]{1,0:T(8,128)(2,1)S(1)}, u32[]{:S(2)}, u32[]{:S(2)}) collective-permute-start(bf16[32,2048]{1,0:T(8,128)(2,1)S(1)} %fusion.25), channel_id=1, source_target_pairs={{0,11},{1,0},{2,1},{3,2},{4,3},{5,4},{6,5},{7,6},{8,7},{9,8},{10,9... | collective-permute-start | bytes 393224 | tf_op jit(solution)/shard_map/ppermute | solution.py:49
  179.0 1.9 collective-permute-start.14
  181.0 5.1 %collective-permute-start.25 = (bf16[32,2048]{1,0:T(8,128)(2,1)S(1)}, bf16[32,2048]{1,0:T(8,128)(2,1)S(1)}, u32[]{:S(2)}, u32[]{:S(2)}) collective-permute-start(bf16[32,2048]{1,0:T(8,128)(2,1)S(1)} %fusion.24), channel_id=1, source_target_pairs={{0,11},{1,0},{2,1},{3,2},{4,3},{5,4},{6,5},{7,6},{8,7},{9,8},{10,9... | collective-permute-start | bytes 393224 | tf_op jit(solution)/shard_map/ppermute | solution.py:49
  187.1 1.9 collective-permute-start.15
  189.1 5.4 %collective-permute-start.26 = (bf16[32,2048]{1,0:T(8,128)(2,1)S(1)}, bf16[32,2048]{1,0:T(8,128)(2,1)S(1)}, u32[]{:S(2)}, u32[]{:S(2)}) collective-permute-start(bf16[32,2048]{1,0:T(8,128)(2,1)S(1)} %fusion.23), channel_id=1, source_target_pairs={{0,11},{1,0},{2,1},{3,2},{4,3},{5,4},{6,5},{7,6},{8,7},{9,8},{10,9... | collective-permute-start | bytes 393224 | tf_op jit(solution)/shard_map/ppermute | solution.py:49
  194.5 1.8 collective-permute-done.15
  196.3 1.9 collective-permute-start.16
  198.3 5.4 %collective-permute-start.27 = (bf16[32,2048]{1,0:T(8,128)(2,1)S(1)}, bf16[32,2048]{1,0:T(8,128)(2,1)S(1)}, u32[]{:S(2)}, u32[]{:S(2)}) collective-permute-start(bf16[32,2048]{1,0:T(8,128)(2,1)S(1)} %fusion.22), channel_id=1, source_target_pairs={{0,11},{1,0},{2,1},{3,2},{4,3},{5,4},{6,5},{7,6},{8,7},{9,8},{10,9... | collective-permute-start | bytes 393224 | tf_op jit(solution)/shard_map/ppermute | solution.py:49
  205.0 1.9 collective-permute-start.17
  206.9 5.5 %collective-permute-start.28 = (bf16[32,2048]{1,0:T(8,128)(2,1)S(1)}, bf16[32,2048]{1,0:T(8,128)(2,1)S(1)}, u32[]{:S(2)}, u32[]{:S(2)}) collective-permute-start(bf16[32,2048]{1,0:T(8,128)(2,1)S(1)} %fusion.21), channel_id=1, source_target_pairs={{0,11},{1,0},{2,1},{3,2},{4,3},{5,4},{6,5},{7,6},{8,7},{9,8},{10,9... | collective-permute-start | bytes 393224 | tf_op jit(solution)/shard_map/ppermute | solution.py:49
  213.1 1.9 collective-permute-done.28
  215.7 127.6 %reduce-scatter.2.cloned.1.call-done = f32[64,256]{1,0:T(8,128)} async-done(((f32[2048,256]{1,0:T(8,128)}), f32[64,256]{1,0:T(8,128)}) %reduce-scatter.2.cloned.1.call-update) | async-done | bytes 65552 | tf_op jit(solution)/shard_map/reduce_scatter | solution.py:132
  (156 shorter events, 42.6 us)
Async XLA Ops:
  7.2 336.1 %reduce-scatter.2.cloned.1.call-start = ((), (), s32[]{:S(2)}) async-start(), calls=%async_computation.1 | async-start | bytes 2162688 | tf_op jit(solution)/shard_map/reduce_scatter | solution.py:132
  18.9 14.8 %copy-start.16 = (f32[2,128,128]{2,1,0:T(8,128)S(1)}, f32[2,128,128]{2,1,0:T(8,128)}, u32[]{:S(2)}) copy-start(f32[2,128,128]{2,1,0:T(8,128)} %copy.108) | copy-start | bytes 393220
  22.0 3.2 collective-permute-start
  25.2 27.3 %copy-start.23 = (bf16[2,2,128,128]{3,2,1,0:T(8,128)(2,1)}, bf16[2,2,128,128]{3,2,1,0:T(8,128)(2,1)S(1)}, u32[]{:S(2)}) copy-start(bf16[2,2,128,128]{3,2,1,0:T(8,128)(2,1)S(1)} %collective-permute-done) | copy-start | bytes 393220
  26.2 7.4 %collective-permute-start.1 = (bf16[2,2,128,128]{3,2,1,0:T(8,128)(2,1)S(1)}, bf16[2,2,128,128]{3,2,1,0:T(8,128)(2,1)S(1)}, u32[]{:S(2)}, u32[]{:S(2)}) collective-permute-start(bf16[2,2,128,128]{3,2,1,0:T(8,128)(2,1)S(1)} %fusion.87), channel_id=1, source_target_pairs={{0,24},{24,0},{12,36},{36,12},{48,72},{72,48},{60,84},{84,60},{96,... | collective-permute-start | bytes 393224 | tf_op jit(solution)/shard_map/ppermute | solution.py:18
  33.6 18.8 %copy-start.30 = (bf16[2,2,128,128]{3,2,1,0:T(8,128)(2,1)}, bf16[2,2,128,128]{3,2,1,0:T(8,128)(2,1)S(1)}, u32[]{:S(2)}) copy-start(bf16[2,2,128,128]{3,2,1,0:T(8,128)(2,1)S(1)} %collective-permute-done.1) | copy-start | bytes 393220
  33.7 10.3 %copy-start.15 = (f32[2,2,128,128]{3,2,1,0:T(8,128)}, f32[2,2,128,128]{3,2,1,0:T(8,128)S(1)}, u32[]{:S(2)}) copy-start(f32[2,2,128,128]{3,2,1,0:T(8,128)S(1)} %get-tuple-element.10) | copy-start | bytes 786436
  33.7 10.3 %collective-permute-start.2 = (bf16[2,2,128,128]{3,2,1,0:T(8,128)(2,1)S(1)}, bf16[2,2,128,128]{3,2,1,0:T(8,128)(2,1)S(1)}, u32[]{:S(2)}, u32[]{:S(2)}) collective-permute-start(bf16[2,2,128,128]{3,2,1,0:T(8,128)(2,1)S(1)} %get-tuple-element.9), channel_id=1, source_target_pairs={{0,48},{48,0},{12,60},{60,12},{24,72},{72,24},{36,84},{84,36},{96,... | collective-permute-start | bytes 393224 | tf_op jit(solution)/shard_map/ppermute | solution.py:18
  44.7 14.4 %collective-permute-start.3 = (bf16[2,2,128,128]{3,2,1,0:T(8,128)(2,1)}, bf16[2,2,128,128]{3,2,1,0:T(8,128)(2,1)}, u32[]{:S(2)}, u32[]{:S(2)}) collective-permute-start(bf16[2,2,128,128]{3,2,1,0:T(8,128)(2,1)} %fusion.89), channel_id=1, source_target_pairs={{0,96},{96,0},{12,108},{108,12},{24,120},{120,24},{36,132},{132,36... | collective-permute-start | bytes 393224 | tf_op jit(solution)/shard_map/ppermute | solution.py:18
  53.0 23.2 %copy-start.12 = (bf16[6,64,2,128]{3,2,1,0:T(2,128)(2,1)S(1)}, bf16[6,64,2,128]{3,2,1,0:T(2,128)(2,1)}, u32[]{:S(2)}) copy-start(bf16[6,64,2,128]{3,2,1,0:T(2,128)(2,1)} %copy-done.11) | copy-start | bytes 589828
  53.1 24.1 %copy-start.24 = (bf16[2,2,128,128]{3,2,1,0:T(8,128)(2,1)S(1)}, bf16[2,2,128,128]{3,2,1,0:T(8,128)(2,1)}, u32[]{:S(2)}) copy-start(bf16[2,2,128,128]{3,2,1,0:T(8,128)(2,1)} %copy-done.23) | copy-start | bytes 393220
  53.1 24.1 %copy-start.31 = (bf16[2,2,128,128]{3,2,1,0:T(8,128)(2,1)S(1)}, bf16[2,2,128,128]{3,2,1,0:T(8,128)(2,1)}, u32[]{:S(2)}) copy-start(bf16[2,2,128,128]{3,2,1,0:T(8,128)(2,1)} %copy-done.30) | copy-start | bytes 393220
  53.1 24.1 %copy-start.22 = (bf16[2,2,128,128]{3,2,1,0:T(8,128)(2,1)S(1)}, bf16[2,2,128,128]{3,2,1,0:T(8,128)(2,1)}, u32[]{:S(2)}) copy-start(bf16[2,2,128,128]{3,2,1,0:T(8,128)(2,1)} %copy-done.21) | copy-start | bytes 393220
  60.2 6.9 %collective-permute-start.4 = (bf16[2,2,128,128]{3,2,1,0:T(8,128)(2,1)S(1)}, bf16[2,2,128,128]{3,2,1,0:T(8,128)(2,1)S(1)}, u32[]{:S(2)}, u32[]{:S(2)}) collective-permute-start(bf16[2,2,128,128]{3,2,1,0:T(8,128)(2,1)S(1)} %fusion.88), channel_id=1, source_target_pairs={{0,192},{192,0},{12,204},{204,12},{24,216},{216,24},{36,228},{228,... | collective-permute-start | bytes 393224 | tf_op jit(solution)/shard_map/ppermute | solution.py:18
  64.8 14.4 %copy-start.17 = (f32[2,128,128]{2,1,0:T(8,128)S(1)}, f32[2,128,128]{2,1,0:T(8,128)}, u32[]{:S(2)}) copy-start(f32[2,128,128]{2,1,0:T(8,128)} %copy.108) | copy-start | bytes 393220
  68.2 10.9 %collective-permute-start.5 = (bf16[2,2,128,128]{3,2,1,0:T(8,128)(2,1)S(1)}, bf16[2,2,128,128]{3,2,1,0:T(8,128)(2,1)S(1)}, u32[]{:S(2)}, u32[]{:S(2)}) collective-permute-start(bf16[2,2,128,128]{3,2,1,0:T(8,128)(2,1)S(1)} %add_convert_fusion), channel_id=1, source_target_pairs={{0,384},{384,0},{12,396},{396,12},{24,408},{408,24},{36,420},{420,... | collective-permute-start | bytes 393224 | tf_op jit(solution)/shard_map/ppermute | solution.py:18
  81.6 3.0 copy-start.13
  81.6 3.0 copy-start.26
  82.9 2.9 copy-start.3
  82.9 2.9 copy-start.6
  82.9 2.9 copy-start.32
  97.1 3.9 %copy-start.4 = (f32[6,2,128,128]{2,3,1,0:T(8,128)S(1)}, f32[6,2,128,128]{2,3,1,0:T(8,128)}, u32[]{:S(2)}) copy-start(f32[6,2,128,128]{2,3,1,0:T(8,128)} %copy-done.3) | copy-start | bytes 2359300
  99.0 3.3 copy-start.2
  99.0 7.0 %collective-permute-start.6 = (f32[32,64,256]{2,1,0:T(8,128)S(1)}, f32[32,64,256]{2,1,0:T(8,128)S(1)}, u32[]{:S(2)}, u32[]{:S(2)}) collective-permute-start(f32[32,64,256]{2,1,0:T(8,128)S(1)} %dynamic-slice_bitcast_fusion), channel_id=1, source_target_pairs={{0,12},{12,0},{1,13},{13,1},{2,14},{14,2},{3,15},{15,3},{4,16},{16... | collective-permute-start | bytes 6291464 | tf_op jit(solution)/shard_map/ppermute | solution.py:129
  109.9 16.4 %collective-permute-start.7 = (bf16[32,2048]{1,0:T(8,128)(2,1)}, bf16[32,2048]{1,0:T(8,128)(2,1)S(1)}, u32[]{:S(2)}, u32[]{:S(2)}) collective-permute-start(bf16[32,2048]{1,0:T(8,128)(2,1)} %dynamic-slice_bitcast_fusion.2), channel_id=1, source_target_pairs={{0,1},{1,2},{2,3},{3,4},{4,5},{5,6},{6,7},{7,8},{8,9},{9,10},{10,1... | collective-permute-start | bytes 393224 | tf_op jit(solution)/shard_map/ppermute | solution.py:48
  111.9 17.3 %collective-permute-start.18 = (bf16[32,2048]{1,0:T(8,128)(2,1)S(1)}, bf16[32,2048]{1,0:T(8,128)(2,1)S(1)}, u32[]{:S(2)}, u32[]{:S(2)}) collective-permute-start(bf16[32,2048]{1,0:T(8,128)(2,1)S(1)} %dynamic-slice_bitcast_fusion.1), channel_id=1, source_target_pairs={{0,11},{1,0},{2,1},{3,2},{4,3},{5,4},{6,5},{7,6},{8,7},{9,8},{10,9... | collective-permute-start | bytes 393224 | tf_op jit(solution)/shard_map/ppermute | solution.py:49
  123.9 32.6 %copy-start.8 = (bf16[12,32,2048]{2,1,0:T(8,128)(2,1)S(1)}, bf16[12,32,2048]{2,1,0:T(8,128)(2,1)}, u32[]{:S(2)}) copy-start(bf16[12,32,2048]{2,1,0:T(8,128)(2,1)} %copy-done.7) | copy-start | bytes 4718596
  123.9 38.8 %copy-start.10 = (bf16[12,32,2048]{2,1,0:T(8,128)(2,1)S(1)}, bf16[12,32,2048]{2,1,0:T(8,128)(2,1)}, u32[]{:S(2)}) copy-start(bf16[12,32,2048]{2,1,0:T(8,128)(2,1)} %copy-done.9) | copy-start | bytes 4718596
  127.2 8.4 %collective-permute-start.8 = (bf16[32,2048]{1,0:T(8,128)(2,1)S(1)}, bf16[32,2048]{1,0:T(8,128)(2,1)S(1)}, u32[]{:S(2)}, u32[]{:S(2)}) collective-permute-start(bf16[32,2048]{1,0:T(8,128)(2,1)S(1)} %fusion.41), channel_id=1, source_target_pairs={{0,1},{1,2},{2,3},{3,4},{4,5},{5,6},{6,7},{7,8},{8,9},{9,10},{10,1... | collective-permute-start | bytes 393224 | tf_op jit(solution)/shard_map/ppermute | solution.py:48
  130.1 8.4 %collective-permute-start.19 = (bf16[32,2048]{1,0:T(8,128)(2,1)S(1)}, bf16[32,2048]{1,0:T(8,128)(2,1)S(1)}, u32[]{:S(2)}, u32[]{:S(2)}) collective-permute-start(bf16[32,2048]{1,0:T(8,128)(2,1)S(1)} %fusion.30), channel_id=1, source_target_pairs={{0,11},{1,0},{2,1},{3,2},{4,3},{5,4},{6,5},{7,6},{8,7},{9,8},{10,9... | collective-permute-start | bytes 393224 | tf_op jit(solution)/shard_map/ppermute | solution.py:49
  136.6 8.1 %collective-permute-start.9 = (bf16[32,2048]{1,0:T(8,128)(2,1)S(1)}, bf16[32,2048]{1,0:T(8,128)(2,1)S(1)}, u32[]{:S(2)}, u32[]{:S(2)}) collective-permute-start(bf16[32,2048]{1,0:T(8,128)(2,1)S(1)} %fusion.40), channel_id=1, source_target_pairs={{0,1},{1,2},{2,3},{3,4},{4,5},{5,6},{6,7},{7,8},{8,9},{9,10},{10,1... | collective-permute-start | bytes 393224 | tf_op jit(solution)/shard_map/ppermute | solution.py:48
  139.5 8.1 %collective-permute-start.20 = (bf16[32,2048]{1,0:T(8,128)(2,1)S(1)}, bf16[32,2048]{1,0:T(8,128)(2,1)S(1)}, u32[]{:S(2)}, u32[]{:S(2)}) collective-permute-start(bf16[32,2048]{1,0:T(8,128)(2,1)S(1)} %fusion.29), channel_id=1, source_target_pairs={{0,11},{1,0},{2,1},{3,2},{4,3},{5,4},{6,5},{7,6},{8,7},{9,8},{10,9... | collective-permute-start | bytes 393224 | tf_op jit(solution)/shard_map/ppermute | solution.py:49
  145.6 8.1 %collective-permute-start.10 = (bf16[32,2048]{1,0:T(8,128)(2,1)S(1)}, bf16[32,2048]{1,0:T(8,128)(2,1)S(1)}, u32[]{:S(2)}, u32[]{:S(2)}) collective-permute-start(bf16[32,2048]{1,0:T(8,128)(2,1)S(1)} %fusion.39), channel_id=1, source_target_pairs={{0,1},{1,2},{2,3},{3,4},{4,5},{5,6},{6,7},{7,8},{8,9},{9,10},{10,1... | collective-permute-start | bytes 393224 | tf_op jit(solution)/shard_map/ppermute | solution.py:48
  148.5 8.1 %collective-permute-start.21 = (bf16[32,2048]{1,0:T(8,128)(2,1)S(1)}, bf16[32,2048]{1,0:T(8,128)(2,1)S(1)}, u32[]{:S(2)}, u32[]{:S(2)}) collective-permute-start(bf16[32,2048]{1,0:T(8,128)(2,1)S(1)} %fusion.28), channel_id=1, source_target_pairs={{0,11},{1,0},{2,1},{3,2},{4,3},{5,4},{6,5},{7,6},{8,7},{9,8},{10,9... | collective-permute-start | bytes 393224 | tf_op jit(solution)/shard_map/ppermute | solution.py:49
  154.6 8.1 %collective-permute-start.11 = (bf16[32,2048]{1,0:T(8,128)(2,1)S(1)}, bf16[32,2048]{1,0:T(8,128)(2,1)S(1)}, u32[]{:S(2)}, u32[]{:S(2)}) collective-permute-start(bf16[32,2048]{1,0:T(8,128)(2,1)S(1)} %fusion.38), channel_id=1, source_target_pairs={{0,1},{1,2},{2,3},{3,4},{4,5},{5,6},{6,7},{7,8},{8,9},{9,10},{10,1... | collective-permute-start | bytes 393224 | tf_op jit(solution)/shard_map/ppermute | solution.py:48
  156.6 8.0 %collective-permute-start.22 = (bf16[32,2048]{1,0:T(8,128)(2,1)S(1)}, bf16[32,2048]{1,0:T(8,128)(2,1)S(1)}, u32[]{:S(2)}, u32[]{:S(2)}) collective-permute-start(bf16[32,2048]{1,0:T(8,128)(2,1)S(1)} %fusion.27), channel_id=1, source_target_pairs={{0,11},{1,0},{2,1},{3,2},{4,3},{5,4},{6,5},{7,6},{8,7},{9,8},{10,9... | collective-permute-start | bytes 393224 | tf_op jit(solution)/shard_map/ppermute | solution.py:49
  162.7 8.1 %collective-permute-start.12 = (bf16[32,2048]{1,0:T(8,128)(2,1)S(1)}, bf16[32,2048]{1,0:T(8,128)(2,1)S(1)}, u32[]{:S(2)}, u32[]{:S(2)}) collective-permute-start(bf16[32,2048]{1,0:T(8,128)(2,1)S(1)} %fusion.37), channel_id=1, source_target_pairs={{0,1},{1,2},{2,3},{3,4},{4,5},{5,6},{6,7},{7,8},{8,9},{9,10},{10,1... | collective-permute-start | bytes 393224 | tf_op jit(solution)/shard_map/ppermute | solution.py:48
  164.7 8.1 %collective-permute-start.23 = (bf16[32,2048]{1,0:T(8,128)(2,1)S(1)}, bf16[32,2048]{1,0:T(8,128)(2,1)S(1)}, u32[]{:S(2)}, u32[]{:S(2)}) collective-permute-start(bf16[32,2048]{1,0:T(8,128)(2,1)S(1)} %fusion.26), channel_id=1, source_target_pairs={{0,11},{1,0},{2,1},{3,2},{4,3},{5,4},{6,5},{7,6},{8,7},{9,8},{10,9... | collective-permute-start | bytes 393224 | tf_op jit(solution)/shard_map/ppermute | solution.py:49
  170.9 8.1 %collective-permute-start.13 = (bf16[32,2048]{1,0:T(8,128)(2,1)S(1)}, bf16[32,2048]{1,0:T(8,128)(2,1)S(1)}, u32[]{:S(2)}, u32[]{:S(2)}) collective-permute-start(bf16[32,2048]{1,0:T(8,128)(2,1)S(1)} %fusion.36), channel_id=1, source_target_pairs={{0,1},{1,2},{2,3},{3,4},{4,5},{5,6},{6,7},{7,8},{8,9},{9,10},{10,1... | collective-permute-start | bytes 393224 | tf_op jit(solution)/shard_map/ppermute | solution.py:48
  172.8 8.1 %collective-permute-start.24 = (bf16[32,2048]{1,0:T(8,128)(2,1)S(1)}, bf16[32,2048]{1,0:T(8,128)(2,1)S(1)}, u32[]{:S(2)}, u32[]{:S(2)}) collective-permute-start(bf16[32,2048]{1,0:T(8,128)(2,1)S(1)} %fusion.25), channel_id=1, source_target_pairs={{0,11},{1,0},{2,1},{3,2},{4,3},{5,4},{6,5},{7,6},{8,7},{9,8},{10,9... | collective-permute-start | bytes 393224 | tf_op jit(solution)/shard_map/ppermute | solution.py:49
  179.0 8.1 %collective-permute-start.14 = (bf16[32,2048]{1,0:T(8,128)(2,1)S(1)}, bf16[32,2048]{1,0:T(8,128)(2,1)S(1)}, u32[]{:S(2)}, u32[]{:S(2)}) collective-permute-start(bf16[32,2048]{1,0:T(8,128)(2,1)S(1)} %fusion.35), channel_id=1, source_target_pairs={{0,1},{1,2},{2,3},{3,4},{4,5},{5,6},{6,7},{7,8},{8,9},{9,10},{10,1... | collective-permute-start | bytes 393224 | tf_op jit(solution)/shard_map/ppermute | solution.py:48
  181.0 8.1 %collective-permute-start.25 = (bf16[32,2048]{1,0:T(8,128)(2,1)S(1)}, bf16[32,2048]{1,0:T(8,128)(2,1)S(1)}, u32[]{:S(2)}, u32[]{:S(2)}) collective-permute-start(bf16[32,2048]{1,0:T(8,128)(2,1)S(1)} %fusion.24), channel_id=1, source_target_pairs={{0,11},{1,0},{2,1},{3,2},{4,3},{5,4},{6,5},{7,6},{8,7},{9,8},{10,9... | collective-permute-start | bytes 393224 | tf_op jit(solution)/shard_map/ppermute | solution.py:49
  187.1 9.2 %collective-permute-start.15 = (bf16[32,2048]{1,0:T(8,128)(2,1)S(1)}, bf16[32,2048]{1,0:T(8,128)(2,1)S(1)}, u32[]{:S(2)}, u32[]{:S(2)}) collective-permute-start(bf16[32,2048]{1,0:T(8,128)(2,1)S(1)} %fusion.34), channel_id=1, source_target_pairs={{0,1},{1,2},{2,3},{3,4},{4,5},{5,6},{6,7},{7,8},{8,9},{9,10},{10,1... | collective-permute-start | bytes 393224 | tf_op jit(solution)/shard_map/ppermute | solution.py:48
  189.1 9.1 %collective-permute-start.26 = (bf16[32,2048]{1,0:T(8,128)(2,1)S(1)}, bf16[32,2048]{1,0:T(8,128)(2,1)S(1)}, u32[]{:S(2)}, u32[]{:S(2)}) collective-permute-start(bf16[32,2048]{1,0:T(8,128)(2,1)S(1)} %fusion.23), channel_id=1, source_target_pairs={{0,11},{1,0},{2,1},{3,2},{4,3},{5,4},{6,5},{7,6},{8,7},{9,8},{10,9... | collective-permute-start | bytes 393224 | tf_op jit(solution)/shard_map/ppermute | solution.py:49
  196.3 8.7 %collective-permute-start.16 = (bf16[32,2048]{1,0:T(8,128)(2,1)S(1)}, bf16[32,2048]{1,0:T(8,128)(2,1)S(1)}, u32[]{:S(2)}, u32[]{:S(2)}) collective-permute-start(bf16[32,2048]{1,0:T(8,128)(2,1)S(1)} %fusion.33), channel_id=1, source_target_pairs={{0,1},{1,2},{2,3},{3,4},{4,5},{5,6},{6,7},{7,8},{8,9},{9,10},{10,1... | collective-permute-start | bytes 393224 | tf_op jit(solution)/shard_map/ppermute | solution.py:48
  198.3 8.6 %collective-permute-start.27 = (bf16[32,2048]{1,0:T(8,128)(2,1)S(1)}, bf16[32,2048]{1,0:T(8,128)(2,1)S(1)}, u32[]{:S(2)}, u32[]{:S(2)}) collective-permute-start(bf16[32,2048]{1,0:T(8,128)(2,1)S(1)} %fusion.22), channel_id=1, source_target_pairs={{0,11},{1,0},{2,1},{3,2},{4,3},{5,4},{6,5},{7,6},{8,7},{9,8},{10,9... | collective-permute-start | bytes 393224 | tf_op jit(solution)/shard_map/ppermute | solution.py:49
  205.0 8.1 %collective-permute-start.17 = (bf16[32,2048]{1,0:T(8,128)(2,1)S(1)}, bf16[32,2048]{1,0:T(8,128)(2,1)S(1)}, u32[]{:S(2)}, u32[]{:S(2)}) collective-permute-start(bf16[32,2048]{1,0:T(8,128)(2,1)S(1)} %fusion.32), channel_id=1, source_target_pairs={{0,1},{1,2},{2,3},{3,4},{4,5},{5,6},{6,7},{7,8},{8,9},{9,10},{10,1... | collective-permute-start | bytes 393224 | tf_op jit(solution)/shard_map/ppermute | solution.py:48
  206.9 8.0 %collective-permute-start.28 = (bf16[32,2048]{1,0:T(8,128)(2,1)S(1)}, bf16[32,2048]{1,0:T(8,128)(2,1)S(1)}, u32[]{:S(2)}, u32[]{:S(2)}) collective-permute-start(bf16[32,2048]{1,0:T(8,128)(2,1)S(1)} %fusion.21), channel_id=1, source_target_pairs={{0,11},{1,0},{2,1},{3,2},{4,3},{5,4},{6,5},{7,6},{8,7},{9,8},{10,9... | collective-permute-start | bytes 393224 | tf_op jit(solution)/shard_map/ppermute | solution.py:49
  (15 other events, 28.5 us)
Sparse Core Ops, SparseCore 0:
  124.0 219.2 reduce-scatter.1

commit v2 on v1

--- a/solution.py
+++ b/solution.py
@@ -29,27 +29,29 @@
     return first + jnp.einsum(form, operand, parts[1], preferred_element_type=jnp.float32)
 
 
-def ring_scatter(partial, count):
-    position = lax.axis_index("head")
-    rows = partial.shape[0] // count
-    half = partial.shape[1] // 2
-    chunks = partial.reshape(count, rows, partial.shape[1])
-    up_own = chunks[:, :, :half]
-    down_own = chunks[:, :, half:]
-    up_route = [(i, (i + 1) % count) for i in range(count)]
-    down_route = [(i, (i - 1) % count) for i in range(count)]
+def halving_order(bits):
+    if bits != 6:
+        return list(range(bits))
+    return [0, 1, 4, 2, 5, 3]
 
-    def pick(own, index):
-        return lax.dynamic_index_in_dim(own, index % count, 0, keepdims=False).astype(jnp.float32)
 
-    up_acc = pick(up_own, position - 1)
-    down_acc = pick(down_own, position + 1)
-    for step in range(count - 1):
-        up_in = lax.ppermute(up_acc.astype(jnp.bfloat16), "head", up_route)
-        down_in = lax.ppermute(down_acc.astype(jnp.bfloat16), "head", down_route)
-        up_acc = up_in.astype(jnp.float32) + pick(up_own, position - 2 - step)
-        down_acc = down_in.astype(jnp.float32) + pick(down_own, position + 2 + step)
-    return jnp.concatenate([up_acc, down_acc], 1).astype(jnp.bfloat16)
+def halving_scatter(partial, count):
+    bits = count.bit_length() - 1
+    position = lax.axis_index(SEQ)
+    cols = partial.shape[1]
+    acc = partial.reshape((2,) * bits + (partial.shape[0] // count, cols))
+    held = list(range(bits - 1, -1, -1))
+    for bit in halving_order(bits):
+        axis = held.index(bit)
+        mine = position >> bit & 1
+        lower = lax.index_in_dim(acc, 0, axis, keepdims=False)
+        upper = lax.index_in_dim(acc, 1, axis, keepdims=False)
+        kept = jnp.where(mine == 1, upper, lower)
+        sent = jnp.where(mine == 1, lower, upper)
+        route = [(i, i ^ 1 << bit) for i in range(count)]
+        acc = kept + lax.ppermute(sent, SEQ, route)
+        held.pop(axis)
+    return acc.reshape(-1, cols)
 
 
 def local(queries, key_rows, value_rows, out_weight, out_grad, seq_count, head_count_axis):
@@ -122,19 +124,9 @@
     weight_partial = lax.dot_general(
         out_grad, attention, (((0,), (0,)), ((), ())), preferred_element_type=jnp.float32
     )
-    core = lax.axis_index("c")
-    halves = weight_partial.reshape(-1, 2, weight_partial.shape[0] // (2 * lax.axis_size("xy")), weight_partial.shape[1])
-    kept = lax.dynamic_index_in_dim(halves, core, 1, keepdims=False)
-    sent = lax.dynamic_index_in_dim(halves, 1 - core, 1, keepdims=False)
-    kept = kept + lax.ppermute(sent, "c", [(0, 1), (1, 0)])
-    kept, partial_output = lax.optimization_barrier((kept, partial_output))
-    output = ring_scatter(partial_output, head_count_axis)
-    weight_grad = lax.psum_scatter(
-        kept.reshape(-1, weight_partial.shape[1]),
-        "xy",
-        scatter_dimension=0,
-        tiled=True,
-    ) * total_rows ** (-0.5)
+    partial_output, weight_partial = lax.optimization_barrier((partial_output, weight_partial))
+    output = lax.psum_scatter(partial_output, "head", scatter_dimension=0, tiled=True)
+    weight_grad = halving_scatter(weight_partial, seq_count) * total_rows ** (-0.5)
     return (
         output,
         query_grad.astype(jnp.bfloat16).reshape(flat_shape),

time: 354 us -> 200 us (0.56)
  waiting for transfers between devices: 160 us -> 77.3 us
  starting transfers between devices: 116 us -> 48.5 us
  local copies, waits for them, and re-layouts: 22.9 us -> 18.1 us
    reduce_scatter x1, waiting for transfers between devices: 128 us -> 0.01 us  [local(): lax.psum_scatter(partial_output, 'head', scatter_dimension=0, tiled=True)]
    ppermute x23 -> x6, starting transfers between devices: 87.5 us -> 20.1 us  [halving_scatter(): acc = kept + lax.ppermute(sent, SEQ, route)]
    ppermute x23 -> x6, waiting for transfers between devices: 12 us -> 55.6 us  [halving_scatter(): acc = kept + lax.ppermute(sent, SEQ, route)]
    convert_element_type x20 -> x0, other arithmetic: 7.08 us -> none  [the longest x10 3.97 us: ring_scatter(): up_in = lax.ppermute(up_acc.astype(jnp.bfloat16), 'head', up_route)]
    dot_general x1 -> x0, local copies, waits for them, and re-layouts: 5.62 us -> none  [local(): lax.dot_general(out_grad, attention, (((0,), (0,)), ((), ())), preferred_...]
    optimization_barrier x0 -> x1, local copies, waits for them, and re-layouts: none -> 5.61 us  [local(): lax.optimization_barrier((partial_output, weight_partial))]
    select_n x0 -> x6, other arithmetic: none -> 4.3 us  [halving_scatter(): sent = jnp.where(mine == 1, lower, upper)]
  transfers between devices with their start and end apart: 30 -> 13, of which waited for: 17 -> 10; matrix products, arithmetic and copies ran while one was open for 5% -> 9% of each run, Pallas kernels for 0% -> 0%
where the time goes in v2:
time: 200 us; the launch traced here: 197 us
  waiting for transfers between devices  77.3 us (39%)
  starting transfers between devices  48.5 us (24%)
  matrix products  21.5 us (11%)
  local copies, waits for them, and re-layouts  18.1 us (9%)
  other arithmetic  16.7 us (8%)
  between operations  14.6 us (7%)
    ppermute x6, waiting for transfers between devices, halving_scatter(): acc = kept + lax.ppermute(sent, SEQ, route)  55.6 us
    ppermute x6, starting transfers between devices, swapped(): return lax.ppermute(block, SEQ, route)  28.3 us
    ppermute x6, waiting for transfers between devices, swapped(): return lax.ppermute(block, SEQ, route)  21.7 us
    ppermute x6, starting transfers between devices, halving_scatter(): acc = kept + lax.ppermute(sent, SEQ, route)  20.1 us
    optimization_barrier x1, local copies, waits for them, and re-layouts, local(): lax.optimization_barrier((partial_output, weight_partial))  5.61 us
    select_n x6, other arithmetic, halving_scatter(): sent = jnp.where(mine == 1, lower, upper)  4.3 us
    dot_general x1, matrix products, local(): lax.dot_general(out_grad, attention, (((0,), (0,)), ((), ())), preferred_...  4.24 us
  transfers between devices with their start and end apart: 13, of which 10 were waited for; matrix products, arithmetic and copies ran while one was open for 9% of the time, Pallas kernels for 0%

profile of v2, /device:TPU:6, one launch (start us, length us, event | category | flops | bytes accessed | tf_op | source)
XLA Modules:
  0.0 196.7 jit_solution(17891867396330383904)
XLA Ops:
  7.2 1.8 reshape.75
  9.0 1.0 reshape.76
  10.0 1.7 reshape.77
  11.7 3.2 %convolution_convert_fusion.1 = bf16[384,256]{1,0:T(8,128)(2,1)} fusion(bf16[384,4096]{1,0:T(8,128)(2,1)S(1)} %copy-done, bf16[4096,256]{1,0:T(8,128)(2,1)} %param.8), kind=kOutput, calls=%fused_computation.38 | convolution fusion | flops 805404672 | bytes 5439488 | tf_op jit(solution)/shard_map/dot_general | solution.py:69
  14.9 1.0 reshape.78
  15.9 2.8 %fusion.83 = (f32[2,128,128]{1,2,0:T(8,128)}, f32[6,2,128,128]{2,3,1,0:T(8,128)}) fusion(bf16[6,64,2,128]{3,2,1,0:T(2,128)(2,1)} %reshape.75, bf16[6,64,2,128]{3,2,1,0:T(2,128)(2,1)S(1)} %reshape.78), kind=kOutput, calls=%fused_computation.132 | convolution fusion | flops 25329664 | bytes 1310720 | tf_op jit(solution)/shard_map/cthd,cthe->chde/dot_general | solution.py:76
  18.7 1.7 copy.142
  20.4 2.2 %fusion.84 = (f32[2,128,128]{2,1,0:T(8,128)S(1)}, f32[6,2,128,128]{3,2,1,0:T(8,128)}) fusion(bf16[6,64,2,128]{3,2,1,0:T(2,128)(2,1)} %reshape.77, bf16[6,64,2,128]{3,2,1,0:T(2,128)(2,1)S(1)} %reshape.76), kind=kOutput, calls=%fused_computation.133 | convolution fusion | flops 25329664 | bytes 1310720 | tf_op jit(solution)/shard_map/cshd,cshe->chde/dot_general | solution.py:73
  22.6 0.9 fusion.29
  23.5 1.9 collective-permute-start
  25.4 1.3 collective-permute-done
  26.7 1.0 fusion.73
  27.7 3.5 %collective-permute-start.1 = (bf16[2,2,128,128]{3,2,1,0:T(8,128)(2,1)S(1)}, bf16[2,2,128,128]{3,2,1,0:T(8,128)(2,1)S(1)}, u32[]{:S(2)}, u32[]{:S(2)}) collective-permute-start(bf16[2,2,128,128]{3,2,1,0:T(8,128)(2,1)S(1)} %fusion.73), channel_id=1, source_target_pairs={{0,24},{24,0},{12,36},{36,12},{48,72},{72,48},{60,84},{84,60},{96,... | collective-permute-start | bytes 393224 | tf_op jit(solution)/shard_map/ppermute | solution.py:18
  31.2 4.0 %collective-permute-done.1 = bf16[2,2,128,128]{3,2,1,0:T(8,128)(2,1)S(1)} collective-permute-done((bf16[2,2,128,128]{3,2,1,0:T(8,128)(2,1)S(1)}, bf16[2,2,128,128]{3,2,1,0:T(8,128)(2,1)S(1)}, u32[]{:S(2)}, u32[]{:S(2)}) %collective-permute-start.1) | collective-permute-done | bytes 131104 | tf_op jit(solution)/shard_map/ppermute | solution.py:18
  35.2 4.5 %collective-permute-start.2 = (bf16[2,2,128,128]{3,2,1,0:T(8,128)(2,1)S(1)}, bf16[2,2,128,128]{3,2,1,0:T(8,128)(2,1)S(1)}, u32[]{:S(2)}, u32[]{:S(2)}) collective-permute-start(bf16[2,2,128,128]{3,2,1,0:T(8,128)(2,1)S(1)} %get-tuple-element.9), channel_id=1, source_target_pairs={{0,48},{48,0},{12,60},{60,12},{24,72},{72,24},{36,84},{84,36},{96,... | collective-permute-start | bytes 393224 | tf_op jit(solution)/shard_map/ppermute | solution.py:18
  39.7 5.8 %collective-permute-done.2 = bf16[2,2,128,128]{3,2,1,0:T(8,128)(2,1)S(1)} collective-permute-done((bf16[2,2,128,128]{3,2,1,0:T(8,128)(2,1)S(1)}, bf16[2,2,128,128]{3,2,1,0:T(8,128)(2,1)S(1)}, u32[]{:S(2)}, u32[]{:S(2)}) %collective-permute-start.2) | collective-permute-done | bytes 131104 | tf_op jit(solution)/shard_map/ppermute | solution.py:18
  45.6 7.7 %collective-permute-start.3 = (bf16[2,2,128,128]{3,2,1,0:T(8,128)(2,1)S(1)}, bf16[2,2,128,128]{3,2,1,0:T(8,128)(2,1)S(1)}, u32[]{:S(2)}, u32[]{:S(2)}) collective-permute-start(bf16[2,2,128,128]{3,2,1,0:T(8,128)(2,1)S(1)} %fusion.76), channel_id=1, source_target_pairs={{0,96},{96,0},{12,108},{108,12},{24,120},{120,24},{36,132},{132,36... | collective-permute-start | bytes 393224 | tf_op jit(solution)/shard_map/ppermute | solution.py:18
  53.3 6.3 %collective-permute-done.3 = bf16[2,2,128,128]{3,2,1,0:T(8,128)(2,1)S(1)} collective-permute-done((bf16[2,2,128,128]{3,2,1,0:T(8,128)(2,1)S(1)}, bf16[2,2,128,128]{3,2,1,0:T(8,128)(2,1)S(1)}, u32[]{:S(2)}, u32[]{:S(2)}) %collective-permute-start.3) | collective-permute-done | bytes 131104 | tf_op jit(solution)/shard_map/ppermute | solution.py:18
  59.6 0.7 fusion.75
  60.4 2.7 %collective-permute-start.4 = (bf16[2,2,128,128]{3,2,1,0:T(8,128)(2,1)}, bf16[2,2,128,128]{3,2,1,0:T(8,128)(2,1)}, u32[]{:S(2)}, u32[]{:S(2)}) collective-permute-start(bf16[2,2,128,128]{3,2,1,0:T(8,128)(2,1)} %fusion.75), channel_id=1, source_target_pairs={{0,192},{192,0},{12,204},{204,12},{24,216},{216,24},{36,228},{228,... | collective-permute-start | bytes 393224 | tf_op jit(solution)/shard_map/ppermute | solution.py:18
  63.2 4.3 %collective-permute-done.4 = bf16[2,2,128,128]{3,2,1,0:T(8,128)(2,1)} collective-permute-done((bf16[2,2,128,128]{3,2,1,0:T(8,128)(2,1)}, bf16[2,2,128,128]{3,2,1,0:T(8,128)(2,1)}, u32[]{:S(2)}, u32[]{:S(2)}) %collective-permute-start.4) | collective-permute-done | bytes 131104 | tf_op jit(solution)/shard_map/ppermute | solution.py:18
  67.5 1.2 add_convert_fusion
  68.7 8.0 %collective-permute-start.5 = (bf16[2,2,128,128]{3,2,1,0:T(8,128)(2,1)S(1)}, bf16[2,2,128,128]{3,2,1,0:T(8,128)(2,1)S(1)}, u32[]{:S(2)}, u32[]{:S(2)}) collective-permute-start(bf16[2,2,128,128]{3,2,1,0:T(8,128)(2,1)S(1)} %add_convert_fusion), channel_id=1, source_target_pairs={{0,384},{384,0},{12,396},{396,12},{24,408},{408,24},{36,420},{420,... | collective-permute-start | bytes 393224 | tf_op jit(solution)/shard_map/ppermute | solution.py:18
  76.7 1.2 fusion.16
  77.9 1.0 convert_element_type.84
  79.0 0.9 convert_element_type.92
  80.0 0.8 fusion.36
  83.2 2.7 %convolution_convert_fusion = bf16[384,4096]{1,0:T(8,128)(2,1)} fusion(bf16[4096,256]{1,0:T(8,128)(2,1)S(1)} %copy-done.12, bf16[48,8,2,128]{3,2,1,0:T(2,128)(2,1)S(1)} %bitcast.155), kind=kOutput, calls=%fused_computation | convolution fusion | flops 806879232 | bytes 5439488 | tf_op jit(solution)/shard_map/dot_general | solution.py:105
  85.9 4.2 %convolution_bitcast_fusion = f32[4096,256]{0,1:T(8,128)} fusion(bf16[384,4096]{1,0:T(8,128)(2,1)S(1)} %copy-done, bf16[48,8,2,128]{3,2,1,0:T(2,128)(2,1)} %bitcast.156), kind=kOutput, calls=%fused_computation.1 | convolution fusion | flops 805306368 | bytes 7536640 | tf_op jit(solution)/shard_map/dot_general | solution.py:124
  90.1 5.6 %copy.167 = f32[4096,256]{1,0:T(8,128)} copy(f32[4096,256]{0,1:T(8,128)} %convolution_bitcast_fusion) | data formatting | bytes 8388608 | tf_op jit(solution)/shard_map/optimization_barrier | solution.py:127
  95.7 4.0 %select_bitcast_fusion = f32[2,2,2,2,2,64,256]{6,5,4,3,2,1,0:T(8,128)} fusion(f32[2,2,2,2,2,2,64,256]{7,6,5,4,3,2,1,0:T(8,128)} %bitcast.150, pred[]{:T(512)S(6)} %eq.12), kind=kLoop, calls=%fused_computation.5 | loop fusion | flops 524288 | bytes 6291457 | tf_op jit(solution)/shard_map/jit(_where)/select_n | solution.py:50
  99.7 1.9 collective-permute-start.6
  101.7 1.8 fusion.15
  103.5 1.6 copy.154
  105.1 1.2 reduce-window_subtract_fusion
  106.4 3.4 %fusion.1 = f32[2,2,2,2,2,64,256]{6,5,4,3,2,1,0:T(8,128)S(1)} fusion(f32[2,2,2,2,2,64,256]{6,5,4,3,2,1,0:T(8,128)} %collective-permute-done.6, f32[2,2,2,2,2,2,64,256]{7,6,5,4,3,2,1,0:T(8,128)} %bitcast.151, pred[]{:T(512)S(6)} %eq.12), kind=kLoop, calls=%fused_computation.4 | loop fusion | flops 1048576 | bytes 8388609 | tf_op jit(solution)/shard_map/add | solution.py:52
  109.9 1.9 collective-permute-start.7
  113.1 24.3 %collective-permute-done.7 = f32[2,2,2,2,64,256]{5,4,3,2,1,0:T(8,128)S(1)} collective-permute-done((f32[2,2,2,2,64,256]{5,4,3,2,1,0:T(8,128)S(1)}, f32[2,2,2,2,64,256]{5,4,3,2,1,0:T(8,128)S(1)}, u32[]{:S(2)}, u32[]{:S(2)}) %collective-permute-start.7) | collective-permute-done | bytes 1048608 | tf_op jit(solution)/shard_map/ppermute | solution.py:52
  137.7 3.5 %collective-permute-start.8 = (f32[2,2,2,64,256]{4,3,2,1,0:T(8,128)S(1)}, f32[2,2,2,64,256]{4,3,2,1,0:T(8,128)S(1)}, u32[]{:S(2)}, u32[]{:S(2)}) collective-permute-start(f32[2,2,2,64,256]{4,3,2,1,0:T(8,128)S(1)} %select_bitcast_fusion.2), channel_id=1, source_target_pairs={{0,192},{12,204},{24,216},{36,228},{48,240},{60,252},{72,264},{84,... | collective-permute-start | bytes 1572872 | tf_op jit(solution)/shard_map/ppermute | solution.py:52
  142.5 10.9 %collective-permute-done.8 = f32[2,2,2,64,256]{4,3,2,1,0:T(8,128)S(1)} collective-permute-done((f32[2,2,2,64,256]{4,3,2,1,0:T(8,128)S(1)}, f32[2,2,2,64,256]{4,3,2,1,0:T(8,128)S(1)}, u32[]{:S(2)}, u32[]{:S(2)}) %collective-permute-start.8) | collective-permute-done | bytes 524320 | tf_op jit(solution)/shard_map/ppermute | solution.py:52
  153.5 1.9 collective-permute-start.9
  155.8 13.4 %collective-permute-done.9 = f32[2,2,64,256]{3,2,1,0:T(8,128)S(1)} collective-permute-done((f32[2,2,64,256]{3,2,1,0:T(8,128)S(1)}, f32[2,2,64,256]{3,2,1,0:T(8,128)S(1)}, u32[]{:S(2)}, u32[]{:S(2)}) %collective-permute-start.9) | collective-permute-done | bytes 262176 | tf_op jit(solution)/shard_map/ppermute | solution.py:52
  169.3 5.7 %collective-permute-start.10 = (f32[2,64,256]{2,1,0:T(8,128)S(1)}, f32[2,64,256]{2,1,0:T(8,128)S(1)}, u32[]{:S(2)}, u32[]{:S(2)}) collective-permute-start(f32[2,64,256]{2,1,0:T(8,128)S(1)} %select_bitcast_fusion.4), channel_id=1, source_target_pairs={{0,384},{12,396},{24,408},{36,420},{48,432},{60,444},{72,456},{84,... | collective-permute-start | bytes 393224 | tf_op jit(solution)/shard_map/ppermute | solution.py:52
  175.2 3.3 %collective-permute-done.10 = f32[2,64,256]{2,1,0:T(8,128)S(1)} collective-permute-done((f32[2,64,256]{2,1,0:T(8,128)S(1)}, f32[2,64,256]{2,1,0:T(8,128)S(1)}, u32[]{:S(2)}, u32[]{:S(2)}) %collective-permute-start.10) | collective-permute-done | bytes 131104 | tf_op jit(solution)/shard_map/ppermute | solution.py:52
  178.5 5.2 %collective-permute-start.11 = (f32[64,256]{1,0:T(8,128)S(1)}, f32[64,256]{1,0:T(8,128)S(1)}, u32[]{:S(2)}, u32[]{:S(2)}) collective-permute-start(f32[64,256]{1,0:T(8,128)S(1)} %select_bitcast_fusion.5), channel_id=1, source_target_pairs={{0,96},{12,108},{24,120},{36,132},{48,144},{60,156},{72,168},{84,1... | collective-permute-start | bytes 196616 | tf_op jit(solution)/shard_map/ppermute | solution.py:52
  183.8 0.8 copy_bitcast_fusion
  184.8 0.7 copy.257
  185.5 3.8 %collective-permute-done.11 = f32[64,256]{1,0:T(8,128)S(1)} collective-permute-done((f32[64,256]{1,0:T(8,128)S(1)}, f32[64,256]{1,0:T(8,128)S(1)}, u32[]{:S(2)}, u32[]{:S(2)}) %collective-permute-start.11) | collective-permute-done | bytes 65568 | tf_op jit(solution)/shard_map/ppermute | solution.py:52
  (85 shorter events, 7.2 us)
Async XLA Ops:
  7.2 4.5 %copy-start = (bf16[384,4096]{1,0:T(8,128)(2,1)S(1)}, bf16[384,4096]{1,0:T(8,128)(2,1)}, u32[]{:S(2)}) copy-start(bf16[384,4096]{1,0:T(8,128)(2,1)} %param.9) | copy-start | bytes 9437188
  7.2 182.7 %reduce-scatter.2.cloned.1.call-start = ((), (), s32[]{:S(2)}) async-start(), calls=%async_computation.1 | async-start | bytes 3407872 | tf_op jit(solution)/shard_map/reduce_scatter | solution.py:128
  20.4 14.8 %copy-start.9 = (f32[2,128,128]{2,1,0:T(8,128)S(1)}, f32[2,128,128]{2,1,0:T(8,128)}, u32[]{:S(2)}) copy-start(f32[2,128,128]{2,1,0:T(8,128)} %copy.142) | copy-start | bytes 393220
  23.5 3.2 %collective-permute-start = (bf16[2,2,128,128]{3,2,1,0:T(8,128)(2,1)S(1)}, bf16[2,2,128,128]{3,2,1,0:T(8,128)(2,1)S(1)}, u32[]{:S(2)}, u32[]{:S(2)}) collective-permute-start(bf16[2,2,128,128]{3,2,1,0:T(8,128)(2,1)S(1)} %fusion.29), channel_id=1, source_target_pairs={{0,12},{12,0},{24,36},{36,24},{48,60},{60,48},{72,84},{84,72},{96,... | collective-permute-start | bytes 393224 | tf_op jit(solution)/shard_map/ppermute | solution.py:18
  26.7 36.4 %copy-start.15 = (bf16[2,2,128,128]{3,2,1,0:T(8,128)(2,1)}, bf16[2,2,128,128]{3,2,1,0:T(8,128)(2,1)S(1)}, u32[]{:S(2)}) copy-start(bf16[2,2,128,128]{3,2,1,0:T(8,128)(2,1)S(1)} %collective-permute-done) | copy-start | bytes 393220
  27.7 7.4 %collective-permute-start.1 = (bf16[2,2,128,128]{3,2,1,0:T(8,128)(2,1)S(1)}, bf16[2,2,128,128]{3,2,1,0:T(8,128)(2,1)S(1)}, u32[]{:S(2)}, u32[]{:S(2)}) collective-permute-start(bf16[2,2,128,128]{3,2,1,0:T(8,128)(2,1)S(1)} %fusion.73), channel_id=1, source_target_pairs={{0,24},{24,0},{12,36},{36,12},{48,72},{72,48},{60,84},{84,60},{96,... | collective-permute-start | bytes 393224 | tf_op jit(solution)/shard_map/ppermute | solution.py:18
  35.2 28.0 %copy-start.21 = (bf16[2,2,128,128]{3,2,1,0:T(8,128)(2,1)}, bf16[2,2,128,128]{3,2,1,0:T(8,128)(2,1)S(1)}, u32[]{:S(2)}) copy-start(bf16[2,2,128,128]{3,2,1,0:T(8,128)(2,1)S(1)} %collective-permute-done.1) | copy-start | bytes 393220
  35.2 24.4 %copy-start.8 = (f32[2,2,128,128]{3,2,1,0:T(8,128)}, f32[2,2,128,128]{3,2,1,0:T(8,128)S(1)}, u32[]{:S(2)}) copy-start(f32[2,2,128,128]{3,2,1,0:T(8,128)S(1)} %get-tuple-element.10) | copy-start | bytes 786436
  35.2 10.3 %collective-permute-start.2 = (bf16[2,2,128,128]{3,2,1,0:T(8,128)(2,1)S(1)}, bf16[2,2,128,128]{3,2,1,0:T(8,128)(2,1)S(1)}, u32[]{:S(2)}, u32[]{:S(2)}) collective-permute-start(bf16[2,2,128,128]{3,2,1,0:T(8,128)(2,1)S(1)} %get-tuple-element.9), channel_id=1, source_target_pairs={{0,48},{48,0},{12,60},{60,12},{24,72},{72,24},{36,84},{84,36},{96,... | collective-permute-start | bytes 393224 | tf_op jit(solution)/shard_map/ppermute | solution.py:18
  45.6 14.8 %copy-start.13 = (bf16[2,2,128,128]{3,2,1,0:T(8,128)(2,1)}, bf16[2,2,128,128]{3,2,1,0:T(8,128)(2,1)S(1)}, u32[]{:S(2)}) copy-start(bf16[2,2,128,128]{3,2,1,0:T(8,128)(2,1)S(1)} %collective-permute-done.2) | copy-start | bytes 393220
  45.6 14.1 %collective-permute-start.3 = (bf16[2,2,128,128]{3,2,1,0:T(8,128)(2,1)S(1)}, bf16[2,2,128,128]{3,2,1,0:T(8,128)(2,1)S(1)}, u32[]{:S(2)}, u32[]{:S(2)}) collective-permute-start(bf16[2,2,128,128]{3,2,1,0:T(8,128)(2,1)S(1)} %fusion.76), channel_id=1, source_target_pairs={{0,96},{96,0},{12,108},{108,12},{24,120},{120,24},{36,132},{132,36... | collective-permute-start | bytes 393224 | tf_op jit(solution)/shard_map/ppermute | solution.py:18
  59.6 3.5 %copy-start.16 = (bf16[2,2,128,128]{3,2,1,0:T(8,128)(2,1)}, bf16[2,2,128,128]{3,2,1,0:T(8,128)(2,1)S(1)}, u32[]{:S(2)}) copy-start(bf16[2,2,128,128]{3,2,1,0:T(8,128)(2,1)S(1)} %collective-permute-done.3) | copy-start | bytes 393220
  60.4 7.2 %collective-permute-start.4 = (bf16[2,2,128,128]{3,2,1,0:T(8,128)(2,1)}, bf16[2,2,128,128]{3,2,1,0:T(8,128)(2,1)}, u32[]{:S(2)}, u32[]{:S(2)}) collective-permute-start(bf16[2,2,128,128]{3,2,1,0:T(8,128)(2,1)} %fusion.75), channel_id=1, source_target_pairs={{0,192},{192,0},{12,204},{204,12},{24,216},{216,24},{36,228},{228,... | collective-permute-start | bytes 393224 | tf_op jit(solution)/shard_map/ppermute | solution.py:18
  63.2 15.8 %copy-start.22 = (bf16[2,2,128,128]{3,2,1,0:T(8,128)(2,1)S(1)}, bf16[2,2,128,128]{3,2,1,0:T(8,128)(2,1)}, u32[]{:S(2)}) copy-start(bf16[2,2,128,128]{3,2,1,0:T(8,128)(2,1)} %copy-done.21) | copy-start | bytes 393220
  63.2 15.8 %copy-start.14 = (bf16[2,2,128,128]{3,2,1,0:T(8,128)(2,1)S(1)}, bf16[2,2,128,128]{3,2,1,0:T(8,128)(2,1)}, u32[]{:S(2)}) copy-start(bf16[2,2,128,128]{3,2,1,0:T(8,128)(2,1)} %copy-done.13) | copy-start | bytes 393220
  63.2 15.8 %copy-start.17 = (bf16[2,2,128,128]{3,2,1,0:T(8,128)(2,1)S(1)}, bf16[2,2,128,128]{3,2,1,0:T(8,128)(2,1)}, u32[]{:S(2)}) copy-start(bf16[2,2,128,128]{3,2,1,0:T(8,128)(2,1)} %copy-done.16) | copy-start | bytes 393220
  63.2 16.8 %copy-start.10 = (f32[2,128,128]{2,1,0:T(8,128)S(1)}, f32[2,128,128]{2,1,0:T(8,128)}, u32[]{:S(2)}) copy-start(f32[2,128,128]{2,1,0:T(8,128)} %copy.142) | copy-start | bytes 393220
  68.7 11.2 %collective-permute-start.5 = (bf16[2,2,128,128]{3,2,1,0:T(8,128)(2,1)S(1)}, bf16[2,2,128,128]{3,2,1,0:T(8,128)(2,1)S(1)}, u32[]{:S(2)}, u32[]{:S(2)}) collective-permute-start(bf16[2,2,128,128]{3,2,1,0:T(8,128)(2,1)S(1)} %add_convert_fusion), channel_id=1, source_target_pairs={{0,384},{384,0},{12,396},{396,12},{24,408},{408,24},{36,420},{420,... | collective-permute-start | bytes 393224 | tf_op jit(solution)/shard_map/ppermute | solution.py:18
  77.9 3.6 %copy-start.18 = (bf16[6,2,64,64]{3,2,1,0:T(8,128)(2,1)}, bf16[6,2,64,64]{3,2,1,0:T(8,128)(2,1)S(1)}, u32[]{:S(2)}) copy-start(bf16[6,2,64,64]{3,2,1,0:T(8,128)(2,1)S(1)} %fusion.16) | copy-start | bytes 294916
  77.9 2.9 %copy-start.3 = (f32[6,2,128,128]{3,2,1,0:T(8,128)S(1)}, f32[6,2,128,128]{3,2,1,0:T(8,128)}, u32[]{:S(2)}) copy-start(f32[6,2,128,128]{3,2,1,0:T(8,128)} %get-tuple-element.16) | copy-start | bytes 2359300
  80.0 0.9 copy-start.4
  80.9 1.5 copy-start.1
  80.9 1.1 copy-start.6
  80.9 2.2 %copy-start.12 = (bf16[4096,256]{1,0:T(8,128)(2,1)S(1)}, bf16[4096,256]{1,0:T(8,128)(2,1)}, u32[]{:S(2)}) copy-start(bf16[4096,256]{1,0:T(8,128)(2,1)} %param.8) | copy-start | bytes 6291460
  82.5 0.7 copy-start.11
  99.7 6.6 %collective-permute-start.6 = (f32[2,2,2,2,2,64,256]{6,5,4,3,2,1,0:T(8,128)}, f32[2,2,2,2,2,64,256]{6,5,4,3,2,1,0:T(8,128)}, u32[]{:S(2)}, u32[]{:S(2)}) collective-permute-start(f32[2,2,2,2,2,64,256]{6,5,4,3,2,1,0:T(8,128)} %select_bitcast_fusion), channel_id=1, source_target_pairs={{0,12},{12,0},{24,36},{36,24},{48,60},{60,48},{72,84},{84,72},{96,... | collective-permute-start | bytes 6291464 | tf_op jit(solution)/shard_map/ppermute | solution.py:52
  109.8 2.5 %copy-start.7 = (bf16[6,64,2,128]{3,2,1,0:T(2,128)(2,1)S(1)}, bf16[6,64,2,128]{3,2,1,0:T(2,128)(2,1)}, u32[]{:S(2)}) copy-start(bf16[6,64,2,128]{3,2,1,0:T(2,128)(2,1)} %reshape.77) | copy-start | bytes 589828
  109.9 27.5 %collective-permute-start.7 = (f32[2,2,2,2,64,256]{5,4,3,2,1,0:T(8,128)S(1)}, f32[2,2,2,2,64,256]{5,4,3,2,1,0:T(8,128)S(1)}, u32[]{:S(2)}, u32[]{:S(2)}) collective-permute-start(f32[2,2,2,2,64,256]{5,4,3,2,1,0:T(8,128)S(1)} %select_bitcast_fusion.1), channel_id=1, source_target_pairs={{0,24},{12,36},{24,0},{36,12},{48,72},{60,84},{72,48},{84,60},{96,... | collective-permute-start | bytes 3145736 | tf_op jit(solution)/shard_map/ppermute | solution.py:52
  113.1 28.1 %copy-start.19 = (bf16[6,2,64,64]{3,2,1,0:T(8,128)(2,1)S(1)}, bf16[6,2,64,64]{3,2,1,0:T(8,128)(2,1)}, u32[]{:S(2)}) copy-start(bf16[6,2,64,64]{3,2,1,0:T(8,128)(2,1)} %copy-done.18) | copy-start | bytes 294916
  137.6 4.1 %copy-start.5 = (bf16[6,64,2,128]{3,2,1,0:T(2,128)(2,1)S(1)}, bf16[6,64,2,128]{3,2,1,0:T(2,128)(2,1)}, u32[]{:S(2)}) copy-start(bf16[6,64,2,128]{3,2,1,0:T(2,128)(2,1)} %reshape.75) | copy-start | bytes 589828
  137.6 4.1 %copy-start.20 = (bf16[6,2,64,64]{3,2,1,0:T(8,128)(2,1)S(1)}, bf16[6,2,64,64]{3,2,1,0:T(8,128)(2,1)}, u32[]{:S(2)}) copy-start(bf16[6,2,64,64]{3,2,1,0:T(8,128)(2,1)} %fusion.15) | copy-start | bytes 294916
  137.6 4.5 %copy-start.2 = (f32[6,2,128,128]{3,2,1,0:T(8,128)S(1)}, f32[6,2,128,128]{3,2,1,0:T(8,128)}, u32[]{:S(2)}) copy-start(f32[6,2,128,128]{3,2,1,0:T(8,128)} %copy-done.1) | copy-start | bytes 2359300
  137.7 15.7 %collective-permute-start.8 = (f32[2,2,2,64,256]{4,3,2,1,0:T(8,128)S(1)}, f32[2,2,2,64,256]{4,3,2,1,0:T(8,128)S(1)}, u32[]{:S(2)}, u32[]{:S(2)}) collective-permute-start(f32[2,2,2,64,256]{4,3,2,1,0:T(8,128)S(1)} %select_bitcast_fusion.2), channel_id=1, source_target_pairs={{0,192},{12,204},{24,216},{36,228},{48,240},{60,252},{72,264},{84,... | collective-permute-start | bytes 1572872 | tf_op jit(solution)/shard_map/ppermute | solution.py:52
  153.5 15.7 %collective-permute-start.9 = (f32[2,2,64,256]{3,2,1,0:T(8,128)S(1)}, f32[2,2,64,256]{3,2,1,0:T(8,128)S(1)}, u32[]{:S(2)}, u32[]{:S(2)}) collective-permute-start(f32[2,2,64,256]{3,2,1,0:T(8,128)S(1)} %select_bitcast_fusion.3), channel_id=1, source_target_pairs={{0,48},{12,60},{24,72},{36,84},{48,0},{60,12},{72,24},{84,36},{96,... | collective-permute-start | bytes 786440 | tf_op jit(solution)/shard_map/ppermute | solution.py:52
  169.3 9.2 %collective-permute-start.10 = (f32[2,64,256]{2,1,0:T(8,128)S(1)}, f32[2,64,256]{2,1,0:T(8,128)S(1)}, u32[]{:S(2)}, u32[]{:S(2)}) collective-permute-start(f32[2,64,256]{2,1,0:T(8,128)S(1)} %select_bitcast_fusion.4), channel_id=1, source_target_pairs={{0,384},{12,396},{24,408},{36,420},{48,432},{60,444},{72,456},{84,... | collective-permute-start | bytes 393224 | tf_op jit(solution)/shard_map/ppermute | solution.py:52
  178.5 10.7 %collective-permute-start.11 = (f32[64,256]{1,0:T(8,128)S(1)}, f32[64,256]{1,0:T(8,128)S(1)}, u32[]{:S(2)}, u32[]{:S(2)}) collective-permute-start(f32[64,256]{1,0:T(8,128)S(1)} %select_bitcast_fusion.5), channel_id=1, source_target_pairs={{0,96},{12,108},{24,120},{36,132},{48,144},{60,156},{72,168},{84,1... | collective-permute-start | bytes 196616 | tf_op jit(solution)/shard_map/ppermute | solution.py:52
Sparse Core Ops, SparseCore 0:
  101.8 65.9 reduce-scatter.1

commit v3 on v2

--- a/solution.py
+++ b/solution.py
@@ -52,6 +52,49 @@
         acc = kept + lax.ppermute(sent, SEQ, route)
         held.pop(axis)
     return acc.reshape(-1, cols)
+
+
+def grid_scatter(partial, x_count, y_count):
+    count = x_count * y_count * 2
+    cols = partial.shape[1]
+    position = lax.axis_index(SEQ)
+    core = position % 2
+    y = position // 2 % y_count
+    x = position // (2 * y_count)
+    index = lambda a, b, c: a * 2 * y_count + b % y_count * 2 + c
+    acc = partial.reshape(x_count, y_count, 2, partial.shape[0] // count, cols)
+    kept = lax.dynamic_index_in_dim(acc, core, 2, keepdims=False)
+    sent = lax.dynamic_index_in_dim(acc, 1 - core, 2, keepdims=False)
+    acc = kept + lax.ppermute(sent, SEQ, [(i, i ^ 1) for i in range(count)])
+    acc = jnp.where(core == 1, jnp.roll(acc, -1, axis=1), acc)
+    acc = acc.reshape(x_count, y_count // 2, 2, acc.shape[2], cols)
+    label = (y - core) % y_count
+    odd = label % 2
+    route = []
+    for a in range(x_count):
+        for b in range(y_count):
+            for c in range(2):
+                other = ((b - c) % y_count ^ 1) + c
+                route.append((index(a, b, c), index(a, other, c)))
+    kept = lax.dynamic_index_in_dim(acc, odd, 2, keepdims=False)
+    sent = lax.dynamic_index_in_dim(acc, 1 - odd, 2, keepdims=False)
+    acc = kept + lax.ppermute(sent, SEQ, route)
+    total = lax.dynamic_index_in_dim(acc, x, 0, keepdims=False)
+    for shift in range(1, x_count):
+        piece = lax.dynamic_index_in_dim(acc, (x + shift) % x_count, 0, keepdims=False)
+        route = [(index(a, b, c), index((a + shift) % x_count, b, c))
+                 for a in range(x_count) for b in range(y_count) for c in range(2)]
+        total = total + lax.ppermute(piece, SEQ, route)
+    acc = total
+    quarter = label // 2
+    groups = y_count // 2
+    total = lax.dynamic_index_in_dim(acc, quarter, 0, keepdims=False)
+    for shift in range(1, groups):
+        piece = lax.dynamic_index_in_dim(acc, (quarter + shift) % groups, 0, keepdims=False)
+        route = [(index(a, b, c), index(a, b + 2 * shift, c))
+                 for a in range(x_count) for b in range(y_count) for c in range(2)]
+        total = total + lax.ppermute(piece, SEQ, route)
+    return total
 
 
 def local(queries, key_rows, value_rows, out_weight, out_grad, seq_count, head_count_axis):
@@ -126,7 +169,11 @@
     )
     partial_output, weight_partial = lax.optimization_barrier((partial_output, weight_partial))
     output = lax.psum_scatter(partial_output, "head", scatter_dimension=0, tiled=True)
-    weight_grad = halving_scatter(weight_partial, seq_count) * total_rows ** (-0.5)
+    if seq_count == 64:
+        weight_grad = grid_scatter(weight_partial, 4, 8)
+    else:
+        weight_grad = halving_scatter(weight_partial, seq_count)
+    weight_grad = weight_grad * total_rows ** (-0.5)
     return (
         output,
         query_grad.astype(jnp.bfloat16).reshape(flat_shape),

time: 200 us -> 177 us (0.89); the launches traced: 197 us -> 176 us
  waiting for transfers between devices: 77.3 us -> 50.3 us
  starting transfers between devices: 48.5 us -> 56.6 us
  other arithmetic: 16.7 us -> 11.5 us
  local copies, waits for them, and re-layouts: 18.1 us -> 22 us
    ppermute x6 -> x8, waiting for transfers between devices: 55.6 us -> 28 us  [the longest x6 14.8 us: grid_scatter(): total = total + lax.ppermute(piece, SEQ, route)]
    ppermute x6 -> x8, starting transfers between devices: 20.1 us -> 28.2 us  [the longest x6 24.3 us: grid_scatter(): total = total + lax.ppermute(piece, SEQ, route)]
    select_n x6 -> x1, other arithmetic: 4.3 us -> 0.37 us  [grid_scatter(): acc = jnp.where(core == 1, jnp.roll(acc, -1, axis=1), acc)]
    squeeze x0 -> x4, local copies, waits for them, and re-layouts: none -> 3.38 us  [the longest x1 3.2 us: grid_scatter(): sent = lax.dynamic_index_in_dim(acc, 1 - core, 2, keepdims=False)]
  transfers between devices with their start and end apart: 13 -> 15, of which waited for: 10 -> 10; matrix products, arithmetic and copies ran while one was open for 9% -> 14% of each run, Pallas kernels for 0% -> 0%
where the time goes in v3:
time: 177 us; the launch traced here: 176 us
  starting transfers between devices  56.6 us (32%)
  waiting for transfers between devices  50.3 us (28%)
  local copies, waits for them, and re-layouts  22 us (12%)
  matrix products  20.7 us (12%)
  between operations  14.9 us (8%)
  other arithmetic  11.5 us (6%)
    ppermute x6, starting transfers between devices, swapped(): return lax.ppermute(block, SEQ, route)  28.4 us
    ppermute x6, starting transfers between devices, grid_scatter(): total = total + lax.ppermute(piece, SEQ, route)  24.3 us
    ppermute x6, waiting for transfers between devices, swapped(): return lax.ppermute(block, SEQ, route)  22.3 us
    ppermute x6, waiting for transfers between devices, grid_scatter(): total = total + lax.ppermute(piece, SEQ, route)  14.8 us
    ppermute x1, waiting for transfers between devices, grid_scatter(): acc = kept + lax.ppermute(sent, SEQ, route)  13.2 us
    optimization_barrier x1, local copies, waits for them, and re-layouts, local(): lax.optimization_barrier((partial_output, weight_partial))  5.61 us
    dot_general x1, matrix products, local(): lax.dot_general(out_grad, attention, (((0,), (0,)), ((), ())), preferred_...  4.22 us
    convert_element_type x6, other arithmetic, local(): totals.astype(jnp.bfloat16)  3.87 us
  transfers between devices with their start and end apart: 15, of which 10 were waited for; matrix products, arithmetic and copies ran while one was open for 14% of the time, Pallas kernels for 0%

profile of v3, /device:TPU:6, one launch (start us, length us, event | category | flops | bytes accessed | tf_op | source)
XLA Modules:
  0.0 175.9 jit_solution(12671459319962576105)
XLA Ops:
  7.2 1.1 reshape.54
  8.4 1.0 reshape.55
  9.3 1.7 reshape.56
  11.0 3.2 %convolution_convert_fusion.1 = bf16[384,256]{1,0:T(8,128)(2,1)} fusion(bf16[384,4096]{1,0:T(8,128)(2,1)S(1)} %copy-done, bf16[4096,256]{1,0:T(8,128)(2,1)} %param.8), kind=kOutput, calls=%fused_computation.37 | convolution fusion | flops 805404672 | bytes 5439488 | tf_op jit(solution)/shard_map/dot_general | solution.py:112
  14.2 1.7 reshape.57
  15.9 2.8 %fusion.79 = (f32[2,128,128]{1,2,0:T(8,128)}, f32[6,2,128,128]{2,3,1,0:T(8,128)}) fusion(bf16[6,64,2,128]{3,2,1,0:T(2,128)(2,1)S(1)} %reshape.54, bf16[6,64,2,128]{3,2,1,0:T(2,128)(2,1)} %reshape.57), kind=kOutput, calls=%fused_computation.129 | convolution fusion | flops 25329664 | bytes 1310720 | tf_op jit(solution)/shard_map/cthd,cthe->chde/dot_general | solution.py:119
  18.7 1.7 copy.110
  20.4 2.2 %fusion.80 = (f32[2,128,128]{2,1,0:T(8,128)S(1)}, f32[6,2,128,128]{3,2,1,0:T(8,128)}) fusion(bf16[6,64,2,128]{3,2,1,0:T(2,128)(2,1)} %reshape.56, bf16[6,64,2,128]{3,2,1,0:T(2,128)(2,1)S(1)} %reshape.55), kind=kOutput, calls=%fused_computation.130 | convolution fusion | flops 25329664 | bytes 1310720 | tf_op jit(solution)/shard_map/cshd,cshe->chde/dot_general | solution.py:116
  22.5 0.9 fusion.23
  23.5 1.9 %collective-permute-start = (bf16[2,2,128,128]{3,2,1,0:T(8,128)(2,1)S(1)}, bf16[2,2,128,128]{3,2,1,0:T(8,128)(2,1)S(1)}, u32[]{:S(2)}, u32[]{:S(2)}) collective-permute-start(bf16[2,2,128,128]{3,2,1,0:T(8,128)(2,1)S(1)} %fusion.23), channel_id=1, source_target_pairs={{0,12},{12,0},{24,36},{36,24},{48,60},{60,48},{72,84},{84,72},{96,... | collective-permute-start | bytes 393224 | tf_op jit(solution)/shard_map/ppermute | solution.py:18
  25.4 1.3 collective-permute-done
  26.7 1.0 fusion.67
  27.7 3.5 %collective-permute-start.1 = (bf16[2,2,128,128]{3,2,1,0:T(8,128)(2,1)S(1)}, bf16[2,2,128,128]{3,2,1,0:T(8,128)(2,1)S(1)}, u32[]{:S(2)}, u32[]{:S(2)}) collective-permute-start(bf16[2,2,128,128]{3,2,1,0:T(8,128)(2,1)S(1)} %fusion.67), channel_id=1, source_target_pairs={{0,24},{24,0},{12,36},{36,12},{48,72},{72,48},{60,84},{84,60},{96,... | collective-permute-start | bytes 393224 | tf_op jit(solution)/shard_map/ppermute | solution.py:18
  31.2 3.9 %collective-permute-done.1 = bf16[2,2,128,128]{3,2,1,0:T(8,128)(2,1)S(1)} collective-permute-done((bf16[2,2,128,128]{3,2,1,0:T(8,128)(2,1)S(1)}, bf16[2,2,128,128]{3,2,1,0:T(8,128)(2,1)S(1)}, u32[]{:S(2)}, u32[]{:S(2)}) %collective-permute-start.1) | collective-permute-done | bytes 131104 | tf_op jit(solution)/shard_map/ppermute | solution.py:18
  35.2 4.5 %collective-permute-start.2 = (bf16[2,2,128,128]{3,2,1,0:T(8,128)(2,1)S(1)}, bf16[2,2,128,128]{3,2,1,0:T(8,128)(2,1)S(1)}, u32[]{:S(2)}, u32[]{:S(2)}) collective-permute-start(bf16[2,2,128,128]{3,2,1,0:T(8,128)(2,1)S(1)} %get-tuple-element.9), channel_id=1, source_target_pairs={{0,48},{48,0},{12,60},{60,12},{24,72},{72,24},{36,84},{84,36},{96,... | collective-permute-start | bytes 393224 | tf_op jit(solution)/shard_map/ppermute | solution.py:18
  39.7 5.8 %collective-permute-done.2 = bf16[2,2,128,128]{3,2,1,0:T(8,128)(2,1)S(1)} collective-permute-done((bf16[2,2,128,128]{3,2,1,0:T(8,128)(2,1)S(1)}, bf16[2,2,128,128]{3,2,1,0:T(8,128)(2,1)S(1)}, u32[]{:S(2)}, u32[]{:S(2)}) %collective-permute-start.2) | collective-permute-done | bytes 131104 | tf_op jit(solution)/shard_map/ppermute | solution.py:18
  45.6 7.7 %collective-permute-start.3 = (bf16[2,2,128,128]{3,2,1,0:T(8,128)(2,1)S(1)}, bf16[2,2,128,128]{3,2,1,0:T(8,128)(2,1)S(1)}, u32[]{:S(2)}, u32[]{:S(2)}) collective-permute-start(bf16[2,2,128,128]{3,2,1,0:T(8,128)(2,1)S(1)} %fusion.72), channel_id=1, source_target_pairs={{0,96},{96,0},{12,108},{108,12},{24,120},{120,24},{36,132},{132,36... | collective-permute-start | bytes 393224 | tf_op jit(solution)/shard_map/ppermute | solution.py:18
  53.3 6.3 %collective-permute-done.3 = bf16[2,2,128,128]{3,2,1,0:T(8,128)(2,1)S(1)} collective-permute-done((bf16[2,2,128,128]{3,2,1,0:T(8,128)(2,1)S(1)}, bf16[2,2,128,128]{3,2,1,0:T(8,128)(2,1)S(1)}, u32[]{:S(2)}, u32[]{:S(2)}) %collective-permute-start.3) | collective-permute-done | bytes 131104 | tf_op jit(solution)/shard_map/ppermute | solution.py:18
  59.6 0.7 fusion.71
  60.4 2.7 %collective-permute-start.4 = (bf16[2,2,128,128]{3,2,1,0:T(8,128)(2,1)}, bf16[2,2,128,128]{3,2,1,0:T(8,128)(2,1)}, u32[]{:S(2)}, u32[]{:S(2)}) collective-permute-start(bf16[2,2,128,128]{3,2,1,0:T(8,128)(2,1)} %fusion.71), channel_id=1, source_target_pairs={{0,192},{192,0},{12,204},{204,12},{24,216},{216,24},{36,228},{228,... | collective-permute-start | bytes 393224 | tf_op jit(solution)/shard_map/ppermute | solution.py:18
  63.2 4.3 %collective-permute-done.4 = bf16[2,2,128,128]{3,2,1,0:T(8,128)(2,1)} collective-permute-done((bf16[2,2,128,128]{3,2,1,0:T(8,128)(2,1)}, bf16[2,2,128,128]{3,2,1,0:T(8,128)(2,1)}, u32[]{:S(2)}, u32[]{:S(2)}) %collective-permute-start.4) | collective-permute-done | bytes 131104 | tf_op jit(solution)/shard_map/ppermute | solution.py:18
  67.5 1.2 add_convert_fusion
  68.7 8.0 %collective-permute-start.5 = (bf16[2,2,128,128]{3,2,1,0:T(8,128)(2,1)S(1)}, bf16[2,2,128,128]{3,2,1,0:T(8,128)(2,1)S(1)}, u32[]{:S(2)}, u32[]{:S(2)}) collective-permute-start(bf16[2,2,128,128]{3,2,1,0:T(8,128)(2,1)S(1)} %add_convert_fusion), channel_id=1, source_target_pairs={{0,384},{384,0},{12,396},{396,12},{24,408},{408,24},{36,420},{420,... | collective-permute-start | bytes 393224 | tf_op jit(solution)/shard_map/ppermute | solution.py:18
  77.0 1.0 convert_element_type.84
  78.1 0.9 convert_element_type.92
  79.7 0.8 fusion.30
  82.1 0.7 copy-done.11
  82.8 2.7 %convolution_convert_fusion = bf16[384,4096]{1,0:T(8,128)(2,1)} fusion(bf16[4096,256]{1,0:T(8,128)(2,1)S(1)} %copy-done.12, bf16[48,8,2,128]{3,2,1,0:T(2,128)(2,1)S(1)} %bitcast.110), kind=kOutput, calls=%fused_computation | convolution fusion | flops 806879232 | bytes 5439488 | tf_op jit(solution)/shard_map/dot_general | solution.py:148
  85.5 4.2 %convolution_bitcast_fusion = f32[4096,256]{0,1:T(8,128)} fusion(bf16[384,4096]{1,0:T(8,128)(2,1)S(1)} %copy-done, bf16[48,8,2,128]{3,2,1,0:T(2,128)(2,1)} %bitcast.111), kind=kOutput, calls=%fused_computation.1 | convolution fusion | flops 805306368 | bytes 7536640 | tf_op jit(solution)/shard_map/dot_general | solution.py:167
  89.8 5.6 %copy.135 = f32[4096,256]{1,0:T(8,128)} copy(f32[4096,256]{0,1:T(8,128)} %convolution_bitcast_fusion) | data formatting | bytes 8388608 | tf_op jit(solution)/shard_map/optimization_barrier | solution.py:170
  95.4 3.2 %dynamic-slice_bitcast_fusion = f32[4,8,64,256]{3,2,1,0:T(8,128)} fusion(f32[4,8,2,64,256]{4,3,2,1,0:T(8,128)} %bitcast.103, s32[]{:T(128)S(6)} %select_n.207), kind=kLoop, calls=%fused_computation.4 | loop fusion | bytes 4194308 | tf_op jit(solution)/shard_map/jit(dynamic_index_in_dim)/squeeze | solution.py:67
  98.6 1.9 %collective-permute-start.6 = (f32[4,8,64,256]{3,2,1,0:T(8,128)}, f32[4,8,64,256]{3,2,1,0:T(8,128)}, u32[]{:S(2)}, u32[]{:S(2)}) collective-permute-start(f32[4,8,64,256]{3,2,1,0:T(8,128)} %dynamic-slice_bitcast_fusion), channel_id=1, source_target_pairs={{0,12},{12,0},{24,36},{36,24},{48,60},{60,48},{72,84},{84,72},{96,... | collective-permute-start | bytes 6291464 | tf_op jit(solution)/shard_map/ppermute | solution.py:68
  100.7 1.9 %fusion.13 = bf16[6,2,64,64]{3,2,1,0:T(8,128)(2,1)} fusion(pred[64,64]{1,0:T(8,128)(4,1)S(1)} %iota_compare_fusion, bf16[6,64,2,128]{3,2,1,0:T(2,128)(2,1)} %reshape.57, bf16[6,64,2,128]{3,2,1,0:T(2,128)(2,1)} %reshape.56), kind=kOutput, calls=%fused_computation.31 | convolution fusion | flops 12730368 | bytes 495616 | tf_op jit(solution)/shard_map/cthe,cshe->chts/dot_general | solution.py:151
  102.7 1.7 copy.122
  104.3 1.4 reduce-window_subtract_fusion
  106.8 2.1 %bitcast_add_fusion = f32[4,8,64,256]{3,2,1,0:T(8,128)S(1)} fusion(f32[4,8,64,256]{3,2,1,0:T(8,128)} %collective-permute-done.6, f32[4,8,2,64,256]{4,3,2,1,0:T(8,128)S(1)} %bitcast.104, s32[]{:T(128)S(6)} %select_n.206), kind=kLoop, calls=%fused_computation.3 | loop fusion | flops 524288 | bytes 6291460 | tf_op jit(solution)/shard_map/add | solution.py:68
  109.6 2.1 %collective-permute-start.7 = (f32[4,4,64,256]{3,2,1,0:T(8,128)S(1)}, f32[4,4,64,256]{3,2,1,0:T(8,128)S(1)}, u32[]{:S(2)}, u32[]{:S(2)}) collective-permute-start(f32[4,4,64,256]{3,2,1,0:T(8,128)S(1)} %dynamic-slice_bitcast_fusion.1), channel_id=1, source_target_pairs={{0,24},{12,180},{24,0},{36,60},{48,72},{60,36},{72,48},{84,108},{9... | collective-permute-start | bytes 3145736 | tf_op jit(solution)/shard_map/ppermute | solution.py:81
  113.2 13.2 %collective-permute-done.7 = f32[4,4,64,256]{3,2,1,0:T(8,128)S(1)} collective-permute-done((f32[4,4,64,256]{3,2,1,0:T(8,128)S(1)}, f32[4,4,64,256]{3,2,1,0:T(8,128)S(1)}, u32[]{:S(2)}, u32[]{:S(2)}) %collective-permute-start.7) | collective-permute-done | bytes 1048608 | tf_op jit(solution)/shard_map/ppermute | solution.py:81
  126.7 6.0 %collective-permute-start.8 = (f32[4,64,256]{2,1,0:T(8,128)S(1)}, f32[4,64,256]{2,1,0:T(8,128)S(1)}, u32[]{:S(2)}, u32[]{:S(2)}) collective-permute-start(f32[4,64,256]{2,1,0:T(8,128)S(1)} %get-tuple-element.13), channel_id=1, source_target_pairs={{0,192},{12,204},{24,216},{36,228},{48,240},{60,252},{72,264},{84,... | collective-permute-start | bytes 786440 | tf_op jit(solution)/shard_map/ppermute | solution.py:87
  132.7 1.9 %collective-permute-start.10 = (f32[4,64,256]{2,1,0:T(8,128)S(1)}, f32[4,64,256]{2,1,0:T(8,128)S(1)}, u32[]{:S(2)}, u32[]{:S(2)}) collective-permute-start(f32[4,64,256]{2,1,0:T(8,128)S(1)} %get-tuple-element.14), channel_id=1, source_target_pairs={{0,576},{12,588},{24,600},{36,612},{48,624},{60,636},{72,648},{84,... | collective-permute-start | bytes 786440 | tf_op jit(solution)/shard_map/ppermute | solution.py:87
  134.6 3.4 %collective-permute-start.9 = (f32[4,64,256]{2,1,0:T(8,128)S(1)}, f32[4,64,256]{2,1,0:T(8,128)S(1)}, u32[]{:S(2)}, u32[]{:S(2)}) collective-permute-start(f32[4,64,256]{2,1,0:T(8,128)S(1)} %get-tuple-element.15), channel_id=1, source_target_pairs={{0,384},{12,396},{24,408},{36,420},{48,432},{60,444},{72,456},{84,... | collective-permute-start | bytes 786440 | tf_op jit(solution)/shard_map/ppermute | solution.py:87
  139.2 10.9 %collective-permute-done.10 = f32[4,64,256]{2,1,0:T(8,128)S(1)} collective-permute-done((f32[4,64,256]{2,1,0:T(8,128)S(1)}, f32[4,64,256]{2,1,0:T(8,128)S(1)}, u32[]{:S(2)}, u32[]{:S(2)}) %collective-permute-start.10) | collective-permute-done | bytes 262176 | tf_op jit(solution)/shard_map/ppermute | solution.py:87
  150.3 1.9 %collective-permute-start.11 = (f32[64,256]{1,0:T(8,128)S(1)}, f32[64,256]{1,0:T(8,128)S(1)}, u32[]{:S(2)}, u32[]{:S(2)}) collective-permute-start(f32[64,256]{1,0:T(8,128)S(1)} %get-tuple-element.16), channel_id=1, source_target_pairs={{0,48},{12,60},{24,72},{36,84},{48,96},{60,108},{72,120},{84,132},... | collective-permute-start | bytes 196616 | tf_op jit(solution)/shard_map/ppermute | solution.py:96
  152.2 6.0 %collective-permute-start.13 = (f32[64,256]{1,0:T(8,128)S(1)}, f32[64,256]{1,0:T(8,128)S(1)}, u32[]{:S(2)}, u32[]{:S(2)}) collective-permute-start(f32[64,256]{1,0:T(8,128)S(1)} %get-tuple-element.17), channel_id=1, source_target_pairs={{0,144},{12,156},{24,168},{36,180},{48,0},{60,12},{72,24},{84,36},... | collective-permute-start | bytes 196616 | tf_op jit(solution)/shard_map/ppermute | solution.py:96
  158.2 5.0 %collective-permute-start.12 = (f32[64,256]{1,0:T(8,128)S(1)}, f32[64,256]{1,0:T(8,128)S(1)}, u32[]{:S(2)}, u32[]{:S(2)}) collective-permute-start(f32[64,256]{1,0:T(8,128)S(1)} %get-tuple-element.18), channel_id=1, source_target_pairs={{0,96},{12,108},{24,120},{36,132},{48,144},{60,156},{72,168},{84,1... | collective-permute-start | bytes 196616 | tf_op jit(solution)/shard_map/ppermute | solution.py:96
  163.2 0.8 copy_bitcast_fusion
  164.2 0.7 copy.205
  164.9 3.5 %collective-permute-done.12 = f32[64,256]{1,0:T(8,128)S(1)} collective-permute-done((f32[64,256]{1,0:T(8,128)S(1)}, f32[64,256]{1,0:T(8,128)S(1)}, u32[]{:S(2)}, u32[]{:S(2)}) %collective-permute-start.12) | collective-permute-done | bytes 65568 | tf_op jit(solution)/shard_map/ppermute | solution.py:96
  (88 shorter events, 8.4 us)
Async XLA Ops:
  7.2 3.8 %copy-start = (bf16[384,4096]{1,0:T(8,128)(2,1)S(1)}, bf16[384,4096]{1,0:T(8,128)(2,1)}, u32[]{:S(2)}) copy-start(bf16[384,4096]{1,0:T(8,128)(2,1)} %param.9) | copy-start | bytes 9437188
  7.2 161.9 %reduce-scatter.2.cloned.1.call-start = ((), (), s32[]{:S(2)}) async-start(), calls=%async_computation.1 | async-start | bytes 3407872 | tf_op jit(solution)/shard_map/reduce_scatter | solution.py:171
  20.4 14.8 %copy-start.9 = (f32[2,128,128]{2,1,0:T(8,128)S(1)}, f32[2,128,128]{2,1,0:T(8,128)}, u32[]{:S(2)}) copy-start(f32[2,128,128]{2,1,0:T(8,128)} %copy.110) | copy-start | bytes 393220
  23.5 3.2 %collective-permute-start = (bf16[2,2,128,128]{3,2,1,0:T(8,128)(2,1)S(1)}, bf16[2,2,128,128]{3,2,1,0:T(8,128)(2,1)S(1)}, u32[]{:S(2)}, u32[]{:S(2)}) collective-permute-start(bf16[2,2,128,128]{3,2,1,0:T(8,128)(2,1)S(1)} %fusion.23), channel_id=1, source_target_pairs={{0,12},{12,0},{24,36},{36,24},{48,60},{60,48},{72,84},{84,72},{96,... | collective-permute-start | bytes 393224 | tf_op jit(solution)/shard_map/ppermute | solution.py:18
  26.7 36.4 %copy-start.15 = (bf16[2,2,128,128]{3,2,1,0:T(8,128)(2,1)}, bf16[2,2,128,128]{3,2,1,0:T(8,128)(2,1)S(1)}, u32[]{:S(2)}) copy-start(bf16[2,2,128,128]{3,2,1,0:T(8,128)(2,1)S(1)} %collective-permute-done) | copy-start | bytes 393220
  27.7 7.4 %collective-permute-start.1 = (bf16[2,2,128,128]{3,2,1,0:T(8,128)(2,1)S(1)}, bf16[2,2,128,128]{3,2,1,0:T(8,128)(2,1)S(1)}, u32[]{:S(2)}, u32[]{:S(2)}) collective-permute-start(bf16[2,2,128,128]{3,2,1,0:T(8,128)(2,1)S(1)} %fusion.67), channel_id=1, source_target_pairs={{0,24},{24,0},{12,36},{36,12},{48,72},{72,48},{60,84},{84,60},{96,... | collective-permute-start | bytes 393224 | tf_op jit(solution)/shard_map/ppermute | solution.py:18
  35.1 28.0 %copy-start.21 = (bf16[2,2,128,128]{3,2,1,0:T(8,128)(2,1)}, bf16[2,2,128,128]{3,2,1,0:T(8,128)(2,1)S(1)}, u32[]{:S(2)}) copy-start(bf16[2,2,128,128]{3,2,1,0:T(8,128)(2,1)S(1)} %collective-permute-done.1) | copy-start | bytes 393220
  35.2 24.4 %copy-start.8 = (f32[2,2,128,128]{3,2,1,0:T(8,128)}, f32[2,2,128,128]{3,2,1,0:T(8,128)S(1)}, u32[]{:S(2)}) copy-start(f32[2,2,128,128]{3,2,1,0:T(8,128)S(1)} %get-tuple-element.10) | copy-start | bytes 786436
  35.2 10.3 %collective-permute-start.2 = (bf16[2,2,128,128]{3,2,1,0:T(8,128)(2,1)S(1)}, bf16[2,2,128,128]{3,2,1,0:T(8,128)(2,1)S(1)}, u32[]{:S(2)}, u32[]{:S(2)}) collective-permute-start(bf16[2,2,128,128]{3,2,1,0:T(8,128)(2,1)S(1)} %get-tuple-element.9), channel_id=1, source_target_pairs={{0,48},{48,0},{12,60},{60,12},{24,72},{72,24},{36,84},{84,36},{96,... | collective-permute-start | bytes 393224 | tf_op jit(solution)/shard_map/ppermute | solution.py:18
  45.5 14.8 %copy-start.13 = (bf16[2,2,128,128]{3,2,1,0:T(8,128)(2,1)}, bf16[2,2,128,128]{3,2,1,0:T(8,128)(2,1)S(1)}, u32[]{:S(2)}) copy-start(bf16[2,2,128,128]{3,2,1,0:T(8,128)(2,1)S(1)} %collective-permute-done.2) | copy-start | bytes 393220
  45.6 14.1 %collective-permute-start.3 = (bf16[2,2,128,128]{3,2,1,0:T(8,128)(2,1)S(1)}, bf16[2,2,128,128]{3,2,1,0:T(8,128)(2,1)S(1)}, u32[]{:S(2)}, u32[]{:S(2)}) collective-permute-start(bf16[2,2,128,128]{3,2,1,0:T(8,128)(2,1)S(1)} %fusion.72), channel_id=1, source_target_pairs={{0,96},{96,0},{12,108},{108,12},{24,120},{120,24},{36,132},{132,36... | collective-permute-start | bytes 393224 | tf_op jit(solution)/shard_map/ppermute | solution.py:18
  59.6 3.5 %copy-start.16 = (bf16[2,2,128,128]{3,2,1,0:T(8,128)(2,1)}, bf16[2,2,128,128]{3,2,1,0:T(8,128)(2,1)S(1)}, u32[]{:S(2)}) copy-start(bf16[2,2,128,128]{3,2,1,0:T(8,128)(2,1)S(1)} %collective-permute-done.3) | copy-start | bytes 393220
  60.4 7.2 %collective-permute-start.4 = (bf16[2,2,128,128]{3,2,1,0:T(8,128)(2,1)}, bf16[2,2,128,128]{3,2,1,0:T(8,128)(2,1)}, u32[]{:S(2)}, u32[]{:S(2)}) collective-permute-start(bf16[2,2,128,128]{3,2,1,0:T(8,128)(2,1)} %fusion.71), channel_id=1, source_target_pairs={{0,192},{192,0},{12,204},{204,12},{24,216},{216,24},{36,228},{228,... | collective-permute-start | bytes 393224 | tf_op jit(solution)/shard_map/ppermute | solution.py:18
  63.1 14.8 %copy-start.22 = (bf16[2,2,128,128]{3,2,1,0:T(8,128)(2,1)S(1)}, bf16[2,2,128,128]{3,2,1,0:T(8,128)(2,1)}, u32[]{:S(2)}) copy-start(bf16[2,2,128,128]{3,2,1,0:T(8,128)(2,1)} %copy-done.21) | copy-start | bytes 393220
  63.1 14.9 %copy-start.14 = (bf16[2,2,128,128]{3,2,1,0:T(8,128)(2,1)S(1)}, bf16[2,2,128,128]{3,2,1,0:T(8,128)(2,1)}, u32[]{:S(2)}) copy-start(bf16[2,2,128,128]{3,2,1,0:T(8,128)(2,1)} %copy-done.13) | copy-start | bytes 393220
  63.2 14.9 %copy-start.17 = (bf16[2,2,128,128]{3,2,1,0:T(8,128)(2,1)S(1)}, bf16[2,2,128,128]{3,2,1,0:T(8,128)(2,1)}, u32[]{:S(2)}) copy-start(bf16[2,2,128,128]{3,2,1,0:T(8,128)(2,1)} %copy-done.16) | copy-start | bytes 393220
  63.2 16.5 %copy-start.10 = (f32[2,128,128]{2,1,0:T(8,128)S(1)}, f32[2,128,128]{2,1,0:T(8,128)}, u32[]{:S(2)}) copy-start(f32[2,128,128]{2,1,0:T(8,128)} %copy.110) | copy-start | bytes 393220
  68.7 10.9 %collective-permute-start.5 = (bf16[2,2,128,128]{3,2,1,0:T(8,128)(2,1)S(1)}, bf16[2,2,128,128]{3,2,1,0:T(8,128)(2,1)S(1)}, u32[]{:S(2)}, u32[]{:S(2)}) collective-permute-start(bf16[2,2,128,128]{3,2,1,0:T(8,128)(2,1)S(1)} %add_convert_fusion), channel_id=1, source_target_pairs={{0,384},{384,0},{12,396},{396,12},{24,408},{408,24},{36,420},{420,... | collective-permute-start | bytes 393224 | tf_op jit(solution)/shard_map/ppermute | solution.py:18
  76.9 4.1 %copy-start.18 = (bf16[6,2,64,64]{3,2,1,0:T(8,128)(2,1)}, bf16[6,2,64,64]{3,2,1,0:T(8,128)(2,1)S(1)}, u32[]{:S(2)}) copy-start(bf16[6,2,64,64]{3,2,1,0:T(8,128)(2,1)S(1)} %fusion.14) | copy-start | bytes 294916
  77.0 3.5 %copy-start.4 = (f32[6,2,128,128]{3,2,1,0:T(8,128)S(1)}, f32[6,2,128,128]{3,2,1,0:T(8,128)}, u32[]{:S(2)}) copy-start(f32[6,2,128,128]{3,2,1,0:T(8,128)} %get-tuple-element.22) | copy-start | bytes 2359300
  80.6 1.6 copy-start.1
  80.6 1.1 copy-start.6
  80.6 2.2 %copy-start.12 = (bf16[4096,256]{1,0:T(8,128)(2,1)S(1)}, bf16[4096,256]{1,0:T(8,128)(2,1)}, u32[]{:S(2)}) copy-start(bf16[4096,256]{1,0:T(8,128)(2,1)} %param.8) | copy-start | bytes 6291460
  82.1 0.7 copy-start.11
  98.6 7.9 %collective-permute-start.6 = (f32[4,8,64,256]{3,2,1,0:T(8,128)}, f32[4,8,64,256]{3,2,1,0:T(8,128)}, u32[]{:S(2)}, u32[]{:S(2)}) collective-permute-start(f32[4,8,64,256]{3,2,1,0:T(8,128)} %dynamic-slice_bitcast_fusion), channel_id=1, source_target_pairs={{0,12},{12,0},{24,36},{36,24},{48,60},{60,48},{72,84},{84,72},{96,... | collective-permute-start | bytes 6291464 | tf_op jit(solution)/shard_map/ppermute | solution.py:68
  104.3 2.5 %copy-start.3 = (f32[4096,256]{1,0:T(8,128)S(1)}, f32[4096,256]{1,0:T(8,128)}, u32[]{:S(2)}) copy-start(f32[4096,256]{1,0:T(8,128)} %copy.135) | copy-start | bytes 12582916
  109.4 2.2 %copy-start.7 = (bf16[6,64,2,128]{3,2,1,0:T(2,128)(2,1)S(1)}, bf16[6,64,2,128]{3,2,1,0:T(2,128)(2,1)}, u32[]{:S(2)}) copy-start(bf16[6,64,2,128]{3,2,1,0:T(2,128)(2,1)} %reshape.56) | copy-start | bytes 589828
  109.4 2.5 %copy-start.5 = (bf16[6,64,2,128]{3,2,1,0:T(2,128)(2,1)S(1)}, bf16[6,64,2,128]{3,2,1,0:T(2,128)(2,1)}, u32[]{:S(2)}) copy-start(bf16[6,64,2,128]{3,2,1,0:T(2,128)(2,1)} %reshape.57) | copy-start | bytes 589828
  109.5 2.5 %copy-start.19 = (bf16[6,2,64,64]{3,2,1,0:T(8,128)(2,1)S(1)}, bf16[6,2,64,64]{3,2,1,0:T(8,128)(2,1)}, u32[]{:S(2)}) copy-start(bf16[6,2,64,64]{3,2,1,0:T(8,128)(2,1)} %copy-done.18) | copy-start | bytes 294916
  109.5 2.7 %copy-start.2 = (f32[6,2,128,128]{3,2,1,0:T(8,128)S(1)}, f32[6,2,128,128]{3,2,1,0:T(8,128)}, u32[]{:S(2)}) copy-start(f32[6,2,128,128]{3,2,1,0:T(8,128)} %copy-done.1) | copy-start | bytes 2359300
  109.6 16.8 %collective-permute-start.7 = (f32[4,4,64,256]{3,2,1,0:T(8,128)S(1)}, f32[4,4,64,256]{3,2,1,0:T(8,128)S(1)}, u32[]{:S(2)}, u32[]{:S(2)}) collective-permute-start(f32[4,4,64,256]{3,2,1,0:T(8,128)S(1)} %dynamic-slice_bitcast_fusion.1), channel_id=1, source_target_pairs={{0,24},{12,180},{24,0},{36,60},{48,72},{60,36},{72,48},{84,108},{9... | collective-permute-start | bytes 3145736 | tf_op jit(solution)/shard_map/ppermute | solution.py:81
  113.2 24.8 %copy-start.20 = (bf16[6,2,64,64]{3,2,1,0:T(8,128)(2,1)S(1)}, bf16[6,2,64,64]{3,2,1,0:T(8,128)(2,1)}, u32[]{:S(2)}) copy-start(bf16[6,2,64,64]{3,2,1,0:T(8,128)(2,1)} %fusion.13) | copy-start | bytes 294916
  126.7 12.6 %collective-permute-start.8 = (f32[4,64,256]{2,1,0:T(8,128)S(1)}, f32[4,64,256]{2,1,0:T(8,128)S(1)}, u32[]{:S(2)}, u32[]{:S(2)}) collective-permute-start(f32[4,64,256]{2,1,0:T(8,128)S(1)} %get-tuple-element.13), channel_id=1, source_target_pairs={{0,192},{12,204},{24,216},{36,228},{48,240},{60,252},{72,264},{84,... | collective-permute-start | bytes 786440 | tf_op jit(solution)/shard_map/ppermute | solution.py:87
  132.7 17.5 %collective-permute-start.10 = (f32[4,64,256]{2,1,0:T(8,128)S(1)}, f32[4,64,256]{2,1,0:T(8,128)S(1)}, u32[]{:S(2)}, u32[]{:S(2)}) collective-permute-start(f32[4,64,256]{2,1,0:T(8,128)S(1)} %get-tuple-element.14), channel_id=1, source_target_pairs={{0,576},{12,588},{24,600},{36,612},{48,624},{60,636},{72,648},{84,... | collective-permute-start | bytes 786440 | tf_op jit(solution)/shard_map/ppermute | solution.py:87
  134.6 15.5 %collective-permute-start.9 = (f32[4,64,256]{2,1,0:T(8,128)S(1)}, f32[4,64,256]{2,1,0:T(8,128)S(1)}, u32[]{:S(2)}, u32[]{:S(2)}) collective-permute-start(f32[4,64,256]{2,1,0:T(8,128)S(1)} %get-tuple-element.15), channel_id=1, source_target_pairs={{0,384},{12,396},{24,408},{36,420},{48,432},{60,444},{72,456},{84,... | collective-permute-start | bytes 786440 | tf_op jit(solution)/shard_map/ppermute | solution.py:87
  150.3 14.6 %collective-permute-start.11 = (f32[64,256]{1,0:T(8,128)S(1)}, f32[64,256]{1,0:T(8,128)S(1)}, u32[]{:S(2)}, u32[]{:S(2)}) collective-permute-start(f32[64,256]{1,0:T(8,128)S(1)} %get-tuple-element.16), channel_id=1, source_target_pairs={{0,48},{12,60},{24,72},{36,84},{48,96},{60,108},{72,120},{84,132},... | collective-permute-start | bytes 196616 | tf_op jit(solution)/shard_map/ppermute | solution.py:96
  152.2 12.7 %collective-permute-start.13 = (f32[64,256]{1,0:T(8,128)S(1)}, f32[64,256]{1,0:T(8,128)S(1)}, u32[]{:S(2)}, u32[]{:S(2)}) collective-permute-start(f32[64,256]{1,0:T(8,128)S(1)} %get-tuple-element.17), channel_id=1, source_target_pairs={{0,144},{12,156},{24,168},{36,180},{48,0},{60,12},{72,24},{84,36},... | collective-permute-start | bytes 196616 | tf_op jit(solution)/shard_map/ppermute | solution.py:96
  158.2 10.2 %collective-permute-start.12 = (f32[64,256]{1,0:T(8,128)S(1)}, f32[64,256]{1,0:T(8,128)S(1)}, u32[]{:S(2)}, u32[]{:S(2)}) collective-permute-start(f32[64,256]{1,0:T(8,128)S(1)} %get-tuple-element.18), channel_id=1, source_target_pairs={{0,96},{12,108},{24,120},{36,132},{48,144},{60,156},{72,168},{84,1... | collective-permute-start | bytes 196616 | tf_op jit(solution)/shard_map/ppermute | solution.py:96
Sparse Core Ops, SparseCore 0:
  89.9 66.0 reduce-scatter.1

commit v4 on v3

--- a/solution.py
+++ b/solution.py
@@ -52,6 +52,10 @@
         acc = kept + lax.ppermute(sent, SEQ, route)
         held.pop(axis)
     return acc.reshape(-1, cols)
+
+
+def wire(block, route):
+    return lax.ppermute(block.astype(jnp.bfloat16), SEQ, route).astype(jnp.float32)
 
 
 def grid_scatter(partial, x_count, y_count):
@@ -78,13 +82,13 @@
                 route.append((index(a, b, c), index(a, other, c)))
     kept = lax.dynamic_index_in_dim(acc, odd, 2, keepdims=False)
     sent = lax.dynamic_index_in_dim(acc, 1 - odd, 2, keepdims=False)
-    acc = kept + lax.ppermute(sent, SEQ, route)
+    acc = kept + wire(sent, route)
     total = lax.dynamic_index_in_dim(acc, x, 0, keepdims=False)
     for shift in range(1, x_count):
         piece = lax.dynamic_index_in_dim(acc, (x + shift) % x_count, 0, keepdims=False)
         route = [(index(a, b, c), index((a + shift) % x_count, b, c))
                  for a in range(x_count) for b in range(y_count) for c in range(2)]
-        total = total + lax.ppermute(piece, SEQ, route)
+        total = total + wire(piece, route)
     acc = total
     quarter = label // 2
     groups = y_count // 2
@@ -93,7 +97,7 @@
         piece = lax.dynamic_index_in_dim(acc, (quarter + shift) % groups, 0, keepdims=False)
         route = [(index(a, b, c), index(a, b + 2 * shift, c))
                  for a in range(x_count) for b in range(y_count) for c in range(2)]
-        total = total + lax.ppermute(piece, SEQ, route)
+        total = total + wire(piece, route)
     return total
 
 
@@ -119,8 +123,20 @@
     query_pairs = jnp.einsum(
         "cthd,cthe->chde", query_blocks, grad_blocks, preferred_element_type=jnp.float32
     )
-    own_state = jnp.sum(key_value, 0)
-    own_pairs = jnp.sum(query_pairs, 0)
+    own_state = jnp.stack([
+        lax.dot_general(
+            key_rows[:, h * HD:(h + 1) * HD], value_rows[:, h * HD:(h + 1) * HD],
+            (((0,), (0,)), ((), ())), preferred_element_type=jnp.float32,
+        )
+        for h in range(head_count)
+    ])
+    own_pairs = jnp.stack([
+        lax.dot_general(
+            queries[:, h * HD:(h + 1) * HD], grad_rows[:, h * HD:(h + 1) * HD],
+            (((0,), (0,)), ((), ())), preferred_element_type=jnp.float32,
+        )
+        for h in range(head_count)
+    ])
     position = lax.axis_index(SEQ)
     level_count = seq_count.bit_length() - 1
     inflow = jnp.zeros_like(own_state)
@@ -164,11 +180,11 @@
         "chts,cthe->cshe", weights, grad_blocks, preferred_element_type=jnp.float32
     )
     value_grad = value_grad + factor * state_product("cshd,chde->cshe", key_blocks, later_parts)
+    partial_output, attention = lax.optimization_barrier((partial_output, attention))
+    output = lax.psum_scatter(partial_output, "head", scatter_dimension=0, tiled=True)
     weight_partial = lax.dot_general(
         out_grad, attention, (((0,), (0,)), ((), ())), preferred_element_type=jnp.float32
     )
-    partial_output, weight_partial = lax.optimization_barrier((partial_output, weight_partial))
-    output = lax.psum_scatter(partial_output, "head", scatter_dimension=0, tiled=True)
     if seq_count == 64:
         weight_grad = grid_scatter(weight_partial, 4, 8)
     else:

time: 177 us -> 164 us (0.927); the launches traced: 176 us -> 161 us
  waiting for transfers between devices: 50.3 us -> 31.2 us
  local copies, waits for them, and re-layouts: 22 us -> 24.6 us
  matrix products: 20.7 us -> 23.1 us
    ppermute x7, waiting for transfers between devices: 28 us -> 13.4 us  [wire(): lax.ppermute(block.astype(jnp.bfloat16), SEQ, route).astype(jnp.float32)]
    unnamed x47 -> x70, local copies, waits for them, and re-layouts: 2.44 us -> 8.28 us
    optimization_barrier x1 -> x0, local copies, waits for them, and re-layouts: 5.61 us -> none  [local(): lax.optimization_barrier((partial_output, weight_partial))]
    dot_general x0 -> x1, local copies, waits for them, and re-layouts: none -> 5.6 us  [local(): lax.dot_general(out_grad, attention, (((0,), (0,)), ((), ())), preferred_...]
    ppermute x6, waiting for transfers between devices: 22.3 us -> 17.8 us  [swapped(): return lax.ppermute(block, SEQ, route)]
    dot_general x0 -> x4, matrix products: none -> 2.89 us  [the longest x2 2.44 us: local(): lax.dot_general(key_rows[:, h * HD:(h + 1) * HD], value_rows[:, h * HD:(h...]
    ppermute x7, starting transfers between devices: 26.3 us -> 24.5 us  [wire(): lax.ppermute(block.astype(jnp.bfloat16), SEQ, route).astype(jnp.float32)]
  transfers between devices with their start and end apart: 15 -> 15, of which waited for: 10 -> 9; matrix products, arithmetic and copies ran while one was open for 14% -> 25% of each run, Pallas kernels for 0% -> 0%
where the time goes in v4:
time: 164 us; the launch traced here: 161 us
  starting transfers between devices  54.9 us (33%)
  waiting for transfers between devices  31.2 us (19%)
  local copies, waits for them, and re-layouts  24.6 us (15%)
  matrix products  23.1 us (14%)
  between operations  14.8 us (9%)
  other arithmetic  12.3 us (8%)
    ppermute x6, starting transfers between devices, swapped(): return lax.ppermute(block, SEQ, route)  28.5 us
    ppermute x7, starting transfers between devices, wire(): lax.ppermute(block.astype(jnp.bfloat16), SEQ, route).astype(jnp.float32)  24.5 us
    ppermute x6, waiting for transfers between devices, swapped(): return lax.ppermute(block, SEQ, route)  17.8 us
    ppermute x7, waiting for transfers between devices, wire(): lax.ppermute(block.astype(jnp.bfloat16), SEQ, route).astype(jnp.float32)  13.4 us
    unnamed x70, local copies, waits for them, and re-layouts  8.28 us
    dot_general x1, local copies, waits for them, and re-layouts, local(): lax.dot_general(out_grad, attention, (((0,), (0,)), ((), ())), preferred_...  5.6 us
    dot_general x1, matrix products, local(): lax.dot_general(out_grad, attention, (((0,), (0,)), ((), ())), preferred_...  4.22 us
    convert_element_type x6, other arithmetic, local(): totals.astype(jnp.bfloat16)  3.73 us
  transfers between devices with their start and end apart: 15, of which 9 were waited for; matrix products, arithmetic and copies ran while one was open for 25% of the time, Pallas kernels for 0%

profile of v4, /device:TPU:6, one launch (start us, length us, event | category | flops | bytes accessed | tf_op | source)
XLA Modules:
  0.0 161.0 jit_solution(8154827127979351299)
XLA Ops:
  7.2 1.3 convolution_bitcast_fusion.5
  8.5 1.1 convolution_bitcast_fusion.6
  9.7 2.6 %convolution_convert_fusion.1 = bf16[384,256]{1,0:T(8,128)(2,1)S(1)} fusion(bf16[384,4096]{1,0:T(8,128)(2,1)S(1)} %copy-done, bf16[4096,256]{1,0:T(8,128)(2,1)} %param.8), kind=kOutput, calls=%fused_computation.37 | convolution fusion | flops 805404672 | bytes 5439488 | tf_op jit(solution)/shard_map/dot_general | solution.py:116
  13.1 1.9 %collective-permute-start = (bf16[2,2,128,128]{3,2,1,0:T(8,128)(2,1)S(1)}, bf16[2,2,128,128]{3,2,1,0:T(8,128)(2,1)S(1)}, u32[]{:S(2)}, u32[]{:S(2)}) collective-permute-start(bf16[2,2,128,128]{3,2,1,0:T(8,128)(2,1)S(1)} %fusion.24), channel_id=1, source_target_pairs={{0,12},{12,0},{24,36},{36,24},{48,60},{60,48},{72,84},{84,72},{96,... | collective-permute-start | bytes 393224 | tf_op jit(solution)/shard_map/ppermute | solution.py:18
  15.0 1.3 collective-permute-done
  16.3 3.5 %collective-permute-start.1 = (bf16[2,2,128,128]{3,2,1,0:T(8,128)(2,1)S(1)}, bf16[2,2,128,128]{3,2,1,0:T(8,128)(2,1)S(1)}, u32[]{:S(2)}, u32[]{:S(2)}) collective-permute-start(bf16[2,2,128,128]{3,2,1,0:T(8,128)(2,1)S(1)} %fusion.77), channel_id=1, source_target_pairs={{0,24},{24,0},{12,36},{36,12},{48,72},{72,48},{60,84},{84,60},{96,... | collective-permute-start | bytes 393224 | tf_op jit(solution)/shard_map/ppermute | solution.py:18
  19.9 3.9 %collective-permute-done.1 = bf16[2,2,128,128]{3,2,1,0:T(8,128)(2,1)S(1)} collective-permute-done((bf16[2,2,128,128]{3,2,1,0:T(8,128)(2,1)S(1)}, bf16[2,2,128,128]{3,2,1,0:T(8,128)(2,1)S(1)}, u32[]{:S(2)}, u32[]{:S(2)}) %collective-permute-start.1) | collective-permute-done | bytes 131104 | tf_op jit(solution)/shard_map/ppermute | solution.py:18
  23.9 4.5 %collective-permute-start.2 = (bf16[2,2,128,128]{3,2,1,0:T(8,128)(2,1)S(1)}, bf16[2,2,128,128]{3,2,1,0:T(8,128)(2,1)S(1)}, u32[]{:S(2)}, u32[]{:S(2)}) collective-permute-start(bf16[2,2,128,128]{3,2,1,0:T(8,128)(2,1)S(1)} %get-tuple-element.9), channel_id=1, source_target_pairs={{0,48},{48,0},{12,60},{60,12},{24,72},{72,24},{36,84},{84,36},{96,... | collective-permute-start | bytes 393224 | tf_op jit(solution)/shard_map/ppermute | solution.py:18
  28.4 5.8 %collective-permute-done.2 = bf16[2,2,128,128]{3,2,1,0:T(8,128)(2,1)S(1)} collective-permute-done((bf16[2,2,128,128]{3,2,1,0:T(8,128)(2,1)S(1)}, bf16[2,2,128,128]{3,2,1,0:T(8,128)(2,1)S(1)}, u32[]{:S(2)}, u32[]{:S(2)}) %collective-permute-start.2) | collective-permute-done | bytes 131104 | tf_op jit(solution)/shard_map/ppermute | solution.py:18
  34.9 7.7 %collective-permute-start.3 = (bf16[2,2,128,128]{3,2,1,0:T(8,128)(2,1)}, bf16[2,2,128,128]{3,2,1,0:T(8,128)(2,1)}, u32[]{:S(2)}, u32[]{:S(2)}) collective-permute-start(bf16[2,2,128,128]{3,2,1,0:T(8,128)(2,1)} %fusion.82), channel_id=1, source_target_pairs={{0,96},{96,0},{12,108},{108,12},{24,120},{120,24},{36,132},{132,36... | collective-permute-start | bytes 393224 | tf_op jit(solution)/shard_map/ppermute | solution.py:18
  42.6 1.0 reshape.66
  43.6 1.1 reshape.65
  44.7 4.6 %collective-permute-done.3 = bf16[2,2,128,128]{3,2,1,0:T(8,128)(2,1)} collective-permute-done((bf16[2,2,128,128]{3,2,1,0:T(8,128)(2,1)}, bf16[2,2,128,128]{3,2,1,0:T(8,128)(2,1)}, u32[]{:S(2)}, u32[]{:S(2)}) %collective-permute-start.3) | collective-permute-done | bytes 131104 | tf_op jit(solution)/shard_map/ppermute | solution.py:18
  49.3 1.7 %fusion.81 = bf16[2,2,128,128]{3,2,1,0:T(8,128)(2,1)} fusion(bf16[2,2,128,128]{3,2,1,0:T(8,128)(2,1)} %collective-permute-done.3, f32[2,2,128,128]{3,2,1,0:T(8,128)} %copy-done.10, bf16[2,2,128,128]{3,2,1,0:T(8,128)(2,1)} %copy-done.14), kind=kLoop, calls=%fused_computation.135 | loop fusion | flops 327680 | bytes 655360 | tf_op jit(solution)/shard_map/convert_element_type | solution.py:146
  51.0 2.7 %collective-permute-start.4 = (bf16[2,2,128,128]{3,2,1,0:T(8,128)(2,1)}, bf16[2,2,128,128]{3,2,1,0:T(8,128)(2,1)}, u32[]{:S(2)}, u32[]{:S(2)}) collective-permute-start(bf16[2,2,128,128]{3,2,1,0:T(8,128)(2,1)} %fusion.81), channel_id=1, source_target_pairs={{0,192},{192,0},{12,204},{204,12},{24,216},{216,24},{36,228},{228,... | collective-permute-start | bytes 393224 | tf_op jit(solution)/shard_map/ppermute | solution.py:18
  53.8 1.2 fusion.51
  55.0 1.0 reshape.64
  56.0 2.2 %collective-permute-done.4 = bf16[2,2,128,128]{3,2,1,0:T(8,128)(2,1)} collective-permute-done((bf16[2,2,128,128]{3,2,1,0:T(8,128)(2,1)}, bf16[2,2,128,128]{3,2,1,0:T(8,128)(2,1)}, u32[]{:S(2)}, u32[]{:S(2)}) %collective-permute-start.4) | collective-permute-done | bytes 131104 | tf_op jit(solution)/shard_map/ppermute | solution.py:18
  58.2 1.2 add_convert_fusion
  59.4 8.1 %collective-permute-start.5 = (bf16[2,2,128,128]{3,2,1,0:T(8,128)(2,1)S(1)}, bf16[2,2,128,128]{3,2,1,0:T(8,128)(2,1)S(1)}, u32[]{:S(2)}, u32[]{:S(2)}) collective-permute-start(bf16[2,2,128,128]{3,2,1,0:T(8,128)(2,1)S(1)} %add_convert_fusion), channel_id=1, source_target_pairs={{0,384},{384,0},{12,396},{396,12},{24,408},{408,24},{36,420},{420,... | collective-permute-start | bytes 393224 | tf_op jit(solution)/shard_map/ppermute | solution.py:18
  67.8 1.0 convert_element_type.147
  68.9 1.1 convert_element_type.153
  69.9 1.0 convert_element_type.155
  74.9 2.6 %convolution_convert_fusion = bf16[384,4096]{1,0:T(8,128)(2,1)} fusion(bf16[4096,256]{1,0:T(8,128)(2,1)S(1)} %copy-done.13, bf16[48,8,2,128]{3,2,1,0:T(2,128)(2,1)S(1)} %bitcast.124), kind=kOutput, calls=%fused_computation | convolution fusion | flops 806879232 | bytes 5439488 | tf_op jit(solution)/shard_map/dot_general | solution.py:164
  77.5 1.6 %copy.133 = bf16[48,8,2,128]{3,1,2,0:T(8,128)(2,1)} copy(bf16[48,8,2,128]{3,2,1,0:T(2,128)(2,1)} %bitcast.125) | data formatting | bytes 393216
  79.2 1.7 %reshape.68 = bf16[6,64,2,128]{3,2,1,0:T(2,128)(2,1)} reshape(bf16[384,256]{1,0:T(8,128)(2,1)} %copy-done.24) | data formatting | bytes 393216 | tf_op jit(solution)/shard_map/reshape | solution.py:119
  80.8 4.2 %convolution_bitcast_fusion = f32[4096,256]{0,1:T(8,128)} fusion(bf16[384,256]{1,0:T(8,128)(2,1)} %bitcast.129, bf16[384,4096]{1,0:T(8,128)(2,1)S(1)} %copy-done), kind=kOutput, calls=%fused_computation.1 | convolution fusion | flops 805306368 | bytes 7536640 | tf_op jit(solution)/shard_map/dot_general | solution.py:185
  85.1 5.6 %copy.72 = f32[4096,256]{1,0:T(8,128)} copy(f32[4096,256]{0,1:T(8,128)} %convolution_bitcast_fusion) | data formatting | bytes 8388608 | tf_op jit(solution)/shard_map/dot_general | solution.py:185
  90.7 3.3 %dynamic-slice_bitcast_fusion = f32[4,8,64,256]{3,2,1,0:T(8,128)} fusion(f32[4,8,2,64,256]{4,3,2,1,0:T(8,128)} %bitcast.120, s32[]{:T(128)S(6)} %select_n.207), kind=kLoop, calls=%fused_computation.4 | loop fusion | bytes 4194308 | tf_op jit(solution)/shard_map/jit(dynamic_index_in_dim)/squeeze | solution.py:71
  93.9 1.9 %collective-permute-start.6 = (f32[4,8,64,256]{3,2,1,0:T(8,128)}, f32[4,8,64,256]{3,2,1,0:T(8,128)}, u32[]{:S(2)}, u32[]{:S(2)}) collective-permute-start(f32[4,8,64,256]{3,2,1,0:T(8,128)} %dynamic-slice_bitcast_fusion), channel_id=1, source_target_pairs={{0,12},{12,0},{24,36},{36,24},{48,60},{60,48},{72,84},{84,72},{96,... | collective-permute-start | bytes 6291464 | tf_op jit(solution)/shard_map/ppermute | solution.py:72
  95.9 0.9 fusion.13
  96.8 2.2 %convolution_bitcast_fusion.1 = f32[6,2,128,128]{2,3,1,0:T(8,128)} fusion(bf16[6,64,2,128]{3,2,1,0:T(2,128)(2,1)} %reshape.68, bf16[6,64,2,128]{3,2,1,0:T(2,128)(2,1)S(1)} %reshape.64), kind=kOutput, calls=%fused_computation.8 | convolution fusion | flops 25165824 | bytes 1179648 | tf_op jit(solution)/shard_map/cthd,cthe->chde/dot_general | solution.py:123
  99.0 1.9 %fusion.30 = f32[2,128,128]{2,1,0:T(8,128)} fusion(f32[2,2,128,128]{3,2,1,0:T(8,128)} %copy-done.22, f32[2,2,128,128]{3,2,1,0:T(8,128)} %copy-done.21, f32[2,2,128,128]{3,2,1,0:T(8,128)} %copy-done.20, f32[2,2,128,128]{3,2,1,0:T(8,128)} %copy-done.19, f32[2,2,128,128]{3,2,1,0:T(8,128)} %copy-done.18, f32[2,2,128,128]{3,2,1,0:T(8,128)} %copy-done.17, ...), kind=kLoop, calls=%fused_computation.66 | loop fusion | flops 425984 | bytes 1048582 | tf_op jit(solution)/shard_map/sub | solution.py:152
  100.9 1.6 %copy.57 = f32[2,128,128]{1,2,0:T(8,128)} copy(f32[2,128,128]{2,1,0:T(8,128)} %fusion.30) | data formatting | bytes 262144 | tf_op jit(solution)/shard_map/sub | solution.py:152
  102.6 1.6 %fusion.44 = f32[6,2,128,64]{2,3,1,0:T(8,128)S(1)} fusion(bf16[6,64,2,128]{3,2,1,0:T(2,128)(2,1)} %reshape.68, f32[6,2,128,128]{3,2,1,0:T(8,128)} %copy-done.1), kind=kOutput, calls=%fused_computation.93 | convolution fusion | flops 25362432 | bytes 1376256 | tf_op jit(solution)/shard_map/cthe,chde->cthd/dot_general | solution.py:28
  104.2 1.9 %fusion.5 = f32[6,64,2,128]{3,1,2,0:T(8,128)S(1)} fusion(f32[6,2,128,64]{2,3,1,0:T(8,128)S(1)} %fusion.44, bf16[6,64,2,128]{3,2,1,0:T(2,128)(2,1)} %reshape.68, f32[6,2,128,128]{3,2,1,0:T(8,128)} %copy-done.1), kind=kOutput, calls=%fused_computation.23 | convolution fusion | flops 26148864 | bytes 1769472 | tf_op jit(solution)/shard_map/cthe,chde->cthd/dot_general | solution.py:29
  107.0 1.6 copy-done.2
  108.5 2.0 %bitcast_add_fusion = f32[4,8,64,256]{3,2,1,0:T(8,128)S(1)} fusion(f32[4,8,64,256]{3,2,1,0:T(8,128)} %collective-permute-done.6, f32[4,8,2,64,256]{4,3,2,1,0:T(8,128)S(1)} %bitcast.121, s32[]{:T(128)S(6)} %select_n.206), kind=kLoop, calls=%fused_computation.3 | loop fusion | flops 524288 | bytes 6291460 | tf_op jit(solution)/shard_map/add | solution.py:72
  111.2 1.9 %collective-permute-start.7 = (bf16[4,4,64,256]{3,2,1,0:T(8,128)(2,1)S(1)}, bf16[4,4,64,256]{3,2,1,0:T(8,128)(2,1)S(1)}, u32[]{:S(2)}, u32[]{:S(2)}) collective-permute-start(bf16[4,4,64,256]{3,2,1,0:T(8,128)(2,1)S(1)} %fusion.20), channel_id=1, source_target_pairs={{0,24},{12,180},{24,0},{36,60},{48,72},{60,36},{72,48},{84,108},{9... | collective-permute-start | bytes 1572872 | tf_op jit(solution)/shard_map/ppermute | solution.py:58
  113.9 8.4 %collective-permute-done.7 = bf16[4,4,64,256]{3,2,1,0:T(8,128)(2,1)S(1)} collective-permute-done((bf16[4,4,64,256]{3,2,1,0:T(8,128)(2,1)S(1)}, bf16[4,4,64,256]{3,2,1,0:T(8,128)(2,1)S(1)}, u32[]{:S(2)}, u32[]{:S(2)}) %collective-permute-start.7) | collective-permute-done | bytes 524320 | tf_op jit(solution)/shard_map/ppermute | solution.py:58
  122.5 3.4 %collective-permute-start.10 = (bf16[4,64,256]{2,1,0:T(8,128)(2,1)S(1)}, bf16[4,64,256]{2,1,0:T(8,128)(2,1)S(1)}, u32[]{:S(2)}, u32[]{:S(2)}) collective-permute-start(bf16[4,64,256]{2,1,0:T(8,128)(2,1)S(1)} %get-tuple-element.12), channel_id=1, source_target_pairs={{0,576},{12,588},{24,600},{36,612},{48,624},{60,636},{72,648},{84,... | collective-permute-start | bytes 393224 | tf_op jit(solution)/shard_map/ppermute | solution.py:58
  125.9 4.8 %collective-permute-start.9 = (bf16[4,64,256]{2,1,0:T(8,128)(2,1)S(1)}, bf16[4,64,256]{2,1,0:T(8,128)(2,1)S(1)}, u32[]{:S(2)}, u32[]{:S(2)}) collective-permute-start(bf16[4,64,256]{2,1,0:T(8,128)(2,1)S(1)} %get-tuple-element.13), channel_id=1, source_target_pairs={{0,384},{12,396},{24,408},{36,420},{48,432},{60,444},{72,456},{84,... | collective-permute-start | bytes 393224 | tf_op jit(solution)/shard_map/ppermute | solution.py:58
  130.8 2.5 %collective-permute-start.8 = (bf16[4,64,256]{2,1,0:T(8,128)(2,1)S(1)}, bf16[4,64,256]{2,1,0:T(8,128)(2,1)S(1)}, u32[]{:S(2)}, u32[]{:S(2)}) collective-permute-start(bf16[4,64,256]{2,1,0:T(8,128)(2,1)S(1)} %get-tuple-element.11), channel_id=1, source_target_pairs={{0,192},{12,204},{24,216},{36,228},{48,240},{60,252},{72,264},{84,... | collective-permute-start | bytes 393224 | tf_op jit(solution)/shard_map/ppermute | solution.py:58
  133.6 2.4 %collective-permute-done.9 = bf16[4,64,256]{2,1,0:T(8,128)(2,1)S(1)} collective-permute-done((bf16[4,64,256]{2,1,0:T(8,128)(2,1)S(1)}, bf16[4,64,256]{2,1,0:T(8,128)(2,1)S(1)}, u32[]{:S(2)}, u32[]{:S(2)}) %collective-permute-start.9) | collective-permute-done | bytes 131104 | tf_op jit(solution)/shard_map/ppermute | solution.py:58
  136.0 2.6 %collective-permute-done.8 = bf16[4,64,256]{2,1,0:T(8,128)(2,1)S(1)} collective-permute-done((bf16[4,64,256]{2,1,0:T(8,128)(2,1)S(1)}, bf16[4,64,256]{2,1,0:T(8,128)(2,1)S(1)}, u32[]{:S(2)}, u32[]{:S(2)}) %collective-permute-start.8) | collective-permute-done | bytes 131104 | tf_op jit(solution)/shard_map/ppermute | solution.py:58
  138.6 1.9 %collective-permute-start.13 = (bf16[64,256]{1,0:T(8,128)(2,1)S(1)}, bf16[64,256]{1,0:T(8,128)(2,1)S(1)}, u32[]{:S(2)}, u32[]{:S(2)}) collective-permute-start(bf16[64,256]{1,0:T(8,128)(2,1)S(1)} %get-tuple-element.15), channel_id=1, source_target_pairs={{0,144},{12,156},{24,168},{36,180},{48,0},{60,12},{72,24},{84,36},... | collective-permute-start | bytes 98312 | tf_op jit(solution)/shard_map/ppermute | solution.py:58
  140.6 5.0 %collective-permute-start.12 = (bf16[64,256]{1,0:T(8,128)(2,1)S(1)}, bf16[64,256]{1,0:T(8,128)(2,1)S(1)}, u32[]{:S(2)}, u32[]{:S(2)}) collective-permute-start(bf16[64,256]{1,0:T(8,128)(2,1)S(1)} %get-tuple-element.16), channel_id=1, source_target_pairs={{0,96},{12,108},{24,120},{36,132},{48,144},{60,156},{72,168},{84,1... | collective-permute-start | bytes 98312 | tf_op jit(solution)/shard_map/ppermute | solution.py:58
  145.5 4.8 %collective-permute-start.11 = (bf16[64,256]{1,0:T(8,128)(2,1)S(1)}, bf16[64,256]{1,0:T(8,128)(2,1)S(1)}, u32[]{:S(2)}, u32[]{:S(2)}) collective-permute-start(bf16[64,256]{1,0:T(8,128)(2,1)S(1)} %get-tuple-element.14), channel_id=1, source_target_pairs={{0,48},{12,60},{24,72},{36,84},{48,96},{60,108},{72,120},{84,132},... | collective-permute-start | bytes 98312 | tf_op jit(solution)/shard_map/ppermute | solution.py:58
  (115 shorter events, 12.1 us)
Async XLA Ops:
  7.2 2.5 %copy-start = (bf16[384,4096]{1,0:T(8,128)(2,1)S(1)}, bf16[384,4096]{1,0:T(8,128)(2,1)}, u32[]{:S(2)}) copy-start(bf16[384,4096]{1,0:T(8,128)(2,1)} %param.9) | copy-start | bytes 9437188
  7.2 146.9 %reduce-scatter.2.cloned.1.call-start = ((), (), s32[]{:S(2)}) async-start(), calls=%async_computation.1 | async-start | bytes 3407872 | tf_op jit(solution)/shard_map/reduce_scatter | solution.py:184
  9.7 2.6 %copy-start.23 = (bf16[384,256]{1,0:T(8,128)(2,1)S(1)}, bf16[384,256]{1,0:T(8,128)(2,1)}, u32[]{:S(2)}) copy-start(bf16[384,256]{1,0:T(8,128)(2,1)} %param.5) | copy-start | bytes 589828
  12.3 0.7 copy-start.24
  12.6 7.3 %copy-start.28 = (f32[128,128]{0,1:T(8,128)}, f32[128,128]{0,1:T(8,128)S(1)}, u32[]{:S(2)}) copy-start(f32[128,128]{0,1:T(8,128)S(1)} %fusion.66) | copy-start | bytes 196612
  12.8 7.0 %copy-start.29 = (f32[128,128]{0,1:T(8,128)}, f32[128,128]{0,1:T(8,128)S(1)}, u32[]{:S(2)}) copy-start(f32[128,128]{0,1:T(8,128)S(1)} %fusion.68) | copy-start | bytes 196612
  13.1 3.2 %collective-permute-start = (bf16[2,2,128,128]{3,2,1,0:T(8,128)(2,1)S(1)}, bf16[2,2,128,128]{3,2,1,0:T(8,128)(2,1)S(1)}, u32[]{:S(2)}, u32[]{:S(2)}) collective-permute-start(bf16[2,2,128,128]{3,2,1,0:T(8,128)(2,1)S(1)} %fusion.24), channel_id=1, source_target_pairs={{0,12},{12,0},{24,36},{36,24},{48,60},{60,48},{72,84},{84,72},{96,... | collective-permute-start | bytes 393224 | tf_op jit(solution)/shard_map/ppermute | solution.py:18
  16.3 18.6 %copy-start.16 = (bf16[2,2,128,128]{3,2,1,0:T(8,128)(2,1)}, bf16[2,2,128,128]{3,2,1,0:T(8,128)(2,1)S(1)}, u32[]{:S(2)}) copy-start(bf16[2,2,128,128]{3,2,1,0:T(8,128)(2,1)S(1)} %collective-permute-done) | copy-start | bytes 393220
  16.3 7.4 %collective-permute-start.1 = (bf16[2,2,128,128]{3,2,1,0:T(8,128)(2,1)S(1)}, bf16[2,2,128,128]{3,2,1,0:T(8,128)(2,1)S(1)}, u32[]{:S(2)}, u32[]{:S(2)}) collective-permute-start(bf16[2,2,128,128]{3,2,1,0:T(8,128)(2,1)S(1)} %fusion.77), channel_id=1, source_target_pairs={{0,24},{24,0},{12,36},{36,12},{48,72},{72,48},{60,84},{84,60},{96,... | collective-permute-start | bytes 393224 | tf_op jit(solution)/shard_map/ppermute | solution.py:18
  23.8 11.1 %copy-start.30 = (bf16[2,2,128,128]{3,2,1,0:T(8,128)(2,1)}, bf16[2,2,128,128]{3,2,1,0:T(8,128)(2,1)S(1)}, u32[]{:S(2)}) copy-start(bf16[2,2,128,128]{3,2,1,0:T(8,128)(2,1)S(1)} %collective-permute-done.1) | copy-start | bytes 393220
  23.8 11.0 %copy-start.10 = (f32[2,2,128,128]{3,2,1,0:T(8,128)}, f32[2,2,128,128]{3,2,1,0:T(8,128)S(1)}, u32[]{:S(2)}) copy-start(f32[2,2,128,128]{3,2,1,0:T(8,128)S(1)} %get-tuple-element.10) | copy-start | bytes 786436
  23.9 10.3 %collective-permute-start.2 = (bf16[2,2,128,128]{3,2,1,0:T(8,128)(2,1)S(1)}, bf16[2,2,128,128]{3,2,1,0:T(8,128)(2,1)S(1)}, u32[]{:S(2)}, u32[]{:S(2)}) collective-permute-start(bf16[2,2,128,128]{3,2,1,0:T(8,128)(2,1)S(1)} %get-tuple-element.9), channel_id=1, source_target_pairs={{0,48},{48,0},{12,60},{60,12},{24,72},{72,24},{36,84},{84,36},{96,... | collective-permute-start | bytes 393224 | tf_op jit(solution)/shard_map/ppermute | solution.py:18
  34.2 8.4 %copy-start.14 = (bf16[2,2,128,128]{3,2,1,0:T(8,128)(2,1)}, bf16[2,2,128,128]{3,2,1,0:T(8,128)(2,1)S(1)}, u32[]{:S(2)}) copy-start(bf16[2,2,128,128]{3,2,1,0:T(8,128)(2,1)S(1)} %collective-permute-done.2) | copy-start | bytes 393220
  34.9 14.4 %collective-permute-start.3 = (bf16[2,2,128,128]{3,2,1,0:T(8,128)(2,1)}, bf16[2,2,128,128]{3,2,1,0:T(8,128)(2,1)}, u32[]{:S(2)}, u32[]{:S(2)}) collective-permute-start(bf16[2,2,128,128]{3,2,1,0:T(8,128)(2,1)} %fusion.82), channel_id=1, source_target_pairs={{0,96},{96,0},{12,108},{108,12},{24,120},{120,24},{36,132},{132,36... | collective-permute-start | bytes 393224 | tf_op jit(solution)/shard_map/ppermute | solution.py:18
  43.6 10.1 %copy-start.4 = (bf16[6,64,2,128]{3,2,1,0:T(2,128)(2,1)}, bf16[6,64,2,128]{3,2,1,0:T(2,128)(2,1)S(1)}, u32[]{:S(2)}) copy-start(bf16[6,64,2,128]{3,2,1,0:T(2,128)(2,1)S(1)} %reshape.66) | copy-start | bytes 589828
  51.0 7.2 %collective-permute-start.4 = (bf16[2,2,128,128]{3,2,1,0:T(8,128)(2,1)}, bf16[2,2,128,128]{3,2,1,0:T(8,128)(2,1)}, u32[]{:S(2)}, u32[]{:S(2)}) collective-permute-start(bf16[2,2,128,128]{3,2,1,0:T(8,128)(2,1)} %fusion.81), channel_id=1, source_target_pairs={{0,192},{192,0},{12,204},{204,12},{24,216},{216,24},{36,228},{228,... | collective-permute-start | bytes 393224 | tf_op jit(solution)/shard_map/ppermute | solution.py:18
  56.0 12.8 %copy-start.31 = (bf16[2,2,128,128]{3,2,1,0:T(8,128)(2,1)S(1)}, bf16[2,2,128,128]{3,2,1,0:T(8,128)(2,1)}, u32[]{:S(2)}) copy-start(bf16[2,2,128,128]{3,2,1,0:T(8,128)(2,1)} %copy-done.30) | copy-start | bytes 393220
  56.0 12.8 %copy-start.15 = (bf16[2,2,128,128]{3,2,1,0:T(8,128)(2,1)S(1)}, bf16[2,2,128,128]{3,2,1,0:T(8,128)(2,1)}, u32[]{:S(2)}) copy-start(bf16[2,2,128,128]{3,2,1,0:T(8,128)(2,1)} %copy-done.14) | copy-start | bytes 393220
  59.4 13.1 %copy-start.3 = (f32[6,2,128,128]{3,2,1,0:T(8,128)S(1)}, f32[6,2,128,128]{3,2,1,0:T(8,128)}, u32[]{:S(2)}) copy-start(f32[6,2,128,128]{3,2,1,0:T(8,128)} %fusion.51) | copy-start | bytes 2359300
  59.4 11.6 %collective-permute-start.5 = (bf16[2,2,128,128]{3,2,1,0:T(8,128)(2,1)S(1)}, bf16[2,2,128,128]{3,2,1,0:T(8,128)(2,1)S(1)}, u32[]{:S(2)}, u32[]{:S(2)}) collective-permute-start(bf16[2,2,128,128]{3,2,1,0:T(8,128)(2,1)S(1)} %add_convert_fusion), channel_id=1, source_target_pairs={{0,384},{384,0},{12,396},{396,12},{24,408},{408,24},{36,420},{420,... | collective-permute-start | bytes 393224 | tf_op jit(solution)/shard_map/ppermute | solution.py:18
  67.7 5.4 %copy-start.25 = (bf16[6,2,64,64]{3,2,1,0:T(8,128)(2,1)}, bf16[6,2,64,64]{3,2,1,0:T(8,128)(2,1)S(1)}, u32[]{:S(2)}) copy-start(bf16[6,2,64,64]{3,2,1,0:T(8,128)(2,1)S(1)} %fusion.14) | copy-start | bytes 294916
  68.8 2.3 %copy-start.17 = (f32[2,2,128,128]{3,2,1,0:T(8,128)}, f32[2,2,128,128]{3,2,1,0:T(8,128)S(1)}, u32[]{:S(2)}) copy-start(f32[2,2,128,128]{3,2,1,0:T(8,128)S(1)} %convert_element_type.147) | copy-start | bytes 786436
  68.8 2.2 %copy-start.18 = (f32[2,2,128,128]{3,2,1,0:T(8,128)}, f32[2,2,128,128]{3,2,1,0:T(8,128)S(1)}, u32[]{:S(2)}) copy-start(f32[2,2,128,128]{3,2,1,0:T(8,128)S(1)} %convert_element_type.149) | copy-start | bytes 786436
  68.8 2.2 %copy-start.19 = (f32[2,2,128,128]{3,2,1,0:T(8,128)}, f32[2,2,128,128]{3,2,1,0:T(8,128)S(1)}, u32[]{:S(2)}) copy-start(f32[2,2,128,128]{3,2,1,0:T(8,128)S(1)} %convert_element_type.151) | copy-start | bytes 786436
  69.9 1.1 copy-start.20
  71.0 0.7 copy-start.21
  71.7 0.7 copy-start.22
  72.6 1.6 copy-start.1
  72.6 1.1 copy-start.5
  72.6 2.2 %copy-start.13 = (bf16[4096,256]{1,0:T(8,128)(2,1)S(1)}, bf16[4096,256]{1,0:T(8,128)(2,1)}, u32[]{:S(2)}) copy-start(bf16[4096,256]{1,0:T(8,128)(2,1)} %param.8) | copy-start | bytes 6291460
  74.2 0.7 copy-start.12
  90.7 5.2 %copy-start.6 = (bf16[6,64,2,128]{3,2,1,0:T(2,128)(2,1)S(1)}, bf16[6,64,2,128]{3,2,1,0:T(2,128)(2,1)}, u32[]{:S(2)}) copy-start(bf16[6,64,2,128]{3,2,1,0:T(2,128)(2,1)} %copy-done.4) | copy-start | bytes 589828
  90.7 5.2 %copy-start.8 = (bf16[6,64,2,128]{3,2,1,0:T(2,128)(2,1)S(1)}, bf16[6,64,2,128]{3,2,1,0:T(2,128)(2,1)}, u32[]{:S(2)}) copy-start(bf16[6,64,2,128]{3,2,1,0:T(2,128)(2,1)} %reshape.68) | copy-start | bytes 589828
  93.9 13.0 %collective-permute-start.6 = (f32[4,8,64,256]{3,2,1,0:T(8,128)}, f32[4,8,64,256]{3,2,1,0:T(8,128)}, u32[]{:S(2)}, u32[]{:S(2)}) collective-permute-start(f32[4,8,64,256]{3,2,1,0:T(8,128)} %dynamic-slice_bitcast_fusion), channel_id=1, source_target_pairs={{0,12},{12,0},{24,36},{36,24},{48,60},{60,48},{72,84},{84,72},{96,... | collective-permute-start | bytes 6291464 | tf_op jit(solution)/shard_map/ppermute | solution.py:72
  102.5 3.5 %copy-start.27 = (bf16[6,2,64,64]{3,2,1,0:T(8,128)(2,1)S(1)}, bf16[6,2,64,64]{3,2,1,0:T(8,128)(2,1)}, u32[]{:S(2)}) copy-start(bf16[6,2,64,64]{3,2,1,0:T(8,128)(2,1)} %fusion.13) | copy-start | bytes 294916
  102.5 3.7 %copy-start.11 = (f32[6,2,128,128]{2,3,1,0:T(8,128)S(1)}, f32[6,2,128,128]{2,3,1,0:T(8,128)}, u32[]{:S(2)}) copy-start(f32[6,2,128,128]{2,3,1,0:T(8,128)} %convolution_bitcast_fusion.1) | copy-start | bytes 2359300
  102.5 3.7 %copy-start.32 = (f32[2,128,128]{1,2,0:T(8,128)S(1)}, f32[2,128,128]{1,2,0:T(8,128)}, u32[]{:S(2)}) copy-start(f32[2,128,128]{1,2,0:T(8,128)} %copy.57) | copy-start | bytes 393220
  104.2 2.3 %copy-start.7 = (bf16[6,64,2,128]{3,2,1,0:T(2,128)(2,1)S(1)}, bf16[6,64,2,128]{3,2,1,0:T(2,128)(2,1)}, u32[]{:S(2)}) copy-start(bf16[6,64,2,128]{3,2,1,0:T(2,128)(2,1)} %copy-done.4) | copy-start | bytes 589828
  106.3 2.2 %copy-start.2 = (f32[4096,256]{1,0:T(8,128)S(1)}, f32[4096,256]{1,0:T(8,128)}, u32[]{:S(2)}) copy-start(f32[4096,256]{1,0:T(8,128)} %copy.72) | copy-start | bytes 12582916
  111.2 11.1 %collective-permute-start.7 = (bf16[4,4,64,256]{3,2,1,0:T(8,128)(2,1)S(1)}, bf16[4,4,64,256]{3,2,1,0:T(8,128)(2,1)S(1)}, u32[]{:S(2)}, u32[]{:S(2)}) collective-permute-start(bf16[4,4,64,256]{3,2,1,0:T(8,128)(2,1)S(1)} %fusion.20), channel_id=1, source_target_pairs={{0,24},{12,180},{24,0},{36,60},{48,72},{60,36},{72,48},{84,108},{9... | collective-permute-start | bytes 1572872 | tf_op jit(solution)/shard_map/ppermute | solution.py:58
  122.4 28.0 %copy-start.9 = (bf16[6,64,2,128]{3,2,1,0:T(2,128)(2,1)S(1)}, bf16[6,64,2,128]{3,2,1,0:T(2,128)(2,1)}, u32[]{:S(2)}) copy-start(bf16[6,64,2,128]{3,2,1,0:T(2,128)(2,1)} %reshape.68) | copy-start | bytes 589828
  122.4 28.0 %copy-start.26 = (bf16[6,2,64,64]{3,2,1,0:T(8,128)(2,1)S(1)}, bf16[6,2,64,64]{3,2,1,0:T(8,128)(2,1)}, u32[]{:S(2)}) copy-start(bf16[6,2,64,64]{3,2,1,0:T(8,128)(2,1)} %copy-done.25) | copy-start | bytes 294916
  122.5 11.1 %collective-permute-start.10 = (bf16[4,64,256]{2,1,0:T(8,128)(2,1)S(1)}, bf16[4,64,256]{2,1,0:T(8,128)(2,1)S(1)}, u32[]{:S(2)}, u32[]{:S(2)}) collective-permute-start(bf16[4,64,256]{2,1,0:T(8,128)(2,1)S(1)} %get-tuple-element.12), channel_id=1, source_target_pairs={{0,576},{12,588},{24,600},{36,612},{48,624},{60,636},{72,648},{84,... | collective-permute-start | bytes 393224 | tf_op jit(solution)/shard_map/ppermute | solution.py:58
  125.9 10.0 %collective-permute-start.9 = (bf16[4,64,256]{2,1,0:T(8,128)(2,1)S(1)}, bf16[4,64,256]{2,1,0:T(8,128)(2,1)S(1)}, u32[]{:S(2)}, u32[]{:S(2)}) collective-permute-start(bf16[4,64,256]{2,1,0:T(8,128)(2,1)S(1)} %get-tuple-element.13), channel_id=1, source_target_pairs={{0,384},{12,396},{24,408},{36,420},{48,432},{60,444},{72,456},{84,... | collective-permute-start | bytes 393224 | tf_op jit(solution)/shard_map/ppermute | solution.py:58
  130.8 7.7 %collective-permute-start.8 = (bf16[4,64,256]{2,1,0:T(8,128)(2,1)S(1)}, bf16[4,64,256]{2,1,0:T(8,128)(2,1)S(1)}, u32[]{:S(2)}, u32[]{:S(2)}) collective-permute-start(bf16[4,64,256]{2,1,0:T(8,128)(2,1)S(1)} %get-tuple-element.11), channel_id=1, source_target_pairs={{0,192},{12,204},{24,216},{36,228},{48,240},{60,252},{72,264},{84,... | collective-permute-start | bytes 393224 | tf_op jit(solution)/shard_map/ppermute | solution.py:58
  138.6 14.8 %collective-permute-start.13 = (bf16[64,256]{1,0:T(8,128)(2,1)S(1)}, bf16[64,256]{1,0:T(8,128)(2,1)S(1)}, u32[]{:S(2)}, u32[]{:S(2)}) collective-permute-start(bf16[64,256]{1,0:T(8,128)(2,1)S(1)} %get-tuple-element.15), channel_id=1, source_target_pairs={{0,144},{12,156},{24,168},{36,180},{48,0},{60,12},{72,24},{84,36},... | collective-permute-start | bytes 98312 | tf_op jit(solution)/shard_map/ppermute | solution.py:58
  140.6 12.8 %collective-permute-start.12 = (bf16[64,256]{1,0:T(8,128)(2,1)S(1)}, bf16[64,256]{1,0:T(8,128)(2,1)S(1)}, u32[]{:S(2)}, u32[]{:S(2)}) collective-permute-start(bf16[64,256]{1,0:T(8,128)(2,1)S(1)} %get-tuple-element.16), channel_id=1, source_target_pairs={{0,96},{12,108},{24,120},{36,132},{48,144},{60,156},{72,168},{84,1... | collective-permute-start | bytes 98312 | tf_op jit(solution)/shard_map/ppermute | solution.py:58
  145.5 7.9 %collective-permute-start.11 = (bf16[64,256]{1,0:T(8,128)(2,1)S(1)}, bf16[64,256]{1,0:T(8,128)(2,1)S(1)}, u32[]{:S(2)}, u32[]{:S(2)}) collective-permute-start(bf16[64,256]{1,0:T(8,128)(2,1)S(1)} %get-tuple-element.14), channel_id=1, source_target_pairs={{0,48},{12,60},{24,72},{36,84},{48,96},{60,108},{72,120},{84,132},... | collective-permute-start | bytes 98312 | tf_op jit(solution)/shard_map/ppermute | solution.py:58
Sparse Core Ops, SparseCore 0:
  79.3 64.9 reduce-scatter.1

commit v5 on v4

--- a/solution.py
+++ b/solution.py
@@ -58,7 +58,7 @@
     return lax.ppermute(block.astype(jnp.bfloat16), SEQ, route).astype(jnp.float32)
 
 
-def grid_scatter(partial, x_count, y_count):
+def grid_scatter(partial, x_count, y_count, ride):
     count = x_count * y_count * 2
     cols = partial.shape[1]
     position = lax.axis_index(SEQ)
@@ -70,6 +70,7 @@
     kept = lax.dynamic_index_in_dim(acc, core, 2, keepdims=False)
     sent = lax.dynamic_index_in_dim(acc, 1 - core, 2, keepdims=False)
     acc = kept + lax.ppermute(sent, SEQ, [(i, i ^ 1) for i in range(count)])
+    acc, ride = lax.optimization_barrier((acc, ride))
     acc = jnp.where(core == 1, jnp.roll(acc, -1, axis=1), acc)
     acc = acc.reshape(x_count, y_count // 2, 2, acc.shape[2], cols)
     label = (y - core) % y_count
@@ -98,7 +99,7 @@
         route = [(index(a, b, c), index(a, b + 2 * shift, c))
                  for a in range(x_count) for b in range(y_count) for c in range(2)]
         total = total + wire(piece, route)
-    return total
+    return total, ride
 
 
 def local(queries, key_rows, value_rows, out_weight, out_grad, seq_count, head_count_axis):
@@ -164,31 +165,33 @@
     partial_output = lax.dot_general(
         attention, out_weight, (((1,), (1,)), ((), ())), preferred_element_type=jnp.float32
     ).astype(jnp.bfloat16)
-    grad_scores = jnp.einsum(
-        "cthe,cshe->chts", grad_blocks, value_blocks, preferred_element_type=jnp.float32
-    )
-    grad_weights = jnp.where(causal, factor * grad_scores, 0.0).astype(jnp.bfloat16)
-    query_grad = jnp.einsum(
-        "chts,cshd->cthd", grad_weights, key_blocks, preferred_element_type=jnp.float32
-    )
-    query_grad = query_grad + factor * state_product("cthe,chde->cthd", grad_blocks, before_parts)
-    key_grad = jnp.einsum(
-        "chts,cthd->cshd", grad_weights, query_blocks, preferred_element_type=jnp.float32
-    )
-    key_grad = key_grad + factor * state_product("cshe,chde->cshd", value_blocks, later_parts)
-    value_grad = jnp.einsum(
-        "chts,cthe->cshe", weights, grad_blocks, preferred_element_type=jnp.float32
-    )
-    value_grad = value_grad + factor * state_product("cshd,chde->cshe", key_blocks, later_parts)
     partial_output, attention = lax.optimization_barrier((partial_output, attention))
     output = lax.psum_scatter(partial_output, "head", scatter_dimension=0, tiled=True)
     weight_partial = lax.dot_general(
         out_grad, attention, (((0,), (0,)), ((), ())), preferred_element_type=jnp.float32
     )
     if seq_count == 64:
-        weight_grad = grid_scatter(weight_partial, 4, 8)
+        weight_grad, (before_parts, later_parts) = grid_scatter(
+            weight_partial, 4, 8, (before_parts, later_parts)
+        )
     else:
         weight_grad = halving_scatter(weight_partial, seq_count)
+    grad_scores = jnp.einsum(
+        "cthe,cshe->chts", grad_blocks, value_blocks, preferred_element_type=jnp.float32
+    )
+    grad_weights = jnp.where(causal, factor * grad_scores, 0.0).astype(jnp.bfloat16)
+    query_grad = jnp.einsum(
+        "chts,cshd->cthd", grad_weights, key_blocks, preferred_element_type=jnp.float32
+    )
+    query_grad = query_grad + factor * state_product("cthe,chde->cthd", grad_blocks, before_parts)
+    key_grad = jnp.einsum(
+        "chts,cthd->cshd", grad_weights, query_blocks, preferred_element_type=jnp.float32
+    )
+    key_grad = key_grad + factor * state_product("cshe,chde->cshd", value_blocks, later_parts)
+    value_grad = jnp.einsum(
+        "chts,cthe->cshe", weights, grad_blocks, preferred_element_type=jnp.float32
+    )
+    value_grad = value_grad + factor * state_product("cshd,chde->cshe", key_blocks, later_parts)
     weight_grad = weight_grad * total_rows ** (-0.5)
     return (
         output,

time: 164 us -> 162 us (0.988)
  local copies, waits for them, and re-layouts: 24.6 us -> 21.1 us
  matrix products: 23.1 us -> 21.4 us
  waiting for transfers between devices: 31.2 us -> 32.9 us
    unnamed x70 -> x76, local copies, waits for them, and re-layouts: 8.28 us -> 4.85 us
  transfers between devices with their start and end apart: 15 -> 15, of which waited for: 9 -> 8; matrix products, arithmetic and copies ran while one was open for 25% -> 25% of each run, Pallas kernels for 0% -> 0%
where the time goes in v5:
time: 162 us; the launch traced here: 160 us
  starting transfers between devices  55.5 us (34%)
  waiting for transfers between devices  32.9 us (20%)
  matrix products  21.4 us (13%)
  local copies, waits for them, and re-layouts  21.1 us (13%)
  between operations  15.1 us (9%)
  other arithmetic  13.9 us (9%)
    ppermute x6, starting transfers between devices, swapped(): return lax.ppermute(block, SEQ, route)  28.5 us
    ppermute x7, starting transfers between devices, wire(): lax.ppermute(block.astype(jnp.bfloat16), SEQ, route).astype(jnp.float32)  25.1 us
    ppermute x6, waiting for transfers between devices, swapped(): return lax.ppermute(block, SEQ, route)  17.9 us
    ppermute x7, waiting for transfers between devices, wire(): lax.ppermute(block.astype(jnp.bfloat16), SEQ, route).astype(jnp.float32)  15 us
    dot_general x1, local copies, waits for them, and re-layouts, local(): lax.dot_general(out_grad, attention, (((0,), (0,)), ((), ())), preferred_...  5.61 us
    unnamed x76, local copies, waits for them, and re-layouts  4.85 us
    dot_general x1, matrix products, local(): lax.dot_general(out_grad, attention, (((0,), (0,)), ((), ())), preferred_...  4.22 us
    convert_element_type x6, other arithmetic, local(): totals.astype(jnp.bfloat16)  3.73 us
  transfers between devices with their start and end apart: 15, of which 8 were waited for; matrix products, arithmetic and copies ran while one was open for 25% of the time, Pallas kernels for 0%

profile of v5, /device:TPU:6, one launch (start us, length us, event | category | flops | bytes accessed | tf_op | source)
XLA Modules:
  0.0 159.8 jit_solution(11780327322315620883)
XLA Ops:
  7.2 1.3 convolution_bitcast_fusion.5
  8.5 1.1 convolution_bitcast_fusion.6
  9.7 2.6 %convolution_convert_fusion.1 = bf16[384,256]{1,0:T(8,128)(2,1)S(1)} fusion(bf16[384,4096]{1,0:T(8,128)(2,1)S(1)} %copy-done, bf16[4096,256]{1,0:T(8,128)(2,1)} %param.8), kind=kOutput, calls=%fused_computation.37 | convolution fusion | flops 805404672 | bytes 5439488 | tf_op jit(solution)/shard_map/dot_general | solution.py:117
  13.1 1.9 %collective-permute-start = (bf16[2,2,128,128]{3,2,1,0:T(8,128)(2,1)S(1)}, bf16[2,2,128,128]{3,2,1,0:T(8,128)(2,1)S(1)}, u32[]{:S(2)}, u32[]{:S(2)}) collective-permute-start(bf16[2,2,128,128]{3,2,1,0:T(8,128)(2,1)S(1)} %fusion.24), channel_id=1, source_target_pairs={{0,12},{12,0},{24,36},{36,24},{48,60},{60,48},{72,84},{84,72},{96,... | collective-permute-start | bytes 393224 | tf_op jit(solution)/shard_map/ppermute | solution.py:18
  15.0 1.3 collective-permute-done
  16.3 3.5 %collective-permute-start.1 = (bf16[2,2,128,128]{3,2,1,0:T(8,128)(2,1)S(1)}, bf16[2,2,128,128]{3,2,1,0:T(8,128)(2,1)S(1)}, u32[]{:S(2)}, u32[]{:S(2)}) collective-permute-start(bf16[2,2,128,128]{3,2,1,0:T(8,128)(2,1)S(1)} %fusion.77), channel_id=1, source_target_pairs={{0,24},{24,0},{12,36},{36,12},{48,72},{72,48},{60,84},{84,60},{96,... | collective-permute-start | bytes 393224 | tf_op jit(solution)/shard_map/ppermute | solution.py:18
  19.9 3.9 %collective-permute-done.1 = bf16[2,2,128,128]{3,2,1,0:T(8,128)(2,1)S(1)} collective-permute-done((bf16[2,2,128,128]{3,2,1,0:T(8,128)(2,1)S(1)}, bf16[2,2,128,128]{3,2,1,0:T(8,128)(2,1)S(1)}, u32[]{:S(2)}, u32[]{:S(2)}) %collective-permute-start.1) | collective-permute-done | bytes 131104 | tf_op jit(solution)/shard_map/ppermute | solution.py:18
  23.9 4.5 %collective-permute-start.2 = (bf16[2,2,128,128]{3,2,1,0:T(8,128)(2,1)S(1)}, bf16[2,2,128,128]{3,2,1,0:T(8,128)(2,1)S(1)}, u32[]{:S(2)}, u32[]{:S(2)}) collective-permute-start(bf16[2,2,128,128]{3,2,1,0:T(8,128)(2,1)S(1)} %get-tuple-element.23), channel_id=1, source_target_pairs={{0,48},{48,0},{12,60},{60,12},{24,72},{72,24},{36,84},{84,36},{96,... | collective-permute-start | bytes 393224 | tf_op jit(solution)/shard_map/ppermute | solution.py:18
  28.4 5.8 %collective-permute-done.2 = bf16[2,2,128,128]{3,2,1,0:T(8,128)(2,1)S(1)} collective-permute-done((bf16[2,2,128,128]{3,2,1,0:T(8,128)(2,1)S(1)}, bf16[2,2,128,128]{3,2,1,0:T(8,128)(2,1)S(1)}, u32[]{:S(2)}, u32[]{:S(2)}) %collective-permute-start.2) | collective-permute-done | bytes 131104 | tf_op jit(solution)/shard_map/ppermute | solution.py:18
  34.9 7.7 %collective-permute-start.3 = (bf16[2,2,128,128]{3,2,1,0:T(8,128)(2,1)}, bf16[2,2,128,128]{3,2,1,0:T(8,128)(2,1)}, u32[]{:S(2)}, u32[]{:S(2)}) collective-permute-start(bf16[2,2,128,128]{3,2,1,0:T(8,128)(2,1)} %fusion.82), channel_id=1, source_target_pairs={{0,96},{96,0},{12,108},{108,12},{24,120},{120,24},{36,132},{132,36... | collective-permute-start | bytes 393224 | tf_op jit(solution)/shard_map/ppermute | solution.py:18
  42.6 1.0 reshape.65
  43.6 1.0 reshape.66
  44.6 4.6 %collective-permute-done.3 = bf16[2,2,128,128]{3,2,1,0:T(8,128)(2,1)} collective-permute-done((bf16[2,2,128,128]{3,2,1,0:T(8,128)(2,1)}, bf16[2,2,128,128]{3,2,1,0:T(8,128)(2,1)}, u32[]{:S(2)}, u32[]{:S(2)}) %collective-permute-start.3) | collective-permute-done | bytes 131104 | tf_op jit(solution)/shard_map/ppermute | solution.py:18
  49.3 1.7 %fusion.81 = bf16[2,2,128,128]{3,2,1,0:T(8,128)(2,1)} fusion(bf16[2,2,128,128]{3,2,1,0:T(8,128)(2,1)} %collective-permute-done.3, f32[2,2,128,128]{3,2,1,0:T(8,128)} %copy-done.6, bf16[2,2,128,128]{3,2,1,0:T(8,128)(2,1)} %copy-done.12), kind=kLoop, calls=%fused_computation.135 | loop fusion | flops 327680 | bytes 655360 | tf_op jit(solution)/shard_map/convert_element_type | solution.py:147
  51.0 2.7 %collective-permute-start.4 = (bf16[2,2,128,128]{3,2,1,0:T(8,128)(2,1)}, bf16[2,2,128,128]{3,2,1,0:T(8,128)(2,1)}, u32[]{:S(2)}, u32[]{:S(2)}) collective-permute-start(bf16[2,2,128,128]{3,2,1,0:T(8,128)(2,1)} %fusion.81), channel_id=1, source_target_pairs={{0,192},{192,0},{12,204},{204,12},{24,216},{216,24},{36,228},{228,... | collective-permute-start | bytes 393224 | tf_op jit(solution)/shard_map/ppermute | solution.py:18
  53.7 1.2 fusion.51
  55.0 1.0 reshape.64
  56.0 2.2 %collective-permute-done.4 = bf16[2,2,128,128]{3,2,1,0:T(8,128)(2,1)} collective-permute-done((bf16[2,2,128,128]{3,2,1,0:T(8,128)(2,1)}, bf16[2,2,128,128]{3,2,1,0:T(8,128)(2,1)}, u32[]{:S(2)}, u32[]{:S(2)}) %collective-permute-start.4) | collective-permute-done | bytes 131104 | tf_op jit(solution)/shard_map/ppermute | solution.py:18
  58.2 1.2 add_convert_fusion
  59.4 8.1 %collective-permute-start.5 = (bf16[2,2,128,128]{3,2,1,0:T(8,128)(2,1)S(1)}, bf16[2,2,128,128]{3,2,1,0:T(8,128)(2,1)S(1)}, u32[]{:S(2)}, u32[]{:S(2)}) collective-permute-start(bf16[2,2,128,128]{3,2,1,0:T(8,128)(2,1)S(1)} %add_convert_fusion), channel_id=1, source_target_pairs={{0,384},{384,0},{12,396},{396,12},{24,408},{408,24},{36,420},{420,... | collective-permute-start | bytes 393224 | tf_op jit(solution)/shard_map/ppermute | solution.py:18
  67.8 1.0 convert_element_type.147
  68.9 1.1 convert_element_type.153
  69.9 1.0 convert_element_type.155
  71.7 0.7 copy-done.25
  73.8 0.7 copy.133
  74.6 2.6 %convolution_convert_fusion = bf16[384,4096]{1,0:T(8,128)(2,1)} fusion(bf16[4096,256]{1,0:T(8,128)(2,1)S(1)} %copy-done.11, bf16[48,8,2,128]{3,2,1,0:T(2,128)(2,1)S(1)} %bitcast.133), kind=kOutput, calls=%fused_computation | convolution fusion | flops 806879232 | bytes 5439488 | tf_op jit(solution)/shard_map/dot_general | solution.py:165
  77.3 4.2 %convolution_bitcast_fusion = f32[4096,256]{0,1:T(8,128)} fusion(bf16[384,256]{1,0:T(8,128)(2,1)} %bitcast.137, bf16[384,4096]{1,0:T(8,128)(2,1)S(1)} %copy-done), kind=kOutput, calls=%fused_computation.1 | convolution fusion | flops 805306368 | bytes 7536640 | tf_op jit(solution)/shard_map/dot_general | solution.py:170
  81.5 5.6 %copy.52 = f32[4096,256]{1,0:T(8,128)} copy(f32[4096,256]{0,1:T(8,128)} %convolution_bitcast_fusion) | data formatting | bytes 8388608 | tf_op jit(solution)/shard_map/dot_general | solution.py:170
  87.1 3.2 %dynamic-slice_bitcast_fusion = f32[4,8,64,256]{3,2,1,0:T(8,128)} fusion(f32[4,8,2,64,256]{4,3,2,1,0:T(8,128)} %bitcast.128, s32[]{:T(128)S(6)} %select_n.200), kind=kLoop, calls=%fused_computation.4 | loop fusion | bytes 4194308 | tf_op jit(solution)/shard_map/jit(dynamic_index_in_dim)/squeeze | solution.py:71
  90.3 1.9 %collective-permute-start.6 = (f32[4,8,64,256]{3,2,1,0:T(8,128)}, f32[4,8,64,256]{3,2,1,0:T(8,128)}, u32[]{:S(2)}, u32[]{:S(2)}) collective-permute-start(f32[4,8,64,256]{3,2,1,0:T(8,128)} %dynamic-slice_bitcast_fusion), channel_id=1, source_target_pairs={{0,12},{12,0},{24,36},{36,24},{48,60},{60,48},{72,84},{84,72},{96,... | collective-permute-start | bytes 6291464 | tf_op jit(solution)/shard_map/ppermute | solution.py:72
  92.4 1.7 %reshape.68 = bf16[6,64,2,128]{3,2,1,0:T(2,128)(2,1)} reshape(bf16[384,256]{1,0:T(8,128)(2,1)} %copy-done.28) | data formatting | bytes 393216 | tf_op jit(solution)/shard_map/reshape | solution.py:120
  94.1 2.1 %fusion.13 = bf16[6,2,64,64]{3,2,1,0:T(8,128)(2,1)} fusion(pred[64,64]{1,0:T(8,128)(4,1)S(1)} %iota_compare_fusion, bf16[6,64,2,128]{3,2,1,0:T(2,128)(2,1)} %reshape.68, bf16[6,64,2,128]{3,2,1,0:T(2,128)(2,1)} %copy-done.2), kind=kOutput, calls=%fused_computation.31 | convolution fusion | flops 12730368 | bytes 495616 | tf_op jit(solution)/shard_map/cthe,cshe->chts/dot_general | solution.py:179
  96.2 2.1 %convolution_bitcast_fusion.1 = f32[6,2,128,128]{2,3,1,0:T(8,128)} fusion(bf16[6,64,2,128]{3,2,1,0:T(2,128)(2,1)} %reshape.68, bf16[6,64,2,128]{3,2,1,0:T(2,128)(2,1)S(1)} %reshape.64), kind=kOutput, calls=%fused_computation.8 | convolution fusion | flops 25165824 | bytes 1179648 | tf_op jit(solution)/shard_map/cthd,cthe->chde/dot_general | solution.py:124
  98.4 1.6 fusion.30
  99.9 1.7 %copy.53 = f32[2,128,128]{1,2,0:T(8,128)} copy(f32[2,128,128]{2,1,0:T(8,128)} %fusion.30) | data formatting | bytes 262144 | tf_op jit(solution)/shard_map/sub | solution.py:153
  101.6 1.3 subtract_convert_fusion
  102.9 2.7 %bitcast_add_fusion = f32[4,8,64,256]{3,2,1,0:T(8,128)S(1)} fusion(f32[4,8,64,256]{3,2,1,0:T(8,128)} %collective-permute-done.6, f32[4,8,2,64,256]{4,3,2,1,0:T(8,128)} %bitcast.129, s32[]{:T(128)S(6)} %select_n.199), kind=kLoop, calls=%fused_computation.3 | loop fusion | flops 524288 | bytes 6291460 | tf_op jit(solution)/shard_map/add | solution.py:72
  106.3 2.1 %collective-permute-start.7 = (bf16[4,4,64,256]{3,2,1,0:T(8,128)(2,1)S(1)}, bf16[4,4,64,256]{3,2,1,0:T(8,128)(2,1)S(1)}, u32[]{:S(2)}, u32[]{:S(2)}) collective-permute-start(bf16[4,4,64,256]{3,2,1,0:T(8,128)(2,1)S(1)} %fusion.20), channel_id=1, source_target_pairs={{0,24},{12,180},{24,0},{36,60},{48,72},{60,36},{72,48},{84,108},{9... | collective-permute-start | bytes 1572872 | tf_op jit(solution)/shard_map/ppermute | solution.py:58
  110.8 6.8 %collective-permute-done.7 = bf16[4,4,64,256]{3,2,1,0:T(8,128)(2,1)S(1)} collective-permute-done((bf16[4,4,64,256]{3,2,1,0:T(8,128)(2,1)S(1)}, bf16[4,4,64,256]{3,2,1,0:T(8,128)(2,1)S(1)}, u32[]{:S(2)}, u32[]{:S(2)}) %collective-permute-start.7) | collective-permute-done | bytes 524320 | tf_op jit(solution)/shard_map/ppermute | solution.py:58
  117.7 4.8 %collective-permute-start.8 = (bf16[4,64,256]{2,1,0:T(8,128)(2,1)S(1)}, bf16[4,64,256]{2,1,0:T(8,128)(2,1)S(1)}, u32[]{:S(2)}, u32[]{:S(2)}) collective-permute-start(bf16[4,64,256]{2,1,0:T(8,128)(2,1)S(1)} %get-tuple-element.25), channel_id=1, source_target_pairs={{0,192},{12,204},{24,216},{36,228},{48,240},{60,252},{72,264},{84,... | collective-permute-start | bytes 393224 | tf_op jit(solution)/shard_map/ppermute | solution.py:58
  122.6 1.9 %collective-permute-start.10 = (bf16[4,64,256]{2,1,0:T(8,128)(2,1)S(1)}, bf16[4,64,256]{2,1,0:T(8,128)(2,1)S(1)}, u32[]{:S(2)}, u32[]{:S(2)}) collective-permute-start(bf16[4,64,256]{2,1,0:T(8,128)(2,1)S(1)} %get-tuple-element.26), channel_id=1, source_target_pairs={{0,576},{12,588},{24,600},{36,612},{48,624},{60,636},{72,648},{84,... | collective-permute-start | bytes 393224 | tf_op jit(solution)/shard_map/ppermute | solution.py:58
  124.5 3.4 %collective-permute-start.9 = (bf16[4,64,256]{2,1,0:T(8,128)(2,1)S(1)}, bf16[4,64,256]{2,1,0:T(8,128)(2,1)S(1)}, u32[]{:S(2)}, u32[]{:S(2)}) collective-permute-start(bf16[4,64,256]{2,1,0:T(8,128)(2,1)S(1)} %get-tuple-element.27), channel_id=1, source_target_pairs={{0,384},{12,396},{24,408},{36,420},{48,432},{60,444},{72,456},{84,... | collective-permute-start | bytes 393224 | tf_op jit(solution)/shard_map/ppermute | solution.py:58
  128.1 6.5 %collective-permute-done.10 = bf16[4,64,256]{2,1,0:T(8,128)(2,1)S(1)} collective-permute-done((bf16[4,64,256]{2,1,0:T(8,128)(2,1)S(1)}, bf16[4,64,256]{2,1,0:T(8,128)(2,1)S(1)}, u32[]{:S(2)}, u32[]{:S(2)}) %collective-permute-start.10) | collective-permute-done | bytes 131104 | tf_op jit(solution)/shard_map/ppermute | solution.py:58
  134.7 1.9 %collective-permute-start.11 = (bf16[64,256]{1,0:T(8,128)(2,1)S(1)}, bf16[64,256]{1,0:T(8,128)(2,1)S(1)}, u32[]{:S(2)}, u32[]{:S(2)}) collective-permute-start(bf16[64,256]{1,0:T(8,128)(2,1)S(1)} %get-tuple-element.28), channel_id=1, source_target_pairs={{0,48},{12,60},{24,72},{36,84},{48,96},{60,108},{72,120},{84,132},... | collective-permute-start | bytes 98312 | tf_op jit(solution)/shard_map/ppermute | solution.py:58
  136.6 6.0 %collective-permute-start.13 = (bf16[64,256]{1,0:T(8,128)(2,1)S(1)}, bf16[64,256]{1,0:T(8,128)(2,1)S(1)}, u32[]{:S(2)}, u32[]{:S(2)}) collective-permute-start(bf16[64,256]{1,0:T(8,128)(2,1)S(1)} %get-tuple-element.29), channel_id=1, source_target_pairs={{0,144},{12,156},{24,168},{36,180},{48,0},{60,12},{72,24},{84,36},... | collective-permute-start | bytes 98312 | tf_op jit(solution)/shard_map/ppermute | solution.py:58
  142.6 5.0 %collective-permute-start.12 = (bf16[64,256]{1,0:T(8,128)(2,1)S(1)}, bf16[64,256]{1,0:T(8,128)(2,1)S(1)}, u32[]{:S(2)}, u32[]{:S(2)}) collective-permute-start(bf16[64,256]{1,0:T(8,128)(2,1)S(1)} %get-tuple-element.30), channel_id=1, source_target_pairs={{0,96},{12,108},{24,120},{36,132},{48,144},{60,156},{72,168},{84,1... | collective-permute-start | bytes 98312 | tf_op jit(solution)/shard_map/ppermute | solution.py:58
  149.9 0.7 copy.131
  150.6 1.7 %collective-permute-done.12 = bf16[64,256]{1,0:T(8,128)(2,1)S(1)} collective-permute-done((bf16[64,256]{1,0:T(8,128)(2,1)S(1)}, bf16[64,256]{1,0:T(8,128)(2,1)S(1)}, u32[]{:S(2)}, u32[]{:S(2)}) %collective-permute-start.12) | collective-permute-done | bytes 32800 | tf_op jit(solution)/shard_map/ppermute | solution.py:58
  (121 shorter events, 10.4 us)
Async XLA Ops:
  7.2 2.5 %copy-start = (bf16[384,4096]{1,0:T(8,128)(2,1)S(1)}, bf16[384,4096]{1,0:T(8,128)(2,1)}, u32[]{:S(2)}) copy-start(bf16[384,4096]{1,0:T(8,128)(2,1)} %param.9) | copy-start | bytes 9437188
  7.2 145.8 %reduce-scatter.2.cloned.1.call-start = ((), (), s32[]{:S(2)}) async-start(), calls=%async_computation.1 | async-start | bytes 3407872 | tf_op jit(solution)/shard_map/reduce_scatter | solution.py:169
  9.7 2.6 %copy-start.27 = (bf16[384,256]{1,0:T(8,128)(2,1)S(1)}, bf16[384,256]{1,0:T(8,128)(2,1)}, u32[]{:S(2)}) copy-start(bf16[384,256]{1,0:T(8,128)(2,1)} %param.5) | copy-start | bytes 589828
  12.6 7.3 %copy-start.32 = (f32[128,128]{0,1:T(8,128)}, f32[128,128]{0,1:T(8,128)S(1)}, u32[]{:S(2)}) copy-start(f32[128,128]{0,1:T(8,128)S(1)} %fusion.66) | copy-start | bytes 196612
  12.8 7.0 %copy-start.33 = (f32[128,128]{0,1:T(8,128)}, f32[128,128]{0,1:T(8,128)S(1)}, u32[]{:S(2)}) copy-start(f32[128,128]{0,1:T(8,128)S(1)} %fusion.68) | copy-start | bytes 196612
  13.1 3.2 %collective-permute-start = (bf16[2,2,128,128]{3,2,1,0:T(8,128)(2,1)S(1)}, bf16[2,2,128,128]{3,2,1,0:T(8,128)(2,1)S(1)}, u32[]{:S(2)}, u32[]{:S(2)}) collective-permute-start(bf16[2,2,128,128]{3,2,1,0:T(8,128)(2,1)S(1)} %fusion.24), channel_id=1, source_target_pairs={{0,12},{12,0},{24,36},{36,24},{48,60},{60,48},{72,84},{84,72},{96,... | collective-permute-start | bytes 393224 | tf_op jit(solution)/shard_map/ppermute | solution.py:18
  16.3 18.6 %copy-start.14 = (bf16[2,2,128,128]{3,2,1,0:T(8,128)(2,1)}, bf16[2,2,128,128]{3,2,1,0:T(8,128)(2,1)S(1)}, u32[]{:S(2)}) copy-start(bf16[2,2,128,128]{3,2,1,0:T(8,128)(2,1)S(1)} %collective-permute-done) | copy-start | bytes 393220
  16.3 7.4 %collective-permute-start.1 = (bf16[2,2,128,128]{3,2,1,0:T(8,128)(2,1)S(1)}, bf16[2,2,128,128]{3,2,1,0:T(8,128)(2,1)S(1)}, u32[]{:S(2)}, u32[]{:S(2)}) collective-permute-start(bf16[2,2,128,128]{3,2,1,0:T(8,128)(2,1)S(1)} %fusion.77), channel_id=1, source_target_pairs={{0,24},{24,0},{12,36},{36,12},{48,72},{72,48},{60,84},{84,60},{96,... | collective-permute-start | bytes 393224 | tf_op jit(solution)/shard_map/ppermute | solution.py:18
  23.8 11.1 %copy-start.34 = (bf16[2,2,128,128]{3,2,1,0:T(8,128)(2,1)}, bf16[2,2,128,128]{3,2,1,0:T(8,128)(2,1)S(1)}, u32[]{:S(2)}) copy-start(bf16[2,2,128,128]{3,2,1,0:T(8,128)(2,1)S(1)} %collective-permute-done.1) | copy-start | bytes 393220
  23.8 11.0 %copy-start.6 = (f32[2,2,128,128]{3,2,1,0:T(8,128)}, f32[2,2,128,128]{3,2,1,0:T(8,128)S(1)}, u32[]{:S(2)}) copy-start(f32[2,2,128,128]{3,2,1,0:T(8,128)S(1)} %get-tuple-element.24) | copy-start | bytes 786436
  23.9 10.3 %collective-permute-start.2 = (bf16[2,2,128,128]{3,2,1,0:T(8,128)(2,1)S(1)}, bf16[2,2,128,128]{3,2,1,0:T(8,128)(2,1)S(1)}, u32[]{:S(2)}, u32[]{:S(2)}) collective-permute-start(bf16[2,2,128,128]{3,2,1,0:T(8,128)(2,1)S(1)} %get-tuple-element.23), channel_id=1, source_target_pairs={{0,48},{48,0},{12,60},{60,12},{24,72},{72,24},{36,84},{84,36},{96,... | collective-permute-start | bytes 393224 | tf_op jit(solution)/shard_map/ppermute | solution.py:18
  34.2 8.4 %copy-start.12 = (bf16[2,2,128,128]{3,2,1,0:T(8,128)(2,1)}, bf16[2,2,128,128]{3,2,1,0:T(8,128)(2,1)S(1)}, u32[]{:S(2)}) copy-start(bf16[2,2,128,128]{3,2,1,0:T(8,128)(2,1)S(1)} %collective-permute-done.2) | copy-start | bytes 393220
  34.9 14.4 %collective-permute-start.3 = (bf16[2,2,128,128]{3,2,1,0:T(8,128)(2,1)}, bf16[2,2,128,128]{3,2,1,0:T(8,128)(2,1)}, u32[]{:S(2)}, u32[]{:S(2)}) collective-permute-start(bf16[2,2,128,128]{3,2,1,0:T(8,128)(2,1)} %fusion.82), channel_id=1, source_target_pairs={{0,96},{96,0},{12,108},{108,12},{24,120},{120,24},{36,132},{132,36... | collective-permute-start | bytes 393224 | tf_op jit(solution)/shard_map/ppermute | solution.py:18
  44.6 10.4 %copy-start.2 = (bf16[6,64,2,128]{3,2,1,0:T(2,128)(2,1)}, bf16[6,64,2,128]{3,2,1,0:T(2,128)(2,1)S(1)}, u32[]{:S(2)}) copy-start(bf16[6,64,2,128]{3,2,1,0:T(2,128)(2,1)S(1)} %reshape.66) | copy-start | bytes 589828
  51.0 7.2 %collective-permute-start.4 = (bf16[2,2,128,128]{3,2,1,0:T(8,128)(2,1)}, bf16[2,2,128,128]{3,2,1,0:T(8,128)(2,1)}, u32[]{:S(2)}, u32[]{:S(2)}) collective-permute-start(bf16[2,2,128,128]{3,2,1,0:T(8,128)(2,1)} %fusion.81), channel_id=1, source_target_pairs={{0,192},{192,0},{12,204},{204,12},{24,216},{216,24},{36,228},{228,... | collective-permute-start | bytes 393224 | tf_op jit(solution)/shard_map/ppermute | solution.py:18
  56.0 12.8 %copy-start.35 = (bf16[2,2,128,128]{3,2,1,0:T(8,128)(2,1)S(1)}, bf16[2,2,128,128]{3,2,1,0:T(8,128)(2,1)}, u32[]{:S(2)}) copy-start(bf16[2,2,128,128]{3,2,1,0:T(8,128)(2,1)} %copy-done.34) | copy-start | bytes 393220
  56.0 12.8 %copy-start.13 = (bf16[2,2,128,128]{3,2,1,0:T(8,128)(2,1)S(1)}, bf16[2,2,128,128]{3,2,1,0:T(8,128)(2,1)}, u32[]{:S(2)}) copy-start(bf16[2,2,128,128]{3,2,1,0:T(8,128)(2,1)} %copy-done.12) | copy-start | bytes 393220
  59.4 13.1 %copy-start.1 = (f32[6,2,128,128]{3,2,1,0:T(8,128)S(1)}, f32[6,2,128,128]{3,2,1,0:T(8,128)}, u32[]{:S(2)}) copy-start(f32[6,2,128,128]{3,2,1,0:T(8,128)} %fusion.51) | copy-start | bytes 2359300
  59.4 11.6 %collective-permute-start.5 = (bf16[2,2,128,128]{3,2,1,0:T(8,128)(2,1)S(1)}, bf16[2,2,128,128]{3,2,1,0:T(8,128)(2,1)S(1)}, u32[]{:S(2)}, u32[]{:S(2)}) collective-permute-start(bf16[2,2,128,128]{3,2,1,0:T(8,128)(2,1)S(1)} %add_convert_fusion), channel_id=1, source_target_pairs={{0,384},{384,0},{12,396},{396,12},{24,408},{408,24},{36,420},{420,... | collective-permute-start | bytes 393224 | tf_op jit(solution)/shard_map/ppermute | solution.py:18
  67.7 5.5 %copy-start.29 = (bf16[6,2,64,64]{3,2,1,0:T(8,128)(2,1)}, bf16[6,2,64,64]{3,2,1,0:T(8,128)(2,1)S(1)}, u32[]{:S(2)}) copy-start(bf16[6,2,64,64]{3,2,1,0:T(8,128)(2,1)S(1)} %fusion.14) | copy-start | bytes 294916
  68.8 2.3 %copy-start.15 = (f32[2,2,128,128]{3,2,1,0:T(8,128)}, f32[2,2,128,128]{3,2,1,0:T(8,128)S(1)}, u32[]{:S(2)}) copy-start(f32[2,2,128,128]{3,2,1,0:T(8,128)S(1)} %convert_element_type.147) | copy-start | bytes 786436
  68.8 2.2 %copy-start.17 = (f32[2,2,128,128]{3,2,1,0:T(8,128)}, f32[2,2,128,128]{3,2,1,0:T(8,128)S(1)}, u32[]{:S(2)}) copy-start(f32[2,2,128,128]{3,2,1,0:T(8,128)S(1)} %convert_element_type.149) | copy-start | bytes 786436
  68.8 2.2 %copy-start.19 = (f32[2,2,128,128]{3,2,1,0:T(8,128)}, f32[2,2,128,128]{3,2,1,0:T(8,128)S(1)}, u32[]{:S(2)}) copy-start(f32[2,2,128,128]{3,2,1,0:T(8,128)S(1)} %convert_element_type.151) | copy-start | bytes 786436
  69.9 1.1 copy-start.21
  72.5 0.9 copy-start.3
  72.7 0.9 copy-start.7
  72.7 1.1 copy-start.9
  72.7 1.9 %copy-start.11 = (bf16[4096,256]{1,0:T(8,128)(2,1)S(1)}, bf16[4096,256]{1,0:T(8,128)(2,1)}, u32[]{:S(2)}) copy-start(bf16[4096,256]{1,0:T(8,128)(2,1)} %param.8) | copy-start | bytes 6291460
  90.3 12.6 %collective-permute-start.6 = (f32[4,8,64,256]{3,2,1,0:T(8,128)}, f32[4,8,64,256]{3,2,1,0:T(8,128)}, u32[]{:S(2)}, u32[]{:S(2)}) collective-permute-start(f32[4,8,64,256]{3,2,1,0:T(8,128)} %dynamic-slice_bitcast_fusion), channel_id=1, source_target_pairs={{0,12},{12,0},{24,36},{36,24},{48,60},{60,48},{72,84},{84,72},{96,... | collective-permute-start | bytes 6291464 | tf_op jit(solution)/shard_map/ppermute | solution.py:72
  94.1 4.2 %copy-start.16 = (f32[2,2,128,128]{3,2,1,0:T(8,128)S(1)}, f32[2,2,128,128]{3,2,1,0:T(8,128)}, u32[]{:S(2)}) copy-start(f32[2,2,128,128]{3,2,1,0:T(8,128)} %copy-done.15) | copy-start | bytes 786436
  94.1 4.2 %copy-start.18 = (f32[2,2,128,128]{3,2,1,0:T(8,128)S(1)}, f32[2,2,128,128]{3,2,1,0:T(8,128)}, u32[]{:S(2)}) copy-start(f32[2,2,128,128]{3,2,1,0:T(8,128)} %copy-done.17) | copy-start | bytes 786436
  94.1 4.2 %copy-start.20 = (f32[2,2,128,128]{3,2,1,0:T(8,128)S(1)}, f32[2,2,128,128]{3,2,1,0:T(8,128)}, u32[]{:S(2)}) copy-start(f32[2,2,128,128]{3,2,1,0:T(8,128)} %copy-done.19) | copy-start | bytes 786436
  94.1 4.2 %copy-start.22 = (f32[2,2,128,128]{3,2,1,0:T(8,128)S(1)}, f32[2,2,128,128]{3,2,1,0:T(8,128)}, u32[]{:S(2)}) copy-start(f32[2,2,128,128]{3,2,1,0:T(8,128)} %copy-done.21) | copy-start | bytes 786436
  94.1 4.2 %copy-start.24 = (f32[2,2,128,128]{3,2,1,0:T(8,128)S(1)}, f32[2,2,128,128]{3,2,1,0:T(8,128)}, u32[]{:S(2)}) copy-start(f32[2,2,128,128]{3,2,1,0:T(8,128)} %copy-done.23) | copy-start | bytes 786436
  94.1 4.2 %copy-start.26 = (f32[2,2,128,128]{3,2,1,0:T(8,128)S(1)}, f32[2,2,128,128]{3,2,1,0:T(8,128)}, u32[]{:S(2)}) copy-start(f32[2,2,128,128]{3,2,1,0:T(8,128)} %copy-done.25) | copy-start | bytes 786436
  106.2 2.5 %copy-start.4 = (bf16[6,64,2,128]{3,2,1,0:T(2,128)(2,1)S(1)}, bf16[6,64,2,128]{3,2,1,0:T(2,128)(2,1)}, u32[]{:S(2)}) copy-start(bf16[6,64,2,128]{3,2,1,0:T(2,128)(2,1)} %copy-done.2) | copy-start | bytes 589828
  106.2 2.8 %copy-start.5 = (bf16[6,64,2,128]{3,2,1,0:T(2,128)(2,1)S(1)}, bf16[6,64,2,128]{3,2,1,0:T(2,128)(2,1)}, u32[]{:S(2)}) copy-start(bf16[6,64,2,128]{3,2,1,0:T(2,128)(2,1)} %reshape.68) | copy-start | bytes 589828
  106.2 2.8 %copy-start.10 = (bf16[6,2,128,128]{3,2,1,0:T(8,128)(2,1)S(1)}, bf16[6,2,128,128]{3,2,1,0:T(8,128)(2,1)}, u32[]{:S(2)}) copy-start(bf16[6,2,128,128]{3,2,1,0:T(8,128)(2,1)} %copy-done.9) | copy-start | bytes 1179652
  106.3 3.5 %copy-start.30 = (bf16[6,2,64,64]{3,2,1,0:T(8,128)(2,1)S(1)}, bf16[6,2,64,64]{3,2,1,0:T(8,128)(2,1)}, u32[]{:S(2)}) copy-start(bf16[6,2,64,64]{3,2,1,0:T(8,128)(2,1)} %copy-done.29) | copy-start | bytes 294916
  106.3 11.2 %collective-permute-start.7 = (bf16[4,4,64,256]{3,2,1,0:T(8,128)(2,1)S(1)}, bf16[4,4,64,256]{3,2,1,0:T(8,128)(2,1)S(1)}, u32[]{:S(2)}, u32[]{:S(2)}) collective-permute-start(bf16[4,4,64,256]{3,2,1,0:T(8,128)(2,1)S(1)} %fusion.20), channel_id=1, source_target_pairs={{0,24},{12,180},{24,0},{36,60},{48,72},{60,36},{72,48},{84,108},{9... | collective-permute-start | bytes 1572872 | tf_op jit(solution)/shard_map/ppermute | solution.py:58
  109.4 1.0 copy-start.8
  110.4 17.5 %copy-start.31 = (bf16[6,2,64,64]{3,2,1,0:T(8,128)(2,1)S(1)}, bf16[6,2,64,64]{3,2,1,0:T(8,128)(2,1)}, u32[]{:S(2)}) copy-start(bf16[6,2,64,64]{3,2,1,0:T(8,128)(2,1)} %fusion.13) | copy-start | bytes 294916
  117.7 10.3 %collective-permute-start.8 = (bf16[4,64,256]{2,1,0:T(8,128)(2,1)S(1)}, bf16[4,64,256]{2,1,0:T(8,128)(2,1)S(1)}, u32[]{:S(2)}, u32[]{:S(2)}) collective-permute-start(bf16[4,64,256]{2,1,0:T(8,128)(2,1)S(1)} %get-tuple-element.25), channel_id=1, source_target_pairs={{0,192},{12,204},{24,216},{36,228},{48,240},{60,252},{72,264},{84,... | collective-permute-start | bytes 393224 | tf_op jit(solution)/shard_map/ppermute | solution.py:58
  122.6 12.0 %collective-permute-start.10 = (bf16[4,64,256]{2,1,0:T(8,128)(2,1)S(1)}, bf16[4,64,256]{2,1,0:T(8,128)(2,1)S(1)}, u32[]{:S(2)}, u32[]{:S(2)}) collective-permute-start(bf16[4,64,256]{2,1,0:T(8,128)(2,1)S(1)} %get-tuple-element.26), channel_id=1, source_target_pairs={{0,576},{12,588},{24,600},{36,612},{48,624},{60,636},{72,648},{84,... | collective-permute-start | bytes 393224 | tf_op jit(solution)/shard_map/ppermute | solution.py:58
  124.5 10.1 %collective-permute-start.9 = (bf16[4,64,256]{2,1,0:T(8,128)(2,1)S(1)}, bf16[4,64,256]{2,1,0:T(8,128)(2,1)S(1)}, u32[]{:S(2)}, u32[]{:S(2)}) collective-permute-start(bf16[4,64,256]{2,1,0:T(8,128)(2,1)S(1)} %get-tuple-element.27), channel_id=1, source_target_pairs={{0,384},{12,396},{24,408},{36,420},{48,432},{60,444},{72,456},{84,... | collective-permute-start | bytes 393224 | tf_op jit(solution)/shard_map/ppermute | solution.py:58
  134.7 16.0 %collective-permute-start.11 = (bf16[64,256]{1,0:T(8,128)(2,1)S(1)}, bf16[64,256]{1,0:T(8,128)(2,1)S(1)}, u32[]{:S(2)}, u32[]{:S(2)}) collective-permute-start(bf16[64,256]{1,0:T(8,128)(2,1)S(1)} %get-tuple-element.28), channel_id=1, source_target_pairs={{0,48},{12,60},{24,72},{36,84},{48,96},{60,108},{72,120},{84,132},... | collective-permute-start | bytes 98312 | tf_op jit(solution)/shard_map/ppermute | solution.py:58
  136.6 14.0 %collective-permute-start.13 = (bf16[64,256]{1,0:T(8,128)(2,1)S(1)}, bf16[64,256]{1,0:T(8,128)(2,1)S(1)}, u32[]{:S(2)}, u32[]{:S(2)}) collective-permute-start(bf16[64,256]{1,0:T(8,128)(2,1)S(1)} %get-tuple-element.29), channel_id=1, source_target_pairs={{0,144},{12,156},{24,168},{36,180},{48,0},{60,12},{72,24},{84,36},... | collective-permute-start | bytes 98312 | tf_op jit(solution)/shard_map/ppermute | solution.py:58
  142.6 9.7 %collective-permute-start.12 = (bf16[64,256]{1,0:T(8,128)(2,1)S(1)}, bf16[64,256]{1,0:T(8,128)(2,1)S(1)}, u32[]{:S(2)}, u32[]{:S(2)}) collective-permute-start(bf16[64,256]{1,0:T(8,128)(2,1)S(1)} %get-tuple-element.30), channel_id=1, source_target_pairs={{0,96},{12,108},{24,120},{36,132},{48,144},{60,156},{72,168},{84,1... | collective-permute-start | bytes 98312 | tf_op jit(solution)/shard_map/ppermute | solution.py:58
  (3 other events, 2.1 us)
Sparse Core Ops, SparseCore 0:
  77.4 65.1 reduce-scatter.1

commit v6 on v5

--- a/solution.py
+++ b/solution.py
@@ -143,12 +143,31 @@
     inflow = jnp.zeros_like(own_state)
     outflow = jnp.zeros_like(own_state)
     totals = jnp.stack([own_state, own_pairs])
-    for level in range(level_count):
+    level = 0
+    while level < level_count:
+        if seq_count == 64 and level == 2:
+            group = position >> level & 3
+            gathered = totals
+            for shift in range(1, 4):
+                route = []
+                for i in range(seq_count):
+                    mine = i >> level & 3
+                    target = i - (mine << level) + ((mine + shift) % 4 << level)
+                    route.append((i, target))
+                other = lax.ppermute(totals.astype(jnp.bfloat16), SEQ, route).astype(jnp.float32)
+                source = (group - shift) % 4
+                inflow = inflow + jnp.where(source < group, other[0], 0.0)
+                outflow = outflow + jnp.where(source > group, other[1], 0.0)
+                gathered = gathered + other
+            totals = gathered
+            level += 2
+            continue
         other = swapped(totals.astype(jnp.bfloat16), seq_count, level).astype(jnp.float32)
         upper_half = position >> level & 1 == 1
         inflow = inflow + jnp.where(upper_half, other[0], 0.0)
         outflow = outflow + jnp.where(upper_half, 0.0, other[1])
         totals = totals + other
+        level += 1
     before = inflow[None] + jnp.cumsum(key_value, 0) - key_value
     later_state = outflow[None] + own_pairs[None] - jnp.cumsum(query_pairs, 0)
     before_parts = split_state(before)

time: 162 us -> 164 us (1.012)
  waiting for transfers between devices: 32.9 us -> 25.8 us
  starting transfers between devices: 55.5 us -> 59.4 us
  other arithmetic: 13.9 us -> 17.1 us
    ppermute x0 -> x3, starting transfers between devices: none -> 14.5 us  [local(): lax.ppermute(totals.astype(jnp.bfloat16), SEQ, route).astype(jnp.float32)]
    ppermute x6 -> x4, waiting for transfers between devices: 17.9 us -> 6.81 us  [swapped(): return lax.ppermute(block, SEQ, route)]
    ppermute x6 -> x4, starting transfers between devices: 28.5 us -> 19.1 us  [swapped(): return lax.ppermute(block, SEQ, route)]
    ppermute x0 -> x3, waiting for transfers between devices: none -> 4.47 us  [local(): lax.ppermute(totals.astype(jnp.bfloat16), SEQ, route).astype(jnp.float32)]
    convert_element_type x0 -> x3, other arithmetic: none -> 3.05 us  [local(): lax.ppermute(totals.astype(jnp.bfloat16), SEQ, route).astype(jnp.float32)]
    convert_element_type x6 -> x5, other arithmetic: 3.73 us -> 3.85 us  [local(): totals.astype(jnp.bfloat16)]
    unnamed x76 -> x74, local copies, waits for them, and re-layouts: 4.85 us -> 4.83 us
  transfers between devices with their start and end apart: 15 -> 16, of which waited for: 8 -> 8; matrix products, arithmetic and copies ran while one was open for 25% -> 28% of each run, Pallas kernels for 0% -> 0%
where the time goes in v6:
time: 164 us; the launch traced here: 161 us
  starting transfers between devices  59.4 us (36%)
  waiting for transfers between devices  25.8 us (16%)
  matrix products  22.3 us (14%)
  local copies, waits for them, and re-layouts  21.7 us (13%)
  other arithmetic  17.1 us (10%)
  between operations  15.1 us (9%)
    ppermute x7, starting transfers between devices, wire(): lax.ppermute(block.astype(jnp.bfloat16), SEQ, route).astype(jnp.float32)  23.9 us
    ppermute x4, starting transfers between devices, swapped(): return lax.ppermute(block, SEQ, route)  19.1 us
    ppermute x7, waiting for transfers between devices, wire(): lax.ppermute(block.astype(jnp.bfloat16), SEQ, route).astype(jnp.float32)  14.5 us
    ppermute x3, starting transfers between devices, local(): lax.ppermute(totals.astype(jnp.bfloat16), SEQ, route).astype(jnp.float32)  14.5 us
    ppermute x4, waiting for transfers between devices, swapped(): return lax.ppermute(block, SEQ, route)  6.81 us
    dot_general x1, local copies, waits for them, and re-layouts, local(): lax.dot_general(out_grad, attention, (((0,), (0,)), ((), ())), preferred_...  5.61 us
    unnamed x74, local copies, waits for them, and re-layouts  4.83 us
    ppermute x3, waiting for transfers between devices, local(): lax.ppermute(totals.astype(jnp.bfloat16), SEQ, route).astype(jnp.float32)  4.47 us
  transfers between devices with their start and end apart: 16, of which 8 were waited for; matrix products, arithmetic and copies ran while one was open for 28% of the time, Pallas kernels for 0%

profile of v6, /device:TPU:6, one launch (start us, length us, event | category | flops | bytes accessed | tf_op | source)
XLA Modules:
  0.0 161.4 jit_solution(12906933786148276183)
XLA Ops:
  7.2 1.3 convolution_bitcast_fusion.5
  8.5 1.1 convolution_bitcast_fusion.6
  9.7 2.6 %convolution_convert_fusion.1 = bf16[384,256]{1,0:T(8,128)(2,1)S(1)} fusion(bf16[384,4096]{1,0:T(8,128)(2,1)S(1)} %copy-done, bf16[4096,256]{1,0:T(8,128)(2,1)} %param.8), kind=kOutput, calls=%fused_computation.37 | convolution fusion | flops 805404672 | bytes 5439488 | tf_op jit(solution)/shard_map/dot_general | solution.py:117
  13.1 1.9 %collective-permute-start = (bf16[2,2,128,128]{3,2,1,0:T(8,128)(2,1)S(1)}, bf16[2,2,128,128]{3,2,1,0:T(8,128)(2,1)S(1)}, u32[]{:S(2)}, u32[]{:S(2)}) collective-permute-start(bf16[2,2,128,128]{3,2,1,0:T(8,128)(2,1)S(1)} %fusion.24), channel_id=1, source_target_pairs={{0,12},{12,0},{24,36},{36,24},{48,60},{60,48},{72,84},{84,72},{96,... | collective-permute-start | bytes 393224 | tf_op jit(solution)/shard_map/ppermute | solution.py:18
  15.0 1.3 collective-permute-done
  16.4 3.5 %collective-permute-start.1 = (bf16[2,2,128,128]{3,2,1,0:T(8,128)(2,1)S(1)}, bf16[2,2,128,128]{3,2,1,0:T(8,128)(2,1)S(1)}, u32[]{:S(2)}, u32[]{:S(2)}) collective-permute-start(bf16[2,2,128,128]{3,2,1,0:T(8,128)(2,1)S(1)} %fusion.79), channel_id=1, source_target_pairs={{0,24},{24,0},{12,36},{36,12},{48,72},{72,48},{60,84},{84,60},{96,... | collective-permute-start | bytes 393224 | tf_op jit(solution)/shard_map/ppermute | solution.py:18
  19.9 4.0 %collective-permute-done.1 = bf16[2,2,128,128]{3,2,1,0:T(8,128)(2,1)S(1)} collective-permute-done((bf16[2,2,128,128]{3,2,1,0:T(8,128)(2,1)S(1)}, bf16[2,2,128,128]{3,2,1,0:T(8,128)(2,1)S(1)}, u32[]{:S(2)}, u32[]{:S(2)}) %collective-permute-start.1) | collective-permute-done | bytes 131104 | tf_op jit(solution)/shard_map/ppermute | solution.py:18
  24.5 6.2 %collective-permute-start.4 = (bf16[2,2,128,128]{3,2,1,0:T(8,128)(2,1)}, bf16[2,2,128,128]{3,2,1,0:T(8,128)(2,1)}, u32[]{:S(2)}, u32[]{:S(2)}) collective-permute-start(bf16[2,2,128,128]{3,2,1,0:T(8,128)(2,1)} %fusion.83), channel_id=1, source_target_pairs={{0,144},{12,156},{24,168},{36,180},{48,0},{60,12},{72,24},{84,36},... | collective-permute-start | bytes 393224 | tf_op jit(solution)/shard_map/ppermute | solution.py:157
  30.7 3.8 %collective-permute-start.3 = (bf16[2,2,128,128]{3,2,1,0:T(8,128)(2,1)}, bf16[2,2,128,128]{3,2,1,0:T(8,128)(2,1)}, u32[]{:S(2)}, u32[]{:S(2)}) collective-permute-start(bf16[2,2,128,128]{3,2,1,0:T(8,128)(2,1)} %fusion.83), channel_id=1, source_target_pairs={{0,96},{12,108},{24,120},{36,132},{48,144},{60,156},{72,168},{84,1... | collective-permute-start | bytes 393224 | tf_op jit(solution)/shard_map/ppermute | solution.py:157
  34.5 4.5 %collective-permute-start.2 = (bf16[2,2,128,128]{3,2,1,0:T(8,128)(2,1)}, bf16[2,2,128,128]{3,2,1,0:T(8,128)(2,1)}, u32[]{:S(2)}, u32[]{:S(2)}) collective-permute-start(bf16[2,2,128,128]{3,2,1,0:T(8,128)(2,1)} %fusion.83), channel_id=1, source_target_pairs={{0,48},{12,60},{24,72},{36,84},{48,96},{60,108},{72,120},{84,132},... | collective-permute-start | bytes 393224 | tf_op jit(solution)/shard_map/ppermute | solution.py:157
  41.0 4.5 %collective-permute-done.3 = bf16[2,2,128,128]{3,2,1,0:T(8,128)(2,1)} collective-permute-done((bf16[2,2,128,128]{3,2,1,0:T(8,128)(2,1)}, bf16[2,2,128,128]{3,2,1,0:T(8,128)(2,1)}, u32[]{:S(2)}, u32[]{:S(2)}) %collective-permute-start.3) | collective-permute-done | bytes 131104 | tf_op jit(solution)/shard_map/ppermute | solution.py:157
  45.5 2.1 %fusion.87 = (bf16[2,2,128,128]{3,2,1,0:T(8,128)(2,1)}, f32[2,2,128,128]{3,2,1,0:T(8,128)}) fusion(bf16[2,2,128,128]{3,2,1,0:T(8,128)(2,1)} %collective-permute-done.4, bf16[2,2,128,128]{3,2,1,0:T(8,128)(2,1)} %collective-permute-done.3, bf16[2,2,128,128]{3,2,1,0:T(8,128)(2,1)} %collective-permute-done.2, bf16[2,2,128,128]{3,2,1,0:T(8,128)(2,1)} %copy-done.13, ...), kind=kLoop, calls=%fused_computation.144 | loop fusion | flops 786432 | bytes 1310720 | tf_op jit(solution)/shard_map/convert_element_type | solution.py:165
  47.6 2.7 %collective-permute-start.5 = (bf16[2,2,128,128]{3,2,1,0:T(8,128)(2,1)}, bf16[2,2,128,128]{3,2,1,0:T(8,128)(2,1)}, u32[]{:S(2)}, u32[]{:S(2)}) collective-permute-start(bf16[2,2,128,128]{3,2,1,0:T(8,128)(2,1)} %get-tuple-element.23), channel_id=1, source_target_pairs={{0,192},{192,0},{12,204},{204,12},{24,216},{216,24},{36,228},{228,... | collective-permute-start | bytes 393224 | tf_op jit(solution)/shard_map/ppermute | solution.py:18
  50.3 1.2 fusion.53
  51.5 1.7 %reshape.64 = bf16[6,64,2,128]{3,2,1,0:T(2,128)(2,1)} reshape(bf16[384,256]{1,0:T(8,128)(2,1)} %param.5) | data formatting | bytes 393216 | tf_op jit(solution)/shard_map/reshape | solution.py:113
  53.2 1.5 collective-permute-done.5
  54.7 1.0 add_convert_fusion
  55.8 10.9 %collective-permute-start.6 = (bf16[2,2,128,128]{3,2,1,0:T(8,128)(2,1)S(1)}, bf16[2,2,128,128]{3,2,1,0:T(8,128)(2,1)S(1)}, u32[]{:S(2)}, u32[]{:S(2)}) collective-permute-start(bf16[2,2,128,128]{3,2,1,0:T(8,128)(2,1)S(1)} %add_convert_fusion), channel_id=1, source_target_pairs={{0,384},{384,0},{12,396},{396,12},{24,408},{408,24},{36,420},{420,... | collective-permute-start | bytes 393224 | tf_op jit(solution)/shard_map/ppermute | solution.py:18
  66.7 1.2 fusion.14
  67.9 1.0 convert_element_type.149
  68.9 1.0 convert_element_type.151
  69.9 1.0 convert_element_type.153
  71.0 1.0 convert_element_type.154
  72.0 1.0 convert_element_type.155
  73.1 1.0 convert_element_type.157
  77.7 2.6 %convolution_convert_fusion = bf16[384,4096]{1,0:T(8,128)(2,1)} fusion(bf16[4096,256]{1,0:T(8,128)(2,1)S(1)} %copy-done.11, bf16[48,8,2,128]{3,2,1,0:T(2,128)(2,1)S(1)} %bitcast.133), kind=kOutput, calls=%fused_computation | convolution fusion | flops 806879232 | bytes 5439488 | tf_op jit(solution)/shard_map/dot_general | solution.py:184
  80.4 4.2 %convolution_bitcast_fusion = f32[4096,256]{0,1:T(8,128)} fusion(bf16[384,256]{1,0:T(8,128)(2,1)} %bitcast.137, bf16[384,4096]{1,0:T(8,128)(2,1)S(1)} %copy-done), kind=kOutput, calls=%fused_computation.1 | convolution fusion | flops 805306368 | bytes 7536640 | tf_op jit(solution)/shard_map/dot_general | solution.py:189
  84.6 5.6 %copy.52 = f32[4096,256]{1,0:T(8,128)} copy(f32[4096,256]{0,1:T(8,128)} %convolution_bitcast_fusion) | data formatting | bytes 8388608 | tf_op jit(solution)/shard_map/dot_general | solution.py:189
  90.2 3.2 %dynamic-slice_bitcast_fusion = f32[4,8,64,256]{3,2,1,0:T(8,128)} fusion(f32[4,8,2,64,256]{4,3,2,1,0:T(8,128)} %bitcast.128, s32[]{:T(128)S(6)} %select_n.235), kind=kLoop, calls=%fused_computation.4 | loop fusion | bytes 4194308 | tf_op jit(solution)/shard_map/jit(dynamic_index_in_dim)/squeeze | solution.py:71
  93.4 1.9 %collective-permute-start.7 = (f32[4,8,64,256]{3,2,1,0:T(8,128)}, f32[4,8,64,256]{3,2,1,0:T(8,128)}, u32[]{:S(2)}, u32[]{:S(2)}) collective-permute-start(f32[4,8,64,256]{3,2,1,0:T(8,128)} %dynamic-slice_bitcast_fusion), channel_id=1, source_target_pairs={{0,12},{12,0},{24,36},{36,24},{48,60},{60,48},{72,84},{84,72},{96,... | collective-permute-start | bytes 6291464 | tf_op jit(solution)/shard_map/ppermute | solution.py:72
  95.6 1.7 %reshape.68 = bf16[6,64,2,128]{3,2,1,0:T(2,128)(2,1)} reshape(bf16[384,256]{1,0:T(8,128)(2,1)} %copy-done.29) | data formatting | bytes 393216 | tf_op jit(solution)/shard_map/reshape | solution.py:120
  97.3 2.0 %fusion.13 = bf16[6,2,64,64]{3,2,1,0:T(8,128)(2,1)} fusion(pred[64,64]{1,0:T(8,128)(4,1)S(1)} %iota_compare_fusion, bf16[6,64,2,128]{3,2,1,0:T(2,128)(2,1)} %reshape.68, bf16[6,64,2,128]{3,2,1,0:T(2,128)(2,1)S(1)} %reshape.66), kind=kOutput, calls=%fused_computation.31 | convolution fusion | flops 12730368 | bytes 495616 | tf_op jit(solution)/shard_map/cthe,cshe->chts/dot_general | solution.py:198
  99.2 2.2 %convolution_bitcast_fusion.1 = f32[6,2,128,128]{2,3,1,0:T(8,128)} fusion(bf16[6,64,2,128]{3,2,1,0:T(2,128)(2,1)} %reshape.68, bf16[6,64,2,128]{3,2,1,0:T(2,128)(2,1)} %reshape.64), kind=kOutput, calls=%fused_computation.8 | convolution fusion | flops 25165824 | bytes 1179648 | tf_op jit(solution)/shard_map/cthd,cthe->chde/dot_general | solution.py:124
  101.5 1.6 fusion.30
  103.1 1.7 %copy.53 = f32[2,128,128]{1,2,0:T(8,128)} copy(f32[2,128,128]{2,1,0:T(8,128)} %fusion.30) | data formatting | bytes 262144 | tf_op jit(solution)/shard_map/sub | solution.py:172
  104.8 1.3 subtract_convert_fusion
  106.1 2.6 %bitcast_add_fusion = f32[4,8,64,256]{3,2,1,0:T(8,128)S(1)} fusion(f32[4,8,64,256]{3,2,1,0:T(8,128)} %collective-permute-done.7, f32[4,8,2,64,256]{4,3,2,1,0:T(8,128)} %bitcast.129, s32[]{:T(128)S(6)} %select_n.234), kind=kLoop, calls=%fused_computation.3 | loop fusion | flops 524288 | bytes 6291460 | tf_op jit(solution)/shard_map/add | solution.py:72
  109.5 4.4 %collective-permute-start.8 = (bf16[4,4,64,256]{3,2,1,0:T(8,128)(2,1)S(1)}, bf16[4,4,64,256]{3,2,1,0:T(8,128)(2,1)S(1)}, u32[]{:S(2)}, u32[]{:S(2)}) collective-permute-start(bf16[4,4,64,256]{3,2,1,0:T(8,128)(2,1)S(1)} %fusion.20), channel_id=1, source_target_pairs={{0,24},{12,180},{24,0},{36,60},{48,72},{60,36},{72,48},{84,108},{9... | collective-permute-start | bytes 1572872 | tf_op jit(solution)/shard_map/ppermute | solution.py:58
  116.3 4.8 %collective-permute-done.8 = bf16[4,4,64,256]{3,2,1,0:T(8,128)(2,1)S(1)} collective-permute-done((bf16[4,4,64,256]{3,2,1,0:T(8,128)(2,1)S(1)}, bf16[4,4,64,256]{3,2,1,0:T(8,128)(2,1)S(1)}, u32[]{:S(2)}, u32[]{:S(2)}) %collective-permute-start.8) | collective-permute-done | bytes 524320 | tf_op jit(solution)/shard_map/ppermute | solution.py:58
  121.3 2.3 %collective-permute-start.9 = (bf16[4,64,256]{2,1,0:T(8,128)(2,1)S(1)}, bf16[4,64,256]{2,1,0:T(8,128)(2,1)S(1)}, u32[]{:S(2)}, u32[]{:S(2)}) collective-permute-start(bf16[4,64,256]{2,1,0:T(8,128)(2,1)S(1)} %get-tuple-element.25), channel_id=1, source_target_pairs={{0,192},{12,204},{24,216},{36,228},{48,240},{60,252},{72,264},{84,... | collective-permute-start | bytes 393224 | tf_op jit(solution)/shard_map/ppermute | solution.py:58
  123.6 3.7 %collective-permute-start.11 = (bf16[4,64,256]{2,1,0:T(8,128)(2,1)S(1)}, bf16[4,64,256]{2,1,0:T(8,128)(2,1)S(1)}, u32[]{:S(2)}, u32[]{:S(2)}) collective-permute-start(bf16[4,64,256]{2,1,0:T(8,128)(2,1)S(1)} %get-tuple-element.26), channel_id=1, source_target_pairs={{0,576},{12,588},{24,600},{36,612},{48,624},{60,636},{72,648},{84,... | collective-permute-start | bytes 393224 | tf_op jit(solution)/shard_map/ppermute | solution.py:58
  127.3 3.1 %collective-permute-start.10 = (bf16[4,64,256]{2,1,0:T(8,128)(2,1)S(1)}, bf16[4,64,256]{2,1,0:T(8,128)(2,1)S(1)}, u32[]{:S(2)}, u32[]{:S(2)}) collective-permute-start(bf16[4,64,256]{2,1,0:T(8,128)(2,1)S(1)} %get-tuple-element.27), channel_id=1, source_target_pairs={{0,384},{12,396},{24,408},{36,420},{48,432},{60,444},{72,456},{84,... | collective-permute-start | bytes 393224 | tf_op jit(solution)/shard_map/ppermute | solution.py:58
  130.6 1.9 %collective-permute-done.11 = bf16[4,64,256]{2,1,0:T(8,128)(2,1)S(1)} collective-permute-done((bf16[4,64,256]{2,1,0:T(8,128)(2,1)S(1)}, bf16[4,64,256]{2,1,0:T(8,128)(2,1)S(1)}, u32[]{:S(2)}, u32[]{:S(2)}) %collective-permute-start.11) | collective-permute-done | bytes 131104 | tf_op jit(solution)/shard_map/ppermute | solution.py:58
  132.5 3.7 %collective-permute-done.10 = bf16[4,64,256]{2,1,0:T(8,128)(2,1)S(1)} collective-permute-done((bf16[4,64,256]{2,1,0:T(8,128)(2,1)S(1)}, bf16[4,64,256]{2,1,0:T(8,128)(2,1)S(1)}, u32[]{:S(2)}, u32[]{:S(2)}) %collective-permute-start.10) | collective-permute-done | bytes 131104 | tf_op jit(solution)/shard_map/ppermute | solution.py:58
  136.2 1.9 %collective-permute-start.12 = (bf16[64,256]{1,0:T(8,128)(2,1)S(1)}, bf16[64,256]{1,0:T(8,128)(2,1)S(1)}, u32[]{:S(2)}, u32[]{:S(2)}) collective-permute-start(bf16[64,256]{1,0:T(8,128)(2,1)S(1)} %get-tuple-element.28), channel_id=1, source_target_pairs={{0,48},{12,60},{24,72},{36,84},{48,96},{60,108},{72,120},{84,132},... | collective-permute-start | bytes 98312 | tf_op jit(solution)/shard_map/ppermute | solution.py:58
  138.2 6.0 %collective-permute-start.14 = (bf16[64,256]{1,0:T(8,128)(2,1)S(1)}, bf16[64,256]{1,0:T(8,128)(2,1)S(1)}, u32[]{:S(2)}, u32[]{:S(2)}) collective-permute-start(bf16[64,256]{1,0:T(8,128)(2,1)S(1)} %get-tuple-element.29), channel_id=1, source_target_pairs={{0,144},{12,156},{24,168},{36,180},{48,0},{60,12},{72,24},{84,36},... | collective-permute-start | bytes 98312 | tf_op jit(solution)/shard_map/ppermute | solution.py:58
  144.2 2.5 %collective-permute-start.13 = (bf16[64,256]{1,0:T(8,128)(2,1)S(1)}, bf16[64,256]{1,0:T(8,128)(2,1)S(1)}, u32[]{:S(2)}, u32[]{:S(2)}) collective-permute-start(bf16[64,256]{1,0:T(8,128)(2,1)S(1)} %get-tuple-element.30), channel_id=1, source_target_pairs={{0,96},{12,108},{24,120},{36,132},{48,144},{60,156},{72,168},{84,1... | collective-permute-start | bytes 98312 | tf_op jit(solution)/shard_map/ppermute | solution.py:58
  149.7 4.2 %collective-permute-done.13 = bf16[64,256]{1,0:T(8,128)(2,1)S(1)} collective-permute-done((bf16[64,256]{1,0:T(8,128)(2,1)S(1)}, bf16[64,256]{1,0:T(8,128)(2,1)S(1)}, u32[]{:S(2)}, u32[]{:S(2)}) %collective-permute-start.13) | collective-permute-done | bytes 32800 | tf_op jit(solution)/shard_map/ppermute | solution.py:58
  (121 shorter events, 14.1 us)
Async XLA Ops:
  7.2 2.5 %copy-start = (bf16[384,4096]{1,0:T(8,128)(2,1)S(1)}, bf16[384,4096]{1,0:T(8,128)(2,1)}, u32[]{:S(2)}) copy-start(bf16[384,4096]{1,0:T(8,128)(2,1)} %param.9) | copy-start | bytes 9437188
  7.2 147.4 %reduce-scatter.2.cloned.1.call-start = ((), (), s32[]{:S(2)}) async-start(), calls=%async_computation.1 | async-start | bytes 3407872 | tf_op jit(solution)/shard_map/reduce_scatter | solution.py:188
  9.7 2.6 %copy-start.28 = (bf16[384,256]{1,0:T(8,128)(2,1)S(1)}, bf16[384,256]{1,0:T(8,128)(2,1)}, u32[]{:S(2)}) copy-start(bf16[384,256]{1,0:T(8,128)(2,1)} %param.5) | copy-start | bytes 589828
  12.6 3.7 %copy-start.33 = (f32[128,128]{0,1:T(8,128)}, f32[128,128]{0,1:T(8,128)S(1)}, u32[]{:S(2)}) copy-start(f32[128,128]{0,1:T(8,128)S(1)} %fusion.68) | copy-start | bytes 196612
  12.8 3.5 %copy-start.34 = (f32[128,128]{0,1:T(8,128)}, f32[128,128]{0,1:T(8,128)S(1)}, u32[]{:S(2)}) copy-start(f32[128,128]{0,1:T(8,128)S(1)} %fusion.70) | copy-start | bytes 196612
  13.0 21.5 %copy-start.9 = (f32[1,2,128,128]{3,2,1,0:T(8,128)}, f32[1,2,128,128]{3,2,1,0:T(8,128)S(1)}, u32[]{:S(2)}) copy-start(f32[1,2,128,128]{3,2,1,0:T(8,128)S(1)} %get-tuple-element.31) | copy-start | bytes 393220
  13.0 21.5 %copy-start.10 = (f32[1,2,128,128]{3,2,1,0:T(8,128)}, f32[1,2,128,128]{3,2,1,0:T(8,128)S(1)}, u32[]{:S(2)}) copy-start(f32[1,2,128,128]{3,2,1,0:T(8,128)S(1)} %get-tuple-element.32) | copy-start | bytes 393220
  13.1 3.2 %collective-permute-start = (bf16[2,2,128,128]{3,2,1,0:T(8,128)(2,1)S(1)}, bf16[2,2,128,128]{3,2,1,0:T(8,128)(2,1)S(1)}, u32[]{:S(2)}, u32[]{:S(2)}) collective-permute-start(bf16[2,2,128,128]{3,2,1,0:T(8,128)(2,1)S(1)} %fusion.24), channel_id=1, source_target_pairs={{0,12},{12,0},{24,36},{36,24},{48,60},{60,48},{72,84},{84,72},{96,... | collective-permute-start | bytes 393224 | tf_op jit(solution)/shard_map/ppermute | solution.py:18
  16.3 22.7 %copy-start.12 = (bf16[2,2,128,128]{3,2,1,0:T(8,128)(2,1)}, bf16[2,2,128,128]{3,2,1,0:T(8,128)(2,1)S(1)}, u32[]{:S(2)}) copy-start(bf16[2,2,128,128]{3,2,1,0:T(8,128)(2,1)S(1)} %collective-permute-done) | copy-start | bytes 393220
  16.4 7.4 %collective-permute-start.1 = (bf16[2,2,128,128]{3,2,1,0:T(8,128)(2,1)S(1)}, bf16[2,2,128,128]{3,2,1,0:T(8,128)(2,1)S(1)}, u32[]{:S(2)}, u32[]{:S(2)}) collective-permute-start(bf16[2,2,128,128]{3,2,1,0:T(8,128)(2,1)S(1)} %fusion.79), channel_id=1, source_target_pairs={{0,24},{24,0},{12,36},{36,12},{48,72},{72,48},{60,84},{84,60},{96,... | collective-permute-start | bytes 393224 | tf_op jit(solution)/shard_map/ppermute | solution.py:18
  23.8 10.7 %copy-start.13 = (bf16[2,2,128,128]{3,2,1,0:T(8,128)(2,1)}, bf16[2,2,128,128]{3,2,1,0:T(8,128)(2,1)S(1)}, u32[]{:S(2)}) copy-start(bf16[2,2,128,128]{3,2,1,0:T(8,128)(2,1)S(1)} %collective-permute-done.1) | copy-start | bytes 393220
  24.5 16.5 %collective-permute-start.4 = (bf16[2,2,128,128]{3,2,1,0:T(8,128)(2,1)}, bf16[2,2,128,128]{3,2,1,0:T(8,128)(2,1)}, u32[]{:S(2)}, u32[]{:S(2)}) collective-permute-start(bf16[2,2,128,128]{3,2,1,0:T(8,128)(2,1)} %fusion.83), channel_id=1, source_target_pairs={{0,144},{12,156},{24,168},{36,180},{48,0},{60,12},{72,24},{84,36},... | collective-permute-start | bytes 393224 | tf_op jit(solution)/shard_map/ppermute | solution.py:157
  30.7 14.8 %collective-permute-start.3 = (bf16[2,2,128,128]{3,2,1,0:T(8,128)(2,1)}, bf16[2,2,128,128]{3,2,1,0:T(8,128)(2,1)}, u32[]{:S(2)}, u32[]{:S(2)}) collective-permute-start(bf16[2,2,128,128]{3,2,1,0:T(8,128)(2,1)} %fusion.83), channel_id=1, source_target_pairs={{0,96},{12,108},{24,120},{36,132},{48,144},{60,156},{72,168},{84,1... | collective-permute-start | bytes 393224 | tf_op jit(solution)/shard_map/ppermute | solution.py:157
  34.5 11.0 %collective-permute-start.2 = (bf16[2,2,128,128]{3,2,1,0:T(8,128)(2,1)}, bf16[2,2,128,128]{3,2,1,0:T(8,128)(2,1)}, u32[]{:S(2)}, u32[]{:S(2)}) collective-permute-start(bf16[2,2,128,128]{3,2,1,0:T(8,128)(2,1)} %fusion.83), channel_id=1, source_target_pairs={{0,48},{12,60},{24,72},{36,84},{48,96},{60,108},{72,120},{84,132},... | collective-permute-start | bytes 393224 | tf_op jit(solution)/shard_map/ppermute | solution.py:157
  47.6 7.2 %collective-permute-start.5 = (bf16[2,2,128,128]{3,2,1,0:T(8,128)(2,1)}, bf16[2,2,128,128]{3,2,1,0:T(8,128)(2,1)}, u32[]{:S(2)}, u32[]{:S(2)}) collective-permute-start(bf16[2,2,128,128]{3,2,1,0:T(8,128)(2,1)} %get-tuple-element.23), channel_id=1, source_target_pairs={{0,192},{192,0},{12,204},{204,12},{24,216},{216,24},{36,228},{228,... | collective-permute-start | bytes 393224 | tf_op jit(solution)/shard_map/ppermute | solution.py:18
  55.8 18.3 %collective-permute-start.6 = (bf16[2,2,128,128]{3,2,1,0:T(8,128)(2,1)S(1)}, bf16[2,2,128,128]{3,2,1,0:T(8,128)(2,1)S(1)}, u32[]{:S(2)}, u32[]{:S(2)}) collective-permute-start(bf16[2,2,128,128]{3,2,1,0:T(8,128)(2,1)S(1)} %add_convert_fusion), channel_id=1, source_target_pairs={{0,384},{384,0},{12,396},{396,12},{24,408},{408,24},{36,420},{420,... | collective-permute-start | bytes 393224 | tf_op jit(solution)/shard_map/ppermute | solution.py:18
  67.9 8.4 %copy-start.30 = (bf16[6,2,64,64]{3,2,1,0:T(8,128)(2,1)}, bf16[6,2,64,64]{3,2,1,0:T(8,128)(2,1)S(1)}, u32[]{:S(2)}) copy-start(bf16[6,2,64,64]{3,2,1,0:T(8,128)(2,1)S(1)} %fusion.14) | copy-start | bytes 294916
  67.9 7.7 %copy-start.1 = (f32[6,2,128,128]{3,2,1,0:T(8,128)S(1)}, f32[6,2,128,128]{3,2,1,0:T(8,128)}, u32[]{:S(2)}) copy-start(f32[6,2,128,128]{3,2,1,0:T(8,128)} %fusion.53) | copy-start | bytes 2359300
  68.9 5.2 %copy-start.14 = (f32[2,2,128,128]{3,2,1,0:T(8,128)}, f32[2,2,128,128]{3,2,1,0:T(8,128)S(1)}, u32[]{:S(2)}) copy-start(f32[2,2,128,128]{3,2,1,0:T(8,128)S(1)} %convert_element_type.149) | copy-start | bytes 786436
  69.9 4.2 %copy-start.16 = (f32[2,2,128,128]{3,2,1,0:T(8,128)}, f32[2,2,128,128]{3,2,1,0:T(8,128)S(1)}, u32[]{:S(2)}) copy-start(f32[2,2,128,128]{3,2,1,0:T(8,128)S(1)} %convert_element_type.151) | copy-start | bytes 786436
  71.0 3.2 %copy-start.18 = (f32[2,2,128,128]{3,2,1,0:T(8,128)}, f32[2,2,128,128]{3,2,1,0:T(8,128)S(1)}, u32[]{:S(2)}) copy-start(f32[2,2,128,128]{3,2,1,0:T(8,128)S(1)} %convert_element_type.153) | copy-start | bytes 786436
  72.0 2.2 %copy-start.20 = (f32[2,2,128,128]{3,2,1,0:T(8,128)}, f32[2,2,128,128]{3,2,1,0:T(8,128)S(1)}, u32[]{:S(2)}) copy-start(f32[2,2,128,128]{3,2,1,0:T(8,128)S(1)} %convert_element_type.154) | copy-start | bytes 786436
  73.0 1.1 copy-start.22
  73.0 2.8 %copy-start.2 = (bf16[6,64,2,128]{3,2,1,0:T(2,128)(2,1)S(1)}, bf16[6,64,2,128]{3,2,1,0:T(2,128)(2,1)}, u32[]{:S(2)}) copy-start(bf16[6,64,2,128]{3,2,1,0:T(2,128)(2,1)} %reshape.64) | copy-start | bytes 589828
  75.8 0.8 copy-start.5
  75.8 1.0 copy-start.7
  75.8 1.9 %copy-start.11 = (bf16[4096,256]{1,0:T(8,128)(2,1)S(1)}, bf16[4096,256]{1,0:T(8,128)(2,1)}, u32[]{:S(2)}) copy-start(bf16[4096,256]{1,0:T(8,128)(2,1)} %param.8) | copy-start | bytes 6291460
  93.4 12.7 %collective-permute-start.7 = (f32[4,8,64,256]{3,2,1,0:T(8,128)}, f32[4,8,64,256]{3,2,1,0:T(8,128)}, u32[]{:S(2)}, u32[]{:S(2)}) collective-permute-start(f32[4,8,64,256]{3,2,1,0:T(8,128)} %dynamic-slice_bitcast_fusion), channel_id=1, source_target_pairs={{0,12},{12,0},{24,36},{36,24},{48,60},{60,48},{72,84},{84,72},{96,... | collective-permute-start | bytes 6291464 | tf_op jit(solution)/shard_map/ppermute | solution.py:72
  97.2 4.3 %copy-start.15 = (f32[2,2,128,128]{3,2,1,0:T(8,128)S(1)}, f32[2,2,128,128]{3,2,1,0:T(8,128)}, u32[]{:S(2)}) copy-start(f32[2,2,128,128]{3,2,1,0:T(8,128)} %copy-done.14) | copy-start | bytes 786436
  97.2 4.3 %copy-start.17 = (f32[2,2,128,128]{3,2,1,0:T(8,128)S(1)}, f32[2,2,128,128]{3,2,1,0:T(8,128)}, u32[]{:S(2)}) copy-start(f32[2,2,128,128]{3,2,1,0:T(8,128)} %copy-done.16) | copy-start | bytes 786436
  97.2 4.3 %copy-start.19 = (f32[2,2,128,128]{3,2,1,0:T(8,128)S(1)}, f32[2,2,128,128]{3,2,1,0:T(8,128)}, u32[]{:S(2)}) copy-start(f32[2,2,128,128]{3,2,1,0:T(8,128)} %copy-done.18) | copy-start | bytes 786436
  97.2 4.3 %copy-start.21 = (f32[2,2,128,128]{3,2,1,0:T(8,128)S(1)}, f32[2,2,128,128]{3,2,1,0:T(8,128)}, u32[]{:S(2)}) copy-start(f32[2,2,128,128]{3,2,1,0:T(8,128)} %copy-done.20) | copy-start | bytes 786436
  97.2 4.3 %copy-start.23 = (f32[2,2,128,128]{3,2,1,0:T(8,128)S(1)}, f32[2,2,128,128]{3,2,1,0:T(8,128)}, u32[]{:S(2)}) copy-start(f32[2,2,128,128]{3,2,1,0:T(8,128)} %copy-done.22) | copy-start | bytes 786436
  97.2 4.3 %copy-start.25 = (f32[2,2,128,128]{3,2,1,0:T(8,128)S(1)}, f32[2,2,128,128]{3,2,1,0:T(8,128)}, u32[]{:S(2)}) copy-start(f32[2,2,128,128]{3,2,1,0:T(8,128)} %copy-done.24) | copy-start | bytes 786436
  97.2 4.3 %copy-start.27 = (f32[2,2,128,128]{3,2,1,0:T(8,128)S(1)}, f32[2,2,128,128]{3,2,1,0:T(8,128)}, u32[]{:S(2)}) copy-start(f32[2,2,128,128]{3,2,1,0:T(8,128)} %copy-done.26) | copy-start | bytes 786436
  109.4 5.2 %copy-start.4 = (bf16[6,64,2,128]{3,2,1,0:T(2,128)(2,1)S(1)}, bf16[6,64,2,128]{3,2,1,0:T(2,128)(2,1)}, u32[]{:S(2)}) copy-start(bf16[6,64,2,128]{3,2,1,0:T(2,128)(2,1)} %reshape.68) | copy-start | bytes 589828
  109.4 5.2 %copy-start.8 = (bf16[6,2,128,128]{3,2,1,0:T(8,128)(2,1)S(1)}, bf16[6,2,128,128]{3,2,1,0:T(8,128)(2,1)}, u32[]{:S(2)}) copy-start(bf16[6,2,128,128]{3,2,1,0:T(8,128)(2,1)} %copy-done.7) | copy-start | bytes 1179652
  109.5 5.8 %copy-start.31 = (bf16[6,2,64,64]{3,2,1,0:T(8,128)(2,1)S(1)}, bf16[6,2,64,64]{3,2,1,0:T(8,128)(2,1)}, u32[]{:S(2)}) copy-start(bf16[6,2,64,64]{3,2,1,0:T(8,128)(2,1)} %copy-done.30) | copy-start | bytes 294916
  109.5 11.6 %collective-permute-start.8 = (bf16[4,4,64,256]{3,2,1,0:T(8,128)(2,1)S(1)}, bf16[4,4,64,256]{3,2,1,0:T(8,128)(2,1)S(1)}, u32[]{:S(2)}, u32[]{:S(2)}) collective-permute-start(bf16[4,4,64,256]{3,2,1,0:T(8,128)(2,1)S(1)} %fusion.20), channel_id=1, source_target_pairs={{0,24},{12,180},{24,0},{36,60},{48,72},{60,36},{72,48},{84,108},{9... | collective-permute-start | bytes 1572872 | tf_op jit(solution)/shard_map/ppermute | solution.py:58
  114.9 1.0 copy-start.6
  115.9 14.4 %copy-start.32 = (bf16[6,2,64,64]{3,2,1,0:T(8,128)(2,1)S(1)}, bf16[6,2,64,64]{3,2,1,0:T(8,128)(2,1)}, u32[]{:S(2)}) copy-start(bf16[6,2,64,64]{3,2,1,0:T(8,128)(2,1)} %fusion.13) | copy-start | bytes 294916
  121.2 25.5 %copy-start.3 = (bf16[6,64,2,128]{3,2,1,0:T(2,128)(2,1)S(1)}, bf16[6,64,2,128]{3,2,1,0:T(2,128)(2,1)}, u32[]{:S(2)}) copy-start(bf16[6,64,2,128]{3,2,1,0:T(2,128)(2,1)} %reshape.64) | copy-start | bytes 589828
  121.3 9.3 %collective-permute-start.9 = (bf16[4,64,256]{2,1,0:T(8,128)(2,1)S(1)}, bf16[4,64,256]{2,1,0:T(8,128)(2,1)S(1)}, u32[]{:S(2)}, u32[]{:S(2)}) collective-permute-start(bf16[4,64,256]{2,1,0:T(8,128)(2,1)S(1)} %get-tuple-element.25), channel_id=1, source_target_pairs={{0,192},{12,204},{24,216},{36,228},{48,240},{60,252},{72,264},{84,... | collective-permute-start | bytes 393224 | tf_op jit(solution)/shard_map/ppermute | solution.py:58
  123.6 8.9 %collective-permute-start.11 = (bf16[4,64,256]{2,1,0:T(8,128)(2,1)S(1)}, bf16[4,64,256]{2,1,0:T(8,128)(2,1)S(1)}, u32[]{:S(2)}, u32[]{:S(2)}) collective-permute-start(bf16[4,64,256]{2,1,0:T(8,128)(2,1)S(1)} %get-tuple-element.26), channel_id=1, source_target_pairs={{0,576},{12,588},{24,600},{36,612},{48,624},{60,636},{72,648},{84,... | collective-permute-start | bytes 393224 | tf_op jit(solution)/shard_map/ppermute | solution.py:58
  127.3 8.9 %collective-permute-start.10 = (bf16[4,64,256]{2,1,0:T(8,128)(2,1)S(1)}, bf16[4,64,256]{2,1,0:T(8,128)(2,1)S(1)}, u32[]{:S(2)}, u32[]{:S(2)}) collective-permute-start(bf16[4,64,256]{2,1,0:T(8,128)(2,1)S(1)} %get-tuple-element.27), channel_id=1, source_target_pairs={{0,384},{12,396},{24,408},{36,420},{48,432},{60,444},{72,456},{84,... | collective-permute-start | bytes 393224 | tf_op jit(solution)/shard_map/ppermute | solution.py:58
  136.2 13.5 %collective-permute-start.12 = (bf16[64,256]{1,0:T(8,128)(2,1)S(1)}, bf16[64,256]{1,0:T(8,128)(2,1)S(1)}, u32[]{:S(2)}, u32[]{:S(2)}) collective-permute-start(bf16[64,256]{1,0:T(8,128)(2,1)S(1)} %get-tuple-element.28), channel_id=1, source_target_pairs={{0,48},{12,60},{24,72},{36,84},{48,96},{60,108},{72,120},{84,132},... | collective-permute-start | bytes 98312 | tf_op jit(solution)/shard_map/ppermute | solution.py:58
  138.2 11.5 %collective-permute-start.14 = (bf16[64,256]{1,0:T(8,128)(2,1)S(1)}, bf16[64,256]{1,0:T(8,128)(2,1)S(1)}, u32[]{:S(2)}, u32[]{:S(2)}) collective-permute-start(bf16[64,256]{1,0:T(8,128)(2,1)S(1)} %get-tuple-element.29), channel_id=1, source_target_pairs={{0,144},{12,156},{24,168},{36,180},{48,0},{60,12},{72,24},{84,36},... | collective-permute-start | bytes 98312 | tf_op jit(solution)/shard_map/ppermute | solution.py:58
  144.2 9.7 %collective-permute-start.13 = (bf16[64,256]{1,0:T(8,128)(2,1)S(1)}, bf16[64,256]{1,0:T(8,128)(2,1)S(1)}, u32[]{:S(2)}, u32[]{:S(2)}) collective-permute-start(bf16[64,256]{1,0:T(8,128)(2,1)S(1)} %get-tuple-element.30), channel_id=1, source_target_pairs={{0,96},{12,108},{24,120},{36,132},{48,144},{60,156},{72,168},{84,1... | collective-permute-start | bytes 98312 | tf_op jit(solution)/shard_map/ppermute | solution.py:58
  (3 other events, 2.1 us)
Sparse Core Ops, SparseCore 0:
  80.5 64.1 reduce-scatter.1

commit v7 on v6

--- a/solution.py
+++ b/solution.py
@@ -168,10 +168,10 @@
         outflow = outflow + jnp.where(upper_half, 0.0, other[1])
         totals = totals + other
         level += 1
-    before = inflow[None] + jnp.cumsum(key_value, 0) - key_value
-    later_state = outflow[None] + own_pairs[None] - jnp.cumsum(query_pairs, 0)
-    before_parts = split_state(before)
-    later_parts = split_state(later_state)
+    local_before = split_state(jnp.cumsum(key_value, 0) - key_value)
+    local_later = split_state(own_pairs[None] - jnp.cumsum(query_pairs, 0))
+    inflow_parts = split_state(inflow)
+    outflow_parts = split_state(outflow)
     scores = jnp.einsum(
         "cthd,cshd->chts", query_blocks, key_blocks, preferred_element_type=jnp.float32
     )
@@ -179,7 +179,10 @@
     within = jnp.einsum(
         "chts,cshe->cthe", weights, value_blocks, preferred_element_type=jnp.float32
     )
-    carried = factor * state_product("cthd,chde->cthe", query_blocks, before_parts)
+    carried = factor * (
+        state_product("cthd,chde->cthe", query_blocks, local_before)
+        + state_product("cthd,hde->cthe", query_blocks, inflow_parts)
+    )
     attention = (within + carried).astype(jnp.bfloat16).reshape(flat_shape)
     partial_output = lax.dot_general(
         attention, out_weight, (((1,), (1,)), ((), ())), preferred_element_type=jnp.float32
@@ -190,8 +193,8 @@
         out_grad, attention, (((0,), (0,)), ((), ())), preferred_element_type=jnp.float32
     )
     if seq_count == 64:
-        weight_grad, (before_parts, later_parts) = grid_scatter(
-            weight_partial, 4, 8, (before_parts, later_parts)
+        weight_grad, (inflow_parts, outflow_parts) = grid_scatter(
+            weight_partial, 4, 8, (inflow_parts, outflow_parts)
         )
     else:
         weight_grad = halving_scatter(weight_partial, seq_count)
@@ -202,15 +205,24 @@
     query_grad = jnp.einsum(
         "chts,cshd->cthd", grad_weights, key_blocks, preferred_element_type=jnp.float32
     )
-    query_grad = query_grad + factor * state_product("cthe,chde->cthd", grad_blocks, before_parts)
+    query_grad = query_grad + factor * (
+        state_product("cthe,chde->cthd", grad_blocks, local_before)
+        + state_product("cthe,hde->cthd", grad_blocks, inflow_parts)
+    )
     key_grad = jnp.einsum(
         "chts,cthd->cshd", grad_weights, query_blocks, preferred_element_type=jnp.float32
     )
-    key_grad = key_grad + factor * state_product("cshe,chde->cshd", value_blocks, later_parts)
+    key_grad = key_grad + factor * (
+        state_product("cshe,chde->cshd", value_blocks, local_later)
+        + state_product("cshe,hde->cshd", value_blocks, outflow_parts)
+    )
     value_grad = jnp.einsum(
         "chts,cthe->cshe", weights, grad_blocks, preferred_element_type=jnp.float32
     )
-    value_grad = value_grad + factor * state_product("cshd,chde->cshe", key_blocks, later_parts)
+    value_grad = value_grad + factor * (
+        state_product("cshd,chde->cshe", key_blocks, local_later)
+        + state_product("cshd,hde->cshe", key_blocks, outflow_parts)
+    )
     weight_grad = weight_grad * total_rows ** (-0.5)
     return (
         output,

time: 164 us -> 183 us (1.12)
  waiting for transfers between devices: 25.8 us -> 35.9 us
  local copies, waits for them, and re-layouts: 21.7 us -> 29.3 us
  other arithmetic: 17.1 us -> 19.1 us
    reduce_scatter x1, waiting for transfers between devices: 0.01 us -> 11.8 us  [local(): lax.psum_scatter(partial_output, 'head', scatter_dimension=0, tiled=True)]
    dot_general x4, matrix products: 1.23 us -> 5.14 us  [state_product(): jnp.einsum(form, operand, parts[0], preferred_element_type=jnp.float32)]
    unnamed x74 -> x92, local copies, waits for them, and re-layouts: 4.83 us -> 8.27 us
    convert_element_type x5, other arithmetic: 3.85 us -> 6.6 us  [local(): totals.astype(jnp.bfloat16)]
    dot_general x2, matrix products: 2.44 us -> 0.41 us  [local(): lax.dot_general(key_rows[:, h * HD:(h + 1) * HD], value_rows[:, h * HD:(h...]
  transfers between devices with their start and end apart: 16 -> 16, of which waited for: 8 -> 10; matrix products, arithmetic and copies ran while one was open for 28% -> 20% of each run, Pallas kernels for 0% -> 0%
where the time goes in v7:
time: 183 us; the launch traced here: 181 us
  starting transfers between devices  58.3 us (32%)
  waiting for transfers between devices  35.9 us (20%)
  local copies, waits for them, and re-layouts  29.3 us (16%)
  matrix products  23.3 us (13%)
  other arithmetic  19.1 us (10%)
  between operations  15 us (8%)
    ppermute x7, starting transfers between devices, wire(): lax.ppermute(block.astype(jnp.bfloat16), SEQ, route).astype(jnp.float32)  22.8 us
    ppermute x4, starting transfers between devices, swapped(): return lax.ppermute(block, SEQ, route)  19.1 us
    ppermute x7, waiting for transfers between devices, wire(): lax.ppermute(block.astype(jnp.bfloat16), SEQ, route).astype(jnp.float32)  14.5 us
    ppermute x3, starting transfers between devices, local(): lax.ppermute(totals.astype(jnp.bfloat16), SEQ, route).astype(jnp.float32)  14.5 us
    reduce_scatter x1, waiting for transfers between devices, local(): lax.psum_scatter(partial_output, 'head', scatter_dimension=0, tiled=True)  11.8 us
    unnamed x92, local copies, waits for them, and re-layouts  8.27 us
    convert_element_type x5, other arithmetic, local(): totals.astype(jnp.bfloat16)  6.6 us
    ppermute x4, waiting for transfers between devices, swapped(): return lax.ppermute(block, SEQ, route)  5.72 us
  transfers between devices with their start and end apart: 16, of which 10 were waited for; matrix products, arithmetic and copies ran while one was open for 20% of the time, Pallas kernels for 0%

profile of v7, /device:TPU:6, one launch (start us, length us, event | category | flops | bytes accessed | tf_op | source)
XLA Modules:
  0.0 180.8 jit_solution(8206029602832004710)
XLA Ops:
  7.2 1.8 %copy-done = bf16[384,4096]{1,0:T(8,128)(2,1)S(1)} copy-done((bf16[384,4096]{1,0:T(8,128)(2,1)S(1)}, bf16[384,4096]{1,0:T(8,128)(2,1)}, u32[]{:S(2)}) %copy-start) | copy-done | bytes 3145752
  9.1 2.6 %convolution_convert_fusion.1 = bf16[384,256]{1,0:T(8,128)(2,1)S(1)} fusion(bf16[384,4096]{1,0:T(8,128)(2,1)S(1)} %copy-done, bf16[4096,256]{1,0:T(8,128)(2,1)} %param.8), kind=kOutput, calls=%fused_computation.42 | convolution fusion | flops 805404672 | bytes 5439488 | tf_op jit(solution)/shard_map/dot_general | solution.py:117
  14.0 1.9 %collective-permute-start = (bf16[2,2,128,128]{3,2,1,0:T(8,128)(2,1)}, bf16[2,2,128,128]{3,2,1,0:T(8,128)(2,1)}, u32[]{:S(2)}, u32[]{:S(2)}) collective-permute-start(bf16[2,2,128,128]{3,2,1,0:T(8,128)(2,1)} %fusion.28), channel_id=1, source_target_pairs={{0,12},{12,0},{24,36},{36,24},{48,60},{60,48},{72,84},{84,72},{96,... | collective-permute-start | bytes 393224 | tf_op jit(solution)/shard_map/ppermute | solution.py:18
  17.6 1.1 fusion.80
  18.7 3.5 %collective-permute-start.1 = (bf16[2,2,128,128]{3,2,1,0:T(8,128)(2,1)S(1)}, bf16[2,2,128,128]{3,2,1,0:T(8,128)(2,1)S(1)}, u32[]{:S(2)}, u32[]{:S(2)}) collective-permute-start(bf16[2,2,128,128]{3,2,1,0:T(8,128)(2,1)S(1)} %fusion.80), channel_id=1, source_target_pairs={{0,24},{24,0},{12,36},{36,12},{48,72},{72,48},{60,84},{84,60},{96,... | collective-permute-start | bytes 393224 | tf_op jit(solution)/shard_map/ppermute | solution.py:18
  22.5 3.6 %collective-permute-done.1 = bf16[2,2,128,128]{3,2,1,0:T(8,128)(2,1)S(1)} collective-permute-done((bf16[2,2,128,128]{3,2,1,0:T(8,128)(2,1)S(1)}, bf16[2,2,128,128]{3,2,1,0:T(8,128)(2,1)S(1)}, u32[]{:S(2)}, u32[]{:S(2)}) %collective-permute-start.1) | collective-permute-done | bytes 131104 | tf_op jit(solution)/shard_map/ppermute | solution.py:18
  26.8 1.7 fusion.84
  28.5 6.2 %collective-permute-start.4 = (bf16[2,2,128,128]{3,2,1,0:T(8,128)(2,1)}, bf16[2,2,128,128]{3,2,1,0:T(8,128)(2,1)}, u32[]{:S(2)}, u32[]{:S(2)}) collective-permute-start(bf16[2,2,128,128]{3,2,1,0:T(8,128)(2,1)} %fusion.84), channel_id=1, source_target_pairs={{0,144},{12,156},{24,168},{36,180},{48,0},{60,12},{72,24},{84,36},... | collective-permute-start | bytes 393224 | tf_op jit(solution)/shard_map/ppermute | solution.py:157
  34.7 3.8 %collective-permute-start.3 = (bf16[2,2,128,128]{3,2,1,0:T(8,128)(2,1)}, bf16[2,2,128,128]{3,2,1,0:T(8,128)(2,1)}, u32[]{:S(2)}, u32[]{:S(2)}) collective-permute-start(bf16[2,2,128,128]{3,2,1,0:T(8,128)(2,1)} %fusion.84), channel_id=1, source_target_pairs={{0,96},{12,108},{24,120},{36,132},{48,144},{60,156},{72,168},{84,1... | collective-permute-start | bytes 393224 | tf_op jit(solution)/shard_map/ppermute | solution.py:157
  38.5 4.5 %collective-permute-start.2 = (bf16[2,2,128,128]{3,2,1,0:T(8,128)(2,1)}, bf16[2,2,128,128]{3,2,1,0:T(8,128)(2,1)}, u32[]{:S(2)}, u32[]{:S(2)}) collective-permute-start(bf16[2,2,128,128]{3,2,1,0:T(8,128)(2,1)} %fusion.84), channel_id=1, source_target_pairs={{0,48},{12,60},{24,72},{36,84},{48,96},{60,108},{72,120},{84,132},... | collective-permute-start | bytes 393224 | tf_op jit(solution)/shard_map/ppermute | solution.py:157
  44.0 1.7 reshape.108
  45.6 3.8 %collective-permute-done.3 = bf16[2,2,128,128]{3,2,1,0:T(8,128)(2,1)} collective-permute-done((bf16[2,2,128,128]{3,2,1,0:T(8,128)(2,1)}, bf16[2,2,128,128]{3,2,1,0:T(8,128)(2,1)}, u32[]{:S(2)}, u32[]{:S(2)}) %collective-permute-start.3) | collective-permute-done | bytes 131104 | tf_op jit(solution)/shard_map/ppermute | solution.py:157
  49.5 2.1 %fusion.93 = (bf16[2,2,128,128]{3,2,1,0:T(8,128)(2,1)}, f32[2,2,128,128]{3,2,1,0:T(8,128)}) fusion(bf16[2,2,128,128]{3,2,1,0:T(8,128)(2,1)} %collective-permute-done.4, bf16[2,2,128,128]{3,2,1,0:T(8,128)(2,1)} %collective-permute-done.3, bf16[2,2,128,128]{3,2,1,0:T(8,128)(2,1)} %collective-permute-done.2, bf16[2,2,128,128]{3,2,1,0:T(8,128)(2,1)} %copy-done.20, ...), kind=kLoop, calls=%fused_computation.158 | loop fusion | flops 786432 | bytes 1310720 | tf_op jit(solution)/shard_map/convert_element_type | solution.py:165
  51.5 2.7 %collective-permute-start.5 = (bf16[2,2,128,128]{3,2,1,0:T(8,128)(2,1)}, bf16[2,2,128,128]{3,2,1,0:T(8,128)(2,1)}, u32[]{:S(2)}, u32[]{:S(2)}) collective-permute-start(bf16[2,2,128,128]{3,2,1,0:T(8,128)(2,1)} %get-tuple-element.23), channel_id=1, source_target_pairs={{0,192},{192,0},{12,204},{204,12},{24,216},{216,24},{36,228},{228,... | collective-permute-start | bytes 393224 | tf_op jit(solution)/shard_map/ppermute | solution.py:18
  54.3 2.2 %fusion.67 = f32[6,2,128,64]{2,3,1,0:T(8,128)} fusion(bf16[6,64,2,128]{3,2,1,0:T(2,128)(2,1)} %reshape.108, f32[6,2,128,128]{3,2,1,0:T(8,128)} %reduce-window_subtract_fusion.1), kind=kOutput, calls=%fused_computation.127 | convolution fusion | flops 25362432 | bytes 1376256 | tf_op jit(solution)/shard_map/cthd,chde->cthe/dot_general | solution.py:28
  57.3 1.5 collective-permute-done.5
  59.7 11.0 %collective-permute-start.6 = (bf16[2,2,128,128]{3,2,1,0:T(8,128)(2,1)S(1)}, bf16[2,2,128,128]{3,2,1,0:T(8,128)(2,1)S(1)}, u32[]{:S(2)}, u32[]{:S(2)}) collective-permute-start(bf16[2,2,128,128]{3,2,1,0:T(8,128)(2,1)S(1)} %add_convert_fusion), channel_id=1, source_target_pairs={{0,384},{384,0},{12,396},{396,12},{24,408},{408,24},{36,420},{420,... | collective-permute-start | bytes 393224 | tf_op jit(solution)/shard_map/ppermute | solution.py:18
  70.7 1.2 fusion.19
  72.9 1.0 convert_element_type.169
  74.0 1.0 convert_element_type.173
  76.1 1.0 convert_element_type.171
  80.9 2.7 %convolution_convert_fusion = bf16[384,4096]{1,0:T(8,128)(2,1)} fusion(bf16[4096,256]{1,0:T(8,128)(2,1)S(1)} %copy-done.13, bf16[48,8,2,128]{3,2,1,0:T(2,128)(2,1)S(1)} %bitcast.194), kind=kOutput, calls=%fused_computation | convolution fusion | flops 806879232 | bytes 5439488 | tf_op jit(solution)/shard_map/dot_general | solution.py:187
  84.6 3.3 %convolution_bitcast_fusion = f32[4096,256]{0,1:T(8,128)} fusion(bf16[384,256]{1,0:T(8,128)(2,1)S(1)} %bitcast.215, bf16[384,4096]{1,0:T(8,128)(2,1)S(1)} %copy-done), kind=kOutput, calls=%fused_computation.1 | convolution fusion | flops 805306368 | bytes 7536640 | tf_op jit(solution)/shard_map/dot_general | solution.py:192
  87.8 5.6 %copy.74 = f32[4096,256]{1,0:T(8,128)} copy(f32[4096,256]{0,1:T(8,128)} %convolution_bitcast_fusion) | data formatting | bytes 8388608 | tf_op jit(solution)/shard_map/dot_general | solution.py:192
  93.4 3.2 %dynamic-slice_bitcast_fusion = f32[4,8,64,256]{3,2,1,0:T(8,128)} fusion(f32[4,8,2,64,256]{4,3,2,1,0:T(8,128)} %bitcast.190, s32[]{:T(128)S(6)} %select_n.250), kind=kLoop, calls=%fused_computation.4 | loop fusion | bytes 4194308 | tf_op jit(solution)/shard_map/jit(dynamic_index_in_dim)/squeeze | solution.py:71
  96.6 1.9 %collective-permute-start.7 = (f32[4,8,64,256]{3,2,1,0:T(8,128)}, f32[4,8,64,256]{3,2,1,0:T(8,128)}, u32[]{:S(2)}, u32[]{:S(2)}) collective-permute-start(f32[4,8,64,256]{3,2,1,0:T(8,128)} %dynamic-slice_bitcast_fusion), channel_id=1, source_target_pairs={{0,12},{12,0},{24,36},{36,24},{48,60},{60,48},{72,84},{84,72},{96,... | collective-permute-start | bytes 6291464 | tf_op jit(solution)/shard_map/ppermute | solution.py:72
  98.6 1.7 reshape.112
  101.6 1.6 copy.75
  103.3 1.7 copy.82
  104.9 2.2 %convolution_bitcast_fusion.1 = f32[6,2,128,128]{2,3,1,0:T(8,128)} fusion(bf16[6,64,2,128]{3,2,1,0:T(2,128)(2,1)} %reshape.112, bf16[6,64,2,128]{3,2,1,0:T(2,128)(2,1)} %reshape.108), kind=kOutput, calls=%fused_computation.7 | convolution fusion | flops 25165824 | bytes 1179648 | tf_op jit(solution)/shard_map/cthd,cthe->chde/dot_general | solution.py:124
  107.2 2.3 %fusion.49 = f32[6,2,128,64]{2,3,1,0:T(8,128)} fusion(bf16[6,64,2,128]{3,2,1,0:T(2,128)(2,1)} %reshape.112, f32[6,2,128,128]{3,2,1,0:T(8,128)} %reduce-window_subtract_fusion.1), kind=kOutput, calls=%fused_computation.109 | convolution fusion | flops 25362432 | bytes 1376256 | tf_op jit(solution)/shard_map/cthe,chde->cthd/dot_general | solution.py:28
  109.5 1.3 fusion.18
  110.8 1.4 reduce-window_subtract_fusion
  113.3 1.9 %bitcast_add_fusion = f32[4,8,64,256]{3,2,1,0:T(8,128)S(1)} fusion(f32[4,8,64,256]{3,2,1,0:T(8,128)} %collective-permute-done.7, f32[4,8,2,64,256]{4,3,2,1,0:T(8,128)S(1)} %bitcast.191, s32[]{:T(128)S(6)} %select_n.249), kind=kLoop, calls=%fused_computation.3 | loop fusion | flops 524288 | bytes 6291460 | tf_op jit(solution)/shard_map/add | solution.py:72
  115.3 1.3 copy-done.3
  121.1 4.3 %collective-permute-start.8 = (bf16[4,4,64,256]{3,2,1,0:T(8,128)(2,1)S(1)}, bf16[4,4,64,256]{3,2,1,0:T(8,128)(2,1)S(1)}, u32[]{:S(2)}, u32[]{:S(2)}) collective-permute-start(bf16[4,4,64,256]{3,2,1,0:T(8,128)(2,1)S(1)} %fusion.24), channel_id=1, source_target_pairs={{0,24},{12,180},{24,0},{36,60},{48,72},{60,36},{72,48},{84,108},{9... | collective-permute-start | bytes 1572872 | tf_op jit(solution)/shard_map/ppermute | solution.py:58
  126.3 6.3 %collective-permute-done.8 = bf16[4,4,64,256]{3,2,1,0:T(8,128)(2,1)S(1)} collective-permute-done((bf16[4,4,64,256]{3,2,1,0:T(8,128)(2,1)S(1)}, bf16[4,4,64,256]{3,2,1,0:T(8,128)(2,1)S(1)}, u32[]{:S(2)}, u32[]{:S(2)}) %collective-permute-start.8) | collective-permute-done | bytes 524320 | tf_op jit(solution)/shard_map/ppermute | solution.py:58
  132.8 3.0 %collective-permute-start.11 = (bf16[4,64,256]{2,1,0:T(8,128)(2,1)S(1)}, bf16[4,64,256]{2,1,0:T(8,128)(2,1)S(1)}, u32[]{:S(2)}, u32[]{:S(2)}) collective-permute-start(bf16[4,64,256]{2,1,0:T(8,128)(2,1)S(1)} %get-tuple-element.26), channel_id=1, source_target_pairs={{0,576},{12,588},{24,600},{36,612},{48,624},{60,636},{72,648},{84,... | collective-permute-start | bytes 393224 | tf_op jit(solution)/shard_map/ppermute | solution.py:58
  135.9 2.5 %collective-permute-start.10 = (bf16[4,64,256]{2,1,0:T(8,128)(2,1)S(1)}, bf16[4,64,256]{2,1,0:T(8,128)(2,1)S(1)}, u32[]{:S(2)}, u32[]{:S(2)}) collective-permute-start(bf16[4,64,256]{2,1,0:T(8,128)(2,1)S(1)} %get-tuple-element.27), channel_id=1, source_target_pairs={{0,384},{12,396},{24,408},{36,420},{48,432},{60,444},{72,456},{84,... | collective-permute-start | bytes 393224 | tf_op jit(solution)/shard_map/ppermute | solution.py:58
  138.4 4.0 %collective-permute-start.9 = (bf16[4,64,256]{2,1,0:T(8,128)(2,1)S(1)}, bf16[4,64,256]{2,1,0:T(8,128)(2,1)S(1)}, u32[]{:S(2)}, u32[]{:S(2)}) collective-permute-start(bf16[4,64,256]{2,1,0:T(8,128)(2,1)S(1)} %get-tuple-element.25), channel_id=1, source_target_pairs={{0,192},{12,204},{24,216},{36,228},{48,240},{60,252},{72,264},{84,... | collective-permute-start | bytes 393224 | tf_op jit(solution)/shard_map/ppermute | solution.py:58
  142.6 2.4 %collective-permute-done.10 = bf16[4,64,256]{2,1,0:T(8,128)(2,1)S(1)} collective-permute-done((bf16[4,64,256]{2,1,0:T(8,128)(2,1)S(1)}, bf16[4,64,256]{2,1,0:T(8,128)(2,1)S(1)}, u32[]{:S(2)}, u32[]{:S(2)}) %collective-permute-start.10) | collective-permute-done | bytes 131104 | tf_op jit(solution)/shard_map/ppermute | solution.py:58
  145.0 2.3 %collective-permute-done.9 = bf16[4,64,256]{2,1,0:T(8,128)(2,1)S(1)} collective-permute-done((bf16[4,64,256]{2,1,0:T(8,128)(2,1)S(1)}, bf16[4,64,256]{2,1,0:T(8,128)(2,1)S(1)}, u32[]{:S(2)}, u32[]{:S(2)}) %collective-permute-start.9) | collective-permute-done | bytes 131104 | tf_op jit(solution)/shard_map/ppermute | solution.py:58
  147.4 1.9 %collective-permute-start.14 = (bf16[64,256]{1,0:T(8,128)(2,1)S(1)}, bf16[64,256]{1,0:T(8,128)(2,1)S(1)}, u32[]{:S(2)}, u32[]{:S(2)}) collective-permute-start(bf16[64,256]{1,0:T(8,128)(2,1)S(1)} %get-tuple-element.29), channel_id=1, source_target_pairs={{0,144},{12,156},{24,168},{36,180},{48,0},{60,12},{72,24},{84,36},... | collective-permute-start | bytes 98312 | tf_op jit(solution)/shard_map/ppermute | solution.py:58
  149.3 3.3 %collective-permute-start.13 = (bf16[64,256]{1,0:T(8,128)(2,1)S(1)}, bf16[64,256]{1,0:T(8,128)(2,1)S(1)}, u32[]{:S(2)}, u32[]{:S(2)}) collective-permute-start(bf16[64,256]{1,0:T(8,128)(2,1)S(1)} %get-tuple-element.30), channel_id=1, source_target_pairs={{0,96},{12,108},{24,120},{36,132},{48,144},{60,156},{72,168},{84,1... | collective-permute-start | bytes 98312 | tf_op jit(solution)/shard_map/ppermute | solution.py:58
  152.6 3.7 %collective-permute-start.12 = (bf16[64,256]{1,0:T(8,128)(2,1)S(1)}, bf16[64,256]{1,0:T(8,128)(2,1)S(1)}, u32[]{:S(2)}, u32[]{:S(2)}) collective-permute-start(bf16[64,256]{1,0:T(8,128)(2,1)S(1)} %get-tuple-element.28), channel_id=1, source_target_pairs={{0,48},{12,60},{24,72},{36,84},{48,96},{60,108},{72,120},{84,132},... | collective-permute-start | bytes 98312 | tf_op jit(solution)/shard_map/ppermute | solution.py:58
  158.0 1.5 collective-permute-done.13
  159.5 2.0 %collective-permute-done.12 = bf16[64,256]{1,0:T(8,128)(2,1)S(1)} collective-permute-done((bf16[64,256]{1,0:T(8,128)(2,1)S(1)}, bf16[64,256]{1,0:T(8,128)(2,1)S(1)}, u32[]{:S(2)}, u32[]{:S(2)}) %collective-permute-start.12) | collective-permute-done | bytes 32800 | tf_op jit(solution)/shard_map/ppermute | solution.py:58
  162.2 11.8 %reduce-scatter.2.cloned.1.call-done = bf16[32,4096]{1,0:T(8,128)(2,1)} async-done(((bf16[384,4096]{1,0:T(8,128)(2,1)}), bf16[32,4096]{1,0:T(8,128)(2,1)}) %reduce-scatter.2.cloned.1.call-update) | async-done | bytes 262160 | tf_op jit(solution)/shard_map/reduce_scatter | solution.py:191
  (155 shorter events, 24.8 us)
Async XLA Ops:
  7.2 1.9 %copy-start = (bf16[384,4096]{1,0:T(8,128)(2,1)S(1)}, bf16[384,4096]{1,0:T(8,128)(2,1)}, u32[]{:S(2)}) copy-start(bf16[384,4096]{1,0:T(8,128)(2,1)} %param.9) | copy-start | bytes 9437188
  7.2 5.0 %copy-start.35 = (bf16[384,256]{1,0:T(8,128)(2,1)S(1)}, bf16[384,256]{1,0:T(8,128)(2,1)}, u32[]{:S(2)}) copy-start(bf16[384,256]{1,0:T(8,128)(2,1)} %param.7) | copy-start | bytes 589828
  7.2 5.0 %copy-start.36 = (bf16[384,256]{1,0:T(8,128)(2,1)S(1)}, bf16[384,256]{1,0:T(8,128)(2,1)}, u32[]{:S(2)}) copy-start(bf16[384,256]{1,0:T(8,128)(2,1)} %param.6) | copy-start | bytes 589828
  7.2 166.8 %reduce-scatter.2.cloned.1.call-start = ((), (), s32[]{:S(2)}) async-start(), calls=%async_computation.1 | async-start | bytes 3407872 | tf_op jit(solution)/shard_map/reduce_scatter | solution.py:191
  9.1 2.6 %copy-start.37 = (bf16[384,256]{1,0:T(8,128)(2,1)S(1)}, bf16[384,256]{1,0:T(8,128)(2,1)}, u32[]{:S(2)}) copy-start(bf16[384,256]{1,0:T(8,128)(2,1)} %param.5) | copy-start | bytes 589828
  11.7 2.3 %copy-start.38 = (bf16[384,256]{1,0:T(8,128)(2,1)}, bf16[384,256]{1,0:T(8,128)(2,1)S(1)}, u32[]{:S(2)}) copy-start(bf16[384,256]{1,0:T(8,128)(2,1)S(1)} %convolution_convert_fusion.1) | copy-start | bytes 589828
  14.0 3.6 %collective-permute-start = (bf16[2,2,128,128]{3,2,1,0:T(8,128)(2,1)}, bf16[2,2,128,128]{3,2,1,0:T(8,128)(2,1)}, u32[]{:S(2)}, u32[]{:S(2)}) collective-permute-start(bf16[2,2,128,128]{3,2,1,0:T(8,128)(2,1)} %fusion.28), channel_id=1, source_target_pairs={{0,12},{12,0},{24,36},{36,24},{48,60},{60,48},{72,84},{84,72},{96,... | collective-permute-start | bytes 393224 | tf_op jit(solution)/shard_map/ppermute | solution.py:18
  18.7 7.4 %collective-permute-start.1 = (bf16[2,2,128,128]{3,2,1,0:T(8,128)(2,1)S(1)}, bf16[2,2,128,128]{3,2,1,0:T(8,128)(2,1)S(1)}, u32[]{:S(2)}, u32[]{:S(2)}) collective-permute-start(bf16[2,2,128,128]{3,2,1,0:T(8,128)(2,1)S(1)} %fusion.80), channel_id=1, source_target_pairs={{0,24},{24,0},{12,36},{36,12},{48,72},{72,48},{60,84},{84,60},{96,... | collective-permute-start | bytes 393224 | tf_op jit(solution)/shard_map/ppermute | solution.py:18
  28.5 17.1 %collective-permute-start.4 = (bf16[2,2,128,128]{3,2,1,0:T(8,128)(2,1)}, bf16[2,2,128,128]{3,2,1,0:T(8,128)(2,1)}, u32[]{:S(2)}, u32[]{:S(2)}) collective-permute-start(bf16[2,2,128,128]{3,2,1,0:T(8,128)(2,1)} %fusion.84), channel_id=1, source_target_pairs={{0,144},{12,156},{24,168},{36,180},{48,0},{60,12},{72,24},{84,36},... | collective-permute-start | bytes 393224 | tf_op jit(solution)/shard_map/ppermute | solution.py:157
  34.7 14.8 %collective-permute-start.3 = (bf16[2,2,128,128]{3,2,1,0:T(8,128)(2,1)}, bf16[2,2,128,128]{3,2,1,0:T(8,128)(2,1)}, u32[]{:S(2)}, u32[]{:S(2)}) collective-permute-start(bf16[2,2,128,128]{3,2,1,0:T(8,128)(2,1)} %fusion.84), channel_id=1, source_target_pairs={{0,96},{12,108},{24,120},{36,132},{48,144},{60,156},{72,168},{84,1... | collective-permute-start | bytes 393224 | tf_op jit(solution)/shard_map/ppermute | solution.py:157
  38.5 11.0 %collective-permute-start.2 = (bf16[2,2,128,128]{3,2,1,0:T(8,128)(2,1)}, bf16[2,2,128,128]{3,2,1,0:T(8,128)(2,1)}, u32[]{:S(2)}, u32[]{:S(2)}) collective-permute-start(bf16[2,2,128,128]{3,2,1,0:T(8,128)(2,1)} %fusion.84), channel_id=1, source_target_pairs={{0,48},{12,60},{24,72},{36,84},{48,96},{60,108},{72,120},{84,132},... | collective-permute-start | bytes 393224 | tf_op jit(solution)/shard_map/ppermute | solution.py:157
  45.6 10.9 %copy-start.6 = (bf16[6,64,2,128]{3,2,1,0:T(2,128)(2,1)S(1)}, bf16[6,64,2,128]{3,2,1,0:T(2,128)(2,1)}, u32[]{:S(2)}) copy-start(bf16[6,64,2,128]{3,2,1,0:T(2,128)(2,1)} %reshape.108) | copy-start | bytes 589828
  51.5 7.2 %collective-permute-start.5 = (bf16[2,2,128,128]{3,2,1,0:T(8,128)(2,1)}, bf16[2,2,128,128]{3,2,1,0:T(8,128)(2,1)}, u32[]{:S(2)}, u32[]{:S(2)}) collective-permute-start(bf16[2,2,128,128]{3,2,1,0:T(8,128)(2,1)} %get-tuple-element.23), channel_id=1, source_target_pairs={{0,192},{192,0},{12,204},{204,12},{24,216},{216,24},{36,228},{228,... | collective-permute-start | bytes 393224 | tf_op jit(solution)/shard_map/ppermute | solution.py:18
  59.7 18.4 %collective-permute-start.6 = (bf16[2,2,128,128]{3,2,1,0:T(8,128)(2,1)S(1)}, bf16[2,2,128,128]{3,2,1,0:T(8,128)(2,1)S(1)}, u32[]{:S(2)}, u32[]{:S(2)}) collective-permute-start(bf16[2,2,128,128]{3,2,1,0:T(8,128)(2,1)S(1)} %add_convert_fusion), channel_id=1, source_target_pairs={{0,384},{384,0},{12,396},{396,12},{24,408},{408,24},{36,420},{420,... | collective-permute-start | bytes 393224 | tf_op jit(solution)/shard_map/ppermute | solution.py:18
  71.9 7.8 %copy-start.39 = (bf16[6,2,64,64]{3,2,1,0:T(8,128)(2,1)}, bf16[6,2,64,64]{3,2,1,0:T(8,128)(2,1)S(1)}, u32[]{:S(2)}) copy-start(bf16[6,2,64,64]{3,2,1,0:T(8,128)(2,1)S(1)} %fusion.19) | copy-start | bytes 294916
  71.9 7.0 %copy-start.16 = (bf16[6,64,2,128]{3,1,0,2:T(8,128)(2,1)S(1)}, bf16[6,64,2,128]{3,1,0,2:T(8,128)(2,1)}, u32[]{:S(2)}) copy-start(bf16[6,64,2,128]{3,1,0,2:T(8,128)(2,1)} %copy.64) | copy-start | bytes 589828
  72.9 6.4 %copy-start.21 = (f32[2,2,128,128]{3,2,1,0:T(8,128)}, f32[2,2,128,128]{3,2,1,0:T(8,128)S(1)}, u32[]{:S(2)}) copy-start(f32[2,2,128,128]{3,2,1,0:T(8,128)S(1)} %convert_element_type.167) | copy-start | bytes 786436
  73.9 5.4 %copy-start.23 = (f32[2,2,128,128]{3,2,1,0:T(8,128)}, f32[2,2,128,128]{3,2,1,0:T(8,128)S(1)}, u32[]{:S(2)}) copy-start(f32[2,2,128,128]{3,2,1,0:T(8,128)S(1)} %convert_element_type.169) | copy-start | bytes 786436
  74.0 5.4 %copy-start.1 = (f32[6,2,128,128]{3,2,1,0:T(8,128)S(1)}, f32[6,2,128,128]{3,2,1,0:T(8,128)}, u32[]{:S(2)}) copy-start(f32[6,2,128,128]{3,2,1,0:T(8,128)} %reduce-window_subtract_fusion.1) | copy-start | bytes 2359300
  74.0 5.4 %copy-start.7 = (bf16[6,64,2,128]{3,2,1,0:T(2,128)(2,1)S(1)}, bf16[6,64,2,128]{3,2,1,0:T(2,128)(2,1)}, u32[]{:S(2)}) copy-start(bf16[6,64,2,128]{3,2,1,0:T(2,128)(2,1)} %reshape.108) | copy-start | bytes 589828
  74.0 5.4 %copy-start.18 = (f32[6,2,128,64]{2,3,1,0:T(8,128)S(1)}, f32[6,2,128,64]{2,3,1,0:T(8,128)}, u32[]{:S(2)}) copy-start(f32[6,2,128,64]{2,3,1,0:T(8,128)} %fusion.67) | copy-start | bytes 1179652
  75.0 4.3 %copy-start.25 = (f32[2,2,128,128]{3,2,1,0:T(8,128)}, f32[2,2,128,128]{3,2,1,0:T(8,128)S(1)}, u32[]{:S(2)}) copy-start(f32[2,2,128,128]{3,2,1,0:T(8,128)S(1)} %convert_element_type.173) | copy-start | bytes 786436
  76.1 3.3 %copy-start.27 = (f32[2,2,128,128]{3,2,1,0:T(8,128)}, f32[2,2,128,128]{3,2,1,0:T(8,128)S(1)}, u32[]{:S(2)}) copy-start(f32[2,2,128,128]{3,2,1,0:T(8,128)S(1)} %convert_element_type.172) | copy-start | bytes 786436
  77.1 2.3 %copy-start.29 = (f32[2,2,128,128]{3,2,1,0:T(8,128)}, f32[2,2,128,128]{3,2,1,0:T(8,128)S(1)}, u32[]{:S(2)}) copy-start(f32[2,2,128,128]{3,2,1,0:T(8,128)S(1)} %convert_element_type.171) | copy-start | bytes 786436
  79.3 1.6 copy-start.13
  96.6 16.4 %collective-permute-start.7 = (f32[4,8,64,256]{3,2,1,0:T(8,128)}, f32[4,8,64,256]{3,2,1,0:T(8,128)}, u32[]{:S(2)}, u32[]{:S(2)}) collective-permute-start(f32[4,8,64,256]{3,2,1,0:T(8,128)} %dynamic-slice_bitcast_fusion), channel_id=1, source_target_pairs={{0,12},{12,0},{24,36},{36,24},{48,60},{60,48},{72,84},{84,72},{96,... | collective-permute-start | bytes 6291464 | tf_op jit(solution)/shard_map/ppermute | solution.py:72
  109.5 3.4 %copy-start.22 = (f32[2,2,128,128]{3,2,1,0:T(8,128)S(1)}, f32[2,2,128,128]{3,2,1,0:T(8,128)}, u32[]{:S(2)}) copy-start(f32[2,2,128,128]{3,2,1,0:T(8,128)} %copy-done.21) | copy-start | bytes 786436
  109.5 3.4 %copy-start.24 = (f32[2,2,128,128]{3,2,1,0:T(8,128)S(1)}, f32[2,2,128,128]{3,2,1,0:T(8,128)}, u32[]{:S(2)}) copy-start(f32[2,2,128,128]{3,2,1,0:T(8,128)} %copy-done.23) | copy-start | bytes 786436
  109.5 3.4 %copy-start.26 = (f32[2,2,128,128]{3,2,1,0:T(8,128)S(1)}, f32[2,2,128,128]{3,2,1,0:T(8,128)}, u32[]{:S(2)}) copy-start(f32[2,2,128,128]{3,2,1,0:T(8,128)} %copy-done.25) | copy-start | bytes 786436
  109.5 3.4 %copy-start.28 = (f32[2,2,128,128]{3,2,1,0:T(8,128)S(1)}, f32[2,2,128,128]{3,2,1,0:T(8,128)}, u32[]{:S(2)}) copy-start(f32[2,2,128,128]{3,2,1,0:T(8,128)} %copy-done.27) | copy-start | bytes 786436
  109.5 3.4 %copy-start.30 = (f32[2,2,128,128]{3,2,1,0:T(8,128)S(1)}, f32[2,2,128,128]{3,2,1,0:T(8,128)}, u32[]{:S(2)}) copy-start(f32[2,2,128,128]{3,2,1,0:T(8,128)} %copy-done.29) | copy-start | bytes 786436
  109.5 3.4 %copy-start.32 = (f32[2,2,128,128]{3,2,1,0:T(8,128)S(1)}, f32[2,2,128,128]{3,2,1,0:T(8,128)}, u32[]{:S(2)}) copy-start(f32[2,2,128,128]{3,2,1,0:T(8,128)} %copy-done.31) | copy-start | bytes 786436
  109.5 3.4 %copy-start.34 = (f32[2,2,128,128]{3,2,1,0:T(8,128)S(1)}, f32[2,2,128,128]{3,2,1,0:T(8,128)}, u32[]{:S(2)}) copy-start(f32[2,2,128,128]{3,2,1,0:T(8,128)} %copy-done.33) | copy-start | bytes 786436
  110.8 2.5 %copy-start.5 = (f32[4096,256]{1,0:T(8,128)S(1)}, f32[4096,256]{1,0:T(8,128)}, u32[]{:S(2)}) copy-start(f32[4096,256]{1,0:T(8,128)} %copy.74) | copy-start | bytes 12582916
  118.4 1.6 copy-start.4
  118.6 2.0 %slice-start.1 = ((f32[4,8,64,256]{3,2,1,0:T(8,128)}), f32[4,7,64,256]{3,2,1,0:T(8,128)S(1)}, s32[]{:S(2)}) async-start(f32[4,8,64,256]{3,2,1,0:T(8,128)} %copy-done.3), calls=%async_computation.3 | async-start | bytes 3670016 | tf_op jit(solution)/shard_map/jit(_roll_static)/slice | solution.py:74
  120.7 4.8 %copy-start.17 = (bf16[6,64,2,128]{3,1,0,2:T(8,128)(2,1)S(1)}, bf16[6,64,2,128]{3,1,0,2:T(8,128)(2,1)}, u32[]{:S(2)}) copy-start(bf16[6,64,2,128]{3,1,0,2:T(8,128)(2,1)} %copy.75) | copy-start | bytes 589828
  120.7 4.8 %copy-start.44 = (bf16[2,128,128]{2,1,0:T(8,128)(2,1)S(1)}, bf16[2,128,128]{2,1,0:T(8,128)(2,1)}, u32[]{:S(2)}) copy-start(bf16[2,128,128]{2,1,0:T(8,128)(2,1)} %copy-done.43) | copy-start | bytes 196612
  120.7 5.0 %copy-start.42 = (bf16[2,128,128]{2,1,0:T(8,128)(2,1)S(1)}, bf16[2,128,128]{2,1,0:T(8,128)(2,1)}, u32[]{:S(2)}) copy-start(bf16[2,128,128]{2,1,0:T(8,128)(2,1)} %copy-done.41) | copy-start | bytes 196612
  121.0 4.9 %copy-start.2 = (f32[6,2,128,128]{3,2,1,0:T(8,128)S(1)}, f32[6,2,128,128]{3,2,1,0:T(8,128)}, u32[]{:S(2)}) copy-start(f32[6,2,128,128]{3,2,1,0:T(8,128)} %reduce-window_subtract_fusion.1) | copy-start | bytes 2359300
  121.0 4.9 %copy-start.19 = (f32[6,2,128,64]{2,3,1,0:T(8,128)S(1)}, f32[6,2,128,64]{2,3,1,0:T(8,128)}, u32[]{:S(2)}) copy-start(f32[6,2,128,64]{2,3,1,0:T(8,128)} %fusion.49) | copy-start | bytes 1179652
  121.1 11.5 %collective-permute-start.8 = (bf16[4,4,64,256]{3,2,1,0:T(8,128)(2,1)S(1)}, bf16[4,4,64,256]{3,2,1,0:T(8,128)(2,1)S(1)}, u32[]{:S(2)}, u32[]{:S(2)}) collective-permute-start(bf16[4,4,64,256]{3,2,1,0:T(8,128)(2,1)S(1)} %fusion.24), channel_id=1, source_target_pairs={{0,24},{12,180},{24,0},{36,60},{48,72},{60,36},{72,48},{84,108},{9... | collective-permute-start | bytes 1572872 | tf_op jit(solution)/shard_map/ppermute | solution.py:58
  132.8 9.8 %collective-permute-start.11 = (bf16[4,64,256]{2,1,0:T(8,128)(2,1)S(1)}, bf16[4,64,256]{2,1,0:T(8,128)(2,1)S(1)}, u32[]{:S(2)}, u32[]{:S(2)}) collective-permute-start(bf16[4,64,256]{2,1,0:T(8,128)(2,1)S(1)} %get-tuple-element.26), channel_id=1, source_target_pairs={{0,576},{12,588},{24,600},{36,612},{48,624},{60,636},{72,648},{84,... | collective-permute-start | bytes 393224 | tf_op jit(solution)/shard_map/ppermute | solution.py:58
  135.9 9.2 %collective-permute-start.10 = (bf16[4,64,256]{2,1,0:T(8,128)(2,1)S(1)}, bf16[4,64,256]{2,1,0:T(8,128)(2,1)S(1)}, u32[]{:S(2)}, u32[]{:S(2)}) collective-permute-start(bf16[4,64,256]{2,1,0:T(8,128)(2,1)S(1)} %get-tuple-element.27), channel_id=1, source_target_pairs={{0,384},{12,396},{24,408},{36,420},{48,432},{60,444},{72,456},{84,... | collective-permute-start | bytes 393224 | tf_op jit(solution)/shard_map/ppermute | solution.py:58
  138.4 8.9 %collective-permute-start.9 = (bf16[4,64,256]{2,1,0:T(8,128)(2,1)S(1)}, bf16[4,64,256]{2,1,0:T(8,128)(2,1)S(1)}, u32[]{:S(2)}, u32[]{:S(2)}) collective-permute-start(bf16[4,64,256]{2,1,0:T(8,128)(2,1)S(1)} %get-tuple-element.25), channel_id=1, source_target_pairs={{0,192},{12,204},{24,216},{36,228},{48,240},{60,252},{72,264},{84,... | collective-permute-start | bytes 393224 | tf_op jit(solution)/shard_map/ppermute | solution.py:58
  147.4 10.6 %collective-permute-start.14 = (bf16[64,256]{1,0:T(8,128)(2,1)S(1)}, bf16[64,256]{1,0:T(8,128)(2,1)S(1)}, u32[]{:S(2)}, u32[]{:S(2)}) collective-permute-start(bf16[64,256]{1,0:T(8,128)(2,1)S(1)} %get-tuple-element.29), channel_id=1, source_target_pairs={{0,144},{12,156},{24,168},{36,180},{48,0},{60,12},{72,24},{84,36},... | collective-permute-start | bytes 98312 | tf_op jit(solution)/shard_map/ppermute | solution.py:58
  149.3 10.2 %collective-permute-start.13 = (bf16[64,256]{1,0:T(8,128)(2,1)S(1)}, bf16[64,256]{1,0:T(8,128)(2,1)S(1)}, u32[]{:S(2)}, u32[]{:S(2)}) collective-permute-start(bf16[64,256]{1,0:T(8,128)(2,1)S(1)} %get-tuple-element.30), channel_id=1, source_target_pairs={{0,96},{12,108},{24,120},{36,132},{48,144},{60,156},{72,168},{84,1... | collective-permute-start | bytes 98312 | tf_op jit(solution)/shard_map/ppermute | solution.py:58
  152.6 8.9 %collective-permute-start.12 = (bf16[64,256]{1,0:T(8,128)(2,1)S(1)}, bf16[64,256]{1,0:T(8,128)(2,1)S(1)}, u32[]{:S(2)}, u32[]{:S(2)}) collective-permute-start(bf16[64,256]{1,0:T(8,128)(2,1)S(1)} %get-tuple-element.28), channel_id=1, source_target_pairs={{0,48},{12,60},{24,72},{36,84},{48,96},{60,108},{72,120},{84,132},... | collective-permute-start | bytes 98312 | tf_op jit(solution)/shard_map/ppermute | solution.py:58
  (15 other events, 14.3 us)
Sparse Core Ops, SparseCore 0:
  109.6 64.3 reduce-scatter.1

commit v8 on v6

--- a/solution.py
+++ b/solution.py
@@ -16,6 +16,10 @@
         if high != low and high < count:
             route += [(low, high), (high, low)]
     return lax.ppermute(block, SEQ, route)
+
+
+def masked(keep, block):
+    return jnp.where(keep, block, jnp.zeros_like(block)).astype(jnp.float32)
 
 
 def split_state(state):
@@ -154,19 +158,19 @@
                     mine = i >> level & 3
                     target = i - (mine << level) + ((mine + shift) % 4 << level)
                     route.append((i, target))
-                other = lax.ppermute(totals.astype(jnp.bfloat16), SEQ, route).astype(jnp.float32)
+                other = lax.ppermute(totals.astype(jnp.bfloat16), SEQ, route)
                 source = (group - shift) % 4
-                inflow = inflow + jnp.where(source < group, other[0], 0.0)
-                outflow = outflow + jnp.where(source > group, other[1], 0.0)
-                gathered = gathered + other
+                inflow = inflow + masked(source < group, other[0])
+                outflow = outflow + masked(source > group, other[1])
+                gathered = gathered + other.astype(jnp.float32)
             totals = gathered
             level += 2
             continue
-        other = swapped(totals.astype(jnp.bfloat16), seq_count, level).astype(jnp.float32)
+        other = swapped(totals.astype(jnp.bfloat16), seq_count, level)
         upper_half = position >> level & 1 == 1
-        inflow = inflow + jnp.where(upper_half, other[0], 0.0)
-        outflow = outflow + jnp.where(upper_half, 0.0, other[1])
-        totals = totals + other
+        inflow = inflow + masked(upper_half, other[0])
+        outflow = outflow + masked(~upper_half, other[1])
+        totals = totals + other.astype(jnp.float32)
         level += 1
     before = inflow[None] + jnp.cumsum(key_value, 0) - key_value
     later_state = outflow[None] + own_pairs[None] - jnp.cumsum(query_pairs, 0)

time: 164 us -> 163 us (level)
  other arithmetic: 17.1 us -> 12.2 us
  waiting for transfers between devices: 25.8 us -> 28.3 us
  starting transfers between devices: 59.4 us -> 61.3 us
    convert_element_type x12 -> x5, other arithmetic: 9.99 us -> 3.88 us  [the longest x4 3.18 us: local(): other = swapped(totals.astype(jnp.bfloat16), seq_count, level)]
    ppermute x7, starting transfers between devices: 23.9 us -> 25.8 us  [wire(): lax.ppermute(block.astype(jnp.bfloat16), SEQ, route).astype(jnp.float32)]
    ppermute x4, waiting for transfers between devices: 6.81 us -> 8.64 us  [swapped(): return lax.ppermute(block, SEQ, route)]
    unnamed x74 -> x48, local copies, waits for them, and re-layouts: 4.83 us -> 4.09 us
  transfers between devices with their start and end apart: 16 -> 16, of which waited for: 8 -> 8; matrix products, arithmetic and copies ran while one was open for 28% -> 25% of each run, Pallas kernels for 0% -> 0%
where the time goes in v8:
time: 163 us; the launch traced here: 160 us
  starting transfers between devices  61.3 us (38%)
  waiting for transfers between devices  28.3 us (17%)
  matrix products  22.2 us (14%)
  local copies, waits for them, and re-layouts  21 us (13%)
  between operations  14.9 us (9%)
  other arithmetic  12.2 us (7%)
    ppermute x7, starting transfers between devices, wire(): lax.ppermute(block.astype(jnp.bfloat16), SEQ, route).astype(jnp.float32)  25.8 us
    ppermute x4, starting transfers between devices, swapped(): return lax.ppermute(block, SEQ, route)  19.1 us
    ppermute x7, waiting for transfers between devices, wire(): lax.ppermute(block.astype(jnp.bfloat16), SEQ, route).astype(jnp.float32)  15.1 us
    ppermute x3, starting transfers between devices, local(): other = lax.ppermute(totals.astype(jnp.bfloat16), SEQ, route)  14.5 us
    ppermute x4, waiting for transfers between devices, swapped(): return lax.ppermute(block, SEQ, route)  8.64 us
    dot_general x1, local copies, waits for them, and re-layouts, local(): lax.dot_general(out_grad, attention, (((0,), (0,)), ((), ())), preferred_...  5.6 us
    ppermute x3, waiting for transfers between devices, local(): other = lax.ppermute(totals.astype(jnp.bfloat16), SEQ, route)  4.47 us
    dot_general x1, matrix products, local(): lax.dot_general(out_grad, attention, (((0,), (0,)), ((), ())), preferred_...  4.23 us
  transfers between devices with their start and end apart: 16, of which 8 were waited for; matrix products, arithmetic and copies ran while one was open for 25% of the time, Pallas kernels for 0%

profile of v8, /device:TPU:6, one launch (start us, length us, event | category | flops | bytes accessed | tf_op | source)
XLA Modules:
  0.0 159.9 jit_solution(2204354528191749402)
XLA Ops:
  7.2 1.3 convolution_bitcast_fusion.5
  8.5 1.1 convolution_bitcast_fusion.6
  9.7 2.6 %convolution_convert_fusion.1 = bf16[384,256]{1,0:T(8,128)(2,1)S(1)} fusion(bf16[384,4096]{1,0:T(8,128)(2,1)S(1)} %copy-done, bf16[4096,256]{1,0:T(8,128)(2,1)} %param.8), kind=kOutput, calls=%fused_computation.37 | convolution fusion | flops 805404672 | bytes 5439488 | tf_op jit(solution)/shard_map/dot_general | solution.py:121
  13.1 1.9 %collective-permute-start = (bf16[2,2,128,128]{3,2,1,0:T(8,128)(2,1)S(1)}, bf16[2,2,128,128]{3,2,1,0:T(8,128)(2,1)S(1)}, u32[]{:S(2)}, u32[]{:S(2)}) collective-permute-start(bf16[2,2,128,128]{3,2,1,0:T(8,128)(2,1)S(1)} %fusion.23), channel_id=1, source_target_pairs={{0,12},{12,0},{24,36},{36,24},{48,60},{60,48},{72,84},{84,72},{96,... | collective-permute-start | bytes 393224 | tf_op jit(solution)/shard_map/ppermute | solution.py:18
  15.0 1.3 collective-permute-done
  16.4 3.5 %collective-permute-start.1 = (bf16[2,2,128,128]{3,2,1,0:T(8,128)(2,1)S(1)}, bf16[2,2,128,128]{3,2,1,0:T(8,128)(2,1)S(1)}, u32[]{:S(2)}, u32[]{:S(2)}) collective-permute-start(bf16[2,2,128,128]{3,2,1,0:T(8,128)(2,1)S(1)} %fusion.70), channel_id=1, source_target_pairs={{0,24},{24,0},{12,36},{36,12},{48,72},{72,48},{60,84},{84,60},{96,... | collective-permute-start | bytes 393224 | tf_op jit(solution)/shard_map/ppermute | solution.py:18
  19.9 4.0 %collective-permute-done.1 = bf16[2,2,128,128]{3,2,1,0:T(8,128)(2,1)S(1)} collective-permute-done((bf16[2,2,128,128]{3,2,1,0:T(8,128)(2,1)S(1)}, bf16[2,2,128,128]{3,2,1,0:T(8,128)(2,1)S(1)}, u32[]{:S(2)}, u32[]{:S(2)}) %collective-permute-start.1) | collective-permute-done | bytes 131104 | tf_op jit(solution)/shard_map/ppermute | solution.py:18
  23.8 0.7 fusion.24
  24.5 6.2 %collective-permute-start.4 = (bf16[2,2,128,128]{3,2,1,0:T(8,128)(2,1)}, bf16[2,2,128,128]{3,2,1,0:T(8,128)(2,1)}, u32[]{:S(2)}, u32[]{:S(2)}) collective-permute-start(bf16[2,2,128,128]{3,2,1,0:T(8,128)(2,1)} %fusion.24), channel_id=1, source_target_pairs={{0,144},{12,156},{24,168},{36,180},{48,0},{60,12},{72,24},{84,36},... | collective-permute-start | bytes 393224 | tf_op jit(solution)/shard_map/ppermute | solution.py:161
  30.7 3.8 %collective-permute-start.3 = (bf16[2,2,128,128]{3,2,1,0:T(8,128)(2,1)}, bf16[2,2,128,128]{3,2,1,0:T(8,128)(2,1)}, u32[]{:S(2)}, u32[]{:S(2)}) collective-permute-start(bf16[2,2,128,128]{3,2,1,0:T(8,128)(2,1)} %fusion.24), channel_id=1, source_target_pairs={{0,96},{12,108},{24,120},{36,132},{48,144},{60,156},{72,168},{84,1... | collective-permute-start | bytes 393224 | tf_op jit(solution)/shard_map/ppermute | solution.py:161
  34.5 4.5 %collective-permute-start.2 = (bf16[2,2,128,128]{3,2,1,0:T(8,128)(2,1)}, bf16[2,2,128,128]{3,2,1,0:T(8,128)(2,1)}, u32[]{:S(2)}, u32[]{:S(2)}) collective-permute-start(bf16[2,2,128,128]{3,2,1,0:T(8,128)(2,1)} %fusion.24), channel_id=1, source_target_pairs={{0,48},{12,60},{24,72},{36,84},{48,96},{60,108},{72,120},{84,132},... | collective-permute-start | bytes 393224 | tf_op jit(solution)/shard_map/ppermute | solution.py:161
  39.0 1.0 reshape.65
  40.0 1.0 reshape.66
  41.0 4.5 %collective-permute-done.3 = bf16[2,2,128,128]{3,2,1,0:T(8,128)(2,1)} collective-permute-done((bf16[2,2,128,128]{3,2,1,0:T(8,128)(2,1)}, bf16[2,2,128,128]{3,2,1,0:T(8,128)(2,1)}, u32[]{:S(2)}, u32[]{:S(2)}) %collective-permute-start.3) | collective-permute-done | bytes 131104 | tf_op jit(solution)/shard_map/ppermute | solution.py:161
  45.5 2.1 %fusion.71 = (bf16[2,2,128,128]{3,2,1,0:T(8,128)(2,1)}, f32[2,2,128,128]{3,2,1,0:T(8,128)}) fusion(bf16[2,2,128,128]{3,2,1,0:T(8,128)(2,1)} %collective-permute-done.4, bf16[2,2,128,128]{3,2,1,0:T(8,128)(2,1)} %collective-permute-done.3, bf16[2,2,128,128]{3,2,1,0:T(8,128)(2,1)} %collective-permute-done.2, bf16[2,2,128,128]{3,2,1,0:T(8,128)(2,1)} %copy-done.13, ...), kind=kLoop, calls=%fused_computation.132 | loop fusion | flops 786432 | bytes 1310720 | tf_op jit(solution)/shard_map/convert_element_type | solution.py:169
  47.6 2.7 %collective-permute-start.5 = (bf16[2,2,128,128]{3,2,1,0:T(8,128)(2,1)}, bf16[2,2,128,128]{3,2,1,0:T(8,128)(2,1)}, u32[]{:S(2)}, u32[]{:S(2)}) collective-permute-start(bf16[2,2,128,128]{3,2,1,0:T(8,128)(2,1)} %get-tuple-element.23), channel_id=1, source_target_pairs={{0,192},{192,0},{12,204},{204,12},{24,216},{216,24},{36,228},{228,... | collective-permute-start | bytes 393224 | tf_op jit(solution)/shard_map/ppermute | solution.py:18
  50.3 1.2 fusion.39
  51.5 1.7 %reshape.64 = bf16[6,64,2,128]{3,2,1,0:T(2,128)(2,1)} reshape(bf16[384,256]{1,0:T(8,128)(2,1)} %param.5) | data formatting | bytes 393216 | tf_op jit(solution)/shard_map/reshape | solution.py:117
  53.2 1.6 collective-permute-done.5
  54.7 1.1 add_convert_fusion
  55.8 10.9 %collective-permute-start.6 = (bf16[2,2,128,128]{3,2,1,0:T(8,128)(2,1)S(1)}, bf16[2,2,128,128]{3,2,1,0:T(8,128)(2,1)S(1)}, u32[]{:S(2)}, u32[]{:S(2)}) collective-permute-start(bf16[2,2,128,128]{3,2,1,0:T(8,128)(2,1)S(1)} %add_convert_fusion), channel_id=1, source_target_pairs={{0,384},{384,0},{12,396},{396,12},{24,408},{408,24},{36,420},{420,... | collective-permute-start | bytes 393224 | tf_op jit(solution)/shard_map/ppermute | solution.py:18
  66.7 1.2 fusion.14
  67.9 1.8 %collective-permute-done.6 = bf16[2,2,128,128]{3,2,1,0:T(8,128)(2,1)S(1)} collective-permute-done((bf16[2,2,128,128]{3,2,1,0:T(8,128)(2,1)S(1)}, bf16[2,2,128,128]{3,2,1,0:T(8,128)(2,1)S(1)}, u32[]{:S(2)}, u32[]{:S(2)}) %collective-permute-start.6) | collective-permute-done | bytes 131104 | tf_op jit(solution)/shard_map/ppermute | solution.py:18
  70.4 1.1 add_bitcast_fusion
  72.9 0.7 copy.133
  73.6 2.7 %convolution_convert_fusion = bf16[384,4096]{1,0:T(8,128)(2,1)} fusion(bf16[4096,256]{1,0:T(8,128)(2,1)S(1)} %copy-done.11, bf16[48,8,2,128]{3,2,1,0:T(2,128)(2,1)S(1)} %bitcast.133), kind=kOutput, calls=%fused_computation | convolution fusion | flops 806879232 | bytes 5439488 | tf_op jit(solution)/shard_map/dot_general | solution.py:188
  76.3 4.2 %convolution_bitcast_fusion = f32[4096,256]{0,1:T(8,128)} fusion(bf16[384,256]{1,0:T(8,128)(2,1)} %bitcast.137, bf16[384,4096]{1,0:T(8,128)(2,1)S(1)} %copy-done), kind=kOutput, calls=%fused_computation.1 | convolution fusion | flops 805306368 | bytes 7536640 | tf_op jit(solution)/shard_map/dot_general | solution.py:193
  80.5 5.6 %copy.52 = f32[4096,256]{1,0:T(8,128)} copy(f32[4096,256]{0,1:T(8,128)} %convolution_bitcast_fusion) | data formatting | bytes 8388608 | tf_op jit(solution)/shard_map/dot_general | solution.py:193
  86.1 3.2 %dynamic-slice_bitcast_fusion = f32[4,8,64,256]{3,2,1,0:T(8,128)} fusion(f32[4,8,2,64,256]{4,3,2,1,0:T(8,128)} %bitcast.128, s32[]{:T(128)S(6)} %select_n.241), kind=kLoop, calls=%fused_computation.4 | loop fusion | bytes 4194308 | tf_op jit(solution)/shard_map/jit(dynamic_index_in_dim)/squeeze | solution.py:75
  89.3 1.9 %collective-permute-start.7 = (f32[4,8,64,256]{3,2,1,0:T(8,128)}, f32[4,8,64,256]{3,2,1,0:T(8,128)}, u32[]{:S(2)}, u32[]{:S(2)}) collective-permute-start(f32[4,8,64,256]{3,2,1,0:T(8,128)} %dynamic-slice_bitcast_fusion), channel_id=1, source_target_pairs={{0,12},{12,0},{24,36},{36,24},{48,60},{60,48},{72,84},{84,72},{96,... | collective-permute-start | bytes 6291464 | tf_op jit(solution)/shard_map/ppermute | solution.py:76
  91.5 1.7 %reshape.68 = bf16[6,64,2,128]{3,2,1,0:T(2,128)(2,1)} reshape(bf16[384,256]{1,0:T(8,128)(2,1)} %copy-done.15) | data formatting | bytes 393216 | tf_op jit(solution)/shard_map/reshape | solution.py:124
  93.2 1.8 %fusion.13 = bf16[6,2,64,64]{3,2,1,0:T(8,128)(2,1)} fusion(pred[64,64]{1,0:T(8,128)(4,1)S(1)} %iota_compare_fusion, bf16[6,64,2,128]{3,2,1,0:T(2,128)(2,1)} %reshape.68, bf16[6,64,2,128]{3,2,1,0:T(2,128)(2,1)S(1)} %reshape.66), kind=kOutput, calls=%fused_computation.31 | convolution fusion | flops 12730368 | bytes 495616 | tf_op jit(solution)/shard_map/cthe,cshe->chts/dot_general | solution.py:202
  95.0 2.3 %convolution_bitcast_fusion.1 = f32[6,2,128,128]{2,3,1,0:T(8,128)} fusion(bf16[6,64,2,128]{3,2,1,0:T(2,128)(2,1)} %reshape.68, bf16[6,64,2,128]{3,2,1,0:T(2,128)(2,1)} %reshape.64), kind=kOutput, calls=%fused_computation.8 | convolution fusion | flops 25165824 | bytes 1179648 | tf_op jit(solution)/shard_map/cthd,cthe->chde/dot_general | solution.py:128
  97.2 1.8 %fusion.28 = f32[2,128,128]{2,1,0:T(8,128)} fusion(f32[1,1,128,128]{3,2,1,0:T(8,128)} %bitcast.139, f32[1,1,128,128]{3,2,1,0:T(8,128)} %bitcast.141, bf16[2,2,128,128]{3,2,1,0:T(8,128)(2,1)} %copy-done.21, bf16[2,2,128,128]{3,2,1,0:T(8,128)(2,1)} %collective-permute-done.5, bf16[2,2,128,128]{3,2,1,0:T(8,128)(2,1)} %collective-permute-done.4, ...), kind=kLoop, calls=%fused_computation.69 | loop fusion | flops 720896 | bytes 720903 | tf_op jit(solution)/shard_map/sub | solution.py:176
  99.1 1.6 %copy.53 = f32[2,128,128]{1,2,0:T(8,128)} copy(f32[2,128,128]{2,1,0:T(8,128)} %fusion.28) | data formatting | bytes 262144 | tf_op jit(solution)/shard_map/sub | solution.py:176
  100.7 1.3 subtract_convert_fusion
  102.1 2.7 %bitcast_add_fusion = f32[4,8,64,256]{3,2,1,0:T(8,128)S(1)} fusion(f32[4,8,64,256]{3,2,1,0:T(8,128)} %collective-permute-done.7, f32[4,8,2,64,256]{4,3,2,1,0:T(8,128)} %bitcast.129, s32[]{:T(128)S(6)} %select_n.240), kind=kLoop, calls=%fused_computation.3 | loop fusion | flops 524288 | bytes 6291460 | tf_op jit(solution)/shard_map/add | solution.py:76
  105.5 4.5 %collective-permute-start.8 = (bf16[4,4,64,256]{3,2,1,0:T(8,128)(2,1)S(1)}, bf16[4,4,64,256]{3,2,1,0:T(8,128)(2,1)S(1)}, u32[]{:S(2)}, u32[]{:S(2)}) collective-permute-start(bf16[4,4,64,256]{3,2,1,0:T(8,128)(2,1)S(1)} %fusion.20), channel_id=1, source_target_pairs={{0,24},{12,180},{24,0},{36,60},{48,72},{60,36},{72,48},{84,108},{9... | collective-permute-start | bytes 1572872 | tf_op jit(solution)/shard_map/ppermute | solution.py:62
  112.3 4.8 %collective-permute-done.8 = bf16[4,4,64,256]{3,2,1,0:T(8,128)(2,1)S(1)} collective-permute-done((bf16[4,4,64,256]{3,2,1,0:T(8,128)(2,1)S(1)}, bf16[4,4,64,256]{3,2,1,0:T(8,128)(2,1)S(1)}, u32[]{:S(2)}, u32[]{:S(2)}) %collective-permute-start.8) | collective-permute-done | bytes 524320 | tf_op jit(solution)/shard_map/ppermute | solution.py:62
  117.3 5.6 %collective-permute-start.9 = (bf16[4,64,256]{2,1,0:T(8,128)(2,1)S(1)}, bf16[4,64,256]{2,1,0:T(8,128)(2,1)S(1)}, u32[]{:S(2)}, u32[]{:S(2)}) collective-permute-start(bf16[4,64,256]{2,1,0:T(8,128)(2,1)S(1)} %get-tuple-element.25), channel_id=1, source_target_pairs={{0,192},{12,204},{24,216},{36,228},{48,240},{60,252},{72,264},{84,... | collective-permute-start | bytes 393224 | tf_op jit(solution)/shard_map/ppermute | solution.py:62
  123.0 1.9 %collective-permute-start.11 = (bf16[4,64,256]{2,1,0:T(8,128)(2,1)S(1)}, bf16[4,64,256]{2,1,0:T(8,128)(2,1)S(1)}, u32[]{:S(2)}, u32[]{:S(2)}) collective-permute-start(bf16[4,64,256]{2,1,0:T(8,128)(2,1)S(1)} %get-tuple-element.26), channel_id=1, source_target_pairs={{0,576},{12,588},{24,600},{36,612},{48,624},{60,636},{72,648},{84,... | collective-permute-start | bytes 393224 | tf_op jit(solution)/shard_map/ppermute | solution.py:62
  124.9 3.7 %collective-permute-start.10 = (bf16[4,64,256]{2,1,0:T(8,128)(2,1)S(1)}, bf16[4,64,256]{2,1,0:T(8,128)(2,1)S(1)}, u32[]{:S(2)}, u32[]{:S(2)}) collective-permute-start(bf16[4,64,256]{2,1,0:T(8,128)(2,1)S(1)} %get-tuple-element.27), channel_id=1, source_target_pairs={{0,384},{12,396},{24,408},{36,420},{48,432},{60,444},{72,456},{84,... | collective-permute-start | bytes 393224 | tf_op jit(solution)/shard_map/ppermute | solution.py:62
  128.8 5.9 %collective-permute-done.11 = bf16[4,64,256]{2,1,0:T(8,128)(2,1)S(1)} collective-permute-done((bf16[4,64,256]{2,1,0:T(8,128)(2,1)S(1)}, bf16[4,64,256]{2,1,0:T(8,128)(2,1)S(1)}, u32[]{:S(2)}, u32[]{:S(2)}) %collective-permute-start.11) | collective-permute-done | bytes 131104 | tf_op jit(solution)/shard_map/ppermute | solution.py:62
  134.7 1.9 %collective-permute-start.12 = (bf16[64,256]{1,0:T(8,128)(2,1)S(1)}, bf16[64,256]{1,0:T(8,128)(2,1)S(1)}, u32[]{:S(2)}, u32[]{:S(2)}) collective-permute-start(bf16[64,256]{1,0:T(8,128)(2,1)S(1)} %get-tuple-element.28), channel_id=1, source_target_pairs={{0,48},{12,60},{24,72},{36,84},{48,96},{60,108},{72,120},{84,132},... | collective-permute-start | bytes 98312 | tf_op jit(solution)/shard_map/ppermute | solution.py:62
  136.7 6.0 %collective-permute-start.14 = (bf16[64,256]{1,0:T(8,128)(2,1)S(1)}, bf16[64,256]{1,0:T(8,128)(2,1)S(1)}, u32[]{:S(2)}, u32[]{:S(2)}) collective-permute-start(bf16[64,256]{1,0:T(8,128)(2,1)S(1)} %get-tuple-element.29), channel_id=1, source_target_pairs={{0,144},{12,156},{24,168},{36,180},{48,0},{60,12},{72,24},{84,36},... | collective-permute-start | bytes 98312 | tf_op jit(solution)/shard_map/ppermute | solution.py:62
  142.7 2.2 %collective-permute-start.13 = (bf16[64,256]{1,0:T(8,128)(2,1)S(1)}, bf16[64,256]{1,0:T(8,128)(2,1)S(1)}, u32[]{:S(2)}, u32[]{:S(2)}) collective-permute-start(bf16[64,256]{1,0:T(8,128)(2,1)S(1)} %get-tuple-element.30), channel_id=1, source_target_pairs={{0,96},{12,108},{24,120},{36,132},{48,144},{60,156},{72,168},{84,1... | collective-permute-start | bytes 98312 | tf_op jit(solution)/shard_map/ppermute | solution.py:62
  145.4 0.7 copy.132
  147.9 4.5 %collective-permute-done.13 = bf16[64,256]{1,0:T(8,128)(2,1)S(1)} collective-permute-done((bf16[64,256]{1,0:T(8,128)(2,1)S(1)}, bf16[64,256]{1,0:T(8,128)(2,1)S(1)}, u32[]{:S(2)}, u32[]{:S(2)}) %collective-permute-start.13) | collective-permute-done | bytes 32800 | tf_op jit(solution)/shard_map/ppermute | solution.py:62
  (88 shorter events, 9.2 us)
Async XLA Ops:
  7.2 2.5 %copy-start = (bf16[384,4096]{1,0:T(8,128)(2,1)S(1)}, bf16[384,4096]{1,0:T(8,128)(2,1)}, u32[]{:S(2)}) copy-start(bf16[384,4096]{1,0:T(8,128)(2,1)} %param.9) | copy-start | bytes 9437188
  7.2 145.9 %reduce-scatter.2.cloned.1.call-start = ((), (), s32[]{:S(2)}) async-start(), calls=%async_computation.1 | async-start | bytes 3407872 | tf_op jit(solution)/shard_map/reduce_scatter | solution.py:192
  9.7 2.6 %copy-start.14 = (bf16[384,256]{1,0:T(8,128)(2,1)S(1)}, bf16[384,256]{1,0:T(8,128)(2,1)}, u32[]{:S(2)}) copy-start(bf16[384,256]{1,0:T(8,128)(2,1)} %param.5) | copy-start | bytes 589828
  12.3 0.7 copy-start.15
  12.6 3.8 %copy-start.19 = (f32[128,128]{0,1:T(8,128)}, f32[128,128]{0,1:T(8,128)S(1)}, u32[]{:S(2)}) copy-start(f32[128,128]{0,1:T(8,128)S(1)} %fusion.54) | copy-start | bytes 196612
  12.8 3.5 %copy-start.20 = (f32[128,128]{0,1:T(8,128)}, f32[128,128]{0,1:T(8,128)S(1)}, u32[]{:S(2)}) copy-start(f32[128,128]{0,1:T(8,128)S(1)} %fusion.56) | copy-start | bytes 196612
  13.0 21.5 %copy-start.9 = (f32[1,2,128,128]{3,2,1,0:T(8,128)}, f32[1,2,128,128]{3,2,1,0:T(8,128)S(1)}, u32[]{:S(2)}) copy-start(f32[1,2,128,128]{3,2,1,0:T(8,128)S(1)} %get-tuple-element.31) | copy-start | bytes 393220
  13.0 21.5 %copy-start.10 = (f32[1,2,128,128]{3,2,1,0:T(8,128)}, f32[1,2,128,128]{3,2,1,0:T(8,128)S(1)}, u32[]{:S(2)}) copy-start(f32[1,2,128,128]{3,2,1,0:T(8,128)S(1)} %get-tuple-element.32) | copy-start | bytes 393220
  13.1 3.2 %collective-permute-start = (bf16[2,2,128,128]{3,2,1,0:T(8,128)(2,1)S(1)}, bf16[2,2,128,128]{3,2,1,0:T(8,128)(2,1)S(1)}, u32[]{:S(2)}, u32[]{:S(2)}) collective-permute-start(bf16[2,2,128,128]{3,2,1,0:T(8,128)(2,1)S(1)} %fusion.23), channel_id=1, source_target_pairs={{0,12},{12,0},{24,36},{36,24},{48,60},{60,48},{72,84},{84,72},{96,... | collective-permute-start | bytes 393224 | tf_op jit(solution)/shard_map/ppermute | solution.py:18
  16.3 22.7 %copy-start.12 = (bf16[2,2,128,128]{3,2,1,0:T(8,128)(2,1)}, bf16[2,2,128,128]{3,2,1,0:T(8,128)(2,1)S(1)}, u32[]{:S(2)}) copy-start(bf16[2,2,128,128]{3,2,1,0:T(8,128)(2,1)S(1)} %collective-permute-done) | copy-start | bytes 393220
  16.4 7.4 %collective-permute-start.1 = (bf16[2,2,128,128]{3,2,1,0:T(8,128)(2,1)S(1)}, bf16[2,2,128,128]{3,2,1,0:T(8,128)(2,1)S(1)}, u32[]{:S(2)}, u32[]{:S(2)}) collective-permute-start(bf16[2,2,128,128]{3,2,1,0:T(8,128)(2,1)S(1)} %fusion.70), channel_id=1, source_target_pairs={{0,24},{24,0},{12,36},{36,12},{48,72},{72,48},{60,84},{84,60},{96,... | collective-permute-start | bytes 393224 | tf_op jit(solution)/shard_map/ppermute | solution.py:18
  23.8 10.7 %copy-start.13 = (bf16[2,2,128,128]{3,2,1,0:T(8,128)(2,1)}, bf16[2,2,128,128]{3,2,1,0:T(8,128)(2,1)S(1)}, u32[]{:S(2)}) copy-start(bf16[2,2,128,128]{3,2,1,0:T(8,128)(2,1)S(1)} %collective-permute-done.1) | copy-start | bytes 393220
  24.5 16.5 %collective-permute-start.4 = (bf16[2,2,128,128]{3,2,1,0:T(8,128)(2,1)}, bf16[2,2,128,128]{3,2,1,0:T(8,128)(2,1)}, u32[]{:S(2)}, u32[]{:S(2)}) collective-permute-start(bf16[2,2,128,128]{3,2,1,0:T(8,128)(2,1)} %fusion.24), channel_id=1, source_target_pairs={{0,144},{12,156},{24,168},{36,180},{48,0},{60,12},{72,24},{84,36},... | collective-permute-start | bytes 393224 | tf_op jit(solution)/shard_map/ppermute | solution.py:161
  30.7 14.8 %collective-permute-start.3 = (bf16[2,2,128,128]{3,2,1,0:T(8,128)(2,1)}, bf16[2,2,128,128]{3,2,1,0:T(8,128)(2,1)}, u32[]{:S(2)}, u32[]{:S(2)}) collective-permute-start(bf16[2,2,128,128]{3,2,1,0:T(8,128)(2,1)} %fusion.24), channel_id=1, source_target_pairs={{0,96},{12,108},{24,120},{36,132},{48,144},{60,156},{72,168},{84,1... | collective-permute-start | bytes 393224 | tf_op jit(solution)/shard_map/ppermute | solution.py:161
  34.5 11.0 %collective-permute-start.2 = (bf16[2,2,128,128]{3,2,1,0:T(8,128)(2,1)}, bf16[2,2,128,128]{3,2,1,0:T(8,128)(2,1)}, u32[]{:S(2)}, u32[]{:S(2)}) collective-permute-start(bf16[2,2,128,128]{3,2,1,0:T(8,128)(2,1)} %fusion.24), channel_id=1, source_target_pairs={{0,48},{12,60},{24,72},{36,84},{48,96},{60,108},{72,120},{84,132},... | collective-permute-start | bytes 393224 | tf_op jit(solution)/shard_map/ppermute | solution.py:161
  47.6 7.2 %collective-permute-start.5 = (bf16[2,2,128,128]{3,2,1,0:T(8,128)(2,1)}, bf16[2,2,128,128]{3,2,1,0:T(8,128)(2,1)}, u32[]{:S(2)}, u32[]{:S(2)}) collective-permute-start(bf16[2,2,128,128]{3,2,1,0:T(8,128)(2,1)} %get-tuple-element.23), channel_id=1, source_target_pairs={{0,192},{192,0},{12,204},{204,12},{24,216},{216,24},{36,228},{228,... | collective-permute-start | bytes 393224 | tf_op jit(solution)/shard_map/ppermute | solution.py:18
  53.2 18.3 %copy-start.1 = (f32[6,2,128,128]{3,2,1,0:T(8,128)S(1)}, f32[6,2,128,128]{3,2,1,0:T(8,128)}, u32[]{:S(2)}) copy-start(f32[6,2,128,128]{3,2,1,0:T(8,128)} %fusion.39) | copy-start | bytes 2359300
  54.7 17.0 %copy-start.2 = (bf16[6,64,2,128]{3,2,1,0:T(2,128)(2,1)S(1)}, bf16[6,64,2,128]{3,2,1,0:T(2,128)(2,1)}, u32[]{:S(2)}) copy-start(bf16[6,64,2,128]{3,2,1,0:T(2,128)(2,1)} %reshape.64) | copy-start | bytes 589828
  55.8 13.9 %collective-permute-start.6 = (bf16[2,2,128,128]{3,2,1,0:T(8,128)(2,1)S(1)}, bf16[2,2,128,128]{3,2,1,0:T(8,128)(2,1)S(1)}, u32[]{:S(2)}, u32[]{:S(2)}) collective-permute-start(bf16[2,2,128,128]{3,2,1,0:T(8,128)(2,1)S(1)} %add_convert_fusion), channel_id=1, source_target_pairs={{0,384},{384,0},{12,396},{396,12},{24,408},{408,24},{36,420},{420,... | collective-permute-start | bytes 393224 | tf_op jit(solution)/shard_map/ppermute | solution.py:18
  67.9 4.3 %copy-start.16 = (bf16[6,2,64,64]{3,2,1,0:T(8,128)(2,1)}, bf16[6,2,64,64]{3,2,1,0:T(8,128)(2,1)S(1)}, u32[]{:S(2)}) copy-start(bf16[6,2,64,64]{3,2,1,0:T(8,128)(2,1)S(1)} %fusion.14) | copy-start | bytes 294916
  69.7 0.6 copy-start.21
  71.7 0.8 copy-start.5
  71.7 1.0 copy-start.7
  71.7 1.9 %copy-start.11 = (bf16[4096,256]{1,0:T(8,128)(2,1)S(1)}, bf16[4096,256]{1,0:T(8,128)(2,1)}, u32[]{:S(2)}) copy-start(bf16[4096,256]{1,0:T(8,128)(2,1)} %param.8) | copy-start | bytes 6291460
  89.3 12.7 %collective-permute-start.7 = (f32[4,8,64,256]{3,2,1,0:T(8,128)}, f32[4,8,64,256]{3,2,1,0:T(8,128)}, u32[]{:S(2)}, u32[]{:S(2)}) collective-permute-start(f32[4,8,64,256]{3,2,1,0:T(8,128)} %dynamic-slice_bitcast_fusion), channel_id=1, source_target_pairs={{0,12},{12,0},{24,36},{36,24},{48,60},{60,48},{72,84},{84,72},{96,... | collective-permute-start | bytes 6291464 | tf_op jit(solution)/shard_map/ppermute | solution.py:76
  105.3 5.2 %copy-start.4 = (bf16[6,64,2,128]{3,2,1,0:T(2,128)(2,1)S(1)}, bf16[6,64,2,128]{3,2,1,0:T(2,128)(2,1)}, u32[]{:S(2)}) copy-start(bf16[6,64,2,128]{3,2,1,0:T(2,128)(2,1)} %reshape.68) | copy-start | bytes 589828
  105.4 5.2 %copy-start.8 = (bf16[6,2,128,128]{3,2,1,0:T(8,128)(2,1)S(1)}, bf16[6,2,128,128]{3,2,1,0:T(8,128)(2,1)}, u32[]{:S(2)}) copy-start(bf16[6,2,128,128]{3,2,1,0:T(8,128)(2,1)} %copy-done.7) | copy-start | bytes 1179652
  105.4 5.9 %copy-start.17 = (bf16[6,2,64,64]{3,2,1,0:T(8,128)(2,1)S(1)}, bf16[6,2,64,64]{3,2,1,0:T(8,128)(2,1)}, u32[]{:S(2)}) copy-start(bf16[6,2,64,64]{3,2,1,0:T(8,128)(2,1)} %copy-done.16) | copy-start | bytes 294916
  105.5 11.7 %collective-permute-start.8 = (bf16[4,4,64,256]{3,2,1,0:T(8,128)(2,1)S(1)}, bf16[4,4,64,256]{3,2,1,0:T(8,128)(2,1)S(1)}, u32[]{:S(2)}, u32[]{:S(2)}) collective-permute-start(bf16[4,4,64,256]{3,2,1,0:T(8,128)(2,1)S(1)} %fusion.20), channel_id=1, source_target_pairs={{0,24},{12,180},{24,0},{36,60},{48,72},{60,36},{72,48},{84,108},{9... | collective-permute-start | bytes 1572872 | tf_op jit(solution)/shard_map/ppermute | solution.py:62
  111.0 1.0 copy-start.6
  112.0 16.6 %copy-start.18 = (bf16[6,2,64,64]{3,2,1,0:T(8,128)(2,1)S(1)}, bf16[6,2,64,64]{3,2,1,0:T(8,128)(2,1)}, u32[]{:S(2)}) copy-start(bf16[6,2,64,64]{3,2,1,0:T(8,128)(2,1)} %fusion.13) | copy-start | bytes 294916
  117.3 27.6 %copy-start.3 = (bf16[6,64,2,128]{3,2,1,0:T(2,128)(2,1)S(1)}, bf16[6,64,2,128]{3,2,1,0:T(2,128)(2,1)}, u32[]{:S(2)}) copy-start(bf16[6,64,2,128]{3,2,1,0:T(2,128)(2,1)} %reshape.64) | copy-start | bytes 589828
  117.3 11.4 %collective-permute-start.9 = (bf16[4,64,256]{2,1,0:T(8,128)(2,1)S(1)}, bf16[4,64,256]{2,1,0:T(8,128)(2,1)S(1)}, u32[]{:S(2)}, u32[]{:S(2)}) collective-permute-start(bf16[4,64,256]{2,1,0:T(8,128)(2,1)S(1)} %get-tuple-element.25), channel_id=1, source_target_pairs={{0,192},{12,204},{24,216},{36,228},{48,240},{60,252},{72,264},{84,... | collective-permute-start | bytes 393224 | tf_op jit(solution)/shard_map/ppermute | solution.py:62
  123.0 11.7 %collective-permute-start.11 = (bf16[4,64,256]{2,1,0:T(8,128)(2,1)S(1)}, bf16[4,64,256]{2,1,0:T(8,128)(2,1)S(1)}, u32[]{:S(2)}, u32[]{:S(2)}) collective-permute-start(bf16[4,64,256]{2,1,0:T(8,128)(2,1)S(1)} %get-tuple-element.26), channel_id=1, source_target_pairs={{0,576},{12,588},{24,600},{36,612},{48,624},{60,636},{72,648},{84,... | collective-permute-start | bytes 393224 | tf_op jit(solution)/shard_map/ppermute | solution.py:62
  124.9 9.7 %collective-permute-start.10 = (bf16[4,64,256]{2,1,0:T(8,128)(2,1)S(1)}, bf16[4,64,256]{2,1,0:T(8,128)(2,1)S(1)}, u32[]{:S(2)}, u32[]{:S(2)}) collective-permute-start(bf16[4,64,256]{2,1,0:T(8,128)(2,1)S(1)} %get-tuple-element.27), channel_id=1, source_target_pairs={{0,384},{12,396},{24,408},{36,420},{48,432},{60,444},{72,456},{84,... | collective-permute-start | bytes 393224 | tf_op jit(solution)/shard_map/ppermute | solution.py:62
  134.7 13.2 %collective-permute-start.12 = (bf16[64,256]{1,0:T(8,128)(2,1)S(1)}, bf16[64,256]{1,0:T(8,128)(2,1)S(1)}, u32[]{:S(2)}, u32[]{:S(2)}) collective-permute-start(bf16[64,256]{1,0:T(8,128)(2,1)S(1)} %get-tuple-element.28), channel_id=1, source_target_pairs={{0,48},{12,60},{24,72},{36,84},{48,96},{60,108},{72,120},{84,132},... | collective-permute-start | bytes 98312 | tf_op jit(solution)/shard_map/ppermute | solution.py:62
  136.7 11.3 %collective-permute-start.14 = (bf16[64,256]{1,0:T(8,128)(2,1)S(1)}, bf16[64,256]{1,0:T(8,128)(2,1)S(1)}, u32[]{:S(2)}, u32[]{:S(2)}) collective-permute-start(bf16[64,256]{1,0:T(8,128)(2,1)S(1)} %get-tuple-element.29), channel_id=1, source_target_pairs={{0,144},{12,156},{24,168},{36,180},{48,0},{60,12},{72,24},{84,36},... | collective-permute-start | bytes 98312 | tf_op jit(solution)/shard_map/ppermute | solution.py:62
  142.7 9.7 %collective-permute-start.13 = (bf16[64,256]{1,0:T(8,128)(2,1)S(1)}, bf16[64,256]{1,0:T(8,128)(2,1)S(1)}, u32[]{:S(2)}, u32[]{:S(2)}) collective-permute-start(bf16[64,256]{1,0:T(8,128)(2,1)S(1)} %get-tuple-element.30), channel_id=1, source_target_pairs={{0,96},{12,108},{24,120},{36,132},{48,144},{60,156},{72,168},{84,1... | collective-permute-start | bytes 98312 | tf_op jit(solution)/shard_map/ppermute | solution.py:62
Sparse Core Ops, SparseCore 0:
  76.4 67.0 reduce-scatter.1

commit v9 on v8

--- a/solution.py
+++ b/solution.py
@@ -64,16 +64,17 @@
 
 def grid_scatter(partial, x_count, y_count, ride):
     count = x_count * y_count * 2
-    cols = partial.shape[1]
     position = lax.axis_index(SEQ)
     core = position % 2
     y = position // 2 % y_count
     x = position // (2 * y_count)
     index = lambda a, b, c: a * 2 * y_count + b % y_count * 2 + c
-    acc = partial.reshape(x_count, y_count, 2, partial.shape[0] // count, cols)
-    kept = lax.dynamic_index_in_dim(acc, core, 2, keepdims=False)
-    sent = lax.dynamic_index_in_dim(acc, 1 - core, 2, keepdims=False)
+    cols = partial.shape[0]
+    half = partial.shape[1] // 2
+    kept = lax.dynamic_slice_in_dim(partial, core * half, half, 1)
+    sent = lax.dynamic_slice_in_dim(partial, (1 - core) * half, half, 1)
     acc = kept + lax.ppermute(sent, SEQ, [(i, i ^ 1) for i in range(count)])
+    acc = acc.reshape(cols, x_count, y_count, half // (x_count * y_count)).transpose(1, 2, 3, 0)
     acc, ride = lax.optimization_barrier((acc, ride))
     acc = jnp.where(core == 1, jnp.roll(acc, -1, axis=1), acc)
     acc = acc.reshape(x_count, y_count // 2, 2, acc.shape[2], cols)
@@ -190,14 +191,20 @@
     ).astype(jnp.bfloat16)
     partial_output, attention = lax.optimization_barrier((partial_output, attention))
     output = lax.psum_scatter(partial_output, "head", scatter_dimension=0, tiled=True)
-    weight_partial = lax.dot_general(
-        out_grad, attention, (((0,), (0,)), ((), ())), preferred_element_type=jnp.float32
-    )
     if seq_count == 64:
+        block = out_grad.shape[1] // seq_count
+        reordered = out_grad.reshape(local_rows, seq_count // 2, 2, block)
+        reordered = reordered.transpose(0, 2, 1, 3).reshape(local_rows, -1)
+        flipped = lax.dot_general(
+            attention, reordered, (((0,), (0,)), ((), ())), preferred_element_type=jnp.float32
+        )
         weight_grad, (before_parts, later_parts) = grid_scatter(
-            weight_partial, 4, 8, (before_parts, later_parts)
+            flipped, 4, 8, (before_parts, later_parts)
         )
     else:
+        weight_partial = lax.dot_general(
+            out_grad, attention, (((0,), (0,)), ((), ())), preferred_element_type=jnp.float32
+        )
         weight_grad = halving_scatter(weight_partial, seq_count)
     grad_scores = jnp.einsum(
         "cthe,cshe->chts", grad_blocks, value_blocks, preferred_element_type=jnp.float32

time: 163 us -> 164 us (level); the launches traced: 160 us -> 163 us
  matrix products: 22.2 us -> 17.6 us
  waiting for transfers between devices: 28.3 us -> 32.6 us
    dot_general x1 -> x0, local copies, waits for them, and re-layouts: 5.6 us -> none  [local(): lax.dot_general(out_grad, attention, (((0,), (0,)), ((), ())), preferred_...]
    unnamed x48 -> x53, local copies, waits for them, and re-layouts: 4.09 us -> 9.16 us
    reduce_scatter x1, waiting for transfers between devices: 0.01 us -> 4.51 us  [local(): lax.psum_scatter(partial_output, 'head', scatter_dimension=0, tiled=True)]
    transpose x0 -> x1, local copies, waits for them, and re-layouts: none -> 3.9 us  [local(): reordered = reordered.transpose(0, 2, 1, 3).reshape(local_rows, -1)]
    squeeze x1 -> x0, local copies, waits for them, and re-layouts: 3.21 us -> none  [grid_scatter(): sent = lax.dynamic_index_in_dim(acc, 1 - core, 2, keepdims=False)]
    add x0 -> x1, local copies, waits for them, and re-layouts: none -> 2.95 us  [grid_scatter(): acc = kept + lax.ppermute(sent, SEQ, [(i, i ^ 1) for i in range(count)])]
    slice x2, local copies, waits for them, and re-layouts: 0.21 us -> 2.81 us  [grid_scatter(): acc = jnp.where(core == 1, jnp.roll(acc, -1, axis=1), acc)]
    ppermute x3, waiting for transfers between devices: 4.47 us -> 6.33 us  [local(): other = lax.ppermute(totals.astype(jnp.bfloat16), SEQ, route)]
  transfers between devices with their start and end apart: 16 -> 16, of which waited for: 8 -> 10; matrix products, arithmetic and copies ran while one was open for 25% -> 20% of each run, Pallas kernels for 0% -> 0%
where the time goes in v9:
time: 164 us; the launch traced here: 163 us
  starting transfers between devices  62 us (38%)
  waiting for transfers between devices  32.6 us (20%)
  local copies, waits for them, and re-layouts  22.6 us (14%)
  matrix products  17.6 us (11%)
  between operations  15.1 us (9%)
  other arithmetic  13.4 us (8%)
    ppermute x7, starting transfers between devices, wire(): lax.ppermute(block.astype(jnp.bfloat16), SEQ, route).astype(jnp.float32)  25.8 us
    ppermute x4, starting transfers between devices, swapped(): return lax.ppermute(block, SEQ, route)  19.7 us
    ppermute x3, starting transfers between devices, local(): other = lax.ppermute(totals.astype(jnp.bfloat16), SEQ, route)  14.5 us
    ppermute x7, waiting for transfers between devices, wire(): lax.ppermute(block.astype(jnp.bfloat16), SEQ, route).astype(jnp.float32)  13.4 us
    unnamed x53, local copies, waits for them, and re-layouts  9.16 us
    ppermute x4, waiting for transfers between devices, swapped(): return lax.ppermute(block, SEQ, route)  8.27 us
    ppermute x3, waiting for transfers between devices, local(): other = lax.ppermute(totals.astype(jnp.bfloat16), SEQ, route)  6.33 us
    reduce_scatter x1, waiting for transfers between devices, local(): lax.psum_scatter(partial_output, 'head', scatter_dimension=0, tiled=True)  4.51 us
  transfers between devices with their start and end apart: 16, of which 10 were waited for; matrix products, arithmetic and copies ran while one was open for 20% of the time, Pallas kernels for 0%

profile of v9, /device:TPU:6, one launch (start us, length us, event | category | flops | bytes accessed | tf_op | source)
XLA Modules:
  0.0 163.2 jit_solution(4815191278858019274)
XLA Ops:
  7.2 1.3 convolution_bitcast_fusion.4
  8.5 1.1 convolution_bitcast_fusion.5
  9.7 2.9 %convolution_convert_fusion.1 = bf16[384,256]{1,0:T(8,128)(2,1)S(1)} fusion(bf16[384,4096]{1,0:T(8,128)(2,1)} %param.9, bf16[4096,256]{1,0:T(8,128)(2,1)S(1)} %copy-done), kind=kOutput, calls=%fused_computation.35 | convolution fusion | flops 805404672 | bytes 5439488 | tf_op jit(solution)/shard_map/dot_general | solution.py:122
  13.2 1.9 %collective-permute-start = (bf16[2,2,128,128]{3,2,1,0:T(8,128)(2,1)S(1)}, bf16[2,2,128,128]{3,2,1,0:T(8,128)(2,1)S(1)}, u32[]{:S(2)}, u32[]{:S(2)}) collective-permute-start(bf16[2,2,128,128]{3,2,1,0:T(8,128)(2,1)S(1)} %fusion.23), channel_id=1, source_target_pairs={{0,12},{12,0},{24,36},{36,24},{48,60},{60,48},{72,84},{84,72},{96,... | collective-permute-start | bytes 393224 | tf_op jit(solution)/shard_map/ppermute | solution.py:18
  15.1 1.3 collective-permute-done
  16.5 3.5 %collective-permute-start.1 = (bf16[2,2,128,128]{3,2,1,0:T(8,128)(2,1)S(1)}, bf16[2,2,128,128]{3,2,1,0:T(8,128)(2,1)S(1)}, u32[]{:S(2)}, u32[]{:S(2)}) collective-permute-start(bf16[2,2,128,128]{3,2,1,0:T(8,128)(2,1)S(1)} %fusion.70), channel_id=1, source_target_pairs={{0,24},{24,0},{12,36},{36,12},{48,72},{72,48},{60,84},{84,60},{96,... | collective-permute-start | bytes 393224 | tf_op jit(solution)/shard_map/ppermute | solution.py:18
  20.0 4.0 %collective-permute-done.1 = bf16[2,2,128,128]{3,2,1,0:T(8,128)(2,1)S(1)} collective-permute-done((bf16[2,2,128,128]{3,2,1,0:T(8,128)(2,1)S(1)}, bf16[2,2,128,128]{3,2,1,0:T(8,128)(2,1)S(1)}, u32[]{:S(2)}, u32[]{:S(2)}) %collective-permute-start.1) | collective-permute-done | bytes 131104 | tf_op jit(solution)/shard_map/ppermute | solution.py:18
  23.9 0.7 fusion.24
  24.6 6.2 %collective-permute-start.4 = (bf16[2,2,128,128]{3,2,1,0:T(8,128)(2,1)}, bf16[2,2,128,128]{3,2,1,0:T(8,128)(2,1)}, u32[]{:S(2)}, u32[]{:S(2)}) collective-permute-start(bf16[2,2,128,128]{3,2,1,0:T(8,128)(2,1)} %fusion.24), channel_id=1, source_target_pairs={{0,144},{12,156},{24,168},{36,180},{48,0},{60,12},{72,24},{84,36},... | collective-permute-start | bytes 393224 | tf_op jit(solution)/shard_map/ppermute | solution.py:162
  30.8 3.8 %collective-permute-start.3 = (bf16[2,2,128,128]{3,2,1,0:T(8,128)(2,1)}, bf16[2,2,128,128]{3,2,1,0:T(8,128)(2,1)}, u32[]{:S(2)}, u32[]{:S(2)}) collective-permute-start(bf16[2,2,128,128]{3,2,1,0:T(8,128)(2,1)} %fusion.24), channel_id=1, source_target_pairs={{0,96},{12,108},{24,120},{36,132},{48,144},{60,156},{72,168},{84,1... | collective-permute-start | bytes 393224 | tf_op jit(solution)/shard_map/ppermute | solution.py:162
  34.6 4.5 %collective-permute-start.2 = (bf16[2,2,128,128]{3,2,1,0:T(8,128)(2,1)}, bf16[2,2,128,128]{3,2,1,0:T(8,128)(2,1)}, u32[]{:S(2)}, u32[]{:S(2)}) collective-permute-start(bf16[2,2,128,128]{3,2,1,0:T(8,128)(2,1)} %fusion.24), channel_id=1, source_target_pairs={{0,48},{12,60},{24,72},{36,84},{48,96},{60,108},{72,120},{84,132},... | collective-permute-start | bytes 393224 | tf_op jit(solution)/shard_map/ppermute | solution.py:162
  39.3 1.9 %collective-permute-done.4 = bf16[2,2,128,128]{3,2,1,0:T(8,128)(2,1)} collective-permute-done((bf16[2,2,128,128]{3,2,1,0:T(8,128)(2,1)}, bf16[2,2,128,128]{3,2,1,0:T(8,128)(2,1)}, u32[]{:S(2)}, u32[]{:S(2)}) %collective-permute-start.4) | collective-permute-done | bytes 131104 | tf_op jit(solution)/shard_map/ppermute | solution.py:162
  41.1 4.5 %collective-permute-done.3 = bf16[2,2,128,128]{3,2,1,0:T(8,128)(2,1)} collective-permute-done((bf16[2,2,128,128]{3,2,1,0:T(8,128)(2,1)}, bf16[2,2,128,128]{3,2,1,0:T(8,128)(2,1)}, u32[]{:S(2)}, u32[]{:S(2)}) %collective-permute-start.3) | collective-permute-done | bytes 131104 | tf_op jit(solution)/shard_map/ppermute | solution.py:162
  45.6 1.9 %fusion.71 = (bf16[2,2,128,128]{3,2,1,0:T(8,128)(2,1)}, f32[2,2,128,128]{3,2,1,0:T(8,128)}) fusion(bf16[2,2,128,128]{3,2,1,0:T(8,128)(2,1)} %collective-permute-done.4, bf16[2,2,128,128]{3,2,1,0:T(8,128)(2,1)} %collective-permute-done.3, bf16[2,2,128,128]{3,2,1,0:T(8,128)(2,1)} %collective-permute-done.2, ...), kind=kLoop, calls=%fused_computation.131 | loop fusion | flops 786432 | bytes 1310720 | tf_op jit(solution)/shard_map/convert_element_type | solution.py:170
  47.5 2.7 %collective-permute-start.5 = (bf16[2,2,128,128]{3,2,1,0:T(8,128)(2,1)}, bf16[2,2,128,128]{3,2,1,0:T(8,128)(2,1)}, u32[]{:S(2)}, u32[]{:S(2)}) collective-permute-start(bf16[2,2,128,128]{3,2,1,0:T(8,128)(2,1)} %get-tuple-element.23), channel_id=1, source_target_pairs={{0,192},{192,0},{12,204},{204,12},{24,216},{216,24},{36,228},{228,... | collective-permute-start | bytes 393224 | tf_op jit(solution)/shard_map/ppermute | solution.py:18
  50.6 1.0 reshape.70
  51.6 4.7 %copy.52 = bf16[384,4096]{0,1:T(8,128)(2,1)} copy(bf16[384,4096]{1,0:T(8,128)(2,1)} %param.9) | data formatting | bytes 6291456 | tf_op args[4]
  56.2 3.9 %copy.53 = bf16[384,2,32,64]{0,3,2,1:T(8,128)(2,1)} copy(bf16[384,2,32,64]{0,3,1,2:T(8,128)(2,1)} %bitcast.132) | data formatting | bytes 6291456 | tf_op jit(solution)/shard_map/transpose | solution.py:197
  60.1 1.0 add_convert_fusion
  61.2 11.5 %collective-permute-start.6 = (bf16[2,2,128,128]{3,2,1,0:T(8,128)(2,1)S(1)}, bf16[2,2,128,128]{3,2,1,0:T(8,128)(2,1)S(1)}, u32[]{:S(2)}, u32[]{:S(2)}) collective-permute-start(bf16[2,2,128,128]{3,2,1,0:T(8,128)(2,1)S(1)} %add_convert_fusion), channel_id=1, source_target_pairs={{0,384},{384,0},{12,396},{396,12},{24,408},{408,24},{36,420},{420,... | collective-permute-start | bytes 393224 | tf_op jit(solution)/shard_map/ppermute | solution.py:18
  73.0 3.0 %collective-permute-done.6 = bf16[2,2,128,128]{3,2,1,0:T(8,128)(2,1)S(1)} collective-permute-done((bf16[2,2,128,128]{3,2,1,0:T(8,128)(2,1)S(1)}, bf16[2,2,128,128]{3,2,1,0:T(8,128)(2,1)S(1)}, u32[]{:S(2)}, u32[]{:S(2)}) %collective-permute-start.6) | collective-permute-done | bytes 131104 | tf_op jit(solution)/shard_map/ppermute | solution.py:18
  76.6 1.1 add_bitcast_fusion
  79.4 2.7 %convolution_convert_fusion = bf16[384,4096]{1,0:T(8,128)(2,1)} fusion(bf16[4096,256]{1,0:T(8,128)(2,1)S(1)} %copy-done, bf16[48,8,2,128]{3,2,1,0:T(2,128)(2,1)S(1)} %bitcast.136), kind=kOutput, calls=%fused_computation | convolution fusion | flops 806879232 | bytes 5439488 | tf_op jit(solution)/shard_map/dot_general | solution.py:189
  82.1 3.2 %fusion.72 = f32[256,4096]{1,0:T(8,128)S(1)} fusion(bf16[384,256]{1,0:T(8,128)(2,1)S(1)} %bitcast.140, bf16[384,4096]{0,1:T(8,128)(2,1)} %bitcast.131), kind=kOutput, calls=%fused_computation.132 | convolution fusion | flops 805306368 | bytes 7536640 | tf_op jit(solution)/shard_map/dot_general | solution.py:198
  85.3 1.6 constant_dynamic-slice_fusion
  86.9 1.0 copy-done.2
  87.9 2.0 %collective-permute-start.7 = (f32[256,2048]{1,0:T(8,128)}, f32[256,2048]{1,0:T(8,128)}, u32[]{:S(2)}, u32[]{:S(2)}) collective-permute-start(f32[256,2048]{1,0:T(8,128)} %constant_dynamic-slice_fusion), channel_id=1, source_target_pairs={{0,12},{12,0},{24,36},{36,24},{48,60},{60,48},{72,84},{84,72},{96,... | collective-permute-start | bytes 6291464 | tf_op jit(solution)/shard_map/ppermute | solution.py:76
  90.3 0.9 fusion.13
  91.3 1.2 convolution_bitcast_fusion
  92.5 1.1 fusion.28
  93.7 2.2 %subtract_convert_fusion = (bf16[6,2,128,128]{2,3,1,0:T(8,128)(2,1)}, bf16[6,2,128,128]{2,3,1,0:T(8,128)(2,1)}) fusion(f32[6,2,128,128]{2,3,1,0:T(8,128)} %convolution_bitcast_fusion, f32[2,128,128]{1,2,0:T(8,128)S(1)} %copy.55), kind=kOutput, calls=%fused_computation.41 | output fusion | flops 1966080 | bytes 1703936 | tf_op jit(solution)/shard_map/jit(cumsum)/reduce_window_sum | solution.py:177
  95.9 3.9 %dynamic-slice_add_fusion = f32[256,2048]{1,0:T(8,128)} fusion(f32[256,2048]{1,0:T(8,128)} %collective-permute-done.7, f32[256,4096]{1,0:T(8,128)} %copy-done.2, s32[]{:T(128)S(6)} %select_n.239), kind=kLoop, calls=%fused_computation.2 | loop fusion | flops 524288 | bytes 6291460 | tf_op jit(solution)/shard_map/add | solution.py:76
  99.7 3.0 %copy.54 = f32[256,2048]{0,1:T(8,128)} copy(f32[256,2048]{1,0:T(8,128)} %dynamic-slice_add_fusion) | data formatting | bytes 4194304 | tf_op jit(solution)/shard_map/add | solution.py:76
  102.7 1.1 slice.97
  103.8 1.7 %slice.96 = f32[4,7,64,256]{3,2,1,0:T(8,128)S(1)} slice(f32[4,8,64,256]{3,2,1,0:T(8,128)} %bitcast.129), slice={[0:4], [1:8], [0:64], [0:256]} | slice | bytes 3670016 | tf_op jit(solution)/shard_map/jit(_roll_static)/slice | solution.py:79
  106.0 4.4 %collective-permute-start.8 = (bf16[4,4,64,256]{3,2,1,0:T(8,128)(2,1)S(1)}, bf16[4,4,64,256]{3,2,1,0:T(8,128)(2,1)S(1)}, u32[]{:S(2)}, u32[]{:S(2)}) collective-permute-start(bf16[4,4,64,256]{3,2,1,0:T(8,128)(2,1)S(1)} %fusion.20), channel_id=1, source_target_pairs={{0,24},{12,180},{24,0},{36,60},{48,72},{60,36},{72,48},{84,108},{9... | collective-permute-start | bytes 1572872 | tf_op jit(solution)/shard_map/ppermute | solution.py:62
  112.8 4.8 %collective-permute-done.8 = bf16[4,4,64,256]{3,2,1,0:T(8,128)(2,1)S(1)} collective-permute-done((bf16[4,4,64,256]{3,2,1,0:T(8,128)(2,1)S(1)}, bf16[4,4,64,256]{3,2,1,0:T(8,128)(2,1)S(1)}, u32[]{:S(2)}, u32[]{:S(2)}) %collective-permute-start.8) | collective-permute-done | bytes 524320 | tf_op jit(solution)/shard_map/ppermute | solution.py:62
  117.8 4.0 %collective-permute-start.9 = (bf16[4,64,256]{2,1,0:T(8,128)(2,1)S(1)}, bf16[4,64,256]{2,1,0:T(8,128)(2,1)S(1)}, u32[]{:S(2)}, u32[]{:S(2)}) collective-permute-start(bf16[4,64,256]{2,1,0:T(8,128)(2,1)S(1)} %get-tuple-element.25), channel_id=1, source_target_pairs={{0,192},{12,204},{24,216},{36,228},{48,240},{60,252},{72,264},{84,... | collective-permute-start | bytes 393224 | tf_op jit(solution)/shard_map/ppermute | solution.py:62
  121.7 1.9 %collective-permute-start.11 = (bf16[4,64,256]{2,1,0:T(8,128)(2,1)S(1)}, bf16[4,64,256]{2,1,0:T(8,128)(2,1)S(1)}, u32[]{:S(2)}, u32[]{:S(2)}) collective-permute-start(bf16[4,64,256]{2,1,0:T(8,128)(2,1)S(1)} %get-tuple-element.26), channel_id=1, source_target_pairs={{0,576},{12,588},{24,600},{36,612},{48,624},{60,636},{72,648},{84,... | collective-permute-start | bytes 393224 | tf_op jit(solution)/shard_map/ppermute | solution.py:62
  123.7 5.1 %collective-permute-start.10 = (bf16[4,64,256]{2,1,0:T(8,128)(2,1)S(1)}, bf16[4,64,256]{2,1,0:T(8,128)(2,1)S(1)}, u32[]{:S(2)}, u32[]{:S(2)}) collective-permute-start(bf16[4,64,256]{2,1,0:T(8,128)(2,1)S(1)} %get-tuple-element.27), channel_id=1, source_target_pairs={{0,384},{12,396},{24,408},{36,420},{48,432},{60,444},{72,456},{84,... | collective-permute-start | bytes 393224 | tf_op jit(solution)/shard_map/ppermute | solution.py:62
  129.0 2.1 %collective-permute-done.11 = bf16[4,64,256]{2,1,0:T(8,128)(2,1)S(1)} collective-permute-done((bf16[4,64,256]{2,1,0:T(8,128)(2,1)S(1)}, bf16[4,64,256]{2,1,0:T(8,128)(2,1)S(1)}, u32[]{:S(2)}, u32[]{:S(2)}) %collective-permute-start.11) | collective-permute-done | bytes 131104 | tf_op jit(solution)/shard_map/ppermute | solution.py:62
  131.1 2.3 %collective-permute-done.10 = bf16[4,64,256]{2,1,0:T(8,128)(2,1)S(1)} collective-permute-done((bf16[4,64,256]{2,1,0:T(8,128)(2,1)S(1)}, bf16[4,64,256]{2,1,0:T(8,128)(2,1)S(1)}, u32[]{:S(2)}, u32[]{:S(2)}) %collective-permute-start.10) | collective-permute-done | bytes 131104 | tf_op jit(solution)/shard_map/ppermute | solution.py:62
  133.5 1.9 %collective-permute-start.12 = (bf16[64,256]{1,0:T(8,128)(2,1)S(1)}, bf16[64,256]{1,0:T(8,128)(2,1)S(1)}, u32[]{:S(2)}, u32[]{:S(2)}) collective-permute-start(bf16[64,256]{1,0:T(8,128)(2,1)S(1)} %get-tuple-element.28), channel_id=1, source_target_pairs={{0,48},{12,60},{24,72},{36,84},{48,96},{60,108},{72,120},{84,132},... | collective-permute-start | bytes 98312 | tf_op jit(solution)/shard_map/ppermute | solution.py:62
  135.5 6.0 %collective-permute-start.14 = (bf16[64,256]{1,0:T(8,128)(2,1)S(1)}, bf16[64,256]{1,0:T(8,128)(2,1)S(1)}, u32[]{:S(2)}, u32[]{:S(2)}) collective-permute-start(bf16[64,256]{1,0:T(8,128)(2,1)S(1)} %get-tuple-element.29), channel_id=1, source_target_pairs={{0,144},{12,156},{24,168},{36,180},{48,0},{60,12},{72,24},{84,36},... | collective-permute-start | bytes 98312 | tf_op jit(solution)/shard_map/ppermute | solution.py:62
  141.5 2.5 %collective-permute-start.13 = (bf16[64,256]{1,0:T(8,128)(2,1)S(1)}, bf16[64,256]{1,0:T(8,128)(2,1)S(1)}, u32[]{:S(2)}, u32[]{:S(2)}) collective-permute-start(bf16[64,256]{1,0:T(8,128)(2,1)S(1)} %get-tuple-element.30), channel_id=1, source_target_pairs={{0,96},{12,108},{24,120},{36,132},{48,144},{60,156},{72,168},{84,1... | collective-permute-start | bytes 98312 | tf_op jit(solution)/shard_map/ppermute | solution.py:62
  144.5 0.7 copy.134
  147.0 4.2 %collective-permute-done.13 = bf16[64,256]{1,0:T(8,128)(2,1)S(1)} collective-permute-done((bf16[64,256]{1,0:T(8,128)(2,1)S(1)}, bf16[64,256]{1,0:T(8,128)(2,1)S(1)}, u32[]{:S(2)}, u32[]{:S(2)}) %collective-permute-start.13) | collective-permute-done | bytes 32800 | tf_op jit(solution)/shard_map/ppermute | solution.py:62
  151.9 4.5 %reduce-scatter.2.cloned.1.call-done = bf16[32,4096]{1,0:T(8,128)(2,1)} async-done(((bf16[384,4096]{1,0:T(8,128)(2,1)}), bf16[32,4096]{1,0:T(8,128)(2,1)}) %reduce-scatter.2.cloned.1.call-update) | async-done | bytes 262160 | tf_op jit(solution)/shard_map/reduce_scatter | solution.py:193
  (94 shorter events, 10.0 us)
Async XLA Ops:
  7.2 2.5 %copy-start = (bf16[4096,256]{1,0:T(8,128)(2,1)S(1)}, bf16[4096,256]{1,0:T(8,128)(2,1)}, u32[]{:S(2)}) copy-start(bf16[4096,256]{1,0:T(8,128)(2,1)} %param.8) | copy-start | bytes 6291460
  7.2 149.2 %reduce-scatter.2.cloned.1.call-start = ((), (), s32[]{:S(2)}) async-start(), calls=%async_computation.1 | async-start | bytes 3407872 | tf_op jit(solution)/shard_map/reduce_scatter | solution.py:193
  9.7 2.9 %copy-start.15 = (bf16[384,256]{1,0:T(8,128)(2,1)S(1)}, bf16[384,256]{1,0:T(8,128)(2,1)}, u32[]{:S(2)}) copy-start(bf16[384,256]{1,0:T(8,128)(2,1)} %param.5) | copy-start | bytes 589828
  12.6 22.0 %copy-start.16 = (bf16[384,256]{1,0:T(8,128)(2,1)}, bf16[384,256]{1,0:T(8,128)(2,1)S(1)}, u32[]{:S(2)}) copy-start(bf16[384,256]{1,0:T(8,128)(2,1)S(1)} %convolution_convert_fusion.1) | copy-start | bytes 589828
  12.6 26.5 %copy-start.13 = (bf16[384,256]{1,0:T(8,128)(2,1)S(1)}, bf16[384,256]{1,0:T(8,128)(2,1)}, u32[]{:S(2)}) copy-start(bf16[384,256]{1,0:T(8,128)(2,1)} %param.6) | copy-start | bytes 589828
  12.6 26.6 %copy-start.14 = (bf16[384,256]{1,0:T(8,128)(2,1)S(1)}, bf16[384,256]{1,0:T(8,128)(2,1)}, u32[]{:S(2)}) copy-start(bf16[384,256]{1,0:T(8,128)(2,1)} %param.7) | copy-start | bytes 589828
  13.1 26.0 %copy-start.21 = (f32[128,128]{0,1:T(8,128)}, f32[128,128]{0,1:T(8,128)S(1)}, u32[]{:S(2)}) copy-start(f32[128,128]{0,1:T(8,128)S(1)} %fusion.56) | copy-start | bytes 196612
  13.2 3.2 %collective-permute-start = (bf16[2,2,128,128]{3,2,1,0:T(8,128)(2,1)S(1)}, bf16[2,2,128,128]{3,2,1,0:T(8,128)(2,1)S(1)}, u32[]{:S(2)}, u32[]{:S(2)}) collective-permute-start(bf16[2,2,128,128]{3,2,1,0:T(8,128)(2,1)S(1)} %fusion.23), channel_id=1, source_target_pairs={{0,12},{12,0},{24,36},{36,24},{48,60},{60,48},{72,84},{84,72},{96,... | collective-permute-start | bytes 393224 | tf_op jit(solution)/shard_map/ppermute | solution.py:18
  16.4 31.0 %copy-start.9 = (bf16[2,2,128,128]{3,2,1,0:T(8,128)(2,1)}, bf16[2,2,128,128]{3,2,1,0:T(8,128)(2,1)S(1)}, u32[]{:S(2)}) copy-start(bf16[2,2,128,128]{3,2,1,0:T(8,128)(2,1)S(1)} %collective-permute-done) | copy-start | bytes 393220
  16.5 7.4 %collective-permute-start.1 = (bf16[2,2,128,128]{3,2,1,0:T(8,128)(2,1)S(1)}, bf16[2,2,128,128]{3,2,1,0:T(8,128)(2,1)S(1)}, u32[]{:S(2)}, u32[]{:S(2)}) collective-permute-start(bf16[2,2,128,128]{3,2,1,0:T(8,128)(2,1)S(1)} %fusion.70), channel_id=1, source_target_pairs={{0,24},{24,0},{12,36},{36,12},{48,72},{72,48},{60,84},{84,60},{96,... | collective-permute-start | bytes 393224 | tf_op jit(solution)/shard_map/ppermute | solution.py:18
  23.9 23.6 %copy-start.11 = (bf16[2,2,128,128]{3,2,1,0:T(8,128)(2,1)}, bf16[2,2,128,128]{3,2,1,0:T(8,128)(2,1)S(1)}, u32[]{:S(2)}) copy-start(bf16[2,2,128,128]{3,2,1,0:T(8,128)(2,1)S(1)} %collective-permute-done.1) | copy-start | bytes 393220
  24.6 16.5 %collective-permute-start.4 = (bf16[2,2,128,128]{3,2,1,0:T(8,128)(2,1)}, bf16[2,2,128,128]{3,2,1,0:T(8,128)(2,1)}, u32[]{:S(2)}, u32[]{:S(2)}) collective-permute-start(bf16[2,2,128,128]{3,2,1,0:T(8,128)(2,1)} %fusion.24), channel_id=1, source_target_pairs={{0,144},{12,156},{24,168},{36,180},{48,0},{60,12},{72,24},{84,36},... | collective-permute-start | bytes 393224 | tf_op jit(solution)/shard_map/ppermute | solution.py:162
  30.8 14.8 %collective-permute-start.3 = (bf16[2,2,128,128]{3,2,1,0:T(8,128)(2,1)}, bf16[2,2,128,128]{3,2,1,0:T(8,128)(2,1)}, u32[]{:S(2)}, u32[]{:S(2)}) collective-permute-start(bf16[2,2,128,128]{3,2,1,0:T(8,128)(2,1)} %fusion.24), channel_id=1, source_target_pairs={{0,96},{12,108},{24,120},{36,132},{48,144},{60,156},{72,168},{84,1... | collective-permute-start | bytes 393224 | tf_op jit(solution)/shard_map/ppermute | solution.py:162
  34.6 11.0 %collective-permute-start.2 = (bf16[2,2,128,128]{3,2,1,0:T(8,128)(2,1)}, bf16[2,2,128,128]{3,2,1,0:T(8,128)(2,1)}, u32[]{:S(2)}, u32[]{:S(2)}) collective-permute-start(bf16[2,2,128,128]{3,2,1,0:T(8,128)(2,1)} %fusion.24), channel_id=1, source_target_pairs={{0,48},{12,60},{24,72},{36,84},{48,96},{60,108},{72,120},{84,132},... | collective-permute-start | bytes 393224 | tf_op jit(solution)/shard_map/ppermute | solution.py:162
  47.5 12.7 %collective-permute-start.5 = (bf16[2,2,128,128]{3,2,1,0:T(8,128)(2,1)}, bf16[2,2,128,128]{3,2,1,0:T(8,128)(2,1)}, u32[]{:S(2)}, u32[]{:S(2)}) collective-permute-start(bf16[2,2,128,128]{3,2,1,0:T(8,128)(2,1)} %get-tuple-element.23), channel_id=1, source_target_pairs={{0,192},{192,0},{12,204},{204,12},{24,216},{216,24},{36,228},{228,... | collective-permute-start | bytes 393224 | tf_op jit(solution)/shard_map/ppermute | solution.py:18
  61.2 14.8 %collective-permute-start.6 = (bf16[2,2,128,128]{3,2,1,0:T(8,128)(2,1)S(1)}, bf16[2,2,128,128]{3,2,1,0:T(8,128)(2,1)S(1)}, u32[]{:S(2)}, u32[]{:S(2)}) collective-permute-start(bf16[2,2,128,128]{3,2,1,0:T(8,128)(2,1)S(1)} %add_convert_fusion), channel_id=1, source_target_pairs={{0,384},{384,0},{12,396},{396,12},{24,408},{408,24},{36,420},{420,... | collective-permute-start | bytes 393224 | tf_op jit(solution)/shard_map/ppermute | solution.py:18
  72.9 6.0 %copy-start.18 = (bf16[6,2,64,64]{3,2,1,0:T(8,128)(2,1)}, bf16[6,2,64,64]{3,2,1,0:T(8,128)(2,1)S(1)}, u32[]{:S(2)}) copy-start(bf16[6,2,64,64]{3,2,1,0:T(8,128)(2,1)S(1)} %fusion.14) | copy-start | bytes 294916
  76.0 0.6 copy-start.23
  77.9 0.8 copy-start.3
  77.9 1.0 copy-start.5
  85.3 2.6 %copy-start.2 = (f32[256,4096]{1,0:T(8,128)}, f32[256,4096]{1,0:T(8,128)S(1)}, u32[]{:S(2)}) copy-start(f32[256,4096]{1,0:T(8,128)S(1)} %fusion.72) | copy-start | bytes 12582916
  87.9 2.4 %copy-start.17 = (bf16[384,256]{1,0:T(8,128)(2,1)S(1)}, bf16[384,256]{1,0:T(8,128)(2,1)}, u32[]{:S(2)}) copy-start(bf16[384,256]{1,0:T(8,128)(2,1)} %copy-done.16) | copy-start | bytes 589828
  87.9 8.0 %collective-permute-start.7 = (f32[256,2048]{1,0:T(8,128)}, f32[256,2048]{1,0:T(8,128)}, u32[]{:S(2)}, u32[]{:S(2)}) collective-permute-start(f32[256,2048]{1,0:T(8,128)} %constant_dynamic-slice_fusion), channel_id=1, source_target_pairs={{0,12},{12,0},{24,36},{36,24},{48,60},{60,48},{72,84},{84,72},{96,... | collective-permute-start | bytes 6291464 | tf_op jit(solution)/shard_map/ppermute | solution.py:76
  89.9 2.5 %copy-start.10 = (bf16[2,2,128,128]{3,2,1,0:T(8,128)(2,1)S(1)}, bf16[2,2,128,128]{3,2,1,0:T(8,128)(2,1)}, u32[]{:S(2)}) copy-start(bf16[2,2,128,128]{3,2,1,0:T(8,128)(2,1)} %copy-done.9) | copy-start | bytes 393220
  89.9 2.5 %copy-start.12 = (bf16[2,2,128,128]{3,2,1,0:T(8,128)(2,1)S(1)}, bf16[2,2,128,128]{3,2,1,0:T(8,128)(2,1)}, u32[]{:S(2)}) copy-start(bf16[2,2,128,128]{3,2,1,0:T(8,128)(2,1)} %copy-done.11) | copy-start | bytes 393220
  90.0 2.5 %copy-start.22 = (f32[128,128]{0,1:T(8,128)S(1)}, f32[128,128]{0,1:T(8,128)}, u32[]{:S(2)}) copy-start(f32[128,128]{0,1:T(8,128)} %copy-done.21) | copy-start | bytes 196612
  102.7 2.8 %copy-start.1 = (f32[256,2048]{0,1:T(8,128)S(1)}, f32[256,2048]{0,1:T(8,128)}, u32[]{:S(2)}) copy-start(f32[256,2048]{0,1:T(8,128)} %copy.54) | copy-start | bytes 6291460
  105.5 4.9 %copy-start.8 = (bf16[6,2,128,128]{2,3,1,0:T(8,128)(2,1)S(1)}, bf16[6,2,128,128]{2,3,1,0:T(8,128)(2,1)}, u32[]{:S(2)}) copy-start(bf16[6,2,128,128]{2,3,1,0:T(8,128)(2,1)} %get-tuple-element.16) | copy-start | bytes 1179652
  105.9 5.1 %copy-start.6 = (bf16[6,2,128,128]{3,2,1,0:T(8,128)(2,1)S(1)}, bf16[6,2,128,128]{3,2,1,0:T(8,128)(2,1)}, u32[]{:S(2)}) copy-start(bf16[6,2,128,128]{3,2,1,0:T(8,128)(2,1)} %copy-done.5) | copy-start | bytes 1179652
  105.9 5.5 %copy-start.7 = (bf16[6,2,128,128]{2,3,1,0:T(8,128)(2,1)S(1)}, bf16[6,2,128,128]{2,3,1,0:T(8,128)(2,1)}, u32[]{:S(2)}) copy-start(bf16[6,2,128,128]{2,3,1,0:T(8,128)(2,1)} %get-tuple-element.17) | copy-start | bytes 1179652
  106.0 5.8 %copy-start.19 = (bf16[6,2,64,64]{3,2,1,0:T(8,128)(2,1)S(1)}, bf16[6,2,64,64]{3,2,1,0:T(8,128)(2,1)}, u32[]{:S(2)}) copy-start(bf16[6,2,64,64]{3,2,1,0:T(8,128)(2,1)} %copy-done.18) | copy-start | bytes 294916
  106.0 11.5 %collective-permute-start.8 = (bf16[4,4,64,256]{3,2,1,0:T(8,128)(2,1)S(1)}, bf16[4,4,64,256]{3,2,1,0:T(8,128)(2,1)S(1)}, u32[]{:S(2)}, u32[]{:S(2)}) collective-permute-start(bf16[4,4,64,256]{3,2,1,0:T(8,128)(2,1)S(1)} %fusion.20), channel_id=1, source_target_pairs={{0,24},{12,180},{24,0},{36,60},{48,72},{60,36},{72,48},{84,108},{9... | collective-permute-start | bytes 1572872 | tf_op jit(solution)/shard_map/ppermute | solution.py:62
  111.4 1.0 copy-start.4
  112.4 16.4 %copy-start.20 = (bf16[6,2,64,64]{3,2,1,0:T(8,128)(2,1)S(1)}, bf16[6,2,64,64]{3,2,1,0:T(8,128)(2,1)}, u32[]{:S(2)}) copy-start(bf16[6,2,64,64]{3,2,1,0:T(8,128)(2,1)} %fusion.13) | copy-start | bytes 294916
  117.8 11.2 %collective-permute-start.9 = (bf16[4,64,256]{2,1,0:T(8,128)(2,1)S(1)}, bf16[4,64,256]{2,1,0:T(8,128)(2,1)S(1)}, u32[]{:S(2)}, u32[]{:S(2)}) collective-permute-start(bf16[4,64,256]{2,1,0:T(8,128)(2,1)S(1)} %get-tuple-element.25), channel_id=1, source_target_pairs={{0,192},{12,204},{24,216},{36,228},{48,240},{60,252},{72,264},{84,... | collective-permute-start | bytes 393224 | tf_op jit(solution)/shard_map/ppermute | solution.py:62
  121.7 9.4 %collective-permute-start.11 = (bf16[4,64,256]{2,1,0:T(8,128)(2,1)S(1)}, bf16[4,64,256]{2,1,0:T(8,128)(2,1)S(1)}, u32[]{:S(2)}, u32[]{:S(2)}) collective-permute-start(bf16[4,64,256]{2,1,0:T(8,128)(2,1)S(1)} %get-tuple-element.26), channel_id=1, source_target_pairs={{0,576},{12,588},{24,600},{36,612},{48,624},{60,636},{72,648},{84,... | collective-permute-start | bytes 393224 | tf_op jit(solution)/shard_map/ppermute | solution.py:62
  123.7 9.8 %collective-permute-start.10 = (bf16[4,64,256]{2,1,0:T(8,128)(2,1)S(1)}, bf16[4,64,256]{2,1,0:T(8,128)(2,1)S(1)}, u32[]{:S(2)}, u32[]{:S(2)}) collective-permute-start(bf16[4,64,256]{2,1,0:T(8,128)(2,1)S(1)} %get-tuple-element.27), channel_id=1, source_target_pairs={{0,384},{12,396},{24,408},{36,420},{48,432},{60,444},{72,456},{84,... | collective-permute-start | bytes 393224 | tf_op jit(solution)/shard_map/ppermute | solution.py:62
  133.5 13.4 %collective-permute-start.12 = (bf16[64,256]{1,0:T(8,128)(2,1)S(1)}, bf16[64,256]{1,0:T(8,128)(2,1)S(1)}, u32[]{:S(2)}, u32[]{:S(2)}) collective-permute-start(bf16[64,256]{1,0:T(8,128)(2,1)S(1)} %get-tuple-element.28), channel_id=1, source_target_pairs={{0,48},{12,60},{24,72},{36,84},{48,96},{60,108},{72,120},{84,132},... | collective-permute-start | bytes 98312 | tf_op jit(solution)/shard_map/ppermute | solution.py:62
  135.5 11.5 %collective-permute-start.14 = (bf16[64,256]{1,0:T(8,128)(2,1)S(1)}, bf16[64,256]{1,0:T(8,128)(2,1)S(1)}, u32[]{:S(2)}, u32[]{:S(2)}) collective-permute-start(bf16[64,256]{1,0:T(8,128)(2,1)S(1)} %get-tuple-element.29), channel_id=1, source_target_pairs={{0,144},{12,156},{24,168},{36,180},{48,0},{60,12},{72,24},{84,36},... | collective-permute-start | bytes 98312 | tf_op jit(solution)/shard_map/ppermute | solution.py:62
  141.5 9.7 %collective-permute-start.13 = (bf16[64,256]{1,0:T(8,128)(2,1)S(1)}, bf16[64,256]{1,0:T(8,128)(2,1)S(1)}, u32[]{:S(2)}, u32[]{:S(2)}) collective-permute-start(bf16[64,256]{1,0:T(8,128)(2,1)S(1)} %get-tuple-element.30), channel_id=1, source_target_pairs={{0,96},{12,108},{24,120},{36,132},{48,144},{60,156},{72,168},{84,1... | collective-permute-start | bytes 98312 | tf_op jit(solution)/shard_map/ppermute | solution.py:62
Sparse Core Ops, SparseCore 0:
  90.0 66.2 reduce-scatter.1

commit v10 on v5

--- a/solution.py
+++ b/solution.py
@@ -171,9 +171,9 @@
         out_grad, attention, (((0,), (0,)), ((), ())), preferred_element_type=jnp.float32
     )
     if seq_count == 64:
-        weight_grad, (before_parts, later_parts) = grid_scatter(
-            weight_partial, 4, 8, (before_parts, later_parts)
-        )
+        weight_grad, (inflow, outflow) = grid_scatter(weight_partial, 4, 8, (inflow, outflow))
+        before_parts = split_state(inflow[None] + jnp.cumsum(key_value, 0) - key_value)
+        later_parts = split_state(outflow[None] + own_pairs[None] - jnp.cumsum(query_pairs, 0))
     else:
         weight_grad = halving_scatter(weight_partial, seq_count)
     grad_scores = jnp.einsum(

time: 162 us -> 167 us (1.031)
  waiting for transfers between devices: 32.9 us -> 35.7 us
  other arithmetic: 13.9 us -> 16.5 us
  local copies, waits for them, and re-layouts: 21.1 us -> 23.2 us
    reduce_scatter x1, waiting for transfers between devices: 0.01 us -> 6.83 us  [local(): lax.psum_scatter(partial_output, 'head', scatter_dimension=0, tiled=True)]
    ppermute x7, waiting for transfers between devices: 15 us -> 10.7 us  [wire(): lax.ppermute(block.astype(jnp.bfloat16), SEQ, route).astype(jnp.float32)]
    select_n x1, other arithmetic: 0.37 us -> 2.73 us  [grid_scatter(): acc = jnp.where(core == 1, jnp.roll(acc, -1, axis=1), acc)]
    slice x2, local copies, waits for them, and re-layouts: 0.21 us -> 2.14 us  [grid_scatter(): acc = jnp.where(core == 1, jnp.roll(acc, -1, axis=1), acc)]
    unnamed x76 -> x68, local copies, waits for them, and re-layouts: 4.85 us -> 5.29 us
  transfers between devices with their start and end apart: 15 -> 15, of which waited for: 8 -> 10; matrix products, arithmetic and copies ran while one was open for 25% -> 18% of each run, Pallas kernels for 0% -> 0%
where the time goes in v10:
time: 167 us; the launch traced here: 165 us
  starting transfers between devices  55.1 us (33%)
  waiting for transfers between devices  35.7 us (21%)
  local copies, waits for them, and re-layouts  23.2 us (14%)
  matrix products  20.3 us (12%)
  other arithmetic  16.5 us (10%)
  between operations  14.7 us (9%)
    ppermute x6, starting transfers between devices, swapped(): return lax.ppermute(block, SEQ, route)  28.4 us
    ppermute x7, starting transfers between devices, wire(): lax.ppermute(block.astype(jnp.bfloat16), SEQ, route).astype(jnp.float32)  24.8 us
    ppermute x6, waiting for transfers between devices, swapped(): return lax.ppermute(block, SEQ, route)  18.1 us
    ppermute x7, waiting for transfers between devices, wire(): lax.ppermute(block.astype(jnp.bfloat16), SEQ, route).astype(jnp.float32)  10.7 us
    reduce_scatter x1, waiting for transfers between devices, local(): lax.psum_scatter(partial_output, 'head', scatter_dimension=0, tiled=True)  6.83 us
    dot_general x1, local copies, waits for them, and re-layouts, local(): lax.dot_general(out_grad, attention, (((0,), (0,)), ((), ())), preferred_...  5.6 us
    unnamed x68, local copies, waits for them, and re-layouts  5.29 us
    convert_element_type x6, other arithmetic, local(): totals.astype(jnp.bfloat16)  4.74 us
  transfers between devices with their start and end apart: 15, of which 10 were waited for; matrix products, arithmetic and copies ran while one was open for 18% of the time, Pallas kernels for 0%

profile of v10, /device:TPU:6, one launch (start us, length us, event | category | flops | bytes accessed | tf_op | source)
XLA Modules:
  0.0 165.5 jit_solution(3462167643092579500)
XLA Ops:
  7.2 1.3 convolution_bitcast_fusion.7
  8.5 1.1 convolution_bitcast_fusion.8
  9.7 2.6 %convolution_convert_fusion.1 = bf16[384,256]{1,0:T(8,128)(2,1)S(1)} fusion(bf16[384,4096]{1,0:T(8,128)(2,1)S(1)} %copy-done, bf16[4096,256]{1,0:T(8,128)(2,1)} %param.8), kind=kOutput, calls=%fused_computation.35 | convolution fusion | flops 805404672 | bytes 5439488 | tf_op jit(solution)/shard_map/dot_general | solution.py:117
  12.9 1.9 %collective-permute-start = (bf16[2,2,128,128]{3,2,1,0:T(8,128)(2,1)S(1)}, bf16[2,2,128,128]{3,2,1,0:T(8,128)(2,1)S(1)}, u32[]{:S(2)}, u32[]{:S(2)}) collective-permute-start(bf16[2,2,128,128]{3,2,1,0:T(8,128)(2,1)S(1)} %fusion.31), channel_id=1, source_target_pairs={{0,12},{12,0},{24,36},{36,24},{48,60},{60,48},{72,84},{84,72},{96,... | collective-permute-start | bytes 393224 | tf_op jit(solution)/shard_map/ppermute | solution.py:18
  14.8 1.3 collective-permute-done
  16.2 3.5 %collective-permute-start.1 = (bf16[2,2,128,128]{3,2,1,0:T(8,128)(2,1)S(1)}, bf16[2,2,128,128]{3,2,1,0:T(8,128)(2,1)S(1)}, u32[]{:S(2)}, u32[]{:S(2)}) collective-permute-start(bf16[2,2,128,128]{3,2,1,0:T(8,128)(2,1)S(1)} %fusion.81), channel_id=1, source_target_pairs={{0,24},{24,0},{12,36},{36,12},{48,72},{72,48},{60,84},{84,60},{96,... | collective-permute-start | bytes 393224 | tf_op jit(solution)/shard_map/ppermute | solution.py:18
  19.7 4.0 %collective-permute-done.1 = bf16[2,2,128,128]{3,2,1,0:T(8,128)(2,1)S(1)} collective-permute-done((bf16[2,2,128,128]{3,2,1,0:T(8,128)(2,1)S(1)}, bf16[2,2,128,128]{3,2,1,0:T(8,128)(2,1)S(1)}, u32[]{:S(2)}, u32[]{:S(2)}) %collective-permute-start.1) | collective-permute-done | bytes 131104 | tf_op jit(solution)/shard_map/ppermute | solution.py:18
  24.5 4.5 %collective-permute-start.2 = (bf16[2,2,128,128]{3,2,1,0:T(8,128)(2,1)}, bf16[2,2,128,128]{3,2,1,0:T(8,128)(2,1)}, u32[]{:S(2)}, u32[]{:S(2)}) collective-permute-start(bf16[2,2,128,128]{3,2,1,0:T(8,128)(2,1)} %get-tuple-element.15), channel_id=1, source_target_pairs={{0,48},{48,0},{12,60},{60,12},{24,72},{72,24},{36,84},{84,36},{96,... | collective-permute-start | bytes 393224 | tf_op jit(solution)/shard_map/ppermute | solution.py:18
  29.0 1.0 reshape.105
  30.0 5.1 %collective-permute-done.2 = bf16[2,2,128,128]{3,2,1,0:T(8,128)(2,1)} collective-permute-done((bf16[2,2,128,128]{3,2,1,0:T(8,128)(2,1)}, bf16[2,2,128,128]{3,2,1,0:T(8,128)(2,1)}, u32[]{:S(2)}, u32[]{:S(2)}) %collective-permute-start.2) | collective-permute-done | bytes 131104 | tf_op jit(solution)/shard_map/ppermute | solution.py:18
  35.1 1.0 fusion.86
  36.1 7.7 %collective-permute-start.3 = (bf16[2,2,128,128]{3,2,1,0:T(8,128)(2,1)S(1)}, bf16[2,2,128,128]{3,2,1,0:T(8,128)(2,1)S(1)}, u32[]{:S(2)}, u32[]{:S(2)}) collective-permute-start(bf16[2,2,128,128]{3,2,1,0:T(8,128)(2,1)S(1)} %fusion.86), channel_id=1, source_target_pairs={{0,96},{96,0},{12,108},{108,12},{24,120},{120,24},{36,132},{132,36... | collective-permute-start | bytes 393224 | tf_op jit(solution)/shard_map/ppermute | solution.py:18
  44.2 6.0 %collective-permute-done.3 = bf16[2,2,128,128]{3,2,1,0:T(8,128)(2,1)S(1)} collective-permute-done((bf16[2,2,128,128]{3,2,1,0:T(8,128)(2,1)S(1)}, bf16[2,2,128,128]{3,2,1,0:T(8,128)(2,1)S(1)}, u32[]{:S(2)}, u32[]{:S(2)}) %collective-permute-start.3) | collective-permute-done | bytes 131104 | tf_op jit(solution)/shard_map/ppermute | solution.py:18
  50.8 1.7 %fusion.85 = bf16[2,2,128,128]{3,2,1,0:T(8,128)(2,1)} fusion(bf16[2,2,128,128]{3,2,1,0:T(8,128)(2,1)S(1)} %collective-permute-done.3, f32[2,2,128,128]{3,2,1,0:T(8,128)} %get-tuple-element.16, bf16[2,2,128,128]{3,2,1,0:T(8,128)(2,1)} %collective-permute-done.2), kind=kLoop, calls=%fused_computation.139 | loop fusion | flops 327680 | bytes 655360 | tf_op jit(solution)/shard_map/convert_element_type | solution.py:147
  52.5 2.7 %collective-permute-start.4 = (bf16[2,2,128,128]{3,2,1,0:T(8,128)(2,1)}, bf16[2,2,128,128]{3,2,1,0:T(8,128)(2,1)}, u32[]{:S(2)}, u32[]{:S(2)}) collective-permute-start(bf16[2,2,128,128]{3,2,1,0:T(8,128)(2,1)} %fusion.85), channel_id=1, source_target_pairs={{0,192},{192,0},{12,204},{204,12},{24,216},{216,24},{36,228},{228,... | collective-permute-start | bytes 393224 | tf_op jit(solution)/shard_map/ppermute | solution.py:18
  55.3 1.0 fusion.94
  56.3 1.7 reshape.104
  57.9 1.7 %collective-permute-done.4 = bf16[2,2,128,128]{3,2,1,0:T(8,128)(2,1)} collective-permute-done((bf16[2,2,128,128]{3,2,1,0:T(8,128)(2,1)}, bf16[2,2,128,128]{3,2,1,0:T(8,128)(2,1)}, u32[]{:S(2)}, u32[]{:S(2)}) %collective-permute-start.4) | collective-permute-done | bytes 131104 | tf_op jit(solution)/shard_map/ppermute | solution.py:18
  59.7 1.2 add_convert_fusion
  60.9 8.0 %collective-permute-start.5 = (bf16[2,2,128,128]{3,2,1,0:T(8,128)(2,1)S(1)}, bf16[2,2,128,128]{3,2,1,0:T(8,128)(2,1)S(1)}, u32[]{:S(2)}, u32[]{:S(2)}) collective-permute-start(bf16[2,2,128,128]{3,2,1,0:T(8,128)(2,1)S(1)} %add_convert_fusion), channel_id=1, source_target_pairs={{0,384},{384,0},{12,396},{396,12},{24,408},{408,24},{36,420},{420,... | collective-permute-start | bytes 393224 | tf_op jit(solution)/shard_map/ppermute | solution.py:18
  68.9 1.2 fusion.13
  70.1 1.1 convert_element_type.156
  71.2 0.9 convert_element_type.160
  72.1 0.9 convert_element_type.164
  75.7 2.6 %convolution_convert_fusion = bf16[384,4096]{1,0:T(8,128)(2,1)} fusion(bf16[4096,256]{1,0:T(8,128)(2,1)S(1)} %copy-done.14, bf16[48,8,2,128]{3,2,1,0:T(2,128)(2,1)S(1)} %bitcast.122), kind=kOutput, calls=%fused_computation | convolution fusion | flops 806879232 | bytes 5439488 | tf_op jit(solution)/shard_map/dot_general | solution.py:165
  78.3 1.0 copy.133
  79.3 3.3 %convolution_bitcast_fusion = f32[4096,256]{0,1:T(8,128)} fusion(bf16[384,256]{1,0:T(8,128)(2,1)S(1)} %bitcast.127, bf16[384,4096]{1,0:T(8,128)(2,1)S(1)} %copy-done), kind=kOutput, calls=%fused_computation.1 | convolution fusion | flops 805306368 | bytes 7536640 | tf_op jit(solution)/shard_map/dot_general | solution.py:170
  82.6 5.6 %copy.52 = f32[4096,256]{1,0:T(8,128)} copy(f32[4096,256]{0,1:T(8,128)} %convolution_bitcast_fusion) | data formatting | bytes 8388608 | tf_op jit(solution)/shard_map/dot_general | solution.py:170
  88.2 3.2 %dynamic-slice_bitcast_fusion = f32[4,8,64,256]{3,2,1,0:T(8,128)} fusion(f32[4,8,2,64,256]{4,3,2,1,0:T(8,128)} %bitcast.118, s32[]{:T(128)S(6)} %select_n.214), kind=kLoop, calls=%fused_computation.4 | loop fusion | bytes 4194308 | tf_op jit(solution)/shard_map/jit(dynamic_index_in_dim)/squeeze | solution.py:71
  91.4 1.9 %collective-permute-start.6 = (f32[4,8,64,256]{3,2,1,0:T(8,128)}, f32[4,8,64,256]{3,2,1,0:T(8,128)}, u32[]{:S(2)}, u32[]{:S(2)}) collective-permute-start(f32[4,8,64,256]{3,2,1,0:T(8,128)} %dynamic-slice_bitcast_fusion), channel_id=1, source_target_pairs={{0,12},{12,0},{24,36},{36,24},{48,60},{60,48},{72,84},{84,72},{96,... | collective-permute-start | bytes 6291464 | tf_op jit(solution)/shard_map/ppermute | solution.py:72
  93.3 1.7 %reshape.108 = bf16[6,64,2,128]{3,2,1,0:T(2,128)(2,1)} reshape(bf16[384,256]{1,0:T(8,128)(2,1)} %copy-done.20) | data formatting | bytes 393216 | tf_op jit(solution)/shard_map/reshape | solution.py:120
  95.0 1.8 %fusion.12 = bf16[6,2,64,64]{3,2,1,0:T(8,128)(2,1)} fusion(pred[64,64]{1,0:T(8,128)(4,1)S(1)} %iota_compare_fusion, bf16[6,64,2,128]{3,2,1,0:T(2,128)(2,1)} %reshape.108, bf16[6,64,2,128]{3,2,1,0:T(2,128)(2,1)S(1)} %reshape.106), kind=kOutput, calls=%fused_computation.29 | convolution fusion | flops 12730368 | bytes 495616 | tf_op jit(solution)/shard_map/cthe,cshe->chts/dot_general | solution.py:179
  96.8 2.2 %convolution_bitcast_fusion.1 = f32[6,2,128,128]{2,3,1,0:T(8,128)} fusion(bf16[6,64,2,128]{3,2,1,0:T(2,128)(2,1)} %reshape.108, bf16[6,64,2,128]{3,2,1,0:T(2,128)(2,1)} %reshape.104), kind=kOutput, calls=%fused_computation.6 | convolution fusion | flops 25165824 | bytes 1179648 | tf_op jit(solution)/shard_map/cthd,cthe->chde/dot_general | solution.py:124
  99.1 2.6 %bitcast_add_fusion = f32[4,8,64,256]{3,2,1,0:T(8,128)S(1)} fusion(f32[4,8,64,256]{3,2,1,0:T(8,128)} %collective-permute-done.6, f32[4,8,2,64,256]{4,3,2,1,0:T(8,128)} %bitcast.119, s32[]{:T(128)S(6)} %select_n.213), kind=kLoop, calls=%fused_computation.3 | loop fusion | flops 524288 | bytes 6291460 | tf_op jit(solution)/shard_map/add | solution.py:72
  102.5 1.4 slice.88
  104.6 1.7 copy.58
  106.2 2.7 %maximum_select_fusion = f32[4,8,64,256]{3,2,1,0:T(8,128)S(1)} fusion(f32[4,8,64,256]{3,2,1,0:T(8,128)} %copy-done.6, f32[4,1,64,256]{3,2,1,0:T(8,128)} %slice.89, f32[4,7,64,256]{3,2,1,0:T(8,128)} %slice.88, pred[]{:T(512)S(6)} %eq.38), kind=kLoop, calls=%fused_computation.2 | loop fusion | flops 1048576 | bytes 6291457 | tf_op jit(solution)/shard_map/jit(_where)/select_n | solution.py:74
  109.0 2.1 %collective-permute-start.7 = (bf16[4,4,64,256]{3,2,1,0:T(8,128)(2,1)S(1)}, bf16[4,4,64,256]{3,2,1,0:T(8,128)(2,1)S(1)}, u32[]{:S(2)}, u32[]{:S(2)}) collective-permute-start(bf16[4,4,64,256]{3,2,1,0:T(8,128)(2,1)S(1)} %fusion.19), channel_id=1, source_target_pairs={{0,24},{12,180},{24,0},{36,60},{48,72},{60,36},{72,48},{84,108},{9... | collective-permute-start | bytes 1572872 | tf_op jit(solution)/shard_map/ppermute | solution.py:58
  114.0 6.2 %collective-permute-done.7 = bf16[4,4,64,256]{3,2,1,0:T(8,128)(2,1)S(1)} collective-permute-done((bf16[4,4,64,256]{3,2,1,0:T(8,128)(2,1)S(1)}, bf16[4,4,64,256]{3,2,1,0:T(8,128)(2,1)S(1)}, u32[]{:S(2)}, u32[]{:S(2)}) %collective-permute-start.7) | collective-permute-done | bytes 524320 | tf_op jit(solution)/shard_map/ppermute | solution.py:58
  120.5 3.5 %collective-permute-start.10 = (bf16[4,64,256]{2,1,0:T(8,128)(2,1)S(1)}, bf16[4,64,256]{2,1,0:T(8,128)(2,1)S(1)}, u32[]{:S(2)}, u32[]{:S(2)}) collective-permute-start(bf16[4,64,256]{2,1,0:T(8,128)(2,1)S(1)} %get-tuple-element.20), channel_id=1, source_target_pairs={{0,576},{12,588},{24,600},{36,612},{48,624},{60,636},{72,648},{84,... | collective-permute-start | bytes 393224 | tf_op jit(solution)/shard_map/ppermute | solution.py:58
  123.9 4.7 %collective-permute-start.9 = (bf16[4,64,256]{2,1,0:T(8,128)(2,1)S(1)}, bf16[4,64,256]{2,1,0:T(8,128)(2,1)S(1)}, u32[]{:S(2)}, u32[]{:S(2)}) collective-permute-start(bf16[4,64,256]{2,1,0:T(8,128)(2,1)S(1)} %get-tuple-element.21), channel_id=1, source_target_pairs={{0,384},{12,396},{24,408},{36,420},{48,432},{60,444},{72,456},{84,... | collective-permute-start | bytes 393224 | tf_op jit(solution)/shard_map/ppermute | solution.py:58
  128.7 2.5 %collective-permute-start.8 = (bf16[4,64,256]{2,1,0:T(8,128)(2,1)S(1)}, bf16[4,64,256]{2,1,0:T(8,128)(2,1)S(1)}, u32[]{:S(2)}, u32[]{:S(2)}) collective-permute-start(bf16[4,64,256]{2,1,0:T(8,128)(2,1)S(1)} %get-tuple-element.19), channel_id=1, source_target_pairs={{0,192},{12,204},{24,216},{36,228},{48,240},{60,252},{72,264},{84,... | collective-permute-start | bytes 393224 | tf_op jit(solution)/shard_map/ppermute | solution.py:58
  131.5 1.4 collective-permute-done.9
  133.0 2.6 %collective-permute-done.8 = bf16[4,64,256]{2,1,0:T(8,128)(2,1)S(1)} collective-permute-done((bf16[4,64,256]{2,1,0:T(8,128)(2,1)S(1)}, bf16[4,64,256]{2,1,0:T(8,128)(2,1)S(1)}, u32[]{:S(2)}, u32[]{:S(2)}) %collective-permute-start.8) | collective-permute-done | bytes 131104 | tf_op jit(solution)/shard_map/ppermute | solution.py:58
  135.7 1.9 %collective-permute-start.13 = (bf16[64,256]{1,0:T(8,128)(2,1)S(1)}, bf16[64,256]{1,0:T(8,128)(2,1)S(1)}, u32[]{:S(2)}, u32[]{:S(2)}) collective-permute-start(bf16[64,256]{1,0:T(8,128)(2,1)S(1)} %get-tuple-element.23), channel_id=1, source_target_pairs={{0,144},{12,156},{24,168},{36,180},{48,0},{60,12},{72,24},{84,36},... | collective-permute-start | bytes 98312 | tf_op jit(solution)/shard_map/ppermute | solution.py:58
  137.6 5.3 %collective-permute-start.12 = (bf16[64,256]{1,0:T(8,128)(2,1)S(1)}, bf16[64,256]{1,0:T(8,128)(2,1)S(1)}, u32[]{:S(2)}, u32[]{:S(2)}) collective-permute-start(bf16[64,256]{1,0:T(8,128)(2,1)S(1)} %get-tuple-element.24), channel_id=1, source_target_pairs={{0,96},{12,108},{24,120},{36,132},{48,144},{60,156},{72,168},{84,1... | collective-permute-start | bytes 98312 | tf_op jit(solution)/shard_map/ppermute | solution.py:58
  142.9 4.8 %collective-permute-start.11 = (bf16[64,256]{1,0:T(8,128)(2,1)S(1)}, bf16[64,256]{1,0:T(8,128)(2,1)S(1)}, u32[]{:S(2)}, u32[]{:S(2)}) collective-permute-start(bf16[64,256]{1,0:T(8,128)(2,1)S(1)} %get-tuple-element.22), channel_id=1, source_target_pairs={{0,48},{12,60},{24,72},{36,84},{48,96},{60,108},{72,120},{84,132},... | collective-permute-start | bytes 98312 | tf_op jit(solution)/shard_map/ppermute | solution.py:58
  151.8 6.8 %reduce-scatter.2.cloned.1.call-done = bf16[32,4096]{1,0:T(8,128)(2,1)} async-done(((bf16[384,4096]{1,0:T(8,128)(2,1)}), bf16[32,4096]{1,0:T(8,128)(2,1)}) %reduce-scatter.2.cloned.1.call-update) | async-done | bytes 262160 | tf_op jit(solution)/shard_map/reduce_scatter | solution.py:169
  (113 shorter events, 14.0 us)
Async XLA Ops:
  7.2 2.5 %copy-start = (bf16[384,4096]{1,0:T(8,128)(2,1)S(1)}, bf16[384,4096]{1,0:T(8,128)(2,1)}, u32[]{:S(2)}) copy-start(bf16[384,4096]{1,0:T(8,128)(2,1)} %param.9) | copy-start | bytes 9437188
  7.2 151.4 %reduce-scatter.2.cloned.1.call-start = ((), (), s32[]{:S(2)}) async-start(), calls=%async_computation.1 | async-start | bytes 3407872 | tf_op jit(solution)/shard_map/reduce_scatter | solution.py:169
  9.7 2.6 %copy-start.19 = (bf16[384,256]{1,0:T(8,128)(2,1)S(1)}, bf16[384,256]{1,0:T(8,128)(2,1)}, u32[]{:S(2)}) copy-start(bf16[384,256]{1,0:T(8,128)(2,1)} %param.5) | copy-start | bytes 589828
  12.3 12.1 %copy-start.20 = (bf16[384,256]{1,0:T(8,128)(2,1)}, bf16[384,256]{1,0:T(8,128)(2,1)S(1)}, u32[]{:S(2)}) copy-start(bf16[384,256]{1,0:T(8,128)(2,1)S(1)} %convolution_convert_fusion.1) | copy-start | bytes 589828
  12.3 16.6 %copy-start.18 = (bf16[384,256]{1,0:T(8,128)(2,1)S(1)}, bf16[384,256]{1,0:T(8,128)(2,1)}, u32[]{:S(2)}) copy-start(bf16[384,256]{1,0:T(8,128)(2,1)} %param.7) | copy-start | bytes 589828
  12.6 3.6 %copy-start.24 = (f32[1,128,128]{2,1,0:T(8,128)}, f32[1,128,128]{2,1,0:T(8,128)S(1)}, u32[]{:S(2)}) copy-start(f32[1,128,128]{2,1,0:T(8,128)S(1)} %convolution_bitcast_fusion.5) | copy-start | bytes 196612
  12.8 3.3 %copy-start.26 = (f32[1,128,128]{2,1,0:T(8,128)}, f32[1,128,128]{2,1,0:T(8,128)S(1)}, u32[]{:S(2)}) copy-start(f32[1,128,128]{2,1,0:T(8,128)S(1)} %convolution_bitcast_fusion.6) | copy-start | bytes 196612
  12.9 3.2 %collective-permute-start = (bf16[2,2,128,128]{3,2,1,0:T(8,128)(2,1)S(1)}, bf16[2,2,128,128]{3,2,1,0:T(8,128)(2,1)S(1)}, u32[]{:S(2)}, u32[]{:S(2)}) collective-permute-start(bf16[2,2,128,128]{3,2,1,0:T(8,128)(2,1)S(1)} %fusion.31), channel_id=1, source_target_pairs={{0,12},{12,0},{24,36},{36,24},{48,60},{60,48},{72,84},{84,72},{96,... | collective-permute-start | bytes 393224 | tf_op jit(solution)/shard_map/ppermute | solution.py:18
  16.1 8.3 %copy-start.15 = (bf16[2,2,128,128]{3,2,1,0:T(8,128)(2,1)}, bf16[2,2,128,128]{3,2,1,0:T(8,128)(2,1)S(1)}, u32[]{:S(2)}) copy-start(bf16[2,2,128,128]{3,2,1,0:T(8,128)(2,1)S(1)} %collective-permute-done) | copy-start | bytes 393220
  16.2 7.4 %collective-permute-start.1 = (bf16[2,2,128,128]{3,2,1,0:T(8,128)(2,1)S(1)}, bf16[2,2,128,128]{3,2,1,0:T(8,128)(2,1)S(1)}, u32[]{:S(2)}, u32[]{:S(2)}) collective-permute-start(bf16[2,2,128,128]{3,2,1,0:T(8,128)(2,1)S(1)} %fusion.81), channel_id=1, source_target_pairs={{0,24},{24,0},{12,36},{36,12},{48,72},{72,48},{60,84},{84,60},{96,... | collective-permute-start | bytes 393224 | tf_op jit(solution)/shard_map/ppermute | solution.py:18
  23.6 0.8 copy-start.28
  24.5 10.6 %collective-permute-start.2 = (bf16[2,2,128,128]{3,2,1,0:T(8,128)(2,1)}, bf16[2,2,128,128]{3,2,1,0:T(8,128)(2,1)}, u32[]{:S(2)}, u32[]{:S(2)}) collective-permute-start(bf16[2,2,128,128]{3,2,1,0:T(8,128)(2,1)} %get-tuple-element.15), channel_id=1, source_target_pairs={{0,48},{48,0},{12,60},{60,12},{24,72},{72,24},{36,84},{84,36},{96,... | collective-permute-start | bytes 393224 | tf_op jit(solution)/shard_map/ppermute | solution.py:18
  36.1 14.1 %collective-permute-start.3 = (bf16[2,2,128,128]{3,2,1,0:T(8,128)(2,1)S(1)}, bf16[2,2,128,128]{3,2,1,0:T(8,128)(2,1)S(1)}, u32[]{:S(2)}, u32[]{:S(2)}) collective-permute-start(bf16[2,2,128,128]{3,2,1,0:T(8,128)(2,1)S(1)} %fusion.86), channel_id=1, source_target_pairs={{0,96},{96,0},{12,108},{108,12},{24,120},{120,24},{36,132},{132,36... | collective-permute-start | bytes 393224 | tf_op jit(solution)/shard_map/ppermute | solution.py:18
  44.2 11.1 %copy-start.1 = (f32[6,2,128,128]{3,2,1,0:T(8,128)}, f32[6,2,128,128]{3,2,1,0:T(8,128)S(1)}, u32[]{:S(2)}) copy-start(f32[6,2,128,128]{3,2,1,0:T(8,128)S(1)} %fusion.58) | copy-start | bytes 2359300
  50.2 0.6 copy-start.16
  52.5 7.2 %collective-permute-start.4 = (bf16[2,2,128,128]{3,2,1,0:T(8,128)(2,1)}, bf16[2,2,128,128]{3,2,1,0:T(8,128)(2,1)}, u32[]{:S(2)}, u32[]{:S(2)}) collective-permute-start(bf16[2,2,128,128]{3,2,1,0:T(8,128)(2,1)} %fusion.85), channel_id=1, source_target_pairs={{0,192},{192,0},{12,204},{204,12},{24,216},{216,24},{36,228},{228,... | collective-permute-start | bytes 393224 | tf_op jit(solution)/shard_map/ppermute | solution.py:18
  57.9 13.2 %copy-start.29 = (bf16[2,2,128,128]{3,2,1,0:T(8,128)(2,1)S(1)}, bf16[2,2,128,128]{3,2,1,0:T(8,128)(2,1)}, u32[]{:S(2)}) copy-start(bf16[2,2,128,128]{3,2,1,0:T(8,128)(2,1)} %copy-done.28) | copy-start | bytes 393220
  57.9 14.2 %copy-start.17 = (bf16[2,2,128,128]{3,2,1,0:T(8,128)(2,1)S(1)}, bf16[2,2,128,128]{3,2,1,0:T(8,128)(2,1)}, u32[]{:S(2)}) copy-start(bf16[2,2,128,128]{3,2,1,0:T(8,128)(2,1)} %copy-done.16) | copy-start | bytes 393220
  60.9 12.2 %collective-permute-start.5 = (bf16[2,2,128,128]{3,2,1,0:T(8,128)(2,1)S(1)}, bf16[2,2,128,128]{3,2,1,0:T(8,128)(2,1)S(1)}, u32[]{:S(2)}, u32[]{:S(2)}) collective-permute-start(bf16[2,2,128,128]{3,2,1,0:T(8,128)(2,1)S(1)} %add_convert_fusion), channel_id=1, source_target_pairs={{0,384},{384,0},{12,396},{396,12},{24,408},{408,24},{36,420},{420,... | collective-permute-start | bytes 393224 | tf_op jit(solution)/shard_map/ppermute | solution.py:18
  70.0 4.3 %copy-start.21 = (bf16[6,2,64,64]{3,2,1,0:T(8,128)(2,1)}, bf16[6,2,64,64]{3,2,1,0:T(8,128)(2,1)S(1)}, u32[]{:S(2)}) copy-start(bf16[6,2,64,64]{3,2,1,0:T(8,128)(2,1)S(1)} %fusion.13) | copy-start | bytes 294916
  70.0 3.8 %copy-start.2 = (f32[6,2,128,128]{3,2,1,0:T(8,128)S(1)}, f32[6,2,128,128]{3,2,1,0:T(8,128)}, u32[]{:S(2)}) copy-start(f32[6,2,128,128]{3,2,1,0:T(8,128)} %copy-done.1) | copy-start | bytes 2359300
  70.0 3.8 %copy-start.4 = (f32[6,2,128,128]{3,2,1,0:T(8,128)S(1)}, f32[6,2,128,128]{3,2,1,0:T(8,128)}, u32[]{:S(2)}) copy-start(f32[6,2,128,128]{3,2,1,0:T(8,128)} %fusion.94) | copy-start | bytes 2359300
  70.1 3.8 %copy-start.7 = (bf16[6,64,2,128]{3,2,1,0:T(2,128)(2,1)S(1)}, bf16[6,64,2,128]{3,2,1,0:T(2,128)(2,1)}, u32[]{:S(2)}) copy-start(bf16[6,64,2,128]{3,2,1,0:T(2,128)(2,1)} %reshape.104) | copy-start | bytes 589828
  73.8 0.7 copy-start.10
  74.1 1.6 copy-start.14
  74.9 0.7 copy-start.13
  91.4 7.7 %collective-permute-start.6 = (f32[4,8,64,256]{3,2,1,0:T(8,128)}, f32[4,8,64,256]{3,2,1,0:T(8,128)}, u32[]{:S(2)}, u32[]{:S(2)}) collective-permute-start(f32[4,8,64,256]{3,2,1,0:T(8,128)} %dynamic-slice_bitcast_fusion), channel_id=1, source_target_pairs={{0,12},{12,0},{24,36},{36,24},{48,60},{60,48},{72,84},{84,72},{96,... | collective-permute-start | bytes 6291464 | tf_op jit(solution)/shard_map/ppermute | solution.py:72
  101.7 2.2 %copy-start.6 = (f32[4,8,64,256]{3,2,1,0:T(8,128)}, f32[4,8,64,256]{3,2,1,0:T(8,128)S(1)}, u32[]{:S(2)}) copy-start(f32[4,8,64,256]{3,2,1,0:T(8,128)S(1)} %bitcast_add_fusion) | copy-start | bytes 6291460
  101.7 2.2 %copy-start.25 = (f32[1,128,128]{2,1,0:T(8,128)S(1)}, f32[1,128,128]{2,1,0:T(8,128)}, u32[]{:S(2)}) copy-start(f32[1,128,128]{2,1,0:T(8,128)} %copy-done.24) | copy-start | bytes 196612
  101.7 2.2 %copy-start.27 = (f32[1,128,128]{2,1,0:T(8,128)S(1)}, f32[1,128,128]{2,1,0:T(8,128)}, u32[]{:S(2)}) copy-start(f32[1,128,128]{2,1,0:T(8,128)} %copy-done.26) | copy-start | bytes 196612
  101.7 2.2 %copy-start.30 = (f32[2,128,128]{2,1,0:T(8,128)S(1)}, f32[2,128,128]{2,1,0:T(8,128)}, u32[]{:S(2)}) copy-start(f32[2,128,128]{2,1,0:T(8,128)} %get-tuple-element.13) | copy-start | bytes 393220
  106.2 4.9 %copy-start.3 = (f32[6,2,128,128]{3,2,1,0:T(8,128)S(1)}, f32[6,2,128,128]{3,2,1,0:T(8,128)}, u32[]{:S(2)}) copy-start(f32[6,2,128,128]{3,2,1,0:T(8,128)} %copy-done.1) | copy-start | bytes 2359300
  106.2 4.9 %copy-start.5 = (f32[6,2,128,128]{3,2,1,0:T(8,128)S(1)}, f32[6,2,128,128]{3,2,1,0:T(8,128)}, u32[]{:S(2)}) copy-start(f32[6,2,128,128]{3,2,1,0:T(8,128)} %fusion.94) | copy-start | bytes 2359300
  106.2 4.9 %copy-start.9 = (bf16[6,64,2,128]{3,2,1,0:T(2,128)(2,1)S(1)}, bf16[6,64,2,128]{3,2,1,0:T(2,128)(2,1)}, u32[]{:S(2)}) copy-start(bf16[6,64,2,128]{3,2,1,0:T(2,128)(2,1)} %reshape.108) | copy-start | bytes 589828
  106.2 4.9 %copy-start.11 = (f32[2,128,128]{2,1,0:T(8,128)S(1)}, f32[2,128,128]{2,1,0:T(8,128)}, u32[]{:S(2)}) copy-start(f32[2,128,128]{2,1,0:T(8,128)} %copy-done.10) | copy-start | bytes 393220
  109.0 2.9 %copy-start.23 = (bf16[6,2,64,64]{3,2,1,0:T(8,128)(2,1)S(1)}, bf16[6,2,64,64]{3,2,1,0:T(8,128)(2,1)}, u32[]{:S(2)}) copy-start(bf16[6,2,64,64]{3,2,1,0:T(8,128)(2,1)} %fusion.12) | copy-start | bytes 294916
  109.0 11.2 %collective-permute-start.7 = (bf16[4,4,64,256]{3,2,1,0:T(8,128)(2,1)S(1)}, bf16[4,4,64,256]{3,2,1,0:T(8,128)(2,1)S(1)}, u32[]{:S(2)}, u32[]{:S(2)}) collective-permute-start(bf16[4,4,64,256]{3,2,1,0:T(8,128)(2,1)S(1)} %fusion.19), channel_id=1, source_target_pairs={{0,24},{12,180},{24,0},{36,60},{48,72},{60,36},{72,48},{84,108},{9... | collective-permute-start | bytes 1572872 | tf_op jit(solution)/shard_map/ppermute | solution.py:58
  111.5 1.1 copy-start.12
  111.5 1.1 copy-start.31
  114.0 17.3 %copy-start.8 = (bf16[6,64,2,128]{3,2,1,0:T(2,128)(2,1)S(1)}, bf16[6,64,2,128]{3,2,1,0:T(2,128)(2,1)}, u32[]{:S(2)}) copy-start(bf16[6,64,2,128]{3,2,1,0:T(2,128)(2,1)} %reshape.104) | copy-start | bytes 589828
  120.4 27.3 %copy-start.22 = (bf16[6,2,64,64]{3,2,1,0:T(8,128)(2,1)S(1)}, bf16[6,2,64,64]{3,2,1,0:T(8,128)(2,1)}, u32[]{:S(2)}) copy-start(bf16[6,2,64,64]{3,2,1,0:T(8,128)(2,1)} %copy-done.21) | copy-start | bytes 294916
  120.5 11.0 %collective-permute-start.10 = (bf16[4,64,256]{2,1,0:T(8,128)(2,1)S(1)}, bf16[4,64,256]{2,1,0:T(8,128)(2,1)S(1)}, u32[]{:S(2)}, u32[]{:S(2)}) collective-permute-start(bf16[4,64,256]{2,1,0:T(8,128)(2,1)S(1)} %get-tuple-element.20), channel_id=1, source_target_pairs={{0,576},{12,588},{24,600},{36,612},{48,624},{60,636},{72,648},{84,... | collective-permute-start | bytes 393224 | tf_op jit(solution)/shard_map/ppermute | solution.py:58
  123.9 9.0 %collective-permute-start.9 = (bf16[4,64,256]{2,1,0:T(8,128)(2,1)S(1)}, bf16[4,64,256]{2,1,0:T(8,128)(2,1)S(1)}, u32[]{:S(2)}, u32[]{:S(2)}) collective-permute-start(bf16[4,64,256]{2,1,0:T(8,128)(2,1)S(1)} %get-tuple-element.21), channel_id=1, source_target_pairs={{0,384},{12,396},{24,408},{36,420},{48,432},{60,444},{72,456},{84,... | collective-permute-start | bytes 393224 | tf_op jit(solution)/shard_map/ppermute | solution.py:58
  128.7 6.9 %collective-permute-start.8 = (bf16[4,64,256]{2,1,0:T(8,128)(2,1)S(1)}, bf16[4,64,256]{2,1,0:T(8,128)(2,1)S(1)}, u32[]{:S(2)}, u32[]{:S(2)}) collective-permute-start(bf16[4,64,256]{2,1,0:T(8,128)(2,1)S(1)} %get-tuple-element.19), channel_id=1, source_target_pairs={{0,192},{12,204},{24,216},{36,228},{48,240},{60,252},{72,264},{84,... | collective-permute-start | bytes 393224 | tf_op jit(solution)/shard_map/ppermute | solution.py:58
  135.7 15.0 %collective-permute-start.13 = (bf16[64,256]{1,0:T(8,128)(2,1)S(1)}, bf16[64,256]{1,0:T(8,128)(2,1)S(1)}, u32[]{:S(2)}, u32[]{:S(2)}) collective-permute-start(bf16[64,256]{1,0:T(8,128)(2,1)S(1)} %get-tuple-element.23), channel_id=1, source_target_pairs={{0,144},{12,156},{24,168},{36,180},{48,0},{60,12},{72,24},{84,36},... | collective-permute-start | bytes 98312 | tf_op jit(solution)/shard_map/ppermute | solution.py:58
  137.6 13.1 %collective-permute-start.12 = (bf16[64,256]{1,0:T(8,128)(2,1)S(1)}, bf16[64,256]{1,0:T(8,128)(2,1)S(1)}, u32[]{:S(2)}, u32[]{:S(2)}) collective-permute-start(bf16[64,256]{1,0:T(8,128)(2,1)S(1)} %get-tuple-element.24), channel_id=1, source_target_pairs={{0,96},{12,108},{24,120},{36,132},{48,144},{60,156},{72,168},{84,1... | collective-permute-start | bytes 98312 | tf_op jit(solution)/shard_map/ppermute | solution.py:58
  142.9 8.3 %collective-permute-start.11 = (bf16[64,256]{1,0:T(8,128)(2,1)S(1)}, bf16[64,256]{1,0:T(8,128)(2,1)S(1)}, u32[]{:S(2)}, u32[]{:S(2)}) collective-permute-start(bf16[64,256]{1,0:T(8,128)(2,1)S(1)} %get-tuple-element.22), channel_id=1, source_target_pairs={{0,48},{12,60},{24,72},{36,84},{48,96},{60,108},{72,120},{84,132},... | collective-permute-start | bytes 98312 | tf_op jit(solution)/shard_map/ppermute | solution.py:58
Sparse Core Ops, SparseCore 0:
  93.5 65.1 reduce-scatter.1

commit v11 on v5

--- a/solution.py
+++ b/solution.py
@@ -67,11 +67,10 @@
     x = position // (2 * y_count)
     index = lambda a, b, c: a * 2 * y_count + b % y_count * 2 + c
     acc = partial.reshape(x_count, y_count, 2, partial.shape[0] // count, cols)
-    kept = lax.dynamic_index_in_dim(acc, core, 2, keepdims=False)
-    sent = lax.dynamic_index_in_dim(acc, 1 - core, 2, keepdims=False)
+    kept = jnp.roll(lax.dynamic_index_in_dim(acc, core, 2, keepdims=False), -core, axis=1)
+    sent = jnp.roll(lax.dynamic_index_in_dim(acc, 1 - core, 2, keepdims=False), core - 1, axis=1)
     acc = kept + lax.ppermute(sent, SEQ, [(i, i ^ 1) for i in range(count)])
     acc, ride = lax.optimization_barrier((acc, ride))
-    acc = jnp.where(core == 1, jnp.roll(acc, -1, axis=1), acc)
     acc = acc.reshape(x_count, y_count // 2, 2, acc.shape[2], cols)
     label = (y - core) % y_count
     odd = label % 2

time: 162 us -> 163 us (level)
  other arithmetic: 13.9 us -> 15.6 us
    concatenate x0 -> x1, other arithmetic: none -> 1.74 us  [grid_scatter(): jnp.roll(lax.dynamic_index_in_dim(acc, 1 - core, 2, keepdims=False), core...]
  transfers between devices with their start and end apart: 15 -> 15, of which waited for: 8 -> 8; matrix products, arithmetic and copies ran while one was open for 25% -> 26% of each run, Pallas kernels for 0% -> 0%
where the time goes in v11:
time: 163 us; the launch traced here: 161 us
  starting transfers between devices  55.5 us (34%)
  waiting for transfers between devices  32.4 us (20%)
  local copies, waits for them, and re-layouts  21.6 us (13%)
  matrix products  21.3 us (13%)
  other arithmetic  15.6 us (10%)
  between operations  15.1 us (9%)
    ppermute x6, starting transfers between devices, swapped(): return lax.ppermute(block, SEQ, route)  28.5 us
    ppermute x7, starting transfers between devices, wire(): lax.ppermute(block.astype(jnp.bfloat16), SEQ, route).astype(jnp.float32)  25.1 us
    ppermute x6, waiting for transfers between devices, swapped(): return lax.ppermute(block, SEQ, route)  17.9 us
    ppermute x7, waiting for transfers between devices, wire(): lax.ppermute(block.astype(jnp.bfloat16), SEQ, route).astype(jnp.float32)  14.5 us
    dot_general x1, local copies, waits for them, and re-layouts, local(): lax.dot_general(out_grad, attention, (((0,), (0,)), ((), ())), preferred_...  5.6 us
    unnamed x76, local copies, waits for them, and re-layouts  4.82 us
    dot_general x1, matrix products, local(): lax.dot_general(out_grad, attention, (((0,), (0,)), ((), ())), preferred_...  4.22 us
    squeeze x1, local copies, waits for them, and re-layouts, grid_scatter(): lax.dynamic_index_in_dim(acc, core, 2, keepdims=False)  3.99 us
  transfers between devices with their start and end apart: 15, of which 8 were waited for; matrix products, arithmetic and copies ran while one was open for 26% of the time, Pallas kernels for 0%

profile of v11, /device:TPU:6, one launch (start us, length us, event | category | flops | bytes accessed | tf_op | source)
XLA Modules:
  0.0 161.5 jit_solution(5158519927279185861)
XLA Ops:
  7.2 1.3 convolution_bitcast_fusion.5
  8.5 1.1 convolution_bitcast_fusion.6
  9.7 2.6 %convolution_convert_fusion.1 = bf16[384,256]{1,0:T(8,128)(2,1)S(1)} fusion(bf16[384,4096]{1,0:T(8,128)(2,1)S(1)} %copy-done, bf16[4096,256]{1,0:T(8,128)(2,1)} %param.10), kind=kOutput, calls=%fused_computation.43 | convolution fusion | flops 805404672 | bytes 5439488 | tf_op jit(solution)/shard_map/dot_general | solution.py:116
  13.1 1.9 %collective-permute-start = (bf16[2,2,128,128]{3,2,1,0:T(8,128)(2,1)S(1)}, bf16[2,2,128,128]{3,2,1,0:T(8,128)(2,1)S(1)}, u32[]{:S(2)}, u32[]{:S(2)}) collective-permute-start(bf16[2,2,128,128]{3,2,1,0:T(8,128)(2,1)S(1)} %fusion.27), channel_id=1, source_target_pairs={{0,12},{12,0},{24,36},{36,24},{48,60},{60,48},{72,84},{84,72},{96,... | collective-permute-start | bytes 393224 | tf_op jit(solution)/shard_map/ppermute | solution.py:18
  15.0 1.3 collective-permute-done
  16.3 3.5 %collective-permute-start.1 = (bf16[2,2,128,128]{3,2,1,0:T(8,128)(2,1)S(1)}, bf16[2,2,128,128]{3,2,1,0:T(8,128)(2,1)S(1)}, u32[]{:S(2)}, u32[]{:S(2)}) collective-permute-start(bf16[2,2,128,128]{3,2,1,0:T(8,128)(2,1)S(1)} %fusion.80), channel_id=1, source_target_pairs={{0,24},{24,0},{12,36},{36,12},{48,72},{72,48},{60,84},{84,60},{96,... | collective-permute-start | bytes 393224 | tf_op jit(solution)/shard_map/ppermute | solution.py:18
  19.9 3.9 %collective-permute-done.1 = bf16[2,2,128,128]{3,2,1,0:T(8,128)(2,1)S(1)} collective-permute-done((bf16[2,2,128,128]{3,2,1,0:T(8,128)(2,1)S(1)}, bf16[2,2,128,128]{3,2,1,0:T(8,128)(2,1)S(1)}, u32[]{:S(2)}, u32[]{:S(2)}) %collective-permute-start.1) | collective-permute-done | bytes 131104 | tf_op jit(solution)/shard_map/ppermute | solution.py:18
  23.9 4.5 %collective-permute-start.2 = (bf16[2,2,128,128]{3,2,1,0:T(8,128)(2,1)S(1)}, bf16[2,2,128,128]{3,2,1,0:T(8,128)(2,1)S(1)}, u32[]{:S(2)}, u32[]{:S(2)}) collective-permute-start(bf16[2,2,128,128]{3,2,1,0:T(8,128)(2,1)S(1)} %get-tuple-element.24), channel_id=1, source_target_pairs={{0,48},{48,0},{12,60},{60,12},{24,72},{72,24},{36,84},{84,36},{96,... | collective-permute-start | bytes 393224 | tf_op jit(solution)/shard_map/ppermute | solution.py:18
  28.4 5.8 %collective-permute-done.2 = bf16[2,2,128,128]{3,2,1,0:T(8,128)(2,1)S(1)} collective-permute-done((bf16[2,2,128,128]{3,2,1,0:T(8,128)(2,1)S(1)}, bf16[2,2,128,128]{3,2,1,0:T(8,128)(2,1)S(1)}, u32[]{:S(2)}, u32[]{:S(2)}) %collective-permute-start.2) | collective-permute-done | bytes 131104 | tf_op jit(solution)/shard_map/ppermute | solution.py:18
  34.9 7.7 %collective-permute-start.3 = (bf16[2,2,128,128]{3,2,1,0:T(8,128)(2,1)}, bf16[2,2,128,128]{3,2,1,0:T(8,128)(2,1)}, u32[]{:S(2)}, u32[]{:S(2)}) collective-permute-start(bf16[2,2,128,128]{3,2,1,0:T(8,128)(2,1)} %fusion.85), channel_id=1, source_target_pairs={{0,96},{96,0},{12,108},{108,12},{24,120},{120,24},{36,132},{132,36... | collective-permute-start | bytes 393224 | tf_op jit(solution)/shard_map/ppermute | solution.py:18
  42.6 1.0 reshape.65
  43.6 1.0 reshape.66
  44.6 4.6 %collective-permute-done.3 = bf16[2,2,128,128]{3,2,1,0:T(8,128)(2,1)} collective-permute-done((bf16[2,2,128,128]{3,2,1,0:T(8,128)(2,1)}, bf16[2,2,128,128]{3,2,1,0:T(8,128)(2,1)}, u32[]{:S(2)}, u32[]{:S(2)}) %collective-permute-start.3) | collective-permute-done | bytes 131104 | tf_op jit(solution)/shard_map/ppermute | solution.py:18
  49.3 1.7 %fusion.84 = bf16[2,2,128,128]{3,2,1,0:T(8,128)(2,1)} fusion(bf16[2,2,128,128]{3,2,1,0:T(8,128)(2,1)} %collective-permute-done.3, f32[2,2,128,128]{3,2,1,0:T(8,128)} %copy-done.6, bf16[2,2,128,128]{3,2,1,0:T(8,128)(2,1)} %copy-done.12), kind=kLoop, calls=%fused_computation.141 | loop fusion | flops 327680 | bytes 655360 | tf_op jit(solution)/shard_map/convert_element_type | solution.py:146
  51.0 2.7 %collective-permute-start.4 = (bf16[2,2,128,128]{3,2,1,0:T(8,128)(2,1)}, bf16[2,2,128,128]{3,2,1,0:T(8,128)(2,1)}, u32[]{:S(2)}, u32[]{:S(2)}) collective-permute-start(bf16[2,2,128,128]{3,2,1,0:T(8,128)(2,1)} %fusion.84), channel_id=1, source_target_pairs={{0,192},{192,0},{12,204},{204,12},{24,216},{216,24},{36,228},{228,... | collective-permute-start | bytes 393224 | tf_op jit(solution)/shard_map/ppermute | solution.py:18
  53.7 1.2 fusion.54
  55.0 1.0 reshape.64
  56.0 2.2 %collective-permute-done.4 = bf16[2,2,128,128]{3,2,1,0:T(8,128)(2,1)} collective-permute-done((bf16[2,2,128,128]{3,2,1,0:T(8,128)(2,1)}, bf16[2,2,128,128]{3,2,1,0:T(8,128)(2,1)}, u32[]{:S(2)}, u32[]{:S(2)}) %collective-permute-start.4) | collective-permute-done | bytes 131104 | tf_op jit(solution)/shard_map/ppermute | solution.py:18
  58.2 1.2 add_convert_fusion
  59.4 8.1 %collective-permute-start.5 = (bf16[2,2,128,128]{3,2,1,0:T(8,128)(2,1)S(1)}, bf16[2,2,128,128]{3,2,1,0:T(8,128)(2,1)S(1)}, u32[]{:S(2)}, u32[]{:S(2)}) collective-permute-start(bf16[2,2,128,128]{3,2,1,0:T(8,128)(2,1)S(1)} %add_convert_fusion), channel_id=1, source_target_pairs={{0,384},{384,0},{12,396},{396,12},{24,408},{408,24},{36,420},{420,... | collective-permute-start | bytes 393224 | tf_op jit(solution)/shard_map/ppermute | solution.py:18
  67.8 1.0 convert_element_type.147
  68.9 1.1 convert_element_type.153
  69.9 1.0 convert_element_type.155
  73.8 0.7 copy.133
  74.6 2.6 %convolution_convert_fusion = bf16[384,4096]{1,0:T(8,128)(2,1)} fusion(bf16[4096,256]{1,0:T(8,128)(2,1)S(1)} %copy-done.11, bf16[48,8,2,128]{3,2,1,0:T(2,128)(2,1)S(1)} %bitcast.132), kind=kOutput, calls=%fused_computation | convolution fusion | flops 806879232 | bytes 5439488 | tf_op jit(solution)/shard_map/dot_general | solution.py:164
  77.2 4.2 %convolution_bitcast_fusion = f32[4096,256]{0,1:T(8,128)} fusion(bf16[384,256]{1,0:T(8,128)(2,1)} %bitcast.136, bf16[384,4096]{1,0:T(8,128)(2,1)S(1)} %copy-done), kind=kOutput, calls=%fused_computation.1 | convolution fusion | flops 805306368 | bytes 7536640 | tf_op jit(solution)/shard_map/dot_general | solution.py:169
  81.4 5.6 %copy.52 = f32[4096,256]{1,0:T(8,128)} copy(f32[4096,256]{0,1:T(8,128)} %convolution_bitcast_fusion) | data formatting | bytes 8388608 | tf_op jit(solution)/shard_map/dot_general | solution.py:169
  87.0 4.0 %dynamic-slice_bitcast_fusion.1 = (f32[4,8,64,256]{3,2,1,0:T(8,128)}, f32[4,8,64,256]{3,2,1,0:T(8,128)S(1)}) fusion(f32[4,8,2,64,256]{4,3,2,1,0:T(8,128)} %bitcast.128, s32[]{:T(128)S(6)} %select_n.200, s32[]{:T(128)S(6)} %select_n.201), kind=kLoop, calls=%fused_computation.10 | loop fusion | bytes 8388616 | tf_op jit(solution)/shard_map/jit(dynamic_index_in_dim)/squeeze | solution.py:70
  91.0 1.7 %fusion = f32[4,8,64,256]{3,2,1,0:T(8,128)} fusion(s32[]{:T(128)S(6)} %select_n.235, f32[4,8,64,256]{3,2,1,0:T(8,128)S(1)} %get-tuple-element.27), kind=kLoop, calls=%fused_computation.6 | loop fusion | flops 524288 | bytes 4194308 | tf_op jit(solution)/shard_map/jit(_roll_dynamic)/concatenate | solution.py:71
  92.8 1.9 %collective-permute-start.6 = (f32[4,8,64,256]{3,2,1,0:T(8,128)}, f32[4,8,64,256]{3,2,1,0:T(8,128)}, u32[]{:S(2)}, u32[]{:S(2)}) collective-permute-start(f32[4,8,64,256]{3,2,1,0:T(8,128)} %fusion), channel_id=1, source_target_pairs={{0,12},{12,0},{24,36},{36,24},{48,60},{60,48},{72,84},{84,72},{96,... | collective-permute-start | bytes 6291464 | tf_op jit(solution)/shard_map/ppermute | solution.py:72
  94.9 1.7 %reshape.68 = bf16[6,64,2,128]{3,2,1,0:T(2,128)(2,1)} reshape(bf16[384,256]{1,0:T(8,128)(2,1)} %copy-done.28) | data formatting | bytes 393216 | tf_op jit(solution)/shard_map/reshape | solution.py:119
  96.6 2.0 %fusion.16 = bf16[6,2,64,64]{3,2,1,0:T(8,128)(2,1)} fusion(pred[64,64]{1,0:T(8,128)(4,1)S(1)} %iota_compare_fusion, bf16[6,64,2,128]{3,2,1,0:T(2,128)(2,1)} %reshape.68, bf16[6,64,2,128]{3,2,1,0:T(2,128)(2,1)} %copy-done.2), kind=kOutput, calls=%fused_computation.37 | convolution fusion | flops 12730368 | bytes 495616 | tf_op jit(solution)/shard_map/cthe,cshe->chts/dot_general | solution.py:178
  98.7 2.1 %convolution_bitcast_fusion.1 = f32[6,2,128,128]{2,3,1,0:T(8,128)} fusion(bf16[6,64,2,128]{3,2,1,0:T(2,128)(2,1)} %reshape.68, bf16[6,64,2,128]{3,2,1,0:T(2,128)(2,1)S(1)} %reshape.64), kind=kOutput, calls=%fused_computation.14 | convolution fusion | flops 25165824 | bytes 1179648 | tf_op jit(solution)/shard_map/cthd,cthe->chde/dot_general | solution.py:123
  100.8 1.6 fusion.33
  102.4 1.7 %copy.53 = f32[2,128,128]{1,2,0:T(8,128)} copy(f32[2,128,128]{2,1,0:T(8,128)} %fusion.33) | data formatting | bytes 262144 | tf_op jit(solution)/shard_map/sub | solution.py:152
  104.1 1.3 subtract_convert_fusion
  105.4 2.9 %fusion.2 = f32[4,8,64,256]{3,2,1,0:T(8,128)S(1)} fusion(f32[4,8,64,256]{3,2,1,0:T(8,128)} %collective-permute-done.6, s32[]{:T(128)S(6)} %select_n.233, f32[4,8,64,256]{3,2,1,0:T(8,128)} %get-tuple-element.26), kind=kLoop, calls=%fused_computation.8 | loop fusion | flops 1048576 | bytes 6291460 | tf_op jit(solution)/shard_map/add | solution.py:72
  108.4 2.1 %collective-permute-start.7 = (bf16[4,4,64,256]{3,2,1,0:T(8,128)(2,1)S(1)}, bf16[4,4,64,256]{3,2,1,0:T(8,128)(2,1)S(1)}, u32[]{:S(2)}, u32[]{:S(2)}) collective-permute-start(bf16[4,4,64,256]{3,2,1,0:T(8,128)(2,1)S(1)} %fusion.23), channel_id=1, source_target_pairs={{0,24},{12,180},{24,0},{36,60},{48,72},{60,36},{72,48},{84,108},{9... | collective-permute-start | bytes 1572872 | tf_op jit(solution)/shard_map/ppermute | solution.py:58
  112.9 6.8 %collective-permute-done.7 = bf16[4,4,64,256]{3,2,1,0:T(8,128)(2,1)S(1)} collective-permute-done((bf16[4,4,64,256]{3,2,1,0:T(8,128)(2,1)S(1)}, bf16[4,4,64,256]{3,2,1,0:T(8,128)(2,1)S(1)}, u32[]{:S(2)}, u32[]{:S(2)}) %collective-permute-start.7) | collective-permute-done | bytes 524320 | tf_op jit(solution)/shard_map/ppermute | solution.py:58
  119.8 4.8 %collective-permute-start.8 = (bf16[4,64,256]{2,1,0:T(8,128)(2,1)S(1)}, bf16[4,64,256]{2,1,0:T(8,128)(2,1)S(1)}, u32[]{:S(2)}, u32[]{:S(2)}) collective-permute-start(bf16[4,64,256]{2,1,0:T(8,128)(2,1)S(1)} %get-tuple-element.28), channel_id=1, source_target_pairs={{0,192},{12,204},{24,216},{36,228},{48,240},{60,252},{72,264},{84,... | collective-permute-start | bytes 393224 | tf_op jit(solution)/shard_map/ppermute | solution.py:58
  124.7 1.9 %collective-permute-start.10 = (bf16[4,64,256]{2,1,0:T(8,128)(2,1)S(1)}, bf16[4,64,256]{2,1,0:T(8,128)(2,1)S(1)}, u32[]{:S(2)}, u32[]{:S(2)}) collective-permute-start(bf16[4,64,256]{2,1,0:T(8,128)(2,1)S(1)} %get-tuple-element.29), channel_id=1, source_target_pairs={{0,576},{12,588},{24,600},{36,612},{48,624},{60,636},{72,648},{84,... | collective-permute-start | bytes 393224 | tf_op jit(solution)/shard_map/ppermute | solution.py:58
  126.6 3.4 %collective-permute-start.9 = (bf16[4,64,256]{2,1,0:T(8,128)(2,1)S(1)}, bf16[4,64,256]{2,1,0:T(8,128)(2,1)S(1)}, u32[]{:S(2)}, u32[]{:S(2)}) collective-permute-start(bf16[4,64,256]{2,1,0:T(8,128)(2,1)S(1)} %get-tuple-element.30), channel_id=1, source_target_pairs={{0,384},{12,396},{24,408},{36,420},{48,432},{60,444},{72,456},{84,... | collective-permute-start | bytes 393224 | tf_op jit(solution)/shard_map/ppermute | solution.py:58
  130.2 6.0 %collective-permute-done.10 = bf16[4,64,256]{2,1,0:T(8,128)(2,1)S(1)} collective-permute-done((bf16[4,64,256]{2,1,0:T(8,128)(2,1)S(1)}, bf16[4,64,256]{2,1,0:T(8,128)(2,1)S(1)}, u32[]{:S(2)}, u32[]{:S(2)}) %collective-permute-start.10) | collective-permute-done | bytes 131104 | tf_op jit(solution)/shard_map/ppermute | solution.py:58
  136.3 1.9 %collective-permute-start.11 = (bf16[64,256]{1,0:T(8,128)(2,1)S(1)}, bf16[64,256]{1,0:T(8,128)(2,1)S(1)}, u32[]{:S(2)}, u32[]{:S(2)}) collective-permute-start(bf16[64,256]{1,0:T(8,128)(2,1)S(1)} %get-tuple-element.31), channel_id=1, source_target_pairs={{0,48},{12,60},{24,72},{36,84},{48,96},{60,108},{72,120},{84,132},... | collective-permute-start | bytes 98312 | tf_op jit(solution)/shard_map/ppermute | solution.py:58
  138.2 6.0 %collective-permute-start.13 = (bf16[64,256]{1,0:T(8,128)(2,1)S(1)}, bf16[64,256]{1,0:T(8,128)(2,1)S(1)}, u32[]{:S(2)}, u32[]{:S(2)}) collective-permute-start(bf16[64,256]{1,0:T(8,128)(2,1)S(1)} %get-tuple-element.32), channel_id=1, source_target_pairs={{0,144},{12,156},{24,168},{36,180},{48,0},{60,12},{72,24},{84,36},... | collective-permute-start | bytes 98312 | tf_op jit(solution)/shard_map/ppermute | solution.py:58
  144.3 5.0 %collective-permute-start.12 = (bf16[64,256]{1,0:T(8,128)(2,1)S(1)}, bf16[64,256]{1,0:T(8,128)(2,1)S(1)}, u32[]{:S(2)}, u32[]{:S(2)}) collective-permute-start(bf16[64,256]{1,0:T(8,128)(2,1)S(1)} %get-tuple-element.33), channel_id=1, source_target_pairs={{0,96},{12,108},{24,120},{36,132},{48,144},{60,156},{72,168},{84,1... | collective-permute-start | bytes 98312 | tf_op jit(solution)/shard_map/ppermute | solution.py:58
  149.7 0.7 copy.132
  152.2 1.7 %collective-permute-done.12 = bf16[64,256]{1,0:T(8,128)(2,1)S(1)} collective-permute-done((bf16[64,256]{1,0:T(8,128)(2,1)S(1)}, bf16[64,256]{1,0:T(8,128)(2,1)S(1)}, u32[]{:S(2)}, u32[]{:S(2)}) %collective-permute-start.12) | collective-permute-done | bytes 32800 | tf_op jit(solution)/shard_map/ppermute | solution.py:58
  (119 shorter events, 10.4 us)
Async XLA Ops:
  7.2 2.5 %copy-start = (bf16[384,4096]{1,0:T(8,128)(2,1)S(1)}, bf16[384,4096]{1,0:T(8,128)(2,1)}, u32[]{:S(2)}) copy-start(bf16[384,4096]{1,0:T(8,128)(2,1)} %param.11) | copy-start | bytes 9437188
  7.2 147.4 %reduce-scatter.2.cloned.1.call-start = ((), (), s32[]{:S(2)}) async-start(), calls=%async_computation.1 | async-start | bytes 3407872 | tf_op jit(solution)/shard_map/reduce_scatter | solution.py:168
  9.7 2.6 %copy-start.27 = (bf16[384,256]{1,0:T(8,128)(2,1)S(1)}, bf16[384,256]{1,0:T(8,128)(2,1)}, u32[]{:S(2)}) copy-start(bf16[384,256]{1,0:T(8,128)(2,1)} %param.7) | copy-start | bytes 589828
  12.6 7.3 %copy-start.32 = (f32[128,128]{0,1:T(8,128)}, f32[128,128]{0,1:T(8,128)S(1)}, u32[]{:S(2)}) copy-start(f32[128,128]{0,1:T(8,128)S(1)} %fusion.69) | copy-start | bytes 196612
  12.8 7.0 %copy-start.33 = (f32[128,128]{0,1:T(8,128)}, f32[128,128]{0,1:T(8,128)S(1)}, u32[]{:S(2)}) copy-start(f32[128,128]{0,1:T(8,128)S(1)} %fusion.71) | copy-start | bytes 196612
  13.1 3.2 %collective-permute-start = (bf16[2,2,128,128]{3,2,1,0:T(8,128)(2,1)S(1)}, bf16[2,2,128,128]{3,2,1,0:T(8,128)(2,1)S(1)}, u32[]{:S(2)}, u32[]{:S(2)}) collective-permute-start(bf16[2,2,128,128]{3,2,1,0:T(8,128)(2,1)S(1)} %fusion.27), channel_id=1, source_target_pairs={{0,12},{12,0},{24,36},{36,24},{48,60},{60,48},{72,84},{84,72},{96,... | collective-permute-start | bytes 393224 | tf_op jit(solution)/shard_map/ppermute | solution.py:18
  16.3 18.6 %copy-start.14 = (bf16[2,2,128,128]{3,2,1,0:T(8,128)(2,1)}, bf16[2,2,128,128]{3,2,1,0:T(8,128)(2,1)S(1)}, u32[]{:S(2)}) copy-start(bf16[2,2,128,128]{3,2,1,0:T(8,128)(2,1)S(1)} %collective-permute-done) | copy-start | bytes 393220
  16.3 7.4 %collective-permute-start.1 = (bf16[2,2,128,128]{3,2,1,0:T(8,128)(2,1)S(1)}, bf16[2,2,128,128]{3,2,1,0:T(8,128)(2,1)S(1)}, u32[]{:S(2)}, u32[]{:S(2)}) collective-permute-start(bf16[2,2,128,128]{3,2,1,0:T(8,128)(2,1)S(1)} %fusion.80), channel_id=1, source_target_pairs={{0,24},{24,0},{12,36},{36,12},{48,72},{72,48},{60,84},{84,60},{96,... | collective-permute-start | bytes 393224 | tf_op jit(solution)/shard_map/ppermute | solution.py:18
  23.8 11.1 %copy-start.34 = (bf16[2,2,128,128]{3,2,1,0:T(8,128)(2,1)}, bf16[2,2,128,128]{3,2,1,0:T(8,128)(2,1)S(1)}, u32[]{:S(2)}) copy-start(bf16[2,2,128,128]{3,2,1,0:T(8,128)(2,1)S(1)} %collective-permute-done.1) | copy-start | bytes 393220
  23.8 11.0 %copy-start.6 = (f32[2,2,128,128]{3,2,1,0:T(8,128)}, f32[2,2,128,128]{3,2,1,0:T(8,128)S(1)}, u32[]{:S(2)}) copy-start(f32[2,2,128,128]{3,2,1,0:T(8,128)S(1)} %get-tuple-element.25) | copy-start | bytes 786436
  23.9 10.3 %collective-permute-start.2 = (bf16[2,2,128,128]{3,2,1,0:T(8,128)(2,1)S(1)}, bf16[2,2,128,128]{3,2,1,0:T(8,128)(2,1)S(1)}, u32[]{:S(2)}, u32[]{:S(2)}) collective-permute-start(bf16[2,2,128,128]{3,2,1,0:T(8,128)(2,1)S(1)} %get-tuple-element.24), channel_id=1, source_target_pairs={{0,48},{48,0},{12,60},{60,12},{24,72},{72,24},{36,84},{84,36},{96,... | collective-permute-start | bytes 393224 | tf_op jit(solution)/shard_map/ppermute | solution.py:18
  34.2 8.4 %copy-start.12 = (bf16[2,2,128,128]{3,2,1,0:T(8,128)(2,1)}, bf16[2,2,128,128]{3,2,1,0:T(8,128)(2,1)S(1)}, u32[]{:S(2)}) copy-start(bf16[2,2,128,128]{3,2,1,0:T(8,128)(2,1)S(1)} %collective-permute-done.2) | copy-start | bytes 393220
  34.9 14.4 %collective-permute-start.3 = (bf16[2,2,128,128]{3,2,1,0:T(8,128)(2,1)}, bf16[2,2,128,128]{3,2,1,0:T(8,128)(2,1)}, u32[]{:S(2)}, u32[]{:S(2)}) collective-permute-start(bf16[2,2,128,128]{3,2,1,0:T(8,128)(2,1)} %fusion.85), channel_id=1, source_target_pairs={{0,96},{96,0},{12,108},{108,12},{24,120},{120,24},{36,132},{132,36... | collective-permute-start | bytes 393224 | tf_op jit(solution)/shard_map/ppermute | solution.py:18
  44.6 10.3 %copy-start.2 = (bf16[6,64,2,128]{3,2,1,0:T(2,128)(2,1)}, bf16[6,64,2,128]{3,2,1,0:T(2,128)(2,1)S(1)}, u32[]{:S(2)}) copy-start(bf16[6,64,2,128]{3,2,1,0:T(2,128)(2,1)S(1)} %reshape.66) | copy-start | bytes 589828
  51.0 7.2 %collective-permute-start.4 = (bf16[2,2,128,128]{3,2,1,0:T(8,128)(2,1)}, bf16[2,2,128,128]{3,2,1,0:T(8,128)(2,1)}, u32[]{:S(2)}, u32[]{:S(2)}) collective-permute-start(bf16[2,2,128,128]{3,2,1,0:T(8,128)(2,1)} %fusion.84), channel_id=1, source_target_pairs={{0,192},{192,0},{12,204},{204,12},{24,216},{216,24},{36,228},{228,... | collective-permute-start | bytes 393224 | tf_op jit(solution)/shard_map/ppermute | solution.py:18
  56.0 12.8 %copy-start.35 = (bf16[2,2,128,128]{3,2,1,0:T(8,128)(2,1)S(1)}, bf16[2,2,128,128]{3,2,1,0:T(8,128)(2,1)}, u32[]{:S(2)}) copy-start(bf16[2,2,128,128]{3,2,1,0:T(8,128)(2,1)} %copy-done.34) | copy-start | bytes 393220
  56.0 12.8 %copy-start.13 = (bf16[2,2,128,128]{3,2,1,0:T(8,128)(2,1)S(1)}, bf16[2,2,128,128]{3,2,1,0:T(8,128)(2,1)}, u32[]{:S(2)}) copy-start(bf16[2,2,128,128]{3,2,1,0:T(8,128)(2,1)} %copy-done.12) | copy-start | bytes 393220
  59.4 13.0 %copy-start.1 = (f32[6,2,128,128]{3,2,1,0:T(8,128)S(1)}, f32[6,2,128,128]{3,2,1,0:T(8,128)}, u32[]{:S(2)}) copy-start(f32[6,2,128,128]{3,2,1,0:T(8,128)} %fusion.54) | copy-start | bytes 2359300
  59.4 11.6 %collective-permute-start.5 = (bf16[2,2,128,128]{3,2,1,0:T(8,128)(2,1)S(1)}, bf16[2,2,128,128]{3,2,1,0:T(8,128)(2,1)S(1)}, u32[]{:S(2)}, u32[]{:S(2)}) collective-permute-start(bf16[2,2,128,128]{3,2,1,0:T(8,128)(2,1)S(1)} %add_convert_fusion), channel_id=1, source_target_pairs={{0,384},{384,0},{12,396},{396,12},{24,408},{408,24},{36,420},{420,... | collective-permute-start | bytes 393224 | tf_op jit(solution)/shard_map/ppermute | solution.py:18
  67.7 5.4 %copy-start.29 = (bf16[6,2,64,64]{3,2,1,0:T(8,128)(2,1)}, bf16[6,2,64,64]{3,2,1,0:T(8,128)(2,1)S(1)}, u32[]{:S(2)}) copy-start(bf16[6,2,64,64]{3,2,1,0:T(8,128)(2,1)S(1)} %fusion.17) | copy-start | bytes 294916
  68.8 2.3 %copy-start.15 = (f32[2,2,128,128]{3,2,1,0:T(8,128)}, f32[2,2,128,128]{3,2,1,0:T(8,128)S(1)}, u32[]{:S(2)}) copy-start(f32[2,2,128,128]{3,2,1,0:T(8,128)S(1)} %convert_element_type.147) | copy-start | bytes 786436
  68.8 2.2 %copy-start.17 = (f32[2,2,128,128]{3,2,1,0:T(8,128)}, f32[2,2,128,128]{3,2,1,0:T(8,128)S(1)}, u32[]{:S(2)}) copy-start(f32[2,2,128,128]{3,2,1,0:T(8,128)S(1)} %convert_element_type.149) | copy-start | bytes 786436
  68.8 2.2 %copy-start.19 = (f32[2,2,128,128]{3,2,1,0:T(8,128)}, f32[2,2,128,128]{3,2,1,0:T(8,128)S(1)}, u32[]{:S(2)}) copy-start(f32[2,2,128,128]{3,2,1,0:T(8,128)S(1)} %convert_element_type.151) | copy-start | bytes 786436
  69.9 1.1 copy-start.21
  72.4 0.9 copy-start.3
  72.6 0.9 copy-start.7
  72.6 1.1 copy-start.9
  72.7 1.9 %copy-start.11 = (bf16[4096,256]{1,0:T(8,128)(2,1)S(1)}, bf16[4096,256]{1,0:T(8,128)(2,1)}, u32[]{:S(2)}) copy-start(bf16[4096,256]{1,0:T(8,128)(2,1)} %param.10) | copy-start | bytes 6291460
  92.8 12.6 %collective-permute-start.6 = (f32[4,8,64,256]{3,2,1,0:T(8,128)}, f32[4,8,64,256]{3,2,1,0:T(8,128)}, u32[]{:S(2)}, u32[]{:S(2)}) collective-permute-start(f32[4,8,64,256]{3,2,1,0:T(8,128)} %fusion), channel_id=1, source_target_pairs={{0,12},{12,0},{24,36},{36,24},{48,60},{60,48},{72,84},{84,72},{96,... | collective-permute-start | bytes 6291464 | tf_op jit(solution)/shard_map/ppermute | solution.py:72
  96.6 4.2 %copy-start.16 = (f32[2,2,128,128]{3,2,1,0:T(8,128)S(1)}, f32[2,2,128,128]{3,2,1,0:T(8,128)}, u32[]{:S(2)}) copy-start(f32[2,2,128,128]{3,2,1,0:T(8,128)} %copy-done.15) | copy-start | bytes 786436
  96.6 4.2 %copy-start.18 = (f32[2,2,128,128]{3,2,1,0:T(8,128)S(1)}, f32[2,2,128,128]{3,2,1,0:T(8,128)}, u32[]{:S(2)}) copy-start(f32[2,2,128,128]{3,2,1,0:T(8,128)} %copy-done.17) | copy-start | bytes 786436
  96.6 4.2 %copy-start.20 = (f32[2,2,128,128]{3,2,1,0:T(8,128)S(1)}, f32[2,2,128,128]{3,2,1,0:T(8,128)}, u32[]{:S(2)}) copy-start(f32[2,2,128,128]{3,2,1,0:T(8,128)} %copy-done.19) | copy-start | bytes 786436
  96.6 4.2 %copy-start.22 = (f32[2,2,128,128]{3,2,1,0:T(8,128)S(1)}, f32[2,2,128,128]{3,2,1,0:T(8,128)}, u32[]{:S(2)}) copy-start(f32[2,2,128,128]{3,2,1,0:T(8,128)} %copy-done.21) | copy-start | bytes 786436
  96.6 4.2 %copy-start.24 = (f32[2,2,128,128]{3,2,1,0:T(8,128)S(1)}, f32[2,2,128,128]{3,2,1,0:T(8,128)}, u32[]{:S(2)}) copy-start(f32[2,2,128,128]{3,2,1,0:T(8,128)} %copy-done.23) | copy-start | bytes 786436
  96.6 4.2 %copy-start.26 = (f32[2,2,128,128]{3,2,1,0:T(8,128)S(1)}, f32[2,2,128,128]{3,2,1,0:T(8,128)}, u32[]{:S(2)}) copy-start(f32[2,2,128,128]{3,2,1,0:T(8,128)} %copy-done.25) | copy-start | bytes 786436
  108.3 2.5 %copy-start.4 = (bf16[6,64,2,128]{3,2,1,0:T(2,128)(2,1)S(1)}, bf16[6,64,2,128]{3,2,1,0:T(2,128)(2,1)}, u32[]{:S(2)}) copy-start(bf16[6,64,2,128]{3,2,1,0:T(2,128)(2,1)} %copy-done.2) | copy-start | bytes 589828
  108.3 2.8 %copy-start.5 = (bf16[6,64,2,128]{3,2,1,0:T(2,128)(2,1)S(1)}, bf16[6,64,2,128]{3,2,1,0:T(2,128)(2,1)}, u32[]{:S(2)}) copy-start(bf16[6,64,2,128]{3,2,1,0:T(2,128)(2,1)} %reshape.68) | copy-start | bytes 589828
  108.4 2.8 %copy-start.10 = (bf16[6,2,128,128]{3,2,1,0:T(8,128)(2,1)S(1)}, bf16[6,2,128,128]{3,2,1,0:T(8,128)(2,1)}, u32[]{:S(2)}) copy-start(bf16[6,2,128,128]{3,2,1,0:T(8,128)(2,1)} %copy-done.9) | copy-start | bytes 1179652
  108.4 3.4 %copy-start.30 = (bf16[6,2,64,64]{3,2,1,0:T(8,128)(2,1)S(1)}, bf16[6,2,64,64]{3,2,1,0:T(8,128)(2,1)}, u32[]{:S(2)}) copy-start(bf16[6,2,64,64]{3,2,1,0:T(8,128)(2,1)} %copy-done.29) | copy-start | bytes 294916
  108.4 11.2 %collective-permute-start.7 = (bf16[4,4,64,256]{3,2,1,0:T(8,128)(2,1)S(1)}, bf16[4,4,64,256]{3,2,1,0:T(8,128)(2,1)S(1)}, u32[]{:S(2)}, u32[]{:S(2)}) collective-permute-start(bf16[4,4,64,256]{3,2,1,0:T(8,128)(2,1)S(1)} %fusion.23), channel_id=1, source_target_pairs={{0,24},{12,180},{24,0},{36,60},{48,72},{60,36},{72,48},{84,108},{9... | collective-permute-start | bytes 1572872 | tf_op jit(solution)/shard_map/ppermute | solution.py:58
  111.5 1.0 copy-start.8
  112.5 17.5 %copy-start.31 = (bf16[6,2,64,64]{3,2,1,0:T(8,128)(2,1)S(1)}, bf16[6,2,64,64]{3,2,1,0:T(8,128)(2,1)}, u32[]{:S(2)}) copy-start(bf16[6,2,64,64]{3,2,1,0:T(8,128)(2,1)} %fusion.16) | copy-start | bytes 294916
  119.8 10.3 %collective-permute-start.8 = (bf16[4,64,256]{2,1,0:T(8,128)(2,1)S(1)}, bf16[4,64,256]{2,1,0:T(8,128)(2,1)S(1)}, u32[]{:S(2)}, u32[]{:S(2)}) collective-permute-start(bf16[4,64,256]{2,1,0:T(8,128)(2,1)S(1)} %get-tuple-element.28), channel_id=1, source_target_pairs={{0,192},{12,204},{24,216},{36,228},{48,240},{60,252},{72,264},{84,... | collective-permute-start | bytes 393224 | tf_op jit(solution)/shard_map/ppermute | solution.py:58
  124.7 11.5 %collective-permute-start.10 = (bf16[4,64,256]{2,1,0:T(8,128)(2,1)S(1)}, bf16[4,64,256]{2,1,0:T(8,128)(2,1)S(1)}, u32[]{:S(2)}, u32[]{:S(2)}) collective-permute-start(bf16[4,64,256]{2,1,0:T(8,128)(2,1)S(1)} %get-tuple-element.29), channel_id=1, source_target_pairs={{0,576},{12,588},{24,600},{36,612},{48,624},{60,636},{72,648},{84,... | collective-permute-start | bytes 393224 | tf_op jit(solution)/shard_map/ppermute | solution.py:58
  126.6 9.6 %collective-permute-start.9 = (bf16[4,64,256]{2,1,0:T(8,128)(2,1)S(1)}, bf16[4,64,256]{2,1,0:T(8,128)(2,1)S(1)}, u32[]{:S(2)}, u32[]{:S(2)}) collective-permute-start(bf16[4,64,256]{2,1,0:T(8,128)(2,1)S(1)} %get-tuple-element.30), channel_id=1, source_target_pairs={{0,384},{12,396},{24,408},{36,420},{48,432},{60,444},{72,456},{84,... | collective-permute-start | bytes 393224 | tf_op jit(solution)/shard_map/ppermute | solution.py:58
  136.3 15.9 %collective-permute-start.11 = (bf16[64,256]{1,0:T(8,128)(2,1)S(1)}, bf16[64,256]{1,0:T(8,128)(2,1)S(1)}, u32[]{:S(2)}, u32[]{:S(2)}) collective-permute-start(bf16[64,256]{1,0:T(8,128)(2,1)S(1)} %get-tuple-element.31), channel_id=1, source_target_pairs={{0,48},{12,60},{24,72},{36,84},{48,96},{60,108},{72,120},{84,132},... | collective-permute-start | bytes 98312 | tf_op jit(solution)/shard_map/ppermute | solution.py:58
  138.2 14.0 %collective-permute-start.13 = (bf16[64,256]{1,0:T(8,128)(2,1)S(1)}, bf16[64,256]{1,0:T(8,128)(2,1)S(1)}, u32[]{:S(2)}, u32[]{:S(2)}) collective-permute-start(bf16[64,256]{1,0:T(8,128)(2,1)S(1)} %get-tuple-element.32), channel_id=1, source_target_pairs={{0,144},{12,156},{24,168},{36,180},{48,0},{60,12},{72,24},{84,36},... | collective-permute-start | bytes 98312 | tf_op jit(solution)/shard_map/ppermute | solution.py:58
  144.3 9.7 %collective-permute-start.12 = (bf16[64,256]{1,0:T(8,128)(2,1)S(1)}, bf16[64,256]{1,0:T(8,128)(2,1)S(1)}, u32[]{:S(2)}, u32[]{:S(2)}) collective-permute-start(bf16[64,256]{1,0:T(8,128)(2,1)S(1)} %get-tuple-element.33), channel_id=1, source_target_pairs={{0,96},{12,108},{24,120},{36,132},{48,144},{60,156},{72,168},{84,1... | collective-permute-start | bytes 98312 | tf_op jit(solution)/shard_map/ppermute | solution.py:58
  (3 other events, 2.1 us)
Sparse Core Ops, SparseCore 0:
  77.3 65.0 reduce-scatter.1

commit v12 on v5

--- a/solution.py
+++ b/solution.py
@@ -67,8 +67,8 @@
     x = position // (2 * y_count)
     index = lambda a, b, c: a * 2 * y_count + b % y_count * 2 + c
     acc = partial.reshape(x_count, y_count, 2, partial.shape[0] // count, cols)
-    kept = lax.dynamic_index_in_dim(acc, core, 2, keepdims=False)
     sent = lax.dynamic_index_in_dim(acc, 1 - core, 2, keepdims=False)
+    kept = lax.dynamic_index_in_dim(lax.optimization_barrier(acc), core, 2, keepdims=False)
     acc = kept + lax.ppermute(sent, SEQ, [(i, i ^ 1) for i in range(count)])
     acc, ride = lax.optimization_barrier((acc, ride))
     acc = jnp.where(core == 1, jnp.roll(acc, -1, axis=1), acc)

time: 162 us -> 162 us (level)
  no operation moved by 1% of the time
where the time goes in v12:
time: 162 us; the launch traced here: 160 us
  starting transfers between devices  55.5 us (34%)
  waiting for transfers between devices  32.9 us (20%)
  matrix products  21.4 us (13%)
  local copies, waits for them, and re-layouts  21.1 us (13%)
  between operations  15.1 us (9%)
  other arithmetic  13.9 us (9%)
    ppermute x6, starting transfers between devices, swapped(): return lax.ppermute(block, SEQ, route)  28.5 us
    ppermute x7, starting transfers between devices, wire(): lax.ppermute(block.astype(jnp.bfloat16), SEQ, route).astype(jnp.float32)  25.1 us
    ppermute x6, waiting for transfers between devices, swapped(): return lax.ppermute(block, SEQ, route)  17.9 us
    ppermute x7, waiting for transfers between devices, wire(): lax.ppermute(block.astype(jnp.bfloat16), SEQ, route).astype(jnp.float32)  15 us
    dot_general x1, local copies, waits for them, and re-layouts, local(): lax.dot_general(out_grad, attention, (((0,), (0,)), ((), ())), preferred_...  5.61 us
    unnamed x76, local copies, waits for them, and re-layouts  4.85 us
    dot_general x1, matrix products, local(): lax.dot_general(out_grad, attention, (((0,), (0,)), ((), ())), preferred_...  4.22 us
    convert_element_type x6, other arithmetic, local(): totals.astype(jnp.bfloat16)  3.73 us
  transfers between devices with their start and end apart: 15, of which 8 were waited for; matrix products, arithmetic and copies ran while one was open for 25% of the time, Pallas kernels for 0%

profile of v12, /device:TPU:6, one launch (start us, length us, event | category | flops | bytes accessed | tf_op | source)
XLA Modules:
  0.0 159.8 jit_solution(11780327322315620883)
XLA Ops:
  7.2 1.3 convolution_bitcast_fusion.5
  8.5 1.1 convolution_bitcast_fusion.6
  9.7 2.6 %convolution_convert_fusion.1 = bf16[384,256]{1,0:T(8,128)(2,1)S(1)} fusion(bf16[384,4096]{1,0:T(8,128)(2,1)S(1)} %copy-done, bf16[4096,256]{1,0:T(8,128)(2,1)} %param.8), kind=kOutput, calls=%fused_computation.37 | convolution fusion | flops 805404672 | bytes 5439488 | tf_op jit(solution)/shard_map/dot_general | solution.py:117
  13.1 1.9 %collective-permute-start = (bf16[2,2,128,128]{3,2,1,0:T(8,128)(2,1)S(1)}, bf16[2,2,128,128]{3,2,1,0:T(8,128)(2,1)S(1)}, u32[]{:S(2)}, u32[]{:S(2)}) collective-permute-start(bf16[2,2,128,128]{3,2,1,0:T(8,128)(2,1)S(1)} %fusion.24), channel_id=1, source_target_pairs={{0,12},{12,0},{24,36},{36,24},{48,60},{60,48},{72,84},{84,72},{96,... | collective-permute-start | bytes 393224 | tf_op jit(solution)/shard_map/ppermute | solution.py:18
  15.0 1.3 collective-permute-done
  16.3 3.5 %collective-permute-start.1 = (bf16[2,2,128,128]{3,2,1,0:T(8,128)(2,1)S(1)}, bf16[2,2,128,128]{3,2,1,0:T(8,128)(2,1)S(1)}, u32[]{:S(2)}, u32[]{:S(2)}) collective-permute-start(bf16[2,2,128,128]{3,2,1,0:T(8,128)(2,1)S(1)} %fusion.77), channel_id=1, source_target_pairs={{0,24},{24,0},{12,36},{36,12},{48,72},{72,48},{60,84},{84,60},{96,... | collective-permute-start | bytes 393224 | tf_op jit(solution)/shard_map/ppermute | solution.py:18
  19.9 3.9 %collective-permute-done.1 = bf16[2,2,128,128]{3,2,1,0:T(8,128)(2,1)S(1)} collective-permute-done((bf16[2,2,128,128]{3,2,1,0:T(8,128)(2,1)S(1)}, bf16[2,2,128,128]{3,2,1,0:T(8,128)(2,1)S(1)}, u32[]{:S(2)}, u32[]{:S(2)}) %collective-permute-start.1) | collective-permute-done | bytes 131104 | tf_op jit(solution)/shard_map/ppermute | solution.py:18
  23.9 4.5 %collective-permute-start.2 = (bf16[2,2,128,128]{3,2,1,0:T(8,128)(2,1)S(1)}, bf16[2,2,128,128]{3,2,1,0:T(8,128)(2,1)S(1)}, u32[]{:S(2)}, u32[]{:S(2)}) collective-permute-start(bf16[2,2,128,128]{3,2,1,0:T(8,128)(2,1)S(1)} %get-tuple-element.23), channel_id=1, source_target_pairs={{0,48},{48,0},{12,60},{60,12},{24,72},{72,24},{36,84},{84,36},{96,... | collective-permute-start | bytes 393224 | tf_op jit(solution)/shard_map/ppermute | solution.py:18
  28.4 5.8 %collective-permute-done.2 = bf16[2,2,128,128]{3,2,1,0:T(8,128)(2,1)S(1)} collective-permute-done((bf16[2,2,128,128]{3,2,1,0:T(8,128)(2,1)S(1)}, bf16[2,2,128,128]{3,2,1,0:T(8,128)(2,1)S(1)}, u32[]{:S(2)}, u32[]{:S(2)}) %collective-permute-start.2) | collective-permute-done | bytes 131104 | tf_op jit(solution)/shard_map/ppermute | solution.py:18
  34.9 7.7 %collective-permute-start.3 = (bf16[2,2,128,128]{3,2,1,0:T(8,128)(2,1)}, bf16[2,2,128,128]{3,2,1,0:T(8,128)(2,1)}, u32[]{:S(2)}, u32[]{:S(2)}) collective-permute-start(bf16[2,2,128,128]{3,2,1,0:T(8,128)(2,1)} %fusion.82), channel_id=1, source_target_pairs={{0,96},{96,0},{12,108},{108,12},{24,120},{120,24},{36,132},{132,36... | collective-permute-start | bytes 393224 | tf_op jit(solution)/shard_map/ppermute | solution.py:18
  42.6 1.0 reshape.65
  43.6 1.0 reshape.66
  44.6 4.6 %collective-permute-done.3 = bf16[2,2,128,128]{3,2,1,0:T(8,128)(2,1)} collective-permute-done((bf16[2,2,128,128]{3,2,1,0:T(8,128)(2,1)}, bf16[2,2,128,128]{3,2,1,0:T(8,128)(2,1)}, u32[]{:S(2)}, u32[]{:S(2)}) %collective-permute-start.3) | collective-permute-done | bytes 131104 | tf_op jit(solution)/shard_map/ppermute | solution.py:18
  49.3 1.7 %fusion.81 = bf16[2,2,128,128]{3,2,1,0:T(8,128)(2,1)} fusion(bf16[2,2,128,128]{3,2,1,0:T(8,128)(2,1)} %collective-permute-done.3, f32[2,2,128,128]{3,2,1,0:T(8,128)} %copy-done.6, bf16[2,2,128,128]{3,2,1,0:T(8,128)(2,1)} %copy-done.12), kind=kLoop, calls=%fused_computation.135 | loop fusion | flops 327680 | bytes 655360 | tf_op jit(solution)/shard_map/convert_element_type | solution.py:147
  51.0 2.7 %collective-permute-start.4 = (bf16[2,2,128,128]{3,2,1,0:T(8,128)(2,1)}, bf16[2,2,128,128]{3,2,1,0:T(8,128)(2,1)}, u32[]{:S(2)}, u32[]{:S(2)}) collective-permute-start(bf16[2,2,128,128]{3,2,1,0:T(8,128)(2,1)} %fusion.81), channel_id=1, source_target_pairs={{0,192},{192,0},{12,204},{204,12},{24,216},{216,24},{36,228},{228,... | collective-permute-start | bytes 393224 | tf_op jit(solution)/shard_map/ppermute | solution.py:18
  53.7 1.2 fusion.51
  55.0 1.0 reshape.64
  56.0 2.2 %collective-permute-done.4 = bf16[2,2,128,128]{3,2,1,0:T(8,128)(2,1)} collective-permute-done((bf16[2,2,128,128]{3,2,1,0:T(8,128)(2,1)}, bf16[2,2,128,128]{3,2,1,0:T(8,128)(2,1)}, u32[]{:S(2)}, u32[]{:S(2)}) %collective-permute-start.4) | collective-permute-done | bytes 131104 | tf_op jit(solution)/shard_map/ppermute | solution.py:18
  58.2 1.2 add_convert_fusion
  59.4 8.1 %collective-permute-start.5 = (bf16[2,2,128,128]{3,2,1,0:T(8,128)(2,1)S(1)}, bf16[2,2,128,128]{3,2,1,0:T(8,128)(2,1)S(1)}, u32[]{:S(2)}, u32[]{:S(2)}) collective-permute-start(bf16[2,2,128,128]{3,2,1,0:T(8,128)(2,1)S(1)} %add_convert_fusion), channel_id=1, source_target_pairs={{0,384},{384,0},{12,396},{396,12},{24,408},{408,24},{36,420},{420,... | collective-permute-start | bytes 393224 | tf_op jit(solution)/shard_map/ppermute | solution.py:18
  67.8 1.0 convert_element_type.147
  68.9 1.1 convert_element_type.153
  69.9 1.0 convert_element_type.155
  71.7 0.7 copy-done.25
  73.8 0.7 copy.133
  74.6 2.6 %convolution_convert_fusion = bf16[384,4096]{1,0:T(8,128)(2,1)} fusion(bf16[4096,256]{1,0:T(8,128)(2,1)S(1)} %copy-done.11, bf16[48,8,2,128]{3,2,1,0:T(2,128)(2,1)S(1)} %bitcast.133), kind=kOutput, calls=%fused_computation | convolution fusion | flops 806879232 | bytes 5439488 | tf_op jit(solution)/shard_map/dot_general | solution.py:165
  77.3 4.2 %convolution_bitcast_fusion = f32[4096,256]{0,1:T(8,128)} fusion(bf16[384,256]{1,0:T(8,128)(2,1)} %bitcast.137, bf16[384,4096]{1,0:T(8,128)(2,1)S(1)} %copy-done), kind=kOutput, calls=%fused_computation.1 | convolution fusion | flops 805306368 | bytes 7536640 | tf_op jit(solution)/shard_map/dot_general | solution.py:170
  81.5 5.6 %copy.52 = f32[4096,256]{1,0:T(8,128)} copy(f32[4096,256]{0,1:T(8,128)} %convolution_bitcast_fusion) | data formatting | bytes 8388608 | tf_op jit(solution)/shard_map/dot_general | solution.py:170
  87.1 3.2 %dynamic-slice_bitcast_fusion = f32[4,8,64,256]{3,2,1,0:T(8,128)} fusion(f32[4,8,2,64,256]{4,3,2,1,0:T(8,128)} %bitcast.128, s32[]{:T(128)S(6)} %select_n.200), kind=kLoop, calls=%fused_computation.4 | loop fusion | bytes 4194308 | tf_op jit(solution)/shard_map/jit(dynamic_index_in_dim)/squeeze | solution.py:70
  90.3 1.9 %collective-permute-start.6 = (f32[4,8,64,256]{3,2,1,0:T(8,128)}, f32[4,8,64,256]{3,2,1,0:T(8,128)}, u32[]{:S(2)}, u32[]{:S(2)}) collective-permute-start(f32[4,8,64,256]{3,2,1,0:T(8,128)} %dynamic-slice_bitcast_fusion), channel_id=1, source_target_pairs={{0,12},{12,0},{24,36},{36,24},{48,60},{60,48},{72,84},{84,72},{96,... | collective-permute-start | bytes 6291464 | tf_op jit(solution)/shard_map/ppermute | solution.py:72
  92.4 1.7 %reshape.68 = bf16[6,64,2,128]{3,2,1,0:T(2,128)(2,1)} reshape(bf16[384,256]{1,0:T(8,128)(2,1)} %copy-done.28) | data formatting | bytes 393216 | tf_op jit(solution)/shard_map/reshape | solution.py:120
  94.1 2.1 %fusion.13 = bf16[6,2,64,64]{3,2,1,0:T(8,128)(2,1)} fusion(pred[64,64]{1,0:T(8,128)(4,1)S(1)} %iota_compare_fusion, bf16[6,64,2,128]{3,2,1,0:T(2,128)(2,1)} %reshape.68, bf16[6,64,2,128]{3,2,1,0:T(2,128)(2,1)} %copy-done.2), kind=kOutput, calls=%fused_computation.31 | convolution fusion | flops 12730368 | bytes 495616 | tf_op jit(solution)/shard_map/cthe,cshe->chts/dot_general | solution.py:179
  96.2 2.1 %convolution_bitcast_fusion.1 = f32[6,2,128,128]{2,3,1,0:T(8,128)} fusion(bf16[6,64,2,128]{3,2,1,0:T(2,128)(2,1)} %reshape.68, bf16[6,64,2,128]{3,2,1,0:T(2,128)(2,1)S(1)} %reshape.64), kind=kOutput, calls=%fused_computation.8 | convolution fusion | flops 25165824 | bytes 1179648 | tf_op jit(solution)/shard_map/cthd,cthe->chde/dot_general | solution.py:124
  98.4 1.6 fusion.30
  99.9 1.7 %copy.53 = f32[2,128,128]{1,2,0:T(8,128)} copy(f32[2,128,128]{2,1,0:T(8,128)} %fusion.30) | data formatting | bytes 262144 | tf_op jit(solution)/shard_map/sub | solution.py:153
  101.6 1.3 subtract_convert_fusion
  102.9 2.7 %bitcast_add_fusion = f32[4,8,64,256]{3,2,1,0:T(8,128)S(1)} fusion(f32[4,8,64,256]{3,2,1,0:T(8,128)} %collective-permute-done.6, f32[4,8,2,64,256]{4,3,2,1,0:T(8,128)} %bitcast.129, s32[]{:T(128)S(6)} %select_n.199), kind=kLoop, calls=%fused_computation.3 | loop fusion | flops 524288 | bytes 6291460 | tf_op jit(solution)/shard_map/add | solution.py:72
  106.3 2.1 %collective-permute-start.7 = (bf16[4,4,64,256]{3,2,1,0:T(8,128)(2,1)S(1)}, bf16[4,4,64,256]{3,2,1,0:T(8,128)(2,1)S(1)}, u32[]{:S(2)}, u32[]{:S(2)}) collective-permute-start(bf16[4,4,64,256]{3,2,1,0:T(8,128)(2,1)S(1)} %fusion.20), channel_id=1, source_target_pairs={{0,24},{12,180},{24,0},{36,60},{48,72},{60,36},{72,48},{84,108},{9... | collective-permute-start | bytes 1572872 | tf_op jit(solution)/shard_map/ppermute | solution.py:58
  110.8 6.8 %collective-permute-done.7 = bf16[4,4,64,256]{3,2,1,0:T(8,128)(2,1)S(1)} collective-permute-done((bf16[4,4,64,256]{3,2,1,0:T(8,128)(2,1)S(1)}, bf16[4,4,64,256]{3,2,1,0:T(8,128)(2,1)S(1)}, u32[]{:S(2)}, u32[]{:S(2)}) %collective-permute-start.7) | collective-permute-done | bytes 524320 | tf_op jit(solution)/shard_map/ppermute | solution.py:58
  117.7 4.8 %collective-permute-start.8 = (bf16[4,64,256]{2,1,0:T(8,128)(2,1)S(1)}, bf16[4,64,256]{2,1,0:T(8,128)(2,1)S(1)}, u32[]{:S(2)}, u32[]{:S(2)}) collective-permute-start(bf16[4,64,256]{2,1,0:T(8,128)(2,1)S(1)} %get-tuple-element.25), channel_id=1, source_target_pairs={{0,192},{12,204},{24,216},{36,228},{48,240},{60,252},{72,264},{84,... | collective-permute-start | bytes 393224 | tf_op jit(solution)/shard_map/ppermute | solution.py:58
  122.6 1.9 %collective-permute-start.10 = (bf16[4,64,256]{2,1,0:T(8,128)(2,1)S(1)}, bf16[4,64,256]{2,1,0:T(8,128)(2,1)S(1)}, u32[]{:S(2)}, u32[]{:S(2)}) collective-permute-start(bf16[4,64,256]{2,1,0:T(8,128)(2,1)S(1)} %get-tuple-element.26), channel_id=1, source_target_pairs={{0,576},{12,588},{24,600},{36,612},{48,624},{60,636},{72,648},{84,... | collective-permute-start | bytes 393224 | tf_op jit(solution)/shard_map/ppermute | solution.py:58
  124.5 3.4 %collective-permute-start.9 = (bf16[4,64,256]{2,1,0:T(8,128)(2,1)S(1)}, bf16[4,64,256]{2,1,0:T(8,128)(2,1)S(1)}, u32[]{:S(2)}, u32[]{:S(2)}) collective-permute-start(bf16[4,64,256]{2,1,0:T(8,128)(2,1)S(1)} %get-tuple-element.27), channel_id=1, source_target_pairs={{0,384},{12,396},{24,408},{36,420},{48,432},{60,444},{72,456},{84,... | collective-permute-start | bytes 393224 | tf_op jit(solution)/shard_map/ppermute | solution.py:58
  128.1 6.5 %collective-permute-done.10 = bf16[4,64,256]{2,1,0:T(8,128)(2,1)S(1)} collective-permute-done((bf16[4,64,256]{2,1,0:T(8,128)(2,1)S(1)}, bf16[4,64,256]{2,1,0:T(8,128)(2,1)S(1)}, u32[]{:S(2)}, u32[]{:S(2)}) %collective-permute-start.10) | collective-permute-done | bytes 131104 | tf_op jit(solution)/shard_map/ppermute | solution.py:58
  134.7 1.9 %collective-permute-start.11 = (bf16[64,256]{1,0:T(8,128)(2,1)S(1)}, bf16[64,256]{1,0:T(8,128)(2,1)S(1)}, u32[]{:S(2)}, u32[]{:S(2)}) collective-permute-start(bf16[64,256]{1,0:T(8,128)(2,1)S(1)} %get-tuple-element.28), channel_id=1, source_target_pairs={{0,48},{12,60},{24,72},{36,84},{48,96},{60,108},{72,120},{84,132},... | collective-permute-start | bytes 98312 | tf_op jit(solution)/shard_map/ppermute | solution.py:58
  136.6 6.0 %collective-permute-start.13 = (bf16[64,256]{1,0:T(8,128)(2,1)S(1)}, bf16[64,256]{1,0:T(8,128)(2,1)S(1)}, u32[]{:S(2)}, u32[]{:S(2)}) collective-permute-start(bf16[64,256]{1,0:T(8,128)(2,1)S(1)} %get-tuple-element.29), channel_id=1, source_target_pairs={{0,144},{12,156},{24,168},{36,180},{48,0},{60,12},{72,24},{84,36},... | collective-permute-start | bytes 98312 | tf_op jit(solution)/shard_map/ppermute | solution.py:58
  142.6 5.0 %collective-permute-start.12 = (bf16[64,256]{1,0:T(8,128)(2,1)S(1)}, bf16[64,256]{1,0:T(8,128)(2,1)S(1)}, u32[]{:S(2)}, u32[]{:S(2)}) collective-permute-start(bf16[64,256]{1,0:T(8,128)(2,1)S(1)} %get-tuple-element.30), channel_id=1, source_target_pairs={{0,96},{12,108},{24,120},{36,132},{48,144},{60,156},{72,168},{84,1... | collective-permute-start | bytes 98312 | tf_op jit(solution)/shard_map/ppermute | solution.py:58
  149.9 0.7 copy.131
  150.6 1.7 %collective-permute-done.12 = bf16[64,256]{1,0:T(8,128)(2,1)S(1)} collective-permute-done((bf16[64,256]{1,0:T(8,128)(2,1)S(1)}, bf16[64,256]{1,0:T(8,128)(2,1)S(1)}, u32[]{:S(2)}, u32[]{:S(2)}) %collective-permute-start.12) | collective-permute-done | bytes 32800 | tf_op jit(solution)/shard_map/ppermute | solution.py:58
  (121 shorter events, 10.4 us)
Async XLA Ops:
  7.2 2.5 %copy-start = (bf16[384,4096]{1,0:T(8,128)(2,1)S(1)}, bf16[384,4096]{1,0:T(8,128)(2,1)}, u32[]{:S(2)}) copy-start(bf16[384,4096]{1,0:T(8,128)(2,1)} %param.9) | copy-start | bytes 9437188
  7.2 145.8 %reduce-scatter.2.cloned.1.call-start = ((), (), s32[]{:S(2)}) async-start(), calls=%async_computation.1 | async-start | bytes 3407872 | tf_op jit(solution)/shard_map/reduce_scatter | solution.py:169
  9.7 2.6 %copy-start.27 = (bf16[384,256]{1,0:T(8,128)(2,1)S(1)}, bf16[384,256]{1,0:T(8,128)(2,1)}, u32[]{:S(2)}) copy-start(bf16[384,256]{1,0:T(8,128)(2,1)} %param.5) | copy-start | bytes 589828
  12.6 7.3 %copy-start.32 = (f32[128,128]{0,1:T(8,128)}, f32[128,128]{0,1:T(8,128)S(1)}, u32[]{:S(2)}) copy-start(f32[128,128]{0,1:T(8,128)S(1)} %fusion.66) | copy-start | bytes 196612
  12.8 7.0 %copy-start.33 = (f32[128,128]{0,1:T(8,128)}, f32[128,128]{0,1:T(8,128)S(1)}, u32[]{:S(2)}) copy-start(f32[128,128]{0,1:T(8,128)S(1)} %fusion.68) | copy-start | bytes 196612
  13.1 3.2 %collective-permute-start = (bf16[2,2,128,128]{3,2,1,0:T(8,128)(2,1)S(1)}, bf16[2,2,128,128]{3,2,1,0:T(8,128)(2,1)S(1)}, u32[]{:S(2)}, u32[]{:S(2)}) collective-permute-start(bf16[2,2,128,128]{3,2,1,0:T(8,128)(2,1)S(1)} %fusion.24), channel_id=1, source_target_pairs={{0,12},{12,0},{24,36},{36,24},{48,60},{60,48},{72,84},{84,72},{96,... | collective-permute-start | bytes 393224 | tf_op jit(solution)/shard_map/ppermute | solution.py:18
  16.3 18.6 %copy-start.14 = (bf16[2,2,128,128]{3,2,1,0:T(8,128)(2,1)}, bf16[2,2,128,128]{3,2,1,0:T(8,128)(2,1)S(1)}, u32[]{:S(2)}) copy-start(bf16[2,2,128,128]{3,2,1,0:T(8,128)(2,1)S(1)} %collective-permute-done) | copy-start | bytes 393220
  16.3 7.4 %collective-permute-start.1 = (bf16[2,2,128,128]{3,2,1,0:T(8,128)(2,1)S(1)}, bf16[2,2,128,128]{3,2,1,0:T(8,128)(2,1)S(1)}, u32[]{:S(2)}, u32[]{:S(2)}) collective-permute-start(bf16[2,2,128,128]{3,2,1,0:T(8,128)(2,1)S(1)} %fusion.77), channel_id=1, source_target_pairs={{0,24},{24,0},{12,36},{36,12},{48,72},{72,48},{60,84},{84,60},{96,... | collective-permute-start | bytes 393224 | tf_op jit(solution)/shard_map/ppermute | solution.py:18
  23.8 11.1 %copy-start.34 = (bf16[2,2,128,128]{3,2,1,0:T(8,128)(2,1)}, bf16[2,2,128,128]{3,2,1,0:T(8,128)(2,1)S(1)}, u32[]{:S(2)}) copy-start(bf16[2,2,128,128]{3,2,1,0:T(8,128)(2,1)S(1)} %collective-permute-done.1) | copy-start | bytes 393220
  23.8 11.0 %copy-start.6 = (f32[2,2,128,128]{3,2,1,0:T(8,128)}, f32[2,2,128,128]{3,2,1,0:T(8,128)S(1)}, u32[]{:S(2)}) copy-start(f32[2,2,128,128]{3,2,1,0:T(8,128)S(1)} %get-tuple-element.24) | copy-start | bytes 786436
  23.9 10.3 %collective-permute-start.2 = (bf16[2,2,128,128]{3,2,1,0:T(8,128)(2,1)S(1)}, bf16[2,2,128,128]{3,2,1,0:T(8,128)(2,1)S(1)}, u32[]{:S(2)}, u32[]{:S(2)}) collective-permute-start(bf16[2,2,128,128]{3,2,1,0:T(8,128)(2,1)S(1)} %get-tuple-element.23), channel_id=1, source_target_pairs={{0,48},{48,0},{12,60},{60,12},{24,72},{72,24},{36,84},{84,36},{96,... | collective-permute-start | bytes 393224 | tf_op jit(solution)/shard_map/ppermute | solution.py:18
  34.2 8.4 %copy-start.12 = (bf16[2,2,128,128]{3,2,1,0:T(8,128)(2,1)}, bf16[2,2,128,128]{3,2,1,0:T(8,128)(2,1)S(1)}, u32[]{:S(2)}) copy-start(bf16[2,2,128,128]{3,2,1,0:T(8,128)(2,1)S(1)} %collective-permute-done.2) | copy-start | bytes 393220
  34.9 14.4 %collective-permute-start.3 = (bf16[2,2,128,128]{3,2,1,0:T(8,128)(2,1)}, bf16[2,2,128,128]{3,2,1,0:T(8,128)(2,1)}, u32[]{:S(2)}, u32[]{:S(2)}) collective-permute-start(bf16[2,2,128,128]{3,2,1,0:T(8,128)(2,1)} %fusion.82), channel_id=1, source_target_pairs={{0,96},{96,0},{12,108},{108,12},{24,120},{120,24},{36,132},{132,36... | collective-permute-start | bytes 393224 | tf_op jit(solution)/shard_map/ppermute | solution.py:18
  44.6 10.4 %copy-start.2 = (bf16[6,64,2,128]{3,2,1,0:T(2,128)(2,1)}, bf16[6,64,2,128]{3,2,1,0:T(2,128)(2,1)S(1)}, u32[]{:S(2)}) copy-start(bf16[6,64,2,128]{3,2,1,0:T(2,128)(2,1)S(1)} %reshape.66) | copy-start | bytes 589828
  51.0 7.2 %collective-permute-start.4 = (bf16[2,2,128,128]{3,2,1,0:T(8,128)(2,1)}, bf16[2,2,128,128]{3,2,1,0:T(8,128)(2,1)}, u32[]{:S(2)}, u32[]{:S(2)}) collective-permute-start(bf16[2,2,128,128]{3,2,1,0:T(8,128)(2,1)} %fusion.81), channel_id=1, source_target_pairs={{0,192},{192,0},{12,204},{204,12},{24,216},{216,24},{36,228},{228,... | collective-permute-start | bytes 393224 | tf_op jit(solution)/shard_map/ppermute | solution.py:18
  56.0 12.8 %copy-start.35 = (bf16[2,2,128,128]{3,2,1,0:T(8,128)(2,1)S(1)}, bf16[2,2,128,128]{3,2,1,0:T(8,128)(2,1)}, u32[]{:S(2)}) copy-start(bf16[2,2,128,128]{3,2,1,0:T(8,128)(2,1)} %copy-done.34) | copy-start | bytes 393220
  56.0 12.8 %copy-start.13 = (bf16[2,2,128,128]{3,2,1,0:T(8,128)(2,1)S(1)}, bf16[2,2,128,128]{3,2,1,0:T(8,128)(2,1)}, u32[]{:S(2)}) copy-start(bf16[2,2,128,128]{3,2,1,0:T(8,128)(2,1)} %copy-done.12) | copy-start | bytes 393220
  59.4 13.1 %copy-start.1 = (f32[6,2,128,128]{3,2,1,0:T(8,128)S(1)}, f32[6,2,128,128]{3,2,1,0:T(8,128)}, u32[]{:S(2)}) copy-start(f32[6,2,128,128]{3,2,1,0:T(8,128)} %fusion.51) | copy-start | bytes 2359300
  59.4 11.6 %collective-permute-start.5 = (bf16[2,2,128,128]{3,2,1,0:T(8,128)(2,1)S(1)}, bf16[2,2,128,128]{3,2,1,0:T(8,128)(2,1)S(1)}, u32[]{:S(2)}, u32[]{:S(2)}) collective-permute-start(bf16[2,2,128,128]{3,2,1,0:T(8,128)(2,1)S(1)} %add_convert_fusion), channel_id=1, source_target_pairs={{0,384},{384,0},{12,396},{396,12},{24,408},{408,24},{36,420},{420,... | collective-permute-start | bytes 393224 | tf_op jit(solution)/shard_map/ppermute | solution.py:18
  67.7 5.5 %copy-start.29 = (bf16[6,2,64,64]{3,2,1,0:T(8,128)(2,1)}, bf16[6,2,64,64]{3,2,1,0:T(8,128)(2,1)S(1)}, u32[]{:S(2)}) copy-start(bf16[6,2,64,64]{3,2,1,0:T(8,128)(2,1)S(1)} %fusion.14) | copy-start | bytes 294916
  68.8 2.3 %copy-start.15 = (f32[2,2,128,128]{3,2,1,0:T(8,128)}, f32[2,2,128,128]{3,2,1,0:T(8,128)S(1)}, u32[]{:S(2)}) copy-start(f32[2,2,128,128]{3,2,1,0:T(8,128)S(1)} %convert_element_type.147) | copy-start | bytes 786436
  68.8 2.2 %copy-start.17 = (f32[2,2,128,128]{3,2,1,0:T(8,128)}, f32[2,2,128,128]{3,2,1,0:T(8,128)S(1)}, u32[]{:S(2)}) copy-start(f32[2,2,128,128]{3,2,1,0:T(8,128)S(1)} %convert_element_type.149) | copy-start | bytes 786436
  68.8 2.2 %copy-start.19 = (f32[2,2,128,128]{3,2,1,0:T(8,128)}, f32[2,2,128,128]{3,2,1,0:T(8,128)S(1)}, u32[]{:S(2)}) copy-start(f32[2,2,128,128]{3,2,1,0:T(8,128)S(1)} %convert_element_type.151) | copy-start | bytes 786436
  69.9 1.1 copy-start.21
  72.5 0.9 copy-start.3
  72.7 0.9 copy-start.7
  72.7 1.1 copy-start.9
  72.7 1.9 %copy-start.11 = (bf16[4096,256]{1,0:T(8,128)(2,1)S(1)}, bf16[4096,256]{1,0:T(8,128)(2,1)}, u32[]{:S(2)}) copy-start(bf16[4096,256]{1,0:T(8,128)(2,1)} %param.8) | copy-start | bytes 6291460
  90.3 12.6 %collective-permute-start.6 = (f32[4,8,64,256]{3,2,1,0:T(8,128)}, f32[4,8,64,256]{3,2,1,0:T(8,128)}, u32[]{:S(2)}, u32[]{:S(2)}) collective-permute-start(f32[4,8,64,256]{3,2,1,0:T(8,128)} %dynamic-slice_bitcast_fusion), channel_id=1, source_target_pairs={{0,12},{12,0},{24,36},{36,24},{48,60},{60,48},{72,84},{84,72},{96,... | collective-permute-start | bytes 6291464 | tf_op jit(solution)/shard_map/ppermute | solution.py:72
  94.1 4.2 %copy-start.16 = (f32[2,2,128,128]{3,2,1,0:T(8,128)S(1)}, f32[2,2,128,128]{3,2,1,0:T(8,128)}, u32[]{:S(2)}) copy-start(f32[2,2,128,128]{3,2,1,0:T(8,128)} %copy-done.15) | copy-start | bytes 786436
  94.1 4.2 %copy-start.18 = (f32[2,2,128,128]{3,2,1,0:T(8,128)S(1)}, f32[2,2,128,128]{3,2,1,0:T(8,128)}, u32[]{:S(2)}) copy-start(f32[2,2,128,128]{3,2,1,0:T(8,128)} %copy-done.17) | copy-start | bytes 786436
  94.1 4.2 %copy-start.20 = (f32[2,2,128,128]{3,2,1,0:T(8,128)S(1)}, f32[2,2,128,128]{3,2,1,0:T(8,128)}, u32[]{:S(2)}) copy-start(f32[2,2,128,128]{3,2,1,0:T(8,128)} %copy-done.19) | copy-start | bytes 786436
  94.1 4.2 %copy-start.22 = (f32[2,2,128,128]{3,2,1,0:T(8,128)S(1)}, f32[2,2,128,128]{3,2,1,0:T(8,128)}, u32[]{:S(2)}) copy-start(f32[2,2,128,128]{3,2,1,0:T(8,128)} %copy-done.21) | copy-start | bytes 786436
  94.1 4.2 %copy-start.24 = (f32[2,2,128,128]{3,2,1,0:T(8,128)S(1)}, f32[2,2,128,128]{3,2,1,0:T(8,128)}, u32[]{:S(2)}) copy-start(f32[2,2,128,128]{3,2,1,0:T(8,128)} %copy-done.23) | copy-start | bytes 786436
  94.1 4.2 %copy-start.26 = (f32[2,2,128,128]{3,2,1,0:T(8,128)S(1)}, f32[2,2,128,128]{3,2,1,0:T(8,128)}, u32[]{:S(2)}) copy-start(f32[2,2,128,128]{3,2,1,0:T(8,128)} %copy-done.25) | copy-start | bytes 786436
  106.2 2.5 %copy-start.4 = (bf16[6,64,2,128]{3,2,1,0:T(2,128)(2,1)S(1)}, bf16[6,64,2,128]{3,2,1,0:T(2,128)(2,1)}, u32[]{:S(2)}) copy-start(bf16[6,64,2,128]{3,2,1,0:T(2,128)(2,1)} %copy-done.2) | copy-start | bytes 589828
  106.2 2.8 %copy-start.5 = (bf16[6,64,2,128]{3,2,1,0:T(2,128)(2,1)S(1)}, bf16[6,64,2,128]{3,2,1,0:T(2,128)(2,1)}, u32[]{:S(2)}) copy-start(bf16[6,64,2,128]{3,2,1,0:T(2,128)(2,1)} %reshape.68) | copy-start | bytes 589828
  106.2 2.8 %copy-start.10 = (bf16[6,2,128,128]{3,2,1,0:T(8,128)(2,1)S(1)}, bf16[6,2,128,128]{3,2,1,0:T(8,128)(2,1)}, u32[]{:S(2)}) copy-start(bf16[6,2,128,128]{3,2,1,0:T(8,128)(2,1)} %copy-done.9) | copy-start | bytes 1179652
  106.3 3.5 %copy-start.30 = (bf16[6,2,64,64]{3,2,1,0:T(8,128)(2,1)S(1)}, bf16[6,2,64,64]{3,2,1,0:T(8,128)(2,1)}, u32[]{:S(2)}) copy-start(bf16[6,2,64,64]{3,2,1,0:T(8,128)(2,1)} %copy-done.29) | copy-start | bytes 294916
  106.3 11.2 %collective-permute-start.7 = (bf16[4,4,64,256]{3,2,1,0:T(8,128)(2,1)S(1)}, bf16[4,4,64,256]{3,2,1,0:T(8,128)(2,1)S(1)}, u32[]{:S(2)}, u32[]{:S(2)}) collective-permute-start(bf16[4,4,64,256]{3,2,1,0:T(8,128)(2,1)S(1)} %fusion.20), channel_id=1, source_target_pairs={{0,24},{12,180},{24,0},{36,60},{48,72},{60,36},{72,48},{84,108},{9... | collective-permute-start | bytes 1572872 | tf_op jit(solution)/shard_map/ppermute | solution.py:58
  109.4 1.0 copy-start.8
  110.4 17.5 %copy-start.31 = (bf16[6,2,64,64]{3,2,1,0:T(8,128)(2,1)S(1)}, bf16[6,2,64,64]{3,2,1,0:T(8,128)(2,1)}, u32[]{:S(2)}) copy-start(bf16[6,2,64,64]{3,2,1,0:T(8,128)(2,1)} %fusion.13) | copy-start | bytes 294916
  117.7 10.3 %collective-permute-start.8 = (bf16[4,64,256]{2,1,0:T(8,128)(2,1)S(1)}, bf16[4,64,256]{2,1,0:T(8,128)(2,1)S(1)}, u32[]{:S(2)}, u32[]{:S(2)}) collective-permute-start(bf16[4,64,256]{2,1,0:T(8,128)(2,1)S(1)} %get-tuple-element.25), channel_id=1, source_target_pairs={{0,192},{12,204},{24,216},{36,228},{48,240},{60,252},{72,264},{84,... | collective-permute-start | bytes 393224 | tf_op jit(solution)/shard_map/ppermute | solution.py:58
  122.6 12.0 %collective-permute-start.10 = (bf16[4,64,256]{2,1,0:T(8,128)(2,1)S(1)}, bf16[4,64,256]{2,1,0:T(8,128)(2,1)S(1)}, u32[]{:S(2)}, u32[]{:S(2)}) collective-permute-start(bf16[4,64,256]{2,1,0:T(8,128)(2,1)S(1)} %get-tuple-element.26), channel_id=1, source_target_pairs={{0,576},{12,588},{24,600},{36,612},{48,624},{60,636},{72,648},{84,... | collective-permute-start | bytes 393224 | tf_op jit(solution)/shard_map/ppermute | solution.py:58
  124.5 10.1 %collective-permute-start.9 = (bf16[4,64,256]{2,1,0:T(8,128)(2,1)S(1)}, bf16[4,64,256]{2,1,0:T(8,128)(2,1)S(1)}, u32[]{:S(2)}, u32[]{:S(2)}) collective-permute-start(bf16[4,64,256]{2,1,0:T(8,128)(2,1)S(1)} %get-tuple-element.27), channel_id=1, source_target_pairs={{0,384},{12,396},{24,408},{36,420},{48,432},{60,444},{72,456},{84,... | collective-permute-start | bytes 393224 | tf_op jit(solution)/shard_map/ppermute | solution.py:58
  134.7 16.0 %collective-permute-start.11 = (bf16[64,256]{1,0:T(8,128)(2,1)S(1)}, bf16[64,256]{1,0:T(8,128)(2,1)S(1)}, u32[]{:S(2)}, u32[]{:S(2)}) collective-permute-start(bf16[64,256]{1,0:T(8,128)(2,1)S(1)} %get-tuple-element.28), channel_id=1, source_target_pairs={{0,48},{12,60},{24,72},{36,84},{48,96},{60,108},{72,120},{84,132},... | collective-permute-start | bytes 98312 | tf_op jit(solution)/shard_map/ppermute | solution.py:58
  136.6 14.0 %collective-permute-start.13 = (bf16[64,256]{1,0:T(8,128)(2,1)S(1)}, bf16[64,256]{1,0:T(8,128)(2,1)S(1)}, u32[]{:S(2)}, u32[]{:S(2)}) collective-permute-start(bf16[64,256]{1,0:T(8,128)(2,1)S(1)} %get-tuple-element.29), channel_id=1, source_target_pairs={{0,144},{12,156},{24,168},{36,180},{48,0},{60,12},{72,24},{84,36},... | collective-permute-start | bytes 98312 | tf_op jit(solution)/shard_map/ppermute | solution.py:58
  142.6 9.7 %collective-permute-start.12 = (bf16[64,256]{1,0:T(8,128)(2,1)S(1)}, bf16[64,256]{1,0:T(8,128)(2,1)S(1)}, u32[]{:S(2)}, u32[]{:S(2)}) collective-permute-start(bf16[64,256]{1,0:T(8,128)(2,1)S(1)} %get-tuple-element.30), channel_id=1, source_target_pairs={{0,96},{12,108},{24,120},{36,132},{48,144},{60,156},{72,168},{84,1... | collective-permute-start | bytes 98312 | tf_op jit(solution)/shard_map/ppermute | solution.py:58
  (3 other events, 2.1 us)
Sparse Core Ops, SparseCore 0:
  77.4 65.1 reduce-scatter.1
